TPU v7x, 128 devices: a whole 4x4x4 slice. The times are simulated.
128 devices in a mesh: sub: 8 (over z, core), rng: 16 (over y, x).
Axes of the slice: x: 4, y: 4, z: 4, core: 2. Of those that a mesh axis runs over, the one named last changes fastest.
Arguments:
- echoes: bfloat16 [2, 4096, 8192], P(None, 'sub', 'rng'), may hold values from -6 to 6
- chirp: bfloat16 [2, 512], replicated, may hold values from -0.1875 to 0.1875
- offsets: int32 [3, 8, 2, 512], P(None, 'sub'), may hold values from 0 to 504
- weights: bfloat16 [3, 8, 2, 2, 512, 8], P(None, 'sub'), may hold values from -1 to 1
- owners: int32 [8, 16, 512, 1], P('sub', 'rng'), may hold values from 0 to 127; in each aligned block of 512 rows (0 to 511, 512 to 1023, ..., all dimensions but the last counted through in order) at most 8 rows name the same one
- targets: int32 [8, 16, 512], P('sub', 'rng'), may hold values from 0 to 511
Outputs:
- tiles: bfloat16 [2, 4096, 8192], P(None, 'sub', 'rng')
Inputs may be any that keep to these rules, and one draw needn't show every extreme that they name: `owners`: within the 512 rows of one device, no tile is named more than 8 times, a bound that some block reaches.
All inputs are finite; a program needn't handle non-finite values.
Results may differ from a plain program's by a relative error of at most 0.0069.
Values may be sent and summed in bfloat16 or wider, within the bound.
No kernel may reach another device: no remote copies, remote signals or barrier semaphores. Data moves between devices by JAX's collectives and lax.ppermute only.
A program may use at most 384 MiB of HBM per device.

v0:
```python
import jax
import jax.numpy as jnp
from jax import lax
from jax.sharding import PartitionSpec as P

RBLK = 512


def shifted(value, axis, steps):
    count = lax.axis_size(axis)
    first, last = (max(0, -steps), min(count, count - steps))
    return lax.ppermute(value, axis, [(source, source + steps) for source in range(first, last)])


def from_partner(value, axis, apart):
    return lax.ppermute(value, axis, [(i, i ^ 1 << apart) for i in range(lax.axis_size(axis))])


def replica_matrix(chirp, block_len):
    taps_len = chirp.shape[1]
    width = block_len + taps_len
    parts = []
    for part in range(2):
        padded = jnp.concatenate([chirp[part], jnp.zeros((width + 1 - taps_len,), chirp.dtype)])
        tiled = jnp.tile(padded, block_len)[: block_len * width].reshape(block_len, width)
        parts.append(tiled.T)
    h_real, h_imag = (parts[0], parts[1])
    upper = jnp.concatenate([h_real, -h_imag], axis=1)
    lower = jnp.concatenate([h_imag, h_real], axis=1)
    return jnp.concatenate([upper, lower], axis=0)


def merge_matrix(starts, kernel):
    beams = starts.shape[0]
    taps_len = kernel.shape[-1]
    spots = starts[:, None] + jnp.arange(taps_len, dtype=jnp.int32)[None, :]
    hit = (spots[:, :, None] == jnp.arange(beams, dtype=jnp.int32)[None, None, :]).astype(
        jnp.float32
    )
    g_real = jnp.einsum("bk,bks->bs", kernel[0].astype(jnp.float32), hit).astype(jnp.bfloat16)
    g_imag = jnp.einsum("bk,bks->bs", kernel[1].astype(jnp.float32), hit).astype(jnp.bfloat16)
    upper = jnp.concatenate([g_real, -g_imag], axis=1)
    lower = jnp.concatenate([g_imag, g_real], axis=1)
    return jnp.concatenate([upper, lower], axis=0)


def group_slots(dest, devices):
    onehot = (dest[:, None] == jnp.arange(devices, dtype=jnp.int32)[None, :]).astype(jnp.int32)
    return jnp.sum((jnp.cumsum(onehot, axis=0) - 1) * onehot, axis=1)


def route_rows(send, labels):
    got, marks = (
        lax.all_to_all(send, ("sub", "rng"), split_axis=0, concat_axis=0, tiled=True),
        lax.all_to_all(labels, ("sub", "rng"), split_axis=0, concat_axis=0, tiled=True),
    )
    return (got, marks)


def on_device(echoes, chirp, offsets, weights, owners, targets):
    p_dev = echoes.shape[1]
    r_dev = echoes.shape[2]
    n_sub = lax.axis_size("sub")
    n_rng = lax.axis_size("rng")
    devices = n_sub * n_rng
    capacity = max(2, 2 * p_dev // devices)
    tail = shifted(echoes, "rng", -1)
    extended = jnp.concatenate([echoes, tail], axis=2)
    matrix = replica_matrix(chirp, RBLK)
    stacked = jnp.concatenate([extended[0], extended[1]], axis=1)
    block_out = jnp.dot(stacked, matrix, preferred_element_type=jnp.float32).astype(jnp.bfloat16)
    pieces = block_out.reshape(p_dev, 2, RBLK)
    image = pieces.transpose(1, 0, 2).reshape(2 * p_dev, r_dev)
    section_count = offsets.shape[0]
    for section in range(section_count):
        partner = from_partner(image, "sub", section)
        mine = merge_matrix(offsets[section, 0, 0], weights[section, 0, 0])
        theirs = merge_matrix(offsets[section, 0, 1], weights[section, 0, 1])
        merged = jnp.dot(mine, image, preferred_element_type=jnp.float32)
        merged = merged + jnp.dot(theirs, partner, preferred_element_type=jnp.float32)
        image = merged.astype(jnp.bfloat16)
    rows = image.reshape(2, p_dev, r_dev).transpose(1, 0, 2).reshape(p_dev, 2 * r_dev)
    dest = owners.reshape(p_dev)
    aim = targets.reshape(p_dev)
    slot = dest * capacity + group_slots(dest, devices)
    pick = jnp.arange(devices * capacity, dtype=jnp.int32)[:, None] == slot[None, :]
    send = jnp.dot(pick.astype(jnp.bfloat16), rows, preferred_element_type=jnp.float32).astype(
        jnp.bfloat16
    )
    labels = jnp.sum(jnp.where(pick, aim[None, :] + 1, 0), axis=1) - 1
    got, marks = route_rows(
        send.reshape(devices, capacity, 2 * r_dev), labels.reshape(devices, capacity)
    )
    got_flat = got.reshape(devices * capacity, 2 * r_dev)
    mark_flat = marks.reshape(devices * capacity)
    place = (jnp.arange(p_dev, dtype=jnp.int32)[:, None] == mark_flat[None, :]).astype(jnp.bfloat16)
    tile = jnp.dot(place, got_flat, preferred_element_type=jnp.float32).astype(jnp.bfloat16)
    return tile.reshape(p_dev, 2, r_dev).transpose(1, 0, 2)


def solution(mesh):
    in_specs = (
        P(None, "sub", "rng"),
        P(),
        P(None, "sub", None, None),
        P(None, "sub", None, None, None, None),
        P("sub", "rng", None, None),
        P("sub", "rng", None),
    )
    out_specs = P(None, "sub", "rng")
    return jax.shard_map(
        on_device, mesh=mesh, in_specs=in_specs, out_specs=out_specs, check_vma=False
    )
```

profile of v0, /device:TPU:1, one launch (start us, length us, event | category | flops | bytes accessed | tf_op | source)
XLA Modules:
  0.0 172.9 jit_solution(7693703797565982493)
XLA Ops:
  0.0 1.3 collective-permute-start
  2.4 0.9 fusion.102
  5.7 13.9 %all-to-all-start = ((s32[128,1,8]{2,1,0:T(1,128)}), s32[128,1,8]{2,1,0:T(1,128)}, u32[]{:S(2)}, u32[]{:S(2)}) async-start(s32[128,1,8]{2,1,0:T(1,128)} %bitcast.6), calls=%async_computation | async-start | bytes 131072 | tf_op jit(solution)/shard_map/all_to_all | solution.py:55
  19.6 1.3 slice_reduce_fusion
  21.1 1.3 tile.21
  23.0 1.0 bitcast_negate_fusion
  25.6 2.2 %fusion.6 = bf16[512,1,512]{2,1,0:T(2,128)(2,1)S(1)} fusion(bf16[512,8,1]{1,2,0:T(2,128)(2,1)S(1)} %copy.36, s32[512,8]{1,0:T(8,128)S(1)} %iota_add_fusion.3), kind=kOutput, calls=%fused_computation.10 | convolution fusion | flops 6291456 | bytes 548864 | tf_op jit(solution)/shard_map/bk,bks->bs/dot_general | solution.py:41
  27.9 1.1 fusion.118
  29.3 2.2 %fusion.4 = bf16[512,1,512]{2,1,0:T(2,128)(2,1)S(1)} fusion(bf16[512,8,1]{1,2,0:T(2,128)(2,1)S(1)} %copy.40, s32[512,8]{1,0:T(8,128)S(1)} %iota_add_fusion.2), kind=kOutput, calls=%fused_computation.7 | convolution fusion | flops 6291456 | bytes 548864 | tf_op jit(solution)/shard_map/bk,bks->bs/dot_general | solution.py:41
  31.5 1.1 fusion.117
  32.9 2.2 %fusion.8 = bf16[512,1,512]{2,1,0:T(2,128)(2,1)S(1)} fusion(bf16[512,8,1]{1,2,0:T(2,128)(2,1)S(1)} %copy.32, s32[512,8]{1,0:T(8,128)S(1)} %iota_add_fusion.4), kind=kOutput, calls=%fused_computation.13 | convolution fusion | flops 6291456 | bytes 548864 | tf_op jit(solution)/shard_map/bk,bks->bs/dot_general | solution.py:41
  35.2 1.1 fusion.116
  36.6 2.2 %fusion.2 = bf16[512,1,512]{2,1,0:T(2,128)(2,1)S(1)} fusion(bf16[512,8,1]{1,2,0:T(2,128)(2,1)S(1)} %copy.44, s32[512,8]{1,0:T(8,128)S(1)} %iota_add_fusion.1), kind=kOutput, calls=%fused_computation.4 | convolution fusion | flops 6291456 | bytes 548864 | tf_op jit(solution)/shard_map/bk,bks->bs/dot_general | solution.py:41
  38.9 1.0 fusion.115
  40.0 1.3 tile.9
  41.5 1.3 reshape.256
  43.1 0.9 copy.30
  44.1 2.2 %fusion.7 = bf16[512,1,512]{2,1,0:T(2,128)(2,1)S(1)} fusion(bf16[512,8,1]{1,2,0:T(2,128)(2,1)S(1)} %copy.34, s32[512,8]{1,0:T(8,128)S(1)} %copy-done.14), kind=kOutput, calls=%fused_computation.11 | convolution fusion | flops 6291456 | bytes 548864 | tf_op jit(solution)/shard_map/bk,bks->bs/dot_general | solution.py:40
  46.4 2.2 %fusion.5 = bf16[512,1,512]{2,1,0:T(2,128)(2,1)S(1)} fusion(bf16[512,8,1]{1,2,0:T(2,128)(2,1)S(1)} %copy.38, s32[512,8]{1,0:T(8,128)S(1)} %copy-done.16), kind=kOutput, calls=%fused_computation.8 | convolution fusion | flops 6291456 | bytes 548864 | tf_op jit(solution)/shard_map/bk,bks->bs/dot_general | solution.py:40
  48.7 2.4 %fusion.9 = bf16[512,1,512]{2,1,0:T(2,128)(2,1)S(1)} fusion(bf16[512,8,1]{1,2,0:T(2,128)(2,1)S(1)} %copy-done.21, s32[512,8]{1,0:T(8,128)S(1)} %copy-done.20), kind=kOutput, calls=%fused_computation.14 | convolution fusion | flops 6291456 | bytes 548864 | tf_op jit(solution)/shard_map/bk,bks->bs/dot_general | solution.py:40
  51.1 1.4 constant_dynamic-update-slice_fusion
  52.7 1.0 copy-done.1
  54.1 2.4 %fusion.92 = bf16[512,1024]{1,0:T(8,128)(2,1)S(1)} fusion(bf16[1024,512]{0,1:T(8,128)(2,1)S(1)} %bitcast.154, bf16[1024,512]{0,1:T(8,128)(2,1)S(1)} %bitcast.153, bf16[1024,512]{0,1:T(8,128)(2,1)S(1)} %copy-done.1, bf16[512,1024]{1,0:T(8,128)(2,1)S(1)} %get-tuple-element.20, bf16[512,1024]{1,0:T(8,128)(2,1)S(1)} %get-tuple-element.19), kind=kOutput, calls=%fused_computation.99 | convolution fusion | flops 2168979456 | bytes 6291456 | tf_op jit(solution)/shard_map/dot_general | solution.py:71
  56.6 1.2 collective-permute-start.1
  57.8 0.9 iota_add_fusion.5
  58.7 0.9 copy.77
  59.6 0.9 copy.76
  60.7 0.9 copy.26
  61.6 2.2 %fusion.3 = bf16[512,1,512]{2,1,0:T(2,128)(2,1)S(1)} fusion(bf16[512,8,1]{1,2,0:T(2,128)(2,1)S(1)} %copy.42, s32[512,8]{1,0:T(8,128)S(1)} %iota_add_fusion.1), kind=kOutput, calls=%fused_computation.5 | convolution fusion | flops 6291456 | bytes 548864 | tf_op jit(solution)/shard_map/bk,bks->bs/dot_general | solution.py:40
  63.8 2.2 %fusion.11 = bf16[512,1,512]{2,1,0:T(2,128)(2,1)S(1)} fusion(bf16[512,8,1]{1,2,0:T(2,128)(2,1)S(1)} %copy-done.22, s32[512,8]{1,0:T(8,128)S(1)} %copy-done.17), kind=kOutput, calls=%fused_computation.17 | convolution fusion | flops 6291456 | bytes 548864 | tf_op jit(solution)/shard_map/bk,bks->bs/dot_general | solution.py:40
  66.2 1.2 fusion.48
  67.5 3.4 %add_convert_fusion.2 = bf16[1024,512]{1,0:T(8,128)(2,1)} fusion(f32[1024,512]{1,0:T(8,128)S(1)} %fusion.48, bf16[1024,512]{1,0:T(8,128)(2,1)} %collective-permute-done.1, bf16[512,512]{1,0:T(8,128)(2,1)S(1)} %bitcast.162, bf16[512,512]{1,0:T(8,128)(2,1)S(1)} %copy-done.12, bf16[512,512]{1,0:T(8,128)(2,1)S(1)} %copy-done.11), kind=kOutput, calls=%fused_computation.94 | convolution fusion | flops 1083179008 | bytes 5767168 | tf_op jit(solution)/shard_map/dot_general | solution.py:80
  72.5 2.2 %fusion.10 = bf16[512,1,512]{2,1,0:T(2,128)(2,1)S(1)} fusion(bf16[512,8,1]{1,2,0:T(2,128)(2,1)S(1)} %copy.28, s32[512,8]{1,0:T(8,128)S(1)} %copy-done.18), kind=kOutput, calls=%fused_computation.16 | convolution fusion | flops 6291456 | bytes 548864 | tf_op jit(solution)/shard_map/bk,bks->bs/dot_general | solution.py:41
  74.8 2.2 %fusion.1 = bf16[512,1,512]{2,1,0:T(2,128)(2,1)S(1)} fusion(bf16[512,8,1]{1,2,0:T(2,128)(2,1)S(1)} %copy.46, s32[512,8]{1,0:T(8,128)S(1)} %iota_add_fusion), kind=kOutput, calls=%fused_computation.2 | convolution fusion | flops 6291456 | bytes 548864 | tf_op jit(solution)/shard_map/bk,bks->bs/dot_general | solution.py:40
  77.1 2.6 %fusion.40 = f32[1024,512]{1,0:T(8,128)S(1)} fusion(bf16[1024,512]{1,0:T(8,128)(2,1)} %add_convert_fusion.2, bf16[512,512]{1,0:T(8,128)(2,1)S(1)} %bitcast.167, bf16[512,512]{1,0:T(8,128)(2,1)S(1)} %copy-done.6, bf16[512,512]{1,0:T(8,128)(2,1)S(1)} %copy-done.5), kind=kOutput, calls=%fused_computation.46 | convolution fusion | flops 1082130432 | bytes 4718592 | tf_op jit(solution)/shard_map/dot_general | solution.py:79
  79.6 15.9 %collective-permute-done.2 = bf16[1024,512]{1,0:T(8,128)(2,1)} collective-permute-done((bf16[1024,512]{1,0:T(8,128)(2,1)}, bf16[1024,512]{1,0:T(8,128)(2,1)}, u32[]{:S(2)}, u32[]{:S(2)}) %collective-permute-start.2) | collective-permute-done | bytes 1048608 | tf_op jit(solution)/shard_map/ppermute | solution.py:16
  95.5 3.4 %add_convert_fusion.1 = bf16[1024,512]{1,0:T(8,128)(2,1)} fusion(f32[1024,512]{1,0:T(8,128)S(1)} %fusion.40, bf16[1024,512]{1,0:T(8,128)(2,1)} %collective-permute-done.2, bf16[512,512]{1,0:T(8,128)(2,1)S(1)} %bitcast.163, bf16[512,512]{1,0:T(8,128)(2,1)S(1)} %copy-done.8, bf16[512,512]{1,0:T(8,128)(2,1)S(1)} %copy-done.7), kind=kOutput, calls=%fused_computation.93 | convolution fusion | flops 1083179008 | bytes 5767168 | tf_op jit(solution)/shard_map/dot_general | solution.py:80
  98.9 2.7 %collective-permute-start.3 = (bf16[1024,512]{1,0:T(8,128)(2,1)}, bf16[1024,512]{1,0:T(8,128)(2,1)}, u32[]{:S(2)}, u32[]{:S(2)}) collective-permute-start(bf16[1024,512]{1,0:T(8,128)(2,1)} %add_convert_fusion.1), channel_id=1, source_target_pairs={{0,64},{16,80},{32,96},{48,112},{64,0},{80,16},{96,32},{112,48},{1... | collective-permute-start | bytes 3145736 | tf_op jit(solution)/shard_map/ppermute | solution.py:16
  102.1 2.5 %fusion = bf16[512,1,512]{2,1,0:T(2,128)(2,1)S(1)} fusion(bf16[512,8,1]{1,2,0:T(2,128)(2,1)S(1)} %copy.48, s32[512,8]{1,0:T(8,128)S(1)} %iota_add_fusion), kind=kOutput, calls=%fused_computation.1 | convolution fusion | flops 6291456 | bytes 548864 | tf_op jit(solution)/shard_map/bk,bks->bs/dot_general | solution.py:41
  104.7 2.5 %fusion.32 = f32[1024,512]{1,0:T(8,128)S(1)} fusion(bf16[1024,512]{1,0:T(8,128)(2,1)} %add_convert_fusion.1, bf16[512,512]{1,0:T(8,128)(2,1)S(1)} %bitcast.165, bf16[512,512]{1,0:T(8,128)(2,1)S(1)} %get-tuple-element.10, bf16[512,512]{1,0:T(8,128)(2,1)S(1)} %get-tuple-element.9), kind=kOutput, calls=%fused_computation.38 | convolution fusion | flops 1082130432 | bytes 4718592 | tf_op jit(solution)/shard_map/dot_general | solution.py:79
  107.2 17.0 %collective-permute-done.3 = bf16[1024,512]{1,0:T(8,128)(2,1)} collective-permute-done((bf16[1024,512]{1,0:T(8,128)(2,1)}, bf16[1024,512]{1,0:T(8,128)(2,1)}, u32[]{:S(2)}, u32[]{:S(2)}) %collective-permute-start.3) | collective-permute-done | bytes 1048608 | tf_op jit(solution)/shard_map/ppermute | solution.py:16
  124.2 2.5 %add_convert_fusion = bf16[1024,512]{1,0:T(8,128)(2,1)S(1)} fusion(f32[1024,512]{1,0:T(8,128)S(1)} %fusion.32, bf16[1024,512]{1,0:T(8,128)(2,1)} %collective-permute-done.3, bf16[512,512]{1,0:T(8,128)(2,1)S(1)} %bitcast.164, bf16[512,512]{1,0:T(8,128)(2,1)S(1)} %get-tuple-element.8, bf16[512,512]{1,0:T(8,128)(2,1)S(1)} %get-tuple-element.7), kind=kOutput, calls=%fused_computation.92 | convolution fusion | flops 1083179008 | bytes 5767168 | tf_op jit(solution)/shard_map/dot_general | solution.py:80
  127.3 2.6 %convert_bitcast_fusion = bf16[128,8,1024]{2,1,0:T(8,128)(2,1)} fusion(bf16[512,1024]{0,1:T(8,128)(2,1)S(1)} %bitcast.160, s32[512]{0:T(512)S(1)} %copy-done.34), kind=kOutput, calls=%fused_computation.91 | convolution fusion | flops 1075314688 | bytes 3147776 | tf_op jit(solution)/shard_map/dot_general | solution.py:87
  129.9 11.0 %all-to-all-start.1 = ((bf16[128,8,1024]{2,1,0:T(8,128)(2,1)}), bf16[128,8,1024]{2,1,0:T(8,128)(2,1)S(1)}, u32[]{:S(2)}, u32[]{:S(2)}) async-start(bf16[128,8,1024]{2,1,0:T(8,128)(2,1)} %convert_bitcast_fusion), calls=%async_computation.1 | async-start | bytes 4194304 | tf_op jit(solution)/shard_map/all_to_all | solution.py:54
  141.5 1.6 reduce.7
  143.2 27.4 %all-to-all-done.1 = bf16[128,8,1024]{2,1,0:T(8,128)(2,1)S(1)} async-done(((bf16[128,8,1024]{2,1,0:T(8,128)(2,1)}), bf16[128,8,1024]{2,1,0:T(8,128)(2,1)S(1)}, u32[]{:S(2)}, u32[]{:S(2)}) %all-to-all-start.1) | async-done | bytes 2097184 | tf_op jit(solution)/shard_map/all_to_all | solution.py:54
  170.6 1.3 fusion.97
  171.9 1.0 copy.72
  (123 shorter events, 11.4 us)
Async XLA Ops:
  0.0 51.1 %collective-permute-start = (bf16[2,512,512]{2,1,0:T(8,128)(2,1)}, bf16[2,512,512]{2,1,0:T(8,128)(2,1)}, u32[]{:S(2)}, u32[]{:S(2)}) collective-permute-start(bf16[2,512,512]{2,1,0:T(8,128)(2,1)} %param.6), channel_id=1, source_target_pairs={{1,0},{2,1},{3,2},{4,3},{5,4},{6,5},{7,6},{8,7},{9,8},{10,9},{11,1... | collective-permute-start | bytes 3145736 | tf_op jit(solution)/shard_map/ppermute | solution.py:12
  4.0 0.7 copy-start.33
  5.7 124.2 %all-to-all-start = ((s32[128,1,8]{2,1,0:T(1,128)}), s32[128,1,8]{2,1,0:T(1,128)}, u32[]{:S(2)}, u32[]{:S(2)}) async-start(s32[128,1,8]{2,1,0:T(1,128)} %bitcast.6), calls=%async_computation | async-start | bytes 131072 | tf_op jit(solution)/shard_map/all_to_all | solution.py:55
  22.5 1.6 copy-start.23
  22.5 2.2 %copy-start.31 = (s32[3,1,2,512]{3,2,1,0:T(2,128)S(1)}, s32[3,1,2,512]{3,2,1,0:T(2,128)}, u32[]{:S(2)}) copy-start(s32[3,1,2,512]{3,2,1,0:T(2,128)} %param.8) | copy-start | bytes 36868
  25.4 2.4 %copy-start.13 = (s32[512,8]{1,0:T(8,128)}, s32[512,8]{1,0:T(8,128)S(1)}, u32[]{:S(2)}) copy-start(s32[512,8]{1,0:T(8,128)S(1)} %iota_add_fusion.3) | copy-start | bytes 49156
  29.1 2.4 %copy-start.15 = (s32[512,8]{1,0:T(8,128)}, s32[512,8]{1,0:T(8,128)S(1)}, u32[]{:S(2)}) copy-start(s32[512,8]{1,0:T(8,128)S(1)} %iota_add_fusion.2) | copy-start | bytes 49156
  32.8 2.4 %copy-start.19 = (s32[512,8]{1,0:T(8,128)}, s32[512,8]{1,0:T(8,128)S(1)}, u32[]{:S(2)}) copy-start(s32[512,8]{1,0:T(8,128)S(1)} %iota_add_fusion.4) | copy-start | bytes 49156
  38.8 1.1 copy-start.35
  41.4 1.3 copy-start.30
  41.4 1.5 copy-start.29
  41.4 1.7 copy-start.28
  41.5 2.5 %copy-start = (bf16[2,512,512]{2,1,0:T(8,128)(2,1)S(1)}, bf16[2,512,512]{2,1,0:T(8,128)(2,1)}, u32[]{:S(2)}) copy-start(bf16[2,512,512]{2,1,0:T(8,128)(2,1)} %param.6) | copy-start | bytes 3145732
  42.7 1.4 copy-start.14
  44.1 2.3 %copy-start.16 = (s32[512,8]{1,0:T(8,128)S(1)}, s32[512,8]{1,0:T(8,128)}, u32[]{:S(2)}) copy-start(s32[512,8]{1,0:T(8,128)} %copy-done.15) | copy-start | bytes 49156
  46.4 2.3 %copy-start.20 = (s32[512,8]{1,0:T(8,128)S(1)}, s32[512,8]{1,0:T(8,128)}, u32[]{:S(2)}) copy-start(s32[512,8]{1,0:T(8,128)} %copy-done.19) | copy-start | bytes 49156
  46.4 2.3 %copy-start.21 = (bf16[512,8,1]{1,2,0:T(2,128)(2,1)S(1)}, bf16[512,8,1]{1,2,0:T(2,128)(2,1)}, u32[]{:S(2)}) copy-start(bf16[512,8,1]{1,2,0:T(2,128)(2,1)} %copy.30) | copy-start | bytes 24580
  52.5 1.2 copy-start.1
  52.5 1.5 copy-start.2
  56.5 1.3 copy-start.32
  56.5 4.0 %copy-start.27 = (bf16[512,8,1]{0,1,2:T(8,128)(2,1)S(1)}, bf16[512,8,1]{0,1,2:T(8,128)(2,1)}, u32[]{:S(2)}) copy-start(bf16[512,8,1]{0,1,2:T(8,128)(2,1)} %get-tuple-element.23) | copy-start | bytes 24580
  56.6 4.1 %copy-start.26 = (bf16[512,8,1]{0,1,2:T(8,128)(2,1)S(1)}, bf16[512,8,1]{0,1,2:T(8,128)(2,1)}, u32[]{:S(2)}) copy-start(bf16[512,8,1]{0,1,2:T(8,128)(2,1)} %get-tuple-element.31) | copy-start | bytes 24580
  56.6 10.8 %collective-permute-start.1 = (bf16[1024,512]{1,0:T(8,128)(2,1)S(1)}, bf16[1024,512]{1,0:T(8,128)(2,1)}, u32[]{:S(2)}, u32[]{:S(2)}) collective-permute-start(bf16[1024,512]{1,0:T(8,128)(2,1)S(1)} %bitcast.155), channel_id=1, source_target_pairs={{0,16},{16,0},{32,48},{48,32},{64,80},{80,64},{96,112},{112,96},{1... | collective-permute-start | bytes 3145736 | tf_op jit(solution)/shard_map/ppermute | solution.py:16
  61.6 2.2 %copy-start.17 = (s32[512,8]{1,0:T(8,128)S(1)}, s32[512,8]{1,0:T(8,128)}, u32[]{:S(2)}) copy-start(s32[512,8]{1,0:T(8,128)} %iota_add_fusion.5) | copy-start | bytes 49156
  61.6 2.2 %copy-start.22 = (bf16[512,8,1]{1,2,0:T(2,128)(2,1)S(1)}, bf16[512,8,1]{1,2,0:T(2,128)(2,1)}, u32[]{:S(2)}) copy-start(bf16[512,8,1]{1,2,0:T(2,128)(2,1)} %copy.26) | copy-start | bytes 24580
  63.8 2.3 %copy-start.4 = (bf16[512,1,512]{2,0,1:T(8,128)(2,1)S(1)}, bf16[512,1,512]{2,0,1:T(8,128)(2,1)}, u32[]{:S(2)}) copy-start(bf16[512,1,512]{2,0,1:T(8,128)(2,1)} %copy.77) | copy-start | bytes 1572868
  63.8 2.3 %copy-start.9 = (bf16[512,512]{1,0:T(8,128)(2,1)S(1)}, bf16[512,512]{1,0:T(8,128)(2,1)}, u32[]{:S(2)}) copy-start(bf16[512,512]{1,0:T(8,128)(2,1)} %get-tuple-element.17) | copy-start | bytes 1572868
  63.8 2.3 %copy-start.10 = (bf16[512,512]{1,0:T(8,128)(2,1)S(1)}, bf16[512,512]{1,0:T(8,128)(2,1)}, u32[]{:S(2)}) copy-start(bf16[512,512]{1,0:T(8,128)(2,1)} %get-tuple-element.18) | copy-start | bytes 1572868
  66.1 1.3 copy-start.3
  66.1 1.3 copy-start.11
  66.2 1.3 copy-start.12
  70.9 1.2 copy-start.25
  70.9 1.4 copy-start.24
  70.9 1.6 copy-start.18
  70.9 24.6 %collective-permute-start.2 = (bf16[1024,512]{1,0:T(8,128)(2,1)}, bf16[1024,512]{1,0:T(8,128)(2,1)}, u32[]{:S(2)}, u32[]{:S(2)}) collective-permute-start(bf16[1024,512]{1,0:T(8,128)(2,1)} %add_convert_fusion.2), channel_id=1, source_target_pairs={{0,32},{16,48},{32,0},{48,16},{64,96},{80,112},{96,64},{112,80},{1... | collective-permute-start | bytes 3145736 | tf_op jit(solution)/shard_map/ppermute | solution.py:16
  74.8 2.3 %copy-start.5 = (bf16[512,512]{1,0:T(8,128)(2,1)S(1)}, bf16[512,512]{1,0:T(8,128)(2,1)}, u32[]{:S(2)}) copy-start(bf16[512,512]{1,0:T(8,128)(2,1)} %get-tuple-element.13) | copy-start | bytes 1572868
  74.8 2.3 %copy-start.6 = (bf16[512,512]{1,0:T(8,128)(2,1)S(1)}, bf16[512,512]{1,0:T(8,128)(2,1)}, u32[]{:S(2)}) copy-start(bf16[512,512]{1,0:T(8,128)(2,1)} %get-tuple-element.14) | copy-start | bytes 1572868
  77.1 18.4 %copy-start.7 = (bf16[512,512]{1,0:T(8,128)(2,1)S(1)}, bf16[512,512]{1,0:T(8,128)(2,1)}, u32[]{:S(2)}) copy-start(bf16[512,512]{1,0:T(8,128)(2,1)} %get-tuple-element.11) | copy-start | bytes 1572868
  77.1 18.4 %copy-start.8 = (bf16[512,512]{1,0:T(8,128)(2,1)S(1)}, bf16[512,512]{1,0:T(8,128)(2,1)}, u32[]{:S(2)}) copy-start(bf16[512,512]{1,0:T(8,128)(2,1)} %get-tuple-element.12) | copy-start | bytes 1572868
  98.9 25.2 %collective-permute-start.3 = (bf16[1024,512]{1,0:T(8,128)(2,1)}, bf16[1024,512]{1,0:T(8,128)(2,1)}, u32[]{:S(2)}, u32[]{:S(2)}) collective-permute-start(bf16[1024,512]{1,0:T(8,128)(2,1)} %add_convert_fusion.1), channel_id=1, source_target_pairs={{0,64},{16,80},{32,96},{48,112},{64,0},{80,16},{96,32},{112,48},{1... | collective-permute-start | bytes 3145736 | tf_op jit(solution)/shard_map/ppermute | solution.py:16
  126.6 0.7 copy-start.34
  129.9 40.7 %all-to-all-start.1 = ((bf16[128,8,1024]{2,1,0:T(8,128)(2,1)}), bf16[128,8,1024]{2,1,0:T(8,128)(2,1)S(1)}, u32[]{:S(2)}, u32[]{:S(2)}) async-start(bf16[128,8,1024]{2,1,0:T(8,128)(2,1)} %convert_bitcast_fusion), calls=%async_computation.1 | async-start | bytes 4194304 | tf_op jit(solution)/shard_map/all_to_all | solution.py:54
where the time goes:
time: 174 us; the launch traced here: 173 us
  waiting for transfers between devices  60.3 us (35%)
  matrix products  49.2 us (28%)
  starting transfers between devices  30.9 us (18%)
  local copies, waits for them, and re-layouts  20.1 us (12%)
  other arithmetic  11.6 us (7%)
    ppermute x3, waiting for transfers between devices, from_partner(): lax.ppermute(value, axis, [(i, i ^ 1 << apart) for i in range(lax.axis_si...  32.9 us
    all_to_all x1, waiting for transfers between devices, route_rows(): lax.all_to_all(send, ('sub', 'rng'), split_axis=0, concat_axis=0, tiled=T...  27.4 us
    all_to_all x1, starting transfers between devices, route_rows(): lax.all_to_all(labels, ('sub', 'rng'), split_axis=0, concat_axis=0, tiled...  13.9 us
    dot_general x6, matrix products, merge_matrix(): jnp.einsum('bk,bks->bs', kernel[1].astype(jnp.float32), hit)  13.7 us
    dot_general x6, matrix products, merge_matrix(): jnp.einsum('bk,bks->bs', kernel[0].astype(jnp.float32), hit)  13.6 us
    all_to_all x1, starting transfers between devices, route_rows(): lax.all_to_all(send, ('sub', 'rng'), split_axis=0, concat_axis=0, tiled=T...  11 us
    dot_general x3, matrix products, on_device(): jnp.dot(theirs, partner, preferred_element_type=jnp.float32)  9.34 us
    dot_general x3, matrix products, on_device(): merged = jnp.dot(mine, image, preferred_element_type=jnp.float32)  6.26 us
  transfers between devices with their start and end apart: 6, of which 3 were waited for; matrix products, arithmetic and copies ran while one was open for 44% of the time, Pallas kernels for 0%

commit v1 on v0

--- a/solution.py
+++ b/solution.py
@@ -33,12 +33,13 @@
 def merge_matrix(starts, kernel):
     beams = starts.shape[0]
     taps_len = kernel.shape[-1]
-    spots = starts[:, None] + jnp.arange(taps_len, dtype=jnp.int32)[None, :]
-    hit = (spots[:, :, None] == jnp.arange(beams, dtype=jnp.int32)[None, None, :]).astype(
-        jnp.float32
-    )
-    g_real = jnp.einsum("bk,bks->bs", kernel[0].astype(jnp.float32), hit).astype(jnp.bfloat16)
-    g_imag = jnp.einsum("bk,bks->bs", kernel[1].astype(jnp.float32), hit).astype(jnp.bfloat16)
+    shift = jnp.arange(beams, dtype=jnp.int32)[None, :] - starts[:, None]
+    g_real = jnp.zeros((beams, beams), kernel.dtype)
+    g_imag = jnp.zeros((beams, beams), kernel.dtype)
+    for tap in range(taps_len):
+        hit = shift == tap
+        g_real = jnp.where(hit, kernel[0][:, tap : tap + 1], g_real)
+        g_imag = jnp.where(hit, kernel[1][:, tap : tap + 1], g_imag)
     upper = jnp.concatenate([g_real, -g_imag], axis=1)
     lower = jnp.concatenate([g_imag, g_real], axis=1)
     return jnp.concatenate([upper, lower], axis=0)
@@ -50,10 +51,10 @@
 
 
 def route_rows(send, labels):
-    got, marks = (
-        lax.all_to_all(send, ("sub", "rng"), split_axis=0, concat_axis=0, tiled=True),
-        lax.all_to_all(labels, ("sub", "rng"), split_axis=0, concat_axis=0, tiled=True),
-    )
+    got = lax.all_to_all(send, ("sub", "rng"), split_axis=0, concat_axis=0, tiled=True)
+    table = lax.all_gather(labels.astype(jnp.float32), ("sub", "rng"), axis=0)
+    me = lax.axis_index("sub") * lax.axis_size("rng") + lax.axis_index("rng")
+    marks = lax.dynamic_index_in_dim(table, me, axis=1, keepdims=False).astype(jnp.int32)
     return (got, marks)
 
 

time: 174 us -> 185 us (1.063)
  blocking collectives: 0 us -> 71.8 us
  matrix products: 49.2 us -> 13.8 us
  waiting for transfers between devices: 60.3 us -> 44.2 us
  starting transfers between devices: 30.9 us -> 21.4 us
  other arithmetic: 11.6 us -> 14.5 us
    all_gather x0 -> x1, blocking collectives: none -> 71.8 us  [route_rows(): table = lax.all_gather(labels.astype(jnp.float32), ('sub', 'rng'), axis=0)]
    all_to_all x1, waiting for transfers between devices: 27.4 us -> 0.01 us  [route_rows(): lax.all_to_all(send, ('sub', 'rng'), split_axis=0, concat_axis=0, tiled=T...]
    dot_general x12 -> x0, matrix products: 27.3 us -> none  [the longest x6 13.7 us: merge_matrix(): jnp.einsum('bk,bks->bs', kernel[1].astype(jnp.float32), hit)]
    all_to_all x1 -> x0, starting transfers between devices: 13.9 us -> none  [route_rows(): lax.all_to_all(labels, ('sub', 'rng'), split_axis=0, concat_axis=0, tiled...]
    neg x6, other arithmetic: 4.48 us -> 11.2 us  [merge_matrix(): upper = jnp.concatenate([g_real, -g_imag], axis=1)]
    ppermute x3, waiting for transfers between devices: 32.9 us -> 39.4 us  [from_partner(): lax.ppermute(value, axis, [(i, i ^ 1 << apart) for i in range(lax.axis_si...]
    dot_general x3, matrix products: 9.34 us -> 3.73 us  [on_device(): jnp.dot(theirs, partner, preferred_element_type=jnp.float32)]
    ppermute x1, waiting for transfers between devices: 0.01 us -> 4.76 us  [shifted(): lax.ppermute(value, axis, [(source, source + steps) for source in range(f...]
  transfers between devices with their start and end apart: 6 -> 5, of which waited for: 3 -> 3; matrix products, arithmetic and copies ran while one was open for 44% -> 16% of each run, Pallas kernels for 0% -> 0%
where the time goes in v1:
time: 185 us
  blocking collectives  71.8 us (39%)
  waiting for transfers between devices  44.2 us (24%)
  starting transfers between devices  21.4 us (12%)
  local copies, waits for them, and re-layouts  18.8 us (10%)
  other arithmetic  14.5 us (8%)
  matrix products  13.8 us (7%)
    all_gather x1, blocking collectives, route_rows(): table = lax.all_gather(labels.astype(jnp.float32), ('sub', 'rng'), axis=0)  71.8 us
    ppermute x3, waiting for transfers between devices, from_partner(): lax.ppermute(value, axis, [(i, i ^ 1 << apart) for i in range(lax.axis_si...  39.4 us
    all_to_all x1, starting transfers between devices, route_rows(): lax.all_to_all(send, ('sub', 'rng'), split_axis=0, concat_axis=0, tiled=T...  12.9 us
    neg x6, other arithmetic, merge_matrix(): upper = jnp.concatenate([g_real, -g_imag], axis=1)  11.2 us
    ppermute x3, starting transfers between devices, from_partner(): lax.ppermute(value, axis, [(i, i ^ 1 << apart) for i in range(lax.axis_si...  7.09 us
    another operation x4, local copies, waits for them, and re-layouts, replica_matrix(): jnp.tile(padded, block_len)[:block_len * width].reshape(block_len, width)  4.78 us
    ppermute x1, waiting for transfers between devices, shifted(): lax.ppermute(value, axis, [(source, source + steps) for source in range(f...  4.76 us
    dot_general x3, matrix products, on_device(): jnp.dot(theirs, partner, preferred_element_type=jnp.float32)  3.73 us
  transfers between devices with their start and end apart: 5, of which 3 were waited for; matrix products, arithmetic and copies ran while one was open for 16% of the time, Pallas kernels for 0%

profile of v1, /device:TPU:1, one launch (start us, length us, event | category | flops | bytes accessed | tf_op | source)
XLA Modules:
  0.0 184.9 jit_solution(3944139202757502713)
XLA Ops:
  0.0 1.4 collective-permute-start
  1.4 1.4 constant_dynamic-update-slice_fusion.1
  2.9 2.3 %tile.9 = bf16[524800]{0:T(1024)(128)(2,1)} reshape(bf16[512,1025]{1,0:T(8,128)(2,1)S(1)} %tile.8) | data formatting | bytes 2099200 | tf_op jit(solution)/shard_map/tile | solution.py:25
  5.2 1.2 slice-done
  6.5 1.3 reshape.124
  7.8 2.3 %tile.21 = bf16[524800]{0:T(1024)(128)(2,1)} reshape(bf16[512,1025]{1,0:T(8,128)(2,1)S(1)} %tile.20) | data formatting | bytes 2099200 | tf_op jit(solution)/shard_map/tile | solution.py:25
  10.1 1.2 slice-done.1
  11.4 1.3 reshape.125
  12.6 0.6 slice_bitcast_fusion.2
  13.2 0.6 fusion.239
  13.9 0.1 copy.20
  14.0 0.2 fusion.223
  14.3 1.3 slice_reduce_fusion.55
  15.7 0.1 slice_reduce_fusion.39
  15.8 0.1 slice_reduce_fusion.71
  15.9 2.6 %fusion.235 = (bf16[512,512]{1,0:T(8,128)(2,1)S(1)}, bf16[512,512]{1,0:T(8,128)(2,1)S(1)}, bf16[512,512]{1,0:T(8,128)(2,1)S(1)}) fusion(bf16[512]{0:T(512)(128)(2,1)S(1)} %get-tuple-element.86, bf16[512]{0:T(512)(128)(2,1)S(1)} %get-tuple-element.87, bf16[512]{0:T(512)(128)(2,1)S(1)} %get-tuple-element.88, bf16[512]{0:T(512)(128)(2,1)S(1)} %get-tuple-element.89, ...), kind=kLoop, calls=%fused_computation.362 | loop fusion | flops 7340032 | bytes 1591296 | tf_op jit(solution)/shard_map/neg | solution.py:43
  18.5 1.7 fusion.236
  20.3 1.7 fusion.234
  22.1 4.8 %collective-permute-done = bf16[2,512,512]{2,1,0:T(8,128)(2,1)} collective-permute-done((bf16[2,512,512]{2,1,0:T(8,128)(2,1)}, bf16[2,512,512]{2,1,0:T(8,128)(2,1)}, u32[]{:S(2)}, u32[]{:S(2)}) %collective-permute-start) | collective-permute-done | bytes 1048608 | tf_op jit(solution)/shard_map/ppermute | solution.py:12
  26.8 1.4 constant_dynamic-update-slice_fusion
  28.2 0.2 slice_bitcast_fusion.1
  28.4 1.0 copy-done.1
  29.4 2.4 %fusion.68 = bf16[512,1024]{1,0:T(8,128)(2,1)S(1)} fusion(bf16[1024,512]{0,1:T(8,128)(2,1)S(1)} %bitcast.81, bf16[1024,512]{0,1:T(8,128)(2,1)S(1)} %bitcast.80, bf16[1024,512]{0,1:T(8,128)(2,1)S(1)} %bitcast_negate_fusion, bf16[512,1024]{1,0:T(8,128)(2,1)S(1)} %get-tuple-element.104, bf16[512,1024]{1,0:T(8,128)(2,1)S(1)} %get-tuple-element.103), kind=kOutput, calls=%fused_computation.69 | convolution fusion | flops 2168979456 | bytes 6291456 | tf_op jit(solution)/shard_map/dot_general | solution.py:72
  31.9 1.7 collective-permute-start.1
  33.7 0.1 slice_reduce_fusion.23
  33.8 0.1 slice_reduce_fusion.87
  33.9 1.7 fusion.237
  35.6 1.2 fusion.24
  36.9 1.2 add_convert_fusion.2
  38.2 2.1 %collective-permute-start.2 = (bf16[1024,512]{1,0:T(8,128)(2,1)S(1)}, bf16[1024,512]{1,0:T(8,128)(2,1)S(1)}, u32[]{:S(2)}, u32[]{:S(2)}) collective-permute-start(bf16[1024,512]{1,0:T(8,128)(2,1)S(1)} %add_convert_fusion.2), channel_id=1, source_target_pairs={{0,32},{16,48},{32,0},{48,16},{64,96},{80,112},{96,64},{112,80},{1... | collective-permute-start | bytes 3145736 | tf_op jit(solution)/shard_map/ppermute | solution.py:16
  40.4 0.2 fusion.222
  40.6 1.7 fusion.233
  42.4 1.2 fusion.16
  43.6 20.0 %collective-permute-done.2 = bf16[1024,512]{1,0:T(8,128)(2,1)S(1)} collective-permute-done((bf16[1024,512]{1,0:T(8,128)(2,1)S(1)}, bf16[1024,512]{1,0:T(8,128)(2,1)S(1)}, u32[]{:S(2)}, u32[]{:S(2)}) %collective-permute-start.2) | collective-permute-done | bytes 1048608 | tf_op jit(solution)/shard_map/ppermute | solution.py:16
  63.6 1.2 add_convert_fusion.1
  64.8 3.2 %collective-permute-start.3 = (bf16[1024,512]{1,0:T(8,128)(2,1)S(1)}, bf16[1024,512]{1,0:T(8,128)(2,1)S(1)}, u32[]{:S(2)}, u32[]{:S(2)}) collective-permute-start(bf16[1024,512]{1,0:T(8,128)(2,1)S(1)} %add_convert_fusion.1), channel_id=1, source_target_pairs={{0,64},{16,80},{32,96},{48,112},{64,0},{80,16},{96,32},{112,48},{1... | collective-permute-start | bytes 3145736 | tf_op jit(solution)/shard_map/ppermute | solution.py:16
  68.1 1.7 fusion.238
  69.8 1.2 fusion.8
  71.0 19.5 %collective-permute-done.3 = bf16[1024,512]{1,0:T(8,128)(2,1)S(1)} collective-permute-done((bf16[1024,512]{1,0:T(8,128)(2,1)S(1)}, bf16[1024,512]{1,0:T(8,128)(2,1)S(1)}, u32[]{:S(2)}, u32[]{:S(2)}) %collective-permute-start.3) | collective-permute-done | bytes 1048608 | tf_op jit(solution)/shard_map/ppermute | solution.py:16
  90.5 1.2 add_convert_fusion
  91.7 0.5 copy.24
  92.3 2.6 %convert_bitcast_fusion = bf16[128,8,1024]{2,1,0:T(8,128)(2,1)} fusion(bf16[512,1024]{0,1:T(8,128)(2,1)S(1)} %bitcast.88, s32[512]{0:T(512)S(1)} %multiply_add_fusion), kind=kOutput, calls=%fused_computation.61 | convolution fusion | flops 1075314688 | bytes 3147776 | tf_op jit(solution)/shard_map/dot_general | solution.py:88
  94.9 12.9 %all-to-all-start = ((bf16[128,8,1024]{2,1,0:T(8,128)(2,1)}), bf16[128,8,1024]{2,1,0:T(8,128)(2,1)S(1)}, u32[]{:S(2)}, u32[]{:S(2)}) async-start(bf16[128,8,1024]{2,1,0:T(8,128)(2,1)} %convert_bitcast_fusion), calls=%async_computation | async-start | bytes 4194304 | tf_op jit(solution)/shard_map/all_to_all | solution.py:54
  107.9 0.3 select_reduce_fusion
  108.3 71.8 %all_gather.4 = f32[128,128,8]{1,2,0:T(8,128)S(1)} all-gather(f32[1,128,8]{1,2,0:T(8,128)S(1)} %copy.22), channel_id=1, replica_groups=mesh['sub'=8,'rng'=16] {'sub','rng'}, dimensions={0}, use_global_device_ids=true | all-gather | bytes 528384 | tf_op jit(solution)/shard_map/all_gather | solution.py:55
  180.1 2.4 %convert_reduce_fusion = s32[128,8]{1,0:T(8,128)S(1)} fusion(f32[128,128,8]{1,2,0:T(8,128)S(1)} %all_gather.4, s32[]{:T(128)S(6)} %select_n.298), kind=kLoop, calls=%fused_computation.227 | loop fusion | flops 1024 | bytes 8196 | tf_op jit(solution)/shard_map/convert_element_type | solution.py:57
  182.6 1.3 fusion.73
  183.8 1.0 copy.30
  (48 shorter events, 0.9 us)
Async XLA Ops:
  0.0 2.8 %copy-start.11 = (bf16[2,512]{1,0:T(2,128)(2,1)S(1)}, bf16[2,512]{1,0:T(2,128)(2,1)}, u32[]{:S(2)}) copy-start(bf16[2,512]{1,0:T(2,128)(2,1)} %param.7) | copy-start | bytes 6148
  0.0 26.8 %collective-permute-start = (bf16[2,512,512]{2,1,0:T(8,128)(2,1)}, bf16[2,512,512]{2,1,0:T(8,128)(2,1)}, u32[]{:S(2)}, u32[]{:S(2)}) collective-permute-start(bf16[2,512,512]{2,1,0:T(8,128)(2,1)} %param.6), channel_id=1, source_target_pairs={{1,0},{2,1},{3,2},{4,3},{5,4},{6,5},{7,6},{8,7},{9,8},{10,9},{11,1... | collective-permute-start | bytes 3145736 | tf_op jit(solution)/shard_map/ppermute | solution.py:12
  5.2 1.2 slice-start
  10.1 1.2 slice-start.1
  10.1 2.5 %copy-start.2 = (bf16[3,1,2,2,512,8]{4,5,3,2,1,0:T(8,128)(2,1)S(1)}, bf16[3,1,2,2,512,8]{4,5,3,2,1,0:T(8,128)(2,1)}, u32[]{:S(2)}) copy-start(bf16[3,1,2,2,512,8]{4,5,3,2,1,0:T(8,128)(2,1)} %param.9) | copy-start | bytes 294916
  10.1 3.1 %copy-start.5 = (s32[3,1,2,512]{3,2,1,0:T(2,128)S(1)}, s32[3,1,2,512]{3,2,1,0:T(2,128)}, u32[]{:S(2)}) copy-start(s32[3,1,2,512]{3,2,1,0:T(2,128)} %param.8) | copy-start | bytes 36868
  10.1 3.7 %copy-start.3 = (s32[1,1,512,1]{2,3,1,0:T(1,128)S(1)}, s32[1,1,512,1]{2,3,1,0:T(1,128)}, u32[]{:S(2)}) copy-start(s32[1,1,512,1]{2,3,1,0:T(1,128)} %param.10) | copy-start | bytes 6148
  12.6 5.8 %copy-start = (bf16[512,1024]{1,0:T(8,128)(2,1)S(1)}, bf16[512,1024]{1,0:T(8,128)(2,1)}, u32[]{:S(2)}) copy-start(bf16[512,1024]{1,0:T(8,128)(2,1)} %reshape.125) | copy-start | bytes 3145732
  14.3 4.2 %copy-start.10 = (s32[1,1,1,512]{3,2,1,0:T(1,128)S(1)}, s32[1,1,1,512]{3,2,1,0:T(1,128)}, u32[]{:S(2)}) copy-start(s32[1,1,1,512]{3,2,1,0:T(1,128)} %get-tuple-element.118) | copy-start | bytes 6148
  18.4 1.9 %copy-start.9 = (s32[1,1,1,512]{3,2,1,0:T(1,128)S(1)}, s32[1,1,1,512]{3,2,1,0:T(1,128)}, u32[]{:S(2)}) copy-start(s32[1,1,1,512]{3,2,1,0:T(1,128)} %get-tuple-element.120) | copy-start | bytes 6148
  28.2 1.2 copy-start.1
  31.8 2.0 %copy-start.8 = (s32[1,1,1,512]{3,2,1,0:T(1,128)S(1)}, s32[1,1,1,512]{3,2,1,0:T(1,128)}, u32[]{:S(2)}) copy-start(s32[1,1,1,512]{3,2,1,0:T(1,128)} %get-tuple-element.122) | copy-start | bytes 6148
  31.9 4.9 %collective-permute-start.1 = (bf16[1024,512]{1,0:T(8,128)(2,1)S(1)}, bf16[1024,512]{1,0:T(8,128)(2,1)S(1)}, u32[]{:S(2)}, u32[]{:S(2)}) collective-permute-start(bf16[1024,512]{1,0:T(8,128)(2,1)S(1)} %bitcast.82), channel_id=1, source_target_pairs={{0,16},{16,0},{32,48},{48,32},{64,80},{80,64},{96,112},{112,96},{1... | collective-permute-start | bytes 3145736 | tf_op jit(solution)/shard_map/ppermute | solution.py:16
  36.9 3.5 %copy-start.4 = (s32[1,1,512,1]{2,3,1,0:T(1,128)S(1)}, s32[1,1,512,1]{2,3,1,0:T(1,128)}, u32[]{:S(2)}) copy-start(s32[1,1,512,1]{2,3,1,0:T(1,128)} %param.10) | copy-start | bytes 6148
  36.9 3.7 %copy-start.7 = (s32[1,1,1,512]{3,2,1,0:T(1,128)S(1)}, s32[1,1,1,512]{3,2,1,0:T(1,128)}, u32[]{:S(2)}) copy-start(s32[1,1,1,512]{3,2,1,0:T(1,128)} %get-tuple-element.121) | copy-start | bytes 6148
  38.2 25.4 %collective-permute-start.2 = (bf16[1024,512]{1,0:T(8,128)(2,1)S(1)}, bf16[1024,512]{1,0:T(8,128)(2,1)S(1)}, u32[]{:S(2)}, u32[]{:S(2)}) collective-permute-start(bf16[1024,512]{1,0:T(8,128)(2,1)S(1)} %add_convert_fusion.2), channel_id=1, source_target_pairs={{0,32},{16,48},{32,0},{48,16},{64,96},{80,112},{96,64},{112,80},{1... | collective-permute-start | bytes 3145736 | tf_op jit(solution)/shard_map/ppermute | solution.py:16
  63.6 4.5 %copy-start.6 = (s32[1,1,1,512]{3,2,1,0:T(1,128)S(1)}, s32[1,1,1,512]{3,2,1,0:T(1,128)}, u32[]{:S(2)}) copy-start(s32[1,1,1,512]{3,2,1,0:T(1,128)} %get-tuple-element.117) | copy-start | bytes 6148
  64.8 25.6 %collective-permute-start.3 = (bf16[1024,512]{1,0:T(8,128)(2,1)S(1)}, bf16[1024,512]{1,0:T(8,128)(2,1)S(1)}, u32[]{:S(2)}, u32[]{:S(2)}) collective-permute-start(bf16[1024,512]{1,0:T(8,128)(2,1)S(1)} %add_convert_fusion.1), channel_id=1, source_target_pairs={{0,64},{16,80},{32,96},{48,112},{64,0},{80,16},{96,32},{112,48},{1... | collective-permute-start | bytes 3145736 | tf_op jit(solution)/shard_map/ppermute | solution.py:16
  94.9 12.9 %copy-start.12 = (s32[1,1,512]{2,1,0:T(1,128)S(1)}, s32[1,1,512]{2,1,0:T(1,128)}, u32[]{:S(2)}) copy-start(s32[1,1,512]{2,1,0:T(1,128)} %param.11) | copy-start | bytes 6148
  94.9 87.6 %all-to-all-start = ((bf16[128,8,1024]{2,1,0:T(8,128)(2,1)}), bf16[128,8,1024]{2,1,0:T(8,128)(2,1)S(1)}, u32[]{:S(2)}, u32[]{:S(2)}) async-start(bf16[128,8,1024]{2,1,0:T(8,128)(2,1)} %convert_bitcast_fusion), calls=%async_computation | async-start | bytes 4194304 | tf_op jit(solution)/shard_map/all_to_all | solution.py:54

commit v2 on v1

--- a/solution.py
+++ b/solution.py
@@ -50,12 +50,13 @@
     return jnp.sum((jnp.cumsum(onehot, axis=0) - 1) * onehot, axis=1)
 
 
-def route_rows(send, labels):
-    got = lax.all_to_all(send, ("sub", "rng"), split_axis=0, concat_axis=0, tiled=True)
-    table = lax.all_gather(labels.astype(jnp.float32), ("sub", "rng"), axis=0)
-    me = lax.axis_index("sub") * lax.axis_size("rng") + lax.axis_index("rng")
-    marks = lax.dynamic_index_in_dim(table, me, axis=1, keepdims=False).astype(jnp.int32)
-    return (got, marks)
+def route_rows(send):
+    n_sub = lax.axis_size("sub")
+    n_rng = lax.axis_size("rng")
+    grid = send.reshape((n_sub, n_rng) + send.shape[1:])
+    grid = lax.all_to_all(grid, "rng", split_axis=1, concat_axis=1, tiled=True)
+    grid = lax.all_to_all(grid, "sub", split_axis=0, concat_axis=0, tiled=True)
+    return grid.reshape(send.shape)
 
 
 def on_device(echoes, chirp, offsets, weights, owners, targets):
@@ -85,17 +86,21 @@
     aim = targets.reshape(p_dev)
     slot = dest * capacity + group_slots(dest, devices)
     pick = jnp.arange(devices * capacity, dtype=jnp.int32)[:, None] == slot[None, :]
+    code = aim + 1
+    lanes = jnp.arange(128, dtype=jnp.int32)[None, :]
+    extra = jnp.where(lanes == 0, (code // 32)[:, None], jnp.where(lanes == 1, (code % 32)[:, None], 0))
+    rows = jnp.concatenate([rows, extra.astype(jnp.bfloat16)], axis=1)
     send = jnp.dot(pick.astype(jnp.bfloat16), rows, preferred_element_type=jnp.float32).astype(
         jnp.bfloat16
     )
-    labels = jnp.sum(jnp.where(pick, aim[None, :] + 1, 0), axis=1) - 1
-    got, marks = route_rows(
-        send.reshape(devices, capacity, 2 * r_dev), labels.reshape(devices, capacity)
-    )
-    got_flat = got.reshape(devices * capacity, 2 * r_dev)
-    mark_flat = marks.reshape(devices * capacity)
+    width = 2 * r_dev
+    got = route_rows(send.reshape(devices, capacity, width + 128))
+    got_flat = got.reshape(devices * capacity, width + 128)
+    head = got_flat[:, width].astype(jnp.int32)
+    low = got_flat[:, width + 1].astype(jnp.int32)
+    mark_flat = head * 32 + low - 1
     place = (jnp.arange(p_dev, dtype=jnp.int32)[:, None] == mark_flat[None, :]).astype(jnp.bfloat16)
-    tile = jnp.dot(place, got_flat, preferred_element_type=jnp.float32).astype(jnp.bfloat16)
+    tile = jnp.dot(place, got_flat[:, :width], preferred_element_type=jnp.float32).astype(jnp.bfloat16)
     return tile.reshape(p_dev, 2, r_dev).transpose(1, 0, 2)
 
 

time: 185 us -> 173 us (0.935)
  starting transfers between devices: 21.4 us -> 8.55 us
  blocking collectives: 71.8 us -> 74.6 us
  other arithmetic: 14.5 us -> 12.1 us
  local copies, waits for them, and re-layouts: 18.8 us -> 20.7 us
    all_to_all x0 -> x2, blocking collectives: none -> 74.6 us  [the longest x1 37.6 us: route_rows(): grid = lax.all_to_all(grid, 'rng', split_axis=1, concat_axis=1, tiled=True)]
    all_gather x1 -> x0, blocking collectives: 71.8 us -> none  [route_rows(): table = lax.all_gather(labels.astype(jnp.float32), ('sub', 'rng'), axis=0)]
    all_to_all x1 -> x0, starting transfers between devices: 12.9 us -> none  [route_rows(): lax.all_to_all(send, ('sub', 'rng'), split_axis=0, concat_axis=0, tiled=T...]
    convert_element_type x2 -> x1, other arithmetic: 2.4 us -> 0.2 us  [on_device(): rows = jnp.concatenate([rows, extra.astype(jnp.bfloat16)], axis=1)]
  transfers between devices with their start and end apart: 5 -> 4, of which waited for: 3 -> 3; matrix products, arithmetic and copies ran while one was open for 16% -> 16% of each run, Pallas kernels for 0% -> 0%
where the time goes in v2:
time: 173 us; the launch traced here: 172 us
  blocking collectives  74.6 us (43%)
  waiting for transfers between devices  43.2 us (25%)
  local copies, waits for them, and re-layouts  20.7 us (12%)
  matrix products  12.7 us (7%)
  other arithmetic  12.1 us (7%)
  starting transfers between devices  8.55 us (5%)
    ppermute x3, waiting for transfers between devices, from_partner(): lax.ppermute(value, axis, [(i, i ^ 1 << apart) for i in range(lax.axis_si...  39.4 us
    all_to_all x1, blocking collectives, route_rows(): grid = lax.all_to_all(grid, 'rng', split_axis=1, concat_axis=1, tiled=True)  37.6 us
    all_to_all x1, blocking collectives, route_rows(): grid = lax.all_to_all(grid, 'sub', split_axis=0, concat_axis=0, tiled=True)  37 us
    neg x6, other arithmetic, merge_matrix(): upper = jnp.concatenate([g_real, -g_imag], axis=1)  11.2 us
    ppermute x3, starting transfers between devices, from_partner(): lax.ppermute(value, axis, [(i, i ^ 1 << apart) for i in range(lax.axis_si...  7.14 us
    another operation x4, local copies, waits for them, and re-layouts, replica_matrix(): jnp.tile(padded, block_len)[:block_len * width].reshape(block_len, width)  4.78 us
    ppermute x1, waiting for transfers between devices, shifted(): lax.ppermute(value, axis, [(source, source + steps) for source in range(f...  3.8 us
    dot_general x3, matrix products, on_device(): merged = jnp.dot(mine, image, preferred_element_type=jnp.float32)  3.73 us
  transfers between devices with their start and end apart: 4, of which 3 were waited for; matrix products, arithmetic and copies ran while one was open for 16% of the time, Pallas kernels for 0%

profile of v2, /device:TPU:1, one launch (start us, length us, event | category | flops | bytes accessed | tf_op | source)
XLA Modules:
  0.0 172.3 jit_solution(13645770832901817952)
XLA Ops:
  0.0 1.4 collective-permute-start
  1.4 1.4 constant_dynamic-update-slice_fusion.1
  2.9 0.2 select_convert_fusion
  3.1 0.8 copy.34
  4.0 2.3 %tile.9 = bf16[524800]{0:T(1024)(128)(2,1)} reshape(bf16[512,1025]{1,0:T(8,128)(2,1)S(1)} %tile.8) | data formatting | bytes 2099200 | tf_op jit(solution)/shard_map/tile | solution.py:25
  6.3 1.2 slice-done
  7.5 1.3 reshape.152
  8.9 2.3 %tile.21 = bf16[524800]{0:T(1024)(128)(2,1)} reshape(bf16[512,1025]{1,0:T(8,128)(2,1)S(1)} %tile.20) | data formatting | bytes 2099200 | tf_op jit(solution)/shard_map/tile | solution.py:25
  11.2 1.2 slice-done.1
  12.4 1.3 reshape.153
  13.7 0.6 slice_bitcast_fusion.2
  14.3 0.6 fusion.244
  15.0 0.2 fusion.225
  15.4 1.3 slice_reduce_fusion.55
  16.8 2.6 %fusion.239 = (bf16[512,512]{1,0:T(8,128)(2,1)S(1)}, bf16[512,512]{1,0:T(8,128)(2,1)S(1)}, bf16[512,512]{1,0:T(8,128)(2,1)S(1)}) fusion(bf16[512]{0:T(512)(128)(2,1)S(1)} %get-tuple-element.86, bf16[512]{0:T(512)(128)(2,1)S(1)} %get-tuple-element.87, bf16[512]{0:T(512)(128)(2,1)S(1)} %get-tuple-element.88, bf16[512]{0:T(512)(128)(2,1)S(1)} %get-tuple-element.89, ...), kind=kLoop, calls=%fused_computation.374 | loop fusion | flops 7340032 | bytes 1591296 | tf_op jit(solution)/shard_map/neg | solution.py:43
  19.5 1.7 %fusion.240 = (bf16[512,512]{1,0:T(8,128)(2,1)S(1)}, bf16[512,512]{1,0:T(8,128)(2,1)S(1)}, bf16[512,512]{1,0:T(8,128)(2,1)S(1)}) fusion(bf16[512]{0:T(512)(128)(2,1)S(1)} %get-tuple-element.70, bf16[512]{0:T(512)(128)(2,1)S(1)} %get-tuple-element.71, bf16[512]{0:T(512)(128)(2,1)S(1)} %get-tuple-element.72, bf16[512]{0:T(512)(128)(2,1)S(1)} %get-tuple-element.73, ...), kind=kLoop, calls=%fused_computation.375 | loop fusion | flops 7340032 | bytes 1591296 | tf_op jit(solution)/shard_map/neg | solution.py:43
  21.3 1.7 %fusion.238 = (bf16[512,512]{1,0:T(8,128)(2,1)S(1)}, bf16[512,512]{1,0:T(8,128)(2,1)S(1)}, bf16[512,512]{1,0:T(8,128)(2,1)S(1)}) fusion(bf16[512]{0:T(512)(128)(2,1)S(1)} %get-tuple-element.54, bf16[512]{0:T(512)(128)(2,1)S(1)} %get-tuple-element.55, bf16[512]{0:T(512)(128)(2,1)S(1)} %get-tuple-element.56, bf16[512]{0:T(512)(128)(2,1)S(1)} %get-tuple-element.57, ...), kind=kLoop, calls=%fused_computation.373 | loop fusion | flops 7340032 | bytes 1591296 | tf_op jit(solution)/shard_map/neg | solution.py:43
  23.0 3.8 %collective-permute-done = bf16[2,512,512]{2,1,0:T(8,128)(2,1)} collective-permute-done((bf16[2,512,512]{2,1,0:T(8,128)(2,1)}, bf16[2,512,512]{2,1,0:T(8,128)(2,1)}, u32[]{:S(2)}, u32[]{:S(2)}) %collective-permute-start) | collective-permute-done | bytes 1048608 | tf_op jit(solution)/shard_map/ppermute | solution.py:12
  26.8 1.4 constant_dynamic-update-slice_fusion
  28.2 0.2 slice_bitcast_fusion.1
  28.4 1.0 copy-done.1
  29.4 2.4 %fusion.67 = bf16[512,1024]{1,0:T(8,128)(2,1)S(1)} fusion(bf16[1024,512]{0,1:T(8,128)(2,1)S(1)} %bitcast.79, bf16[1024,512]{0,1:T(8,128)(2,1)S(1)} %bitcast.75, bf16[1024,512]{0,1:T(8,128)(2,1)S(1)} %bitcast_negate_fusion, bf16[512,1024]{1,0:T(8,128)(2,1)S(1)} %get-tuple-element.106, bf16[512,1024]{1,0:T(8,128)(2,1)S(1)} %get-tuple-element.105), kind=kOutput, calls=%fused_computation.67 | convolution fusion | flops 2168979456 | bytes 6291456 | tf_op jit(solution)/shard_map/dot_general | solution.py:73
  31.9 1.7 %collective-permute-start.1 = (bf16[1024,512]{1,0:T(8,128)(2,1)S(1)}, bf16[1024,512]{1,0:T(8,128)(2,1)S(1)}, u32[]{:S(2)}, u32[]{:S(2)}) collective-permute-start(bf16[1024,512]{1,0:T(8,128)(2,1)S(1)} %bitcast.80), channel_id=1, source_target_pairs={{0,16},{16,0},{32,48},{48,32},{64,80},{80,64},{96,112},{112,96},{1... | collective-permute-start | bytes 3145736 | tf_op jit(solution)/shard_map/ppermute | solution.py:16
  33.9 1.7 %fusion.241 = (bf16[512,512]{1,0:T(8,128)(2,1)S(1)}, bf16[512,512]{1,0:T(8,128)(2,1)S(1)}, bf16[512,512]{1,0:T(8,128)(2,1)S(1)}) fusion(bf16[512]{0:T(512)(128)(2,1)S(1)} %get-tuple-element.38, bf16[512]{0:T(512)(128)(2,1)S(1)} %get-tuple-element.39, bf16[512]{0:T(512)(128)(2,1)S(1)} %get-tuple-element.40, bf16[512]{0:T(512)(128)(2,1)S(1)} %get-tuple-element.41, ...), kind=kLoop, calls=%fused_computation.376 | loop fusion | flops 7340032 | bytes 1591296 | tf_op jit(solution)/shard_map/neg | solution.py:43
  35.6 1.2 fusion.26
  36.9 1.2 add_convert_fusion.2
  38.2 2.1 %collective-permute-start.2 = (bf16[1024,512]{1,0:T(8,128)(2,1)S(1)}, bf16[1024,512]{1,0:T(8,128)(2,1)S(1)}, u32[]{:S(2)}, u32[]{:S(2)}) collective-permute-start(bf16[1024,512]{1,0:T(8,128)(2,1)S(1)} %add_convert_fusion.2), channel_id=1, source_target_pairs={{0,32},{16,48},{32,0},{48,16},{64,96},{80,112},{96,64},{112,80},{1... | collective-permute-start | bytes 3145736 | tf_op jit(solution)/shard_map/ppermute | solution.py:16
  40.4 0.2 fusion.224
  40.6 1.7 %fusion.237 = (bf16[512,512]{1,0:T(8,128)(2,1)S(1)}, bf16[512,512]{1,0:T(8,128)(2,1)S(1)}, bf16[512,512]{1,0:T(8,128)(2,1)S(1)}) fusion(bf16[512]{0:T(512)(128)(2,1)S(1)} %get-tuple-element.22, bf16[512]{0:T(512)(128)(2,1)S(1)} %get-tuple-element.23, bf16[512]{0:T(512)(128)(2,1)S(1)} %get-tuple-element.24, bf16[512]{0:T(512)(128)(2,1)S(1)} %get-tuple-element.25, ...), kind=kLoop, calls=%fused_computation.372 | loop fusion | flops 7340032 | bytes 1591296 | tf_op jit(solution)/shard_map/neg | solution.py:43
  42.4 1.2 fusion.18
  43.6 19.9 %collective-permute-done.2 = bf16[1024,512]{1,0:T(8,128)(2,1)S(1)} collective-permute-done((bf16[1024,512]{1,0:T(8,128)(2,1)S(1)}, bf16[1024,512]{1,0:T(8,128)(2,1)S(1)}, u32[]{:S(2)}, u32[]{:S(2)}) %collective-permute-start.2) | collective-permute-done | bytes 1048608 | tf_op jit(solution)/shard_map/ppermute | solution.py:16
  63.6 1.2 add_convert_fusion.1
  64.8 3.3 %collective-permute-start.3 = (bf16[1024,512]{1,0:T(8,128)(2,1)S(1)}, bf16[1024,512]{1,0:T(8,128)(2,1)S(1)}, u32[]{:S(2)}, u32[]{:S(2)}) collective-permute-start(bf16[1024,512]{1,0:T(8,128)(2,1)S(1)} %add_convert_fusion.1), channel_id=1, source_target_pairs={{0,64},{16,80},{32,96},{48,112},{64,0},{80,16},{96,32},{112,48},{1... | collective-permute-start | bytes 3145736 | tf_op jit(solution)/shard_map/ppermute | solution.py:16
  68.1 1.7 fusion.242
  69.8 1.2 fusion.10
  71.0 19.5 %collective-permute-done.3 = bf16[1024,512]{1,0:T(8,128)(2,1)S(1)} collective-permute-done((bf16[1024,512]{1,0:T(8,128)(2,1)S(1)}, bf16[1024,512]{1,0:T(8,128)(2,1)S(1)}, u32[]{:S(2)}, u32[]{:S(2)}) %collective-permute-start.3) | collective-permute-done | bytes 1048608 | tf_op jit(solution)/shard_map/ppermute | solution.py:16
  90.5 1.2 add_convert_fusion
  91.8 0.5 copy.33
  92.3 0.3 copy-done.2
  92.7 1.6 convolution_convert_fusion
  94.2 0.3 copy.35
  94.6 37.6 %all_to_all.10 = bf16[8,16,8,1152]{3,2,0,1:T(8,128)(2,1)S(1)} all-to-all(bf16[8,16,8,1152]{3,2,0,1:T(8,128)(2,1)S(1)} %copy.35), channel_id=1, replica_groups=mesh['sub'=8,'rng'=16] {'rng'}, dimensions={1} | all-to-all | bytes 4718592 | tf_op jit(solution)/shard_map/all_to_all | solution.py:57
  132.2 0.3 copy.36
  132.5 37.0 %all_to_all.11 = bf16[8,16,8,1152]{3,2,1,0:T(8,128)(2,1)S(1)} all-to-all(bf16[8,16,8,1152]{3,2,1,0:T(8,128)(2,1)S(1)} %copy.36), channel_id=1, replica_groups=mesh['sub'=8,'rng'=16] {'sub'}, dimensions={0} | all-to-all | bytes 4718592 | tf_op jit(solution)/shard_map/all_to_all | solution.py:58
  169.5 0.1 fusion.243
  169.8 0.1 copy.40
  170.0 1.2 fusion.72
  171.2 1.0 copy.46
  (53 shorter events, 1.3 us)
Async XLA Ops:
  0.0 2.8 %copy-start.13 = (s32[1,1,512]{2,1,0:T(1,128)S(1)}, s32[1,1,512]{2,1,0:T(1,128)}, u32[]{:S(2)}) copy-start(s32[1,1,512]{2,1,0:T(1,128)} %param.11) | copy-start | bytes 6148
  0.0 3.8 %copy-start.12 = (bf16[2,512]{1,0:T(2,128)(2,1)S(1)}, bf16[2,512]{1,0:T(2,128)(2,1)}, u32[]{:S(2)}) copy-start(bf16[2,512]{1,0:T(2,128)(2,1)} %param.7) | copy-start | bytes 6148
  0.0 26.8 %collective-permute-start = (bf16[2,512,512]{2,1,0:T(8,128)(2,1)}, bf16[2,512,512]{2,1,0:T(8,128)(2,1)}, u32[]{:S(2)}, u32[]{:S(2)}) collective-permute-start(bf16[2,512,512]{2,1,0:T(8,128)(2,1)} %param.6), channel_id=1, source_target_pairs={{1,0},{2,1},{3,2},{4,3},{5,4},{6,5},{7,6},{8,7},{9,8},{10,9},{11,1... | collective-permute-start | bytes 3145736 | tf_op jit(solution)/shard_map/ppermute | solution.py:12
  6.3 1.2 slice-start
  11.2 1.2 slice-start.1
  11.2 2.5 %copy-start.3 = (bf16[3,1,2,2,512,8]{4,5,3,2,1,0:T(8,128)(2,1)S(1)}, bf16[3,1,2,2,512,8]{4,5,3,2,1,0:T(8,128)(2,1)}, u32[]{:S(2)}) copy-start(bf16[3,1,2,2,512,8]{4,5,3,2,1,0:T(8,128)(2,1)} %param.9) | copy-start | bytes 294916
  11.2 3.1 %copy-start.6 = (s32[3,1,2,512]{3,2,1,0:T(2,128)S(1)}, s32[3,1,2,512]{3,2,1,0:T(2,128)}, u32[]{:S(2)}) copy-start(s32[3,1,2,512]{3,2,1,0:T(2,128)} %param.8) | copy-start | bytes 36868
  11.2 3.7 %copy-start.4 = (s32[1,1,512,1]{2,3,1,0:T(1,128)S(1)}, s32[1,1,512,1]{2,3,1,0:T(1,128)}, u32[]{:S(2)}) copy-start(s32[1,1,512,1]{2,3,1,0:T(1,128)} %param.10) | copy-start | bytes 6148
  13.7 5.8 %copy-start = (bf16[512,1024]{1,0:T(8,128)(2,1)S(1)}, bf16[512,1024]{1,0:T(8,128)(2,1)}, u32[]{:S(2)}) copy-start(bf16[512,1024]{1,0:T(8,128)(2,1)} %reshape.153) | copy-start | bytes 3145732
  15.3 4.2 %copy-start.11 = (s32[1,1,1,512]{3,2,1,0:T(1,128)S(1)}, s32[1,1,1,512]{3,2,1,0:T(1,128)}, u32[]{:S(2)}) copy-start(s32[1,1,1,512]{3,2,1,0:T(1,128)} %get-tuple-element.120) | copy-start | bytes 6148
  19.4 1.9 %copy-start.10 = (s32[1,1,1,512]{3,2,1,0:T(1,128)S(1)}, s32[1,1,1,512]{3,2,1,0:T(1,128)}, u32[]{:S(2)}) copy-start(s32[1,1,1,512]{3,2,1,0:T(1,128)} %get-tuple-element.122) | copy-start | bytes 6148
  28.2 1.2 copy-start.1
  31.8 2.0 %copy-start.9 = (s32[1,1,1,512]{3,2,1,0:T(1,128)S(1)}, s32[1,1,1,512]{3,2,1,0:T(1,128)}, u32[]{:S(2)}) copy-start(s32[1,1,1,512]{3,2,1,0:T(1,128)} %get-tuple-element.124) | copy-start | bytes 6148
  31.9 5.0 %collective-permute-start.1 = (bf16[1024,512]{1,0:T(8,128)(2,1)S(1)}, bf16[1024,512]{1,0:T(8,128)(2,1)S(1)}, u32[]{:S(2)}, u32[]{:S(2)}) collective-permute-start(bf16[1024,512]{1,0:T(8,128)(2,1)S(1)} %bitcast.80), channel_id=1, source_target_pairs={{0,16},{16,0},{32,48},{48,32},{64,80},{80,64},{96,112},{112,96},{1... | collective-permute-start | bytes 3145736 | tf_op jit(solution)/shard_map/ppermute | solution.py:16
  36.9 3.5 %copy-start.5 = (s32[1,1,512,1]{2,3,1,0:T(1,128)S(1)}, s32[1,1,512,1]{2,3,1,0:T(1,128)}, u32[]{:S(2)}) copy-start(s32[1,1,512,1]{2,3,1,0:T(1,128)} %param.10) | copy-start | bytes 6148
  36.9 3.7 %copy-start.8 = (s32[1,1,1,512]{3,2,1,0:T(1,128)S(1)}, s32[1,1,1,512]{3,2,1,0:T(1,128)}, u32[]{:S(2)}) copy-start(s32[1,1,1,512]{3,2,1,0:T(1,128)} %get-tuple-element.123) | copy-start | bytes 6148
  38.2 25.4 %collective-permute-start.2 = (bf16[1024,512]{1,0:T(8,128)(2,1)S(1)}, bf16[1024,512]{1,0:T(8,128)(2,1)S(1)}, u32[]{:S(2)}, u32[]{:S(2)}) collective-permute-start(bf16[1024,512]{1,0:T(8,128)(2,1)S(1)} %add_convert_fusion.2), channel_id=1, source_target_pairs={{0,32},{16,48},{32,0},{48,16},{64,96},{80,112},{96,64},{112,80},{1... | collective-permute-start | bytes 3145736 | tf_op jit(solution)/shard_map/ppermute | solution.py:16
  63.6 4.5 %copy-start.7 = (s32[1,1,1,512]{3,2,1,0:T(1,128)S(1)}, s32[1,1,1,512]{3,2,1,0:T(1,128)}, u32[]{:S(2)}) copy-start(s32[1,1,1,512]{3,2,1,0:T(1,128)} %get-tuple-element.119) | copy-start | bytes 6148
  64.8 25.7 %collective-permute-start.3 = (bf16[1024,512]{1,0:T(8,128)(2,1)S(1)}, bf16[1024,512]{1,0:T(8,128)(2,1)S(1)}, u32[]{:S(2)}, u32[]{:S(2)}) collective-permute-start(bf16[1024,512]{1,0:T(8,128)(2,1)S(1)} %add_convert_fusion.1), channel_id=1, source_target_pairs={{0,64},{16,80},{32,96},{48,112},{64,0},{80,16},{96,32},{112,48},{1... | collective-permute-start | bytes 3145736 | tf_op jit(solution)/shard_map/ppermute | solution.py:16
  91.7 0.9 copy-start.2

commit v3 on v2

--- a/solution.py
+++ b/solution.py
@@ -51,12 +51,7 @@
 
 
 def route_rows(send):
-    n_sub = lax.axis_size("sub")
-    n_rng = lax.axis_size("rng")
-    grid = send.reshape((n_sub, n_rng) + send.shape[1:])
-    grid = lax.all_to_all(grid, "rng", split_axis=1, concat_axis=1, tiled=True)
-    grid = lax.all_to_all(grid, "sub", split_axis=0, concat_axis=0, tiled=True)
-    return grid.reshape(send.shape)
+    return lax.all_to_all(send, ("sub", "rng"), split_axis=0, concat_axis=0, tiled=True)
 
 
 def on_device(echoes, chirp, offsets, weights, owners, targets):

time: 173 us -> 143 us (0.83)
  blocking collectives: 74.6 us -> 45.1 us
    all_to_all x2 -> x1, blocking collectives: 74.6 us -> 45.1 us  [route_rows(): lax.all_to_all(send, ('sub', 'rng'), split_axis=0, concat_axis=0, tiled=T...]
  transfers between devices with their start and end apart: 4 -> 4, of which waited for: 3 -> 3; matrix products, arithmetic and copies ran while one was open for 16% -> 20% of each run, Pallas kernels for 0% -> 0%
where the time goes in v3:
time: 143 us; the launch traced here: 142 us
  blocking collectives  45.1 us (32%)
  waiting for transfers between devices  43.2 us (30%)
  local copies, waits for them, and re-layouts  20.1 us (14%)
  matrix products  12.7 us (9%)
  other arithmetic  12.1 us (8%)
  starting transfers between devices  8.55 us (6%)
    all_to_all x1, blocking collectives, route_rows(): lax.all_to_all(send, ('sub', 'rng'), split_axis=0, concat_axis=0, tiled=T...  45.1 us
    ppermute x3, waiting for transfers between devices, from_partner(): lax.ppermute(value, axis, [(i, i ^ 1 << apart) for i in range(lax.axis_si...  39.4 us
    neg x6, other arithmetic, merge_matrix(): upper = jnp.concatenate([g_real, -g_imag], axis=1)  11.2 us
    ppermute x3, starting transfers between devices, from_partner(): lax.ppermute(value, axis, [(i, i ^ 1 << apart) for i in range(lax.axis_si...  7.14 us
    another operation x4, local copies, waits for them, and re-layouts, replica_matrix(): jnp.tile(padded, block_len)[:block_len * width].reshape(block_len, width)  4.78 us
    ppermute x1, waiting for transfers between devices, shifted(): lax.ppermute(value, axis, [(source, source + steps) for source in range(f...  3.8 us
    dot_general x3, matrix products, on_device(): merged = jnp.dot(mine, image, preferred_element_type=jnp.float32)  3.73 us
    dot_general x3, matrix products, on_device(): jnp.dot(theirs, partner, preferred_element_type=jnp.float32)  3.73 us
  transfers between devices with their start and end apart: 4, of which 3 were waited for; matrix products, arithmetic and copies ran while one was open for 20% of the time, Pallas kernels for 0%

profile of v3, /device:TPU:1, one launch (start us, length us, event | category | flops | bytes accessed | tf_op | source)
XLA Modules:
  0.0 142.1 jit_solution(3840718535190976441)
XLA Ops:
  0.0 1.4 collective-permute-start
  1.4 1.4 constant_dynamic-update-slice_fusion.1
  2.9 0.2 select_convert_fusion
  3.1 0.8 copy.26
  4.0 2.3 %tile.9 = bf16[524800]{0:T(1024)(128)(2,1)} reshape(bf16[512,1025]{1,0:T(8,128)(2,1)S(1)} %tile.8) | data formatting | bytes 2099200 | tf_op jit(solution)/shard_map/tile | solution.py:25
  6.3 1.2 slice-done
  7.5 1.3 reshape.158
  8.9 2.3 %tile.21 = bf16[524800]{0:T(1024)(128)(2,1)} reshape(bf16[512,1025]{1,0:T(8,128)(2,1)S(1)} %tile.20) | data formatting | bytes 2099200 | tf_op jit(solution)/shard_map/tile | solution.py:25
  11.2 1.2 slice-done.1
  12.4 1.3 reshape.159
  13.7 0.6 slice_bitcast_fusion.2
  14.3 0.6 fusion.245
  14.9 0.1 copy.22
  15.0 0.2 fusion.226
  15.4 1.3 slice_reduce_fusion.55
  16.6 0.1 slice_reduce_fusion.39
  16.8 2.6 %fusion.240 = (bf16[512,512]{1,0:T(8,128)(2,1)S(1)}, bf16[512,512]{1,0:T(8,128)(2,1)S(1)}, bf16[512,512]{1,0:T(8,128)(2,1)S(1)}) fusion(bf16[512]{0:T(512)(128)(2,1)S(1)} %get-tuple-element.86, bf16[512]{0:T(512)(128)(2,1)S(1)} %get-tuple-element.87, bf16[512]{0:T(512)(128)(2,1)S(1)} %get-tuple-element.88, bf16[512]{0:T(512)(128)(2,1)S(1)} %get-tuple-element.89, ...), kind=kLoop, calls=%fused_computation.375 | loop fusion | flops 7340032 | bytes 1591296 | tf_op jit(solution)/shard_map/neg | solution.py:43
  19.5 1.7 %fusion.241 = (bf16[512,512]{1,0:T(8,128)(2,1)S(1)}, bf16[512,512]{1,0:T(8,128)(2,1)S(1)}, bf16[512,512]{1,0:T(8,128)(2,1)S(1)}) fusion(bf16[512]{0:T(512)(128)(2,1)S(1)} %get-tuple-element.70, bf16[512]{0:T(512)(128)(2,1)S(1)} %get-tuple-element.71, bf16[512]{0:T(512)(128)(2,1)S(1)} %get-tuple-element.72, bf16[512]{0:T(512)(128)(2,1)S(1)} %get-tuple-element.73, ...), kind=kLoop, calls=%fused_computation.376 | loop fusion | flops 7340032 | bytes 1591296 | tf_op jit(solution)/shard_map/neg | solution.py:43
  21.3 1.7 %fusion.239 = (bf16[512,512]{1,0:T(8,128)(2,1)S(1)}, bf16[512,512]{1,0:T(8,128)(2,1)S(1)}, bf16[512,512]{1,0:T(8,128)(2,1)S(1)}) fusion(bf16[512]{0:T(512)(128)(2,1)S(1)} %get-tuple-element.54, bf16[512]{0:T(512)(128)(2,1)S(1)} %get-tuple-element.55, bf16[512]{0:T(512)(128)(2,1)S(1)} %get-tuple-element.56, bf16[512]{0:T(512)(128)(2,1)S(1)} %get-tuple-element.57, ...), kind=kLoop, calls=%fused_computation.374 | loop fusion | flops 7340032 | bytes 1591296 | tf_op jit(solution)/shard_map/neg | solution.py:43
  23.0 3.8 %collective-permute-done = bf16[2,512,512]{2,1,0:T(8,128)(2,1)} collective-permute-done((bf16[2,512,512]{2,1,0:T(8,128)(2,1)}, bf16[2,512,512]{2,1,0:T(8,128)(2,1)}, u32[]{:S(2)}, u32[]{:S(2)}) %collective-permute-start) | collective-permute-done | bytes 1048608 | tf_op jit(solution)/shard_map/ppermute | solution.py:12
  26.8 1.4 constant_dynamic-update-slice_fusion
  28.2 0.2 slice_bitcast_fusion.1
  28.4 1.0 copy-done.1
  29.4 2.4 %fusion.68 = bf16[512,1024]{1,0:T(8,128)(2,1)S(1)} fusion(bf16[1024,512]{0,1:T(8,128)(2,1)S(1)} %bitcast.79, bf16[1024,512]{0,1:T(8,128)(2,1)S(1)} %bitcast.76, bf16[1024,512]{0,1:T(8,128)(2,1)S(1)} %bitcast_negate_fusion, bf16[512,1024]{1,0:T(8,128)(2,1)S(1)} %get-tuple-element.106, bf16[512,1024]{1,0:T(8,128)(2,1)S(1)} %get-tuple-element.105), kind=kOutput, calls=%fused_computation.68 | convolution fusion | flops 2168979456 | bytes 6291456 | tf_op jit(solution)/shard_map/dot_general | solution.py:68
  31.9 1.7 %collective-permute-start.1 = (bf16[1024,512]{1,0:T(8,128)(2,1)S(1)}, bf16[1024,512]{1,0:T(8,128)(2,1)S(1)}, u32[]{:S(2)}, u32[]{:S(2)}) collective-permute-start(bf16[1024,512]{1,0:T(8,128)(2,1)S(1)} %bitcast.80), channel_id=1, source_target_pairs={{0,16},{16,0},{32,48},{48,32},{64,80},{80,64},{96,112},{112,96},{1... | collective-permute-start | bytes 3145736 | tf_op jit(solution)/shard_map/ppermute | solution.py:16
  33.9 1.7 %fusion.242 = (bf16[512,512]{1,0:T(8,128)(2,1)S(1)}, bf16[512,512]{1,0:T(8,128)(2,1)S(1)}, bf16[512,512]{1,0:T(8,128)(2,1)S(1)}) fusion(bf16[512]{0:T(512)(128)(2,1)S(1)} %get-tuple-element.38, bf16[512]{0:T(512)(128)(2,1)S(1)} %get-tuple-element.39, bf16[512]{0:T(512)(128)(2,1)S(1)} %get-tuple-element.40, bf16[512]{0:T(512)(128)(2,1)S(1)} %get-tuple-element.41, ...), kind=kLoop, calls=%fused_computation.377 | loop fusion | flops 7340032 | bytes 1591296 | tf_op jit(solution)/shard_map/neg | solution.py:43
  35.6 1.2 fusion.27
  36.9 1.2 add_convert_fusion.2
  38.2 2.1 %collective-permute-start.2 = (bf16[1024,512]{1,0:T(8,128)(2,1)S(1)}, bf16[1024,512]{1,0:T(8,128)(2,1)S(1)}, u32[]{:S(2)}, u32[]{:S(2)}) collective-permute-start(bf16[1024,512]{1,0:T(8,128)(2,1)S(1)} %add_convert_fusion.2), channel_id=1, source_target_pairs={{0,32},{16,48},{32,0},{48,16},{64,96},{80,112},{96,64},{112,80},{1... | collective-permute-start | bytes 3145736 | tf_op jit(solution)/shard_map/ppermute | solution.py:16
  40.4 0.2 fusion.225
  40.6 1.7 %fusion.238 = (bf16[512,512]{1,0:T(8,128)(2,1)S(1)}, bf16[512,512]{1,0:T(8,128)(2,1)S(1)}, bf16[512,512]{1,0:T(8,128)(2,1)S(1)}) fusion(bf16[512]{0:T(512)(128)(2,1)S(1)} %get-tuple-element.22, bf16[512]{0:T(512)(128)(2,1)S(1)} %get-tuple-element.23, bf16[512]{0:T(512)(128)(2,1)S(1)} %get-tuple-element.24, bf16[512]{0:T(512)(128)(2,1)S(1)} %get-tuple-element.25, ...), kind=kLoop, calls=%fused_computation.373 | loop fusion | flops 7340032 | bytes 1591296 | tf_op jit(solution)/shard_map/neg | solution.py:43
  42.4 1.2 fusion.19
  43.6 19.9 %collective-permute-done.2 = bf16[1024,512]{1,0:T(8,128)(2,1)S(1)} collective-permute-done((bf16[1024,512]{1,0:T(8,128)(2,1)S(1)}, bf16[1024,512]{1,0:T(8,128)(2,1)S(1)}, u32[]{:S(2)}, u32[]{:S(2)}) %collective-permute-start.2) | collective-permute-done | bytes 1048608 | tf_op jit(solution)/shard_map/ppermute | solution.py:16
  63.6 1.2 add_convert_fusion.1
  64.8 3.3 %collective-permute-start.3 = (bf16[1024,512]{1,0:T(8,128)(2,1)S(1)}, bf16[1024,512]{1,0:T(8,128)(2,1)S(1)}, u32[]{:S(2)}, u32[]{:S(2)}) collective-permute-start(bf16[1024,512]{1,0:T(8,128)(2,1)S(1)} %add_convert_fusion.1), channel_id=1, source_target_pairs={{0,64},{16,80},{32,96},{48,112},{64,0},{80,16},{96,32},{112,48},{1... | collective-permute-start | bytes 3145736 | tf_op jit(solution)/shard_map/ppermute | solution.py:16
  68.1 1.7 %fusion.243 = (bf16[512,512]{1,0:T(8,128)(2,1)S(1)}, bf16[512,512]{1,0:T(8,128)(2,1)S(1)}, bf16[512,512]{1,0:T(8,128)(2,1)S(1)}) fusion(bf16[512]{0:T(512)(128)(2,1)S(1)} %get-tuple-element.6, bf16[512]{0:T(512)(128)(2,1)S(1)} %get-tuple-element.7, bf16[512]{0:T(512)(128)(2,1)S(1)} %get-tuple-element.8, bf16[512]{0:T(512)(128)(2,1)S(1)} %get-tuple-element.9, ...), kind=kLoop, calls=%fused_computation.378 | loop fusion | flops 7340032 | bytes 1591296 | tf_op jit(solution)/shard_map/neg | solution.py:43
  69.8 1.2 fusion.11
  71.0 19.5 %collective-permute-done.3 = bf16[1024,512]{1,0:T(8,128)(2,1)S(1)} collective-permute-done((bf16[1024,512]{1,0:T(8,128)(2,1)S(1)}, bf16[1024,512]{1,0:T(8,128)(2,1)S(1)}, u32[]{:S(2)}, u32[]{:S(2)}) %collective-permute-start.3) | collective-permute-done | bytes 1048608 | tf_op jit(solution)/shard_map/ppermute | solution.py:16
  90.5 1.2 add_convert_fusion
  91.8 0.5 copy.25
  92.3 0.3 copy-done.2
  92.7 1.6 %fusion.8 = bf16[128,8,1152]{2,1,0:T(8,128)(2,1)S(1)} fusion(bf16[512,128]{0,1:T(8,128)(2,1)S(1)} %copy-done.2, bf16[512,1024]{0,1:T(8,128)(2,1)S(1)} %bitcast.85, s32[512]{0:T(512)S(1)} %multiply_add_fusion), kind=kOutput, calls=%fused_computation.9 | convolution fusion | flops 1212022784 | bytes 3540992 | tf_op jit(solution)/shard_map/dot_general | solution.py:88
  94.2 45.1 %all_to_all.5 = bf16[128,8,1152]{2,1,0:T(8,128)(2,1)S(1)} all-to-all(bf16[128,8,1152]{2,1,0:T(8,128)(2,1)S(1)} %fusion.8), channel_id=1, replica_groups=mesh['sub'=8,'rng'=16] {'sub','rng'}, dimensions={0} | all-to-all | bytes 4718592 | tf_op jit(solution)/shard_map/all_to_all | solution.py:54
  139.4 0.1 fusion.244
  139.5 0.1 copy.31
  139.7 0.1 copy.30
  139.9 1.2 fusion.73
  141.1 1.0 copy.36
  (50 shorter events, 1.0 us)
Async XLA Ops:
  0.0 2.8 %copy-start.13 = (s32[1,1,512]{2,1,0:T(1,128)S(1)}, s32[1,1,512]{2,1,0:T(1,128)}, u32[]{:S(2)}) copy-start(s32[1,1,512]{2,1,0:T(1,128)} %param.11) | copy-start | bytes 6148
  0.0 3.8 %copy-start.12 = (bf16[2,512]{1,0:T(2,128)(2,1)S(1)}, bf16[2,512]{1,0:T(2,128)(2,1)}, u32[]{:S(2)}) copy-start(bf16[2,512]{1,0:T(2,128)(2,1)} %param.7) | copy-start | bytes 6148
  0.0 26.8 %collective-permute-start = (bf16[2,512,512]{2,1,0:T(8,128)(2,1)}, bf16[2,512,512]{2,1,0:T(8,128)(2,1)}, u32[]{:S(2)}, u32[]{:S(2)}) collective-permute-start(bf16[2,512,512]{2,1,0:T(8,128)(2,1)} %param.6), channel_id=1, source_target_pairs={{1,0},{2,1},{3,2},{4,3},{5,4},{6,5},{7,6},{8,7},{9,8},{10,9},{11,1... | collective-permute-start | bytes 3145736 | tf_op jit(solution)/shard_map/ppermute | solution.py:12
  6.3 1.2 slice-start
  11.2 1.2 slice-start.1
  11.2 2.5 %copy-start.3 = (bf16[3,1,2,2,512,8]{4,5,3,2,1,0:T(8,128)(2,1)S(1)}, bf16[3,1,2,2,512,8]{4,5,3,2,1,0:T(8,128)(2,1)}, u32[]{:S(2)}) copy-start(bf16[3,1,2,2,512,8]{4,5,3,2,1,0:T(8,128)(2,1)} %param.9) | copy-start | bytes 294916
  11.2 3.1 %copy-start.6 = (s32[3,1,2,512]{3,2,1,0:T(2,128)S(1)}, s32[3,1,2,512]{3,2,1,0:T(2,128)}, u32[]{:S(2)}) copy-start(s32[3,1,2,512]{3,2,1,0:T(2,128)} %param.8) | copy-start | bytes 36868
  11.2 3.7 %copy-start.4 = (s32[1,1,512,1]{2,3,1,0:T(1,128)S(1)}, s32[1,1,512,1]{2,3,1,0:T(1,128)}, u32[]{:S(2)}) copy-start(s32[1,1,512,1]{2,3,1,0:T(1,128)} %param.10) | copy-start | bytes 6148
  13.7 5.8 %copy-start = (bf16[512,1024]{1,0:T(8,128)(2,1)S(1)}, bf16[512,1024]{1,0:T(8,128)(2,1)}, u32[]{:S(2)}) copy-start(bf16[512,1024]{1,0:T(8,128)(2,1)} %reshape.159) | copy-start | bytes 3145732
  15.3 4.2 %copy-start.11 = (s32[1,1,1,512]{3,2,1,0:T(1,128)S(1)}, s32[1,1,1,512]{3,2,1,0:T(1,128)}, u32[]{:S(2)}) copy-start(s32[1,1,1,512]{3,2,1,0:T(1,128)} %get-tuple-element.120) | copy-start | bytes 6148
  19.4 1.9 %copy-start.10 = (s32[1,1,1,512]{3,2,1,0:T(1,128)S(1)}, s32[1,1,1,512]{3,2,1,0:T(1,128)}, u32[]{:S(2)}) copy-start(s32[1,1,1,512]{3,2,1,0:T(1,128)} %get-tuple-element.122) | copy-start | bytes 6148
  28.2 1.2 copy-start.1
  31.8 2.0 %copy-start.9 = (s32[1,1,1,512]{3,2,1,0:T(1,128)S(1)}, s32[1,1,1,512]{3,2,1,0:T(1,128)}, u32[]{:S(2)}) copy-start(s32[1,1,1,512]{3,2,1,0:T(1,128)} %get-tuple-element.124) | copy-start | bytes 6148
  31.9 5.0 %collective-permute-start.1 = (bf16[1024,512]{1,0:T(8,128)(2,1)S(1)}, bf16[1024,512]{1,0:T(8,128)(2,1)S(1)}, u32[]{:S(2)}, u32[]{:S(2)}) collective-permute-start(bf16[1024,512]{1,0:T(8,128)(2,1)S(1)} %bitcast.80), channel_id=1, source_target_pairs={{0,16},{16,0},{32,48},{48,32},{64,80},{80,64},{96,112},{112,96},{1... | collective-permute-start | bytes 3145736 | tf_op jit(solution)/shard_map/ppermute | solution.py:16
  36.9 3.5 %copy-start.5 = (s32[1,1,512,1]{2,3,1,0:T(1,128)S(1)}, s32[1,1,512,1]{2,3,1,0:T(1,128)}, u32[]{:S(2)}) copy-start(s32[1,1,512,1]{2,3,1,0:T(1,128)} %param.10) | copy-start | bytes 6148
  36.9 3.7 %copy-start.8 = (s32[1,1,1,512]{3,2,1,0:T(1,128)S(1)}, s32[1,1,1,512]{3,2,1,0:T(1,128)}, u32[]{:S(2)}) copy-start(s32[1,1,1,512]{3,2,1,0:T(1,128)} %get-tuple-element.123) | copy-start | bytes 6148
  38.2 25.4 %collective-permute-start.2 = (bf16[1024,512]{1,0:T(8,128)(2,1)S(1)}, bf16[1024,512]{1,0:T(8,128)(2,1)S(1)}, u32[]{:S(2)}, u32[]{:S(2)}) collective-permute-start(bf16[1024,512]{1,0:T(8,128)(2,1)S(1)} %add_convert_fusion.2), channel_id=1, source_target_pairs={{0,32},{16,48},{32,0},{48,16},{64,96},{80,112},{96,64},{112,80},{1... | collective-permute-start | bytes 3145736 | tf_op jit(solution)/shard_map/ppermute | solution.py:16
  63.6 4.5 %copy-start.7 = (s32[1,1,1,512]{3,2,1,0:T(1,128)S(1)}, s32[1,1,1,512]{3,2,1,0:T(1,128)}, u32[]{:S(2)}) copy-start(s32[1,1,1,512]{3,2,1,0:T(1,128)} %get-tuple-element.119) | copy-start | bytes 6148
  64.8 25.7 %collective-permute-start.3 = (bf16[1024,512]{1,0:T(8,128)(2,1)S(1)}, bf16[1024,512]{1,0:T(8,128)(2,1)S(1)}, u32[]{:S(2)}, u32[]{:S(2)}) collective-permute-start(bf16[1024,512]{1,0:T(8,128)(2,1)S(1)} %add_convert_fusion.1), channel_id=1, source_target_pairs={{0,64},{16,80},{32,96},{48,112},{64,0},{80,16},{96,32},{112,48},{1... | collective-permute-start | bytes 3145736 | tf_op jit(solution)/shard_map/ppermute | solution.py:16
  91.7 0.9 copy-start.2

commit v4 on v3

--- a/solution.py
+++ b/solution.py
@@ -54,6 +54,9 @@
     return lax.all_to_all(send, ("sub", "rng"), split_axis=0, concat_axis=0, tiled=True)
 
 
+CHUNKS = 2
+
+
 def on_device(echoes, chirp, offsets, weights, owners, targets):
     p_dev = echoes.shape[1]
     r_dev = echoes.shape[2]
@@ -61,42 +64,52 @@
     n_rng = lax.axis_size("rng")
     devices = n_sub * n_rng
     capacity = max(2, 2 * p_dev // devices)
-    tail = shifted(echoes, "rng", -1)
-    extended = jnp.concatenate([echoes, tail], axis=2)
-    matrix = replica_matrix(chirp, RBLK)
-    stacked = jnp.concatenate([extended[0], extended[1]], axis=1)
-    block_out = jnp.dot(stacked, matrix, preferred_element_type=jnp.float32).astype(jnp.bfloat16)
-    pieces = block_out.reshape(p_dev, 2, RBLK)
-    image = pieces.transpose(1, 0, 2).reshape(2 * p_dev, r_dev)
+    width = r_dev // CHUNKS
+    tails = [shifted(echoes[:, :, c * width : (c + 1) * width], "rng", -1) for c in range(CHUNKS)]
+    matrix = replica_matrix(chirp, width)
+    images = []
+    for c in range(CHUNKS):
+        window = jnp.concatenate([echoes[:, :, c * width :]] + tails[: c + 1], axis=2)
+        stacked = jnp.concatenate([window[0], window[1]], axis=1)
+        block_out = jnp.dot(stacked, matrix, preferred_element_type=jnp.float32).astype(jnp.bfloat16)
+        images.append(block_out.reshape(p_dev, 2, width).transpose(1, 0, 2).reshape(2 * p_dev, width))
     section_count = offsets.shape[0]
     for section in range(section_count):
-        partner = from_partner(image, "sub", section)
         mine = merge_matrix(offsets[section, 0, 0], weights[section, 0, 0])
         theirs = merge_matrix(offsets[section, 0, 1], weights[section, 0, 1])
-        merged = jnp.dot(mine, image, preferred_element_type=jnp.float32)
-        merged = merged + jnp.dot(theirs, partner, preferred_element_type=jnp.float32)
-        image = merged.astype(jnp.bfloat16)
-    rows = image.reshape(2, p_dev, r_dev).transpose(1, 0, 2).reshape(p_dev, 2 * r_dev)
+        partners = [from_partner(image, "sub", section) for image in images]
+        merged = []
+        for image, partner in zip(images, partners):
+            acc = jnp.dot(mine, image, preferred_element_type=jnp.float32)
+            acc = acc + jnp.dot(theirs, partner, preferred_element_type=jnp.float32)
+            merged.append(acc.astype(jnp.bfloat16))
+        images = merged
     dest = owners.reshape(p_dev)
     aim = targets.reshape(p_dev)
     slot = dest * capacity + group_slots(dest, devices)
-    pick = jnp.arange(devices * capacity, dtype=jnp.int32)[:, None] == slot[None, :]
+    pick = (jnp.arange(devices * capacity, dtype=jnp.int32)[:, None] == slot[None, :]).astype(
+        jnp.bfloat16
+    )
     code = aim + 1
     lanes = jnp.arange(128, dtype=jnp.int32)[None, :]
     extra = jnp.where(lanes == 0, (code // 32)[:, None], jnp.where(lanes == 1, (code % 32)[:, None], 0))
-    rows = jnp.concatenate([rows, extra.astype(jnp.bfloat16)], axis=1)
-    send = jnp.dot(pick.astype(jnp.bfloat16), rows, preferred_element_type=jnp.float32).astype(
-        jnp.bfloat16
-    )
-    width = 2 * r_dev
-    got = route_rows(send.reshape(devices, capacity, width + 128))
-    got_flat = got.reshape(devices * capacity, width + 128)
-    head = got_flat[:, width].astype(jnp.int32)
-    low = got_flat[:, width + 1].astype(jnp.int32)
+    received = []
+    for c, image in enumerate(images):
+        rows = image.reshape(2, p_dev, width).transpose(1, 0, 2).reshape(p_dev, 2 * width)
+        if c == 0:
+            rows = jnp.concatenate([rows, extra.astype(jnp.bfloat16)], axis=1)
+        send = jnp.dot(pick, rows, preferred_element_type=jnp.float32).astype(jnp.bfloat16)
+        got = route_rows(send.reshape(devices, capacity, rows.shape[1]))
+        received.append(got.reshape(devices * capacity, rows.shape[1]))
+    head = received[0][:, 2 * width].astype(jnp.int32)
+    low = received[0][:, 2 * width + 1].astype(jnp.int32)
     mark_flat = head * 32 + low - 1
     place = (jnp.arange(p_dev, dtype=jnp.int32)[:, None] == mark_flat[None, :]).astype(jnp.bfloat16)
-    tile = jnp.dot(place, got_flat[:, :width], preferred_element_type=jnp.float32).astype(jnp.bfloat16)
-    return tile.reshape(p_dev, 2, r_dev).transpose(1, 0, 2)
+    tiles = []
+    for got in received:
+        tile = jnp.dot(place, got[:, : 2 * width], preferred_element_type=jnp.float32)
+        tiles.append(tile.astype(jnp.bfloat16).reshape(p_dev, 2, width))
+    return jnp.concatenate(tiles, axis=2).transpose(1, 0, 2)
 
 
 def solution(mesh):

time: 143 us -> 156 us (1.091)
  blocking collectives: 45.1 us -> 0 us
  starting transfers between devices: 8.55 us -> 35.4 us
  waiting for transfers between devices: 43.2 us -> 57.7 us
  matrix products: 12.7 us -> 23.5 us
  other arithmetic: 12.1 us -> 21.5 us
  local copies, waits for them, and re-layouts: 20.1 us -> 16.1 us
    all_to_all x1 -> x0, blocking collectives: 45.1 us -> none  [route_rows(): lax.all_to_all(send, ('sub', 'rng'), split_axis=0, concat_axis=0, tiled=T...]
    all_to_all x0 -> x2, starting transfers between devices: none -> 22 us  [route_rows(): lax.all_to_all(send, ('sub', 'rng'), split_axis=0, concat_axis=0, tiled=T...]
    all_to_all x0 -> x2, waiting for transfers between devices: none -> 17.4 us  [route_rows(): lax.all_to_all(send, ('sub', 'rng'), split_axis=0, concat_axis=0, tiled=T...]
    dot_general x8 -> x16, matrix products: 10.3 us -> 21.5 us  [the longest x6 8.45 us: on_device(): acc = jnp.dot(mine, image, preferred_element_type=jnp.float32)]
    neg x6, other arithmetic: 11.2 us -> 16.6 us  [merge_matrix(): upper = jnp.concatenate([g_real, -g_imag], axis=1)]
    ppermute x1 -> x2, waiting for transfers between devices: 3.8 us -> 0.01 us  [shifted(): lax.ppermute(value, axis, [(source, source + steps) for source in range(f...]
    ppermute x3 -> x6, starting transfers between devices: 7.14 us -> 10.7 us  [from_partner(): lax.ppermute(value, axis, [(i, i ^ 1 << apart) for i in range(lax.axis_si...]
    another operation x4, local copies, waits for them, and re-layouts: 4.78 us -> 1.46 us  [replica_matrix(): jnp.tile(padded, block_len)[:block_len * width].reshape(block_len, width)]
  transfers between devices with their start and end apart: 4 -> 10, of which waited for: 3 -> 4; matrix products, arithmetic and copies ran while one was open for 20% -> 35% of each run, Pallas kernels for 0% -> 0%
where the time goes in v4:
time: 156 us; the launch traced here: 155 us
  waiting for transfers between devices  57.7 us (37%)
  starting transfers between devices  35.4 us (23%)
  matrix products  23.5 us (15%)
  other arithmetic  21.5 us (14%)
  local copies, waits for them, and re-layouts  16.1 us (10%)
    ppermute x6, waiting for transfers between devices, from_partner(): lax.ppermute(value, axis, [(i, i ^ 1 << apart) for i in range(lax.axis_si...  40.3 us
    all_to_all x2, starting transfers between devices, route_rows(): lax.all_to_all(send, ('sub', 'rng'), split_axis=0, concat_axis=0, tiled=T...  22 us
    all_to_all x2, waiting for transfers between devices, route_rows(): lax.all_to_all(send, ('sub', 'rng'), split_axis=0, concat_axis=0, tiled=T...  17.4 us
    neg x6, other arithmetic, merge_matrix(): upper = jnp.concatenate([g_real, -g_imag], axis=1)  16.6 us
    ppermute x6, starting transfers between devices, from_partner(): lax.ppermute(value, axis, [(i, i ^ 1 << apart) for i in range(lax.axis_si...  10.7 us
    dot_general x6, matrix products, on_device(): acc = jnp.dot(mine, image, preferred_element_type=jnp.float32)  8.45 us
    dot_general x6, matrix products, on_device(): acc = acc + jnp.dot(theirs, partner, preferred_element_type=jnp.float32)  7.67 us
    dot_general x2, matrix products, on_device(): jnp.dot(pick, rows, preferred_element_type=jnp.float32).astype(jnp.bfloat16)  3.83 us
  transfers between devices with their start and end apart: 10, of which 4 were waited for; matrix products, arithmetic and copies ran while one was open for 35% of the time, Pallas kernels for 0%

profile of v4, /device:TPU:1, one launch (start us, length us, event | category | flops | bytes accessed | tf_op | source)
XLA Modules:
  0.0 155.0 jit_solution(15879273857336568277)
XLA Ops:
  0.0 2.1 %fusion.216 = (bf16[2,512,256]{2,1,0:T(8,128)(2,1)}, bf16[2,512,256]{2,1,0:T(8,128)(2,1)S(1)}) fusion(bf16[2,512,512]{2,1,0:T(8,128)(2,1)} %param.6), kind=kLoop, calls=%fused_computation.370 | loop fusion | bytes 2097152 | tf_op jit(solution)/shard_map/slice | solution.py:68
  2.2 1.4 collective-permute-start
  3.6 1.3 collective-permute-start.4
  8.1 0.8 slice.683
  8.8 1.3 reshape.180
  10.2 0.9 bitcast_negate_fusion
  12.0 1.1 reshape.179
  14.6 0.8 copy.33
  15.9 2.8 %fusion.211 = (bf16[512,512]{1,0:T(8,128)(2,1)}, bf16[512,512]{1,0:T(8,128)(2,1)}, bf16[512,512]{1,0:T(8,128)(2,1)}) fusion(bf16[512]{0:T(512)(128)(2,1)S(1)} %get-tuple-element.86, bf16[512]{0:T(512)(128)(2,1)S(1)} %get-tuple-element.87, bf16[512]{0:T(512)(128)(2,1)S(1)} %get-tuple-element.88, bf16[512]{0:T(512)(128)(2,1)S(1)} %get-tuple-element.89, ...), kind=kLoop, calls=%fused_computation.365 | loop fusion | flops 7340032 | bytes 1591296 | tf_op jit(solution)/shard_map/neg | solution.py:43
  18.7 2.8 %fusion.212 = (bf16[512,512]{1,0:T(8,128)(2,1)}, bf16[512,512]{1,0:T(8,128)(2,1)}, bf16[512,512]{1,0:T(8,128)(2,1)}) fusion(bf16[512]{0:T(512)(128)(2,1)S(1)} %get-tuple-element.70, bf16[512]{0:T(512)(128)(2,1)S(1)} %get-tuple-element.71, bf16[512]{0:T(512)(128)(2,1)S(1)} %get-tuple-element.72, bf16[512]{0:T(512)(128)(2,1)S(1)} %get-tuple-element.73, ...), kind=kLoop, calls=%fused_computation.366 | loop fusion | flops 7340032 | bytes 1591296 | tf_op jit(solution)/shard_map/neg | solution.py:43
  21.5 2.8 %fusion.210 = (bf16[512,512]{1,0:T(8,128)(2,1)}, bf16[512,512]{1,0:T(8,128)(2,1)}, bf16[512,512]{1,0:T(8,128)(2,1)}) fusion(bf16[512]{0:T(512)(128)(2,1)S(1)} %get-tuple-element.54, bf16[512]{0:T(512)(128)(2,1)S(1)} %get-tuple-element.55, bf16[512]{0:T(512)(128)(2,1)S(1)} %get-tuple-element.56, bf16[512]{0:T(512)(128)(2,1)S(1)} %get-tuple-element.57, ...), kind=kLoop, calls=%fused_computation.364 | loop fusion | flops 7340032 | bytes 1591296 | tf_op jit(solution)/shard_map/neg | solution.py:43
  24.3 2.7 %fusion.213 = (bf16[512,512]{1,0:T(8,128)(2,1)S(1)}, bf16[512,512]{1,0:T(8,128)(2,1)}, bf16[512,512]{1,0:T(8,128)(2,1)}) fusion(bf16[512]{0:T(512)(128)(2,1)S(1)} %get-tuple-element.38, bf16[512]{0:T(512)(128)(2,1)S(1)} %get-tuple-element.39, bf16[512]{0:T(512)(128)(2,1)S(1)} %get-tuple-element.40, bf16[512]{0:T(512)(128)(2,1)S(1)} %get-tuple-element.41, ...), kind=kLoop, calls=%fused_computation.367 | loop fusion | flops 7340032 | bytes 1591296 | tf_op jit(solution)/shard_map/neg | solution.py:43
  27.0 2.8 %fusion.209 = (bf16[512,512]{1,0:T(8,128)(2,1)}, bf16[512,512]{1,0:T(8,128)(2,1)}, bf16[512,512]{1,0:T(8,128)(2,1)}) fusion(bf16[512]{0:T(512)(128)(2,1)S(1)} %get-tuple-element.22, bf16[512]{0:T(512)(128)(2,1)S(1)} %get-tuple-element.23, bf16[512]{0:T(512)(128)(2,1)S(1)} %get-tuple-element.24, bf16[512]{0:T(512)(128)(2,1)S(1)} %get-tuple-element.25, ...), kind=kLoop, calls=%fused_computation.363 | loop fusion | flops 7340032 | bytes 1591296 | tf_op jit(solution)/shard_map/neg | solution.py:43
  29.9 2.8 %fusion.214 = (bf16[512,512]{1,0:T(8,128)(2,1)}, bf16[512,512]{1,0:T(8,128)(2,1)}, bf16[512,512]{1,0:T(8,128)(2,1)}) fusion(bf16[512]{0:T(512)(128)(2,1)S(1)} %get-tuple-element.6, bf16[512]{0:T(512)(128)(2,1)S(1)} %get-tuple-element.7, bf16[512]{0:T(512)(128)(2,1)S(1)} %get-tuple-element.8, bf16[512]{0:T(512)(128)(2,1)S(1)} %get-tuple-element.9, ...), kind=kLoop, calls=%fused_computation.368 | loop fusion | flops 7340032 | bytes 1591296 | tf_op jit(solution)/shard_map/neg | solution.py:43
  32.8 0.9 copy-done.2
  33.9 1.0 fusion.21
  35.0 1.0 copy.31
  36.0 1.4 collective-permute-start.1
  37.4 1.1 pad_maximum_fusion
  38.6 0.9 copy-done.26
  39.6 1.0 fusion.18
  40.6 1.0 copy.36
  41.7 1.7 %fusion.184 = f32[1024,256]{1,0:T(8,128)S(1)} fusion(bf16[1024,256]{1,0:T(8,128)(2,1)} %bitcast.20, bf16[512,512]{1,0:T(8,128)(2,1)S(1)} %copy-done.7, bf16[512,512]{1,0:T(8,128)(2,1)S(1)} %copy-done.6, bf16[512,512]{1,0:T(8,128)(2,1)S(1)} %copy-done.5), kind=kOutput, calls=%fused_computation.207 | convolution fusion | flops 545259520 | bytes 3145728 | tf_op jit(solution)/shard_map/dot_general | solution.py:83
  43.4 1.9 %fusion.183 = f32[1024,256]{1,0:T(8,128)S(1)} fusion(bf16[1024,256]{1,0:T(8,128)(2,1)} %bitcast.43, bf16[512,512]{1,0:T(8,128)(2,1)S(1)} %copy-done.7, bf16[512,512]{1,0:T(8,128)(2,1)S(1)} %copy-done.6, bf16[512,512]{1,0:T(8,128)(2,1)S(1)} %copy-done.5), kind=kOutput, calls=%fused_computation.206 | convolution fusion | flops 545259520 | bytes 3145728 | tf_op jit(solution)/shard_map/dot_general | solution.py:83
  45.4 1.9 %fusion.24 = bf16[1024,256]{1,0:T(8,128)(2,1)S(1)} fusion(f32[1024,256]{1,0:T(8,128)S(1)} %fusion.184, bf16[1024,256]{1,0:T(8,128)(2,1)} %collective-permute-done.1, bf16[512,512]{1,0:T(8,128)(2,1)S(1)} %copy-done.10, bf16[512,512]{1,0:T(8,128)(2,1)S(1)} %copy-done.9, bf16[512,512]{1,0:T(8,128)(2,1)S(1)} %copy-done.8), kind=kOutput, calls=%fused_computation.36 | convolution fusion | flops 545783808 | bytes 3670016 | tf_op jit(solution)/shard_map/dot_general | solution.py:84
  47.3 2.0 %collective-permute-start.2 = (bf16[1024,256]{1,0:T(8,128)(2,1)S(1)}, bf16[1024,256]{1,0:T(8,128)(2,1)S(1)}, u32[]{:S(2)}, u32[]{:S(2)}) collective-permute-start(bf16[1024,256]{1,0:T(8,128)(2,1)S(1)} %fusion.24), channel_id=1, source_target_pairs={{0,32},{16,48},{32,0},{48,16},{64,96},{80,112},{96,64},{112,80},{1... | collective-permute-start | bytes 1572872 | tf_op jit(solution)/shard_map/ppermute | solution.py:16
  49.3 0.7 fusion.186
  50.0 1.5 fusion.27
  51.5 9.5 %collective-permute-done.2 = bf16[1024,256]{1,0:T(8,128)(2,1)S(1)} collective-permute-done((bf16[1024,256]{1,0:T(8,128)(2,1)S(1)}, bf16[1024,256]{1,0:T(8,128)(2,1)S(1)}, u32[]{:S(2)}, u32[]{:S(2)}) %collective-permute-start.2) | collective-permute-done | bytes 524320 | tf_op jit(solution)/shard_map/ppermute | solution.py:16
  61.1 0.7 fusion.25
  61.8 3.2 %collective-permute-start.3 = (bf16[1024,256]{1,0:T(8,128)(2,1)S(1)}, bf16[1024,256]{1,0:T(8,128)(2,1)S(1)}, u32[]{:S(2)}, u32[]{:S(2)}) collective-permute-start(bf16[1024,256]{1,0:T(8,128)(2,1)S(1)} %fusion.25), channel_id=1, source_target_pairs={{0,64},{16,80},{32,96},{48,112},{64,0},{80,16},{96,32},{112,48},{1... | collective-permute-start | bytes 1572872 | tf_op jit(solution)/shard_map/ppermute | solution.py:16
  65.0 2.7 %fusion.185 = f32[1024,256]{1,0:T(8,128)} fusion(bf16[1024,256]{1,0:T(8,128)(2,1)} %fusion.27, bf16[512,512]{1,0:T(8,128)(2,1)S(1)} %copy-done.13, bf16[512,512]{1,0:T(8,128)(2,1)S(1)} %copy-done.12, bf16[512,512]{1,0:T(8,128)(2,1)S(1)} %copy-done.11), kind=kOutput, calls=%fused_computation.208 | convolution fusion | flops 545259520 | bytes 3145728 | tf_op jit(solution)/shard_map/dot_general | solution.py:83
  67.8 0.7 collective-permute-start.6
  68.5 0.7 fusion.188
  69.3 6.7 %collective-permute-done.3 = bf16[1024,256]{1,0:T(8,128)(2,1)S(1)} collective-permute-done((bf16[1024,256]{1,0:T(8,128)(2,1)S(1)}, bf16[1024,256]{1,0:T(8,128)(2,1)S(1)}, u32[]{:S(2)}, u32[]{:S(2)}) %collective-permute-start.3) | collective-permute-done | bytes 524320 | tf_op jit(solution)/shard_map/ppermute | solution.py:16
  76.0 0.7 fusion.26
  77.0 2.1 %fusion.14 = bf16[128,8,640]{2,1,0:T(8,128)(2,1)} fusion(s32[512]{0:T(512)S(1)} %copy-done.44, bf16[512,128]{0,1:T(8,128)(2,1)S(1)} %copy-done.29, bf16[512,512]{0,1:T(8,128)(2,1)S(1)} %bitcast.102), kind=kOutput, calls=%fused_computation.24 | convolution fusion | flops 673579008 | bytes 1968128 | tf_op jit(solution)/shard_map/dot_general | solution.py:101
  79.1 16.1 %all-to-all-start = ((bf16[128,8,640]{2,1,0:T(8,128)(2,1)}), bf16[128,8,640]{2,1,0:T(8,128)(2,1)S(1)}, u32[]{:S(2)}, u32[]{:S(2)}) async-start(bf16[128,8,640]{2,1,0:T(8,128)(2,1)} %fusion.14), calls=%async_computation | async-start | bytes 2621440 | tf_op jit(solution)/shard_map/all_to_all | solution.py:54
  95.2 2.2 %fusion.28 = bf16[1024,256]{1,0:T(8,128)(2,1)S(1)} fusion(f32[1024,256]{1,0:T(8,128)} %fusion.185, bf16[1024,256]{1,0:T(8,128)(2,1)} %collective-permute-done.6, bf16[512,512]{1,0:T(8,128)(2,1)S(1)} %copy-done.4, bf16[512,512]{1,0:T(8,128)(2,1)S(1)} %copy-done.3, bf16[512,512]{1,0:T(8,128)(2,1)S(1)} %get-tuple-element.133), kind=kOutput, calls=%fused_computation.40 | convolution fusion | flops 545783808 | bytes 3670016 | tf_op jit(solution)/shard_map/dot_general | solution.py:84
  97.4 3.3 %collective-permute-start.7 = (bf16[1024,256]{1,0:T(8,128)(2,1)S(1)}, bf16[1024,256]{1,0:T(8,128)(2,1)S(1)}, u32[]{:S(2)}, u32[]{:S(2)}) collective-permute-start(bf16[1024,256]{1,0:T(8,128)(2,1)S(1)} %fusion.28), channel_id=1, source_target_pairs={{0,64},{16,80},{32,96},{48,112},{64,0},{80,16},{96,32},{112,48},{1... | collective-permute-start | bytes 1572872 | tf_op jit(solution)/shard_map/ppermute | solution.py:16
  101.5 24.0 %collective-permute-done.7 = bf16[1024,256]{1,0:T(8,128)(2,1)S(1)} collective-permute-done((bf16[1024,256]{1,0:T(8,128)(2,1)S(1)}, bf16[1024,256]{1,0:T(8,128)(2,1)S(1)}, u32[]{:S(2)}, u32[]{:S(2)}) %collective-permute-start.7) | collective-permute-done | bytes 524320 | tf_op jit(solution)/shard_map/ppermute | solution.py:16
  125.5 0.7 fusion.29
  126.4 1.7 %fusion.15 = bf16[128,8,512]{2,1,0:T(8,128)(2,1)} fusion(bf16[512,512]{0,1:T(8,128)(2,1)S(1)} %bitcast.103, s32[512]{0:T(512)S(1)} %copy-done.44), kind=kOutput, calls=%fused_computation.25 | convolution fusion | flops 537919488 | bytes 1574912 | tf_op jit(solution)/shard_map/dot_general | solution.py:101
  128.2 5.9 %all-to-all-start.1 = ((bf16[128,8,512]{2,1,0:T(8,128)(2,1)}), bf16[128,8,512]{2,1,0:T(8,128)(2,1)S(1)}, u32[]{:S(2)}, u32[]{:S(2)}) async-start(bf16[128,8,512]{2,1,0:T(8,128)(2,1)} %fusion.15), calls=%async_computation.1 | async-start | bytes 2097152 | tf_op jit(solution)/shard_map/all_to_all | solution.py:54
  134.5 0.8 fusion.16
  135.5 17.4 %all-to-all-done.1 = bf16[128,8,512]{2,1,0:T(8,128)(2,1)S(1)} async-done(((bf16[128,8,512]{2,1,0:T(8,128)(2,1)}), bf16[128,8,512]{2,1,0:T(8,128)(2,1)S(1)}, u32[]{:S(2)}, u32[]{:S(2)}) %all-to-all-start.1) | async-done | bytes 1048608 | tf_op jit(solution)/shard_map/all_to_all | solution.py:54
  152.9 0.8 fusion.17
  153.9 1.1 maximum_bitcast_fusion
  (143 shorter events, 8.8 us)
Async XLA Ops:
  0.0 4.9 %copy-start = (bf16[2,512,512]{2,1,0:T(8,128)(2,1)S(1)}, bf16[2,512,512]{2,1,0:T(8,128)(2,1)}, u32[]{:S(2)}) copy-start(bf16[2,512,512]{2,1,0:T(8,128)(2,1)} %param.6) | copy-start | bytes 3145732
  2.2 3.3 %copy-start.30 = (bf16[3,1,2,2,512,8]{4,5,3,2,1,0:T(8,128)(2,1)S(1)}, bf16[3,1,2,2,512,8]{4,5,3,2,1,0:T(8,128)(2,1)}, u32[]{:S(2)}) copy-start(bf16[3,1,2,2,512,8]{4,5,3,2,1,0:T(8,128)(2,1)} %param.9) | copy-start | bytes 294916
  2.2 4.0 %copy-start.35 = (s32[3,1,2,512]{3,2,1,0:T(2,128)S(1)}, s32[3,1,2,512]{3,2,1,0:T(2,128)}, u32[]{:S(2)}) copy-start(s32[3,1,2,512]{3,2,1,0:T(2,128)} %param.8) | copy-start | bytes 36868
  2.2 4.6 %copy-start.42 = (bf16[2,512]{1,0:T(2,128)(2,1)S(1)}, bf16[2,512]{1,0:T(2,128)(2,1)}, u32[]{:S(2)}) copy-start(bf16[2,512]{1,0:T(2,128)(2,1)} %param.7) | copy-start | bytes 6148
  2.2 30.5 %collective-permute-start = (bf16[2,512,256]{2,1,0:T(8,128)(2,1)}, bf16[2,512,256]{2,1,0:T(8,128)(2,1)S(1)}, u32[]{:S(2)}, u32[]{:S(2)}) collective-permute-start(bf16[2,512,256]{2,1,0:T(8,128)(2,1)} %get-tuple-element.109), channel_id=1, source_target_pairs={{1,0},{2,1},{3,2},{4,3},{5,4},{6,5},{7,6},{8,7},{9,8},{10,9},{11,1... | collective-permute-start | bytes 1572872 | tf_op jit(solution)/shard_map/ppermute | solution.py:12
  3.6 33.8 %collective-permute-start.4 = (bf16[2,512,256]{2,1,0:T(8,128)(2,1)S(1)}, bf16[2,512,256]{2,1,0:T(8,128)(2,1)}, u32[]{:S(2)}, u32[]{:S(2)}) collective-permute-start(bf16[2,512,256]{2,1,0:T(8,128)(2,1)S(1)} %get-tuple-element.110), channel_id=1, source_target_pairs={{1,0},{2,1},{3,2},{4,3},{5,4},{6,5},{7,6},{8,7},{9,8},{10,9},{11,1... | collective-permute-start | bytes 1572872 | tf_op jit(solution)/shard_map/ppermute | solution.py:12
  8.0 3.1 %copy-start.43 = (bf16[512]{0:T(512)(128)(2,1)S(1)}, bf16[512]{0:T(512)(128)(2,1)}, u32[]{:S(2)}) copy-start(bf16[512]{0:T(512)(128)(2,1)} %get-tuple-element.102) | copy-start | bytes 3076
  11.1 2.0 %copy-start.34 = (s32[1,1,512,1]{2,3,1,0:T(1,128)S(1)}, s32[1,1,512,1]{2,3,1,0:T(1,128)}, u32[]{:S(2)}) copy-start(s32[1,1,512,1]{2,3,1,0:T(1,128)} %param.10) | copy-start | bytes 6148
  11.9 2.5 %copy-start.45 = (s32[1,1,512]{2,1,0:T(1,128)S(1)}, s32[1,1,512]{2,1,0:T(1,128)}, u32[]{:S(2)}) copy-start(s32[1,1,512]{2,1,0:T(1,128)} %param.11) | copy-start | bytes 6148
  11.9 2.5 %copy-start.46 = (pred[128]{0:T(512)(128)(4,1)S(1)}, pred[128]{0:T(512)(128)(4,1)}, u32[]{:S(2)}) copy-start(pred[128]{0:T(512)(128)(4,1)} %get-tuple-element.149) | copy-start | bytes 388
  11.9 2.5 %copy-start.47 = (pred[128]{0:T(512)(128)(4,1)S(1)}, pred[128]{0:T(512)(128)(4,1)}, u32[]{:S(2)}) copy-start(pred[128]{0:T(512)(128)(4,1)} %get-tuple-element.150) | copy-start | bytes 388
  11.9 3.5 %copy-start.32 = (bf16[512,8]{0,1:T(8,128)(2,1)S(1)}, bf16[512,8]{0,1:T(8,128)(2,1)}, u32[]{:S(2)}) copy-start(bf16[512,8]{0,1:T(8,128)(2,1)} %get-tuple-element.116) | copy-start | bytes 24580
  11.9 3.4 %copy-start.33 = (bf16[512,8]{0,1:T(8,128)(2,1)S(1)}, bf16[512,8]{0,1:T(8,128)(2,1)}, u32[]{:S(2)}) copy-start(bf16[512,8]{0,1:T(8,128)(2,1)} %get-tuple-element.117) | copy-start | bytes 24580
  11.9 3.5 %copy-start.31 = (bf16[512,8]{0,1:T(8,128)(2,1)S(1)}, bf16[512,8]{0,1:T(8,128)(2,1)}, u32[]{:S(2)}) copy-start(bf16[512,8]{0,1:T(8,128)(2,1)} %get-tuple-element.115) | copy-start | bytes 24580
  12.0 4.0 %copy-start.41 = (s32[1,1,1,512]{3,2,1,0:T(1,128)S(1)}, s32[1,1,1,512]{3,2,1,0:T(1,128)}, u32[]{:S(2)}) copy-start(s32[1,1,1,512]{3,2,1,0:T(1,128)} %get-tuple-element.125) | copy-start | bytes 6148
  13.5 5.2 %copy-start.40 = (s32[1,1,1,512]{3,2,1,0:T(1,128)S(1)}, s32[1,1,1,512]{3,2,1,0:T(1,128)}, u32[]{:S(2)}) copy-start(s32[1,1,1,512]{3,2,1,0:T(1,128)} %get-tuple-element.124) | copy-start | bytes 6148
  15.9 5.6 %copy-start.39 = (s32[1,1,1,512]{3,2,1,0:T(1,128)S(1)}, s32[1,1,1,512]{3,2,1,0:T(1,128)}, u32[]{:S(2)}) copy-start(s32[1,1,1,512]{3,2,1,0:T(1,128)} %get-tuple-element.126) | copy-start | bytes 6148
  18.7 5.6 %copy-start.38 = (s32[1,1,1,512]{3,2,1,0:T(1,128)S(1)}, s32[1,1,1,512]{3,2,1,0:T(1,128)}, u32[]{:S(2)}) copy-start(s32[1,1,1,512]{3,2,1,0:T(1,128)} %get-tuple-element.128) | copy-start | bytes 6148
  21.5 5.5 %copy-start.37 = (s32[1,1,1,512]{3,2,1,0:T(1,128)S(1)}, s32[1,1,1,512]{3,2,1,0:T(1,128)}, u32[]{:S(2)}) copy-start(s32[1,1,1,512]{3,2,1,0:T(1,128)} %get-tuple-element.127) | copy-start | bytes 6148
  24.3 5.5 %copy-start.36 = (s32[1,1,1,512]{3,2,1,0:T(1,128)S(1)}, s32[1,1,1,512]{3,2,1,0:T(1,128)}, u32[]{:S(2)}) copy-start(s32[1,1,1,512]{3,2,1,0:T(1,128)} %get-tuple-element.123) | copy-start | bytes 6148
  36.0 9.3 %collective-permute-start.1 = (bf16[1024,256]{1,0:T(8,128)(2,1)}, bf16[1024,256]{1,0:T(8,128)(2,1)}, u32[]{:S(2)}, u32[]{:S(2)}) collective-permute-start(bf16[1024,256]{1,0:T(8,128)(2,1)} %bitcast.20), channel_id=1, source_target_pairs={{0,16},{16,0},{32,48},{48,32},{64,80},{80,64},{96,112},{112,96},{1... | collective-permute-start | bytes 1572872 | tf_op jit(solution)/shard_map/ppermute | solution.py:16
  39.6 2.0 %copy-start.5 = (bf16[512,512]{1,0:T(8,128)(2,1)S(1)}, bf16[512,512]{1,0:T(8,128)(2,1)}, u32[]{:S(2)}) copy-start(bf16[512,512]{1,0:T(8,128)(2,1)} %get-tuple-element.139) | copy-start | bytes 1572868
  39.6 2.0 %copy-start.6 = (bf16[512,512]{1,0:T(8,128)(2,1)S(1)}, bf16[512,512]{1,0:T(8,128)(2,1)}, u32[]{:S(2)}) copy-start(bf16[512,512]{1,0:T(8,128)(2,1)} %get-tuple-element.140) | copy-start | bytes 1572868
  39.6 2.0 %copy-start.7 = (bf16[512,512]{1,0:T(8,128)(2,1)S(1)}, bf16[512,512]{1,0:T(8,128)(2,1)}, u32[]{:S(2)}) copy-start(bf16[512,512]{1,0:T(8,128)(2,1)} %get-tuple-element.148) | copy-start | bytes 1572868
  41.6 8.4 %collective-permute-start.5 = (bf16[1024,256]{1,0:T(8,128)(2,1)}, bf16[1024,256]{1,0:T(8,128)(2,1)S(1)}, u32[]{:S(2)}, u32[]{:S(2)}) collective-permute-start(bf16[1024,256]{1,0:T(8,128)(2,1)} %bitcast.43), channel_id=1, source_target_pairs={{0,16},{16,0},{32,48},{48,32},{64,80},{80,64},{96,112},{112,96},{1... | collective-permute-start | bytes 1572872 | tf_op jit(solution)/shard_map/ppermute | solution.py:16
  43.4 1.9 %copy-start.8 = (bf16[512,512]{1,0:T(8,128)(2,1)S(1)}, bf16[512,512]{1,0:T(8,128)(2,1)}, u32[]{:S(2)}) copy-start(bf16[512,512]{1,0:T(8,128)(2,1)} %get-tuple-element.137) | copy-start | bytes 1572868
  45.4 3.9 %copy-start.11 = (bf16[512,512]{1,0:T(8,128)(2,1)S(1)}, bf16[512,512]{1,0:T(8,128)(2,1)}, u32[]{:S(2)}) copy-start(bf16[512,512]{1,0:T(8,128)(2,1)} %get-tuple-element.135) | copy-start | bytes 1572868
  45.4 3.9 %copy-start.12 = (bf16[512,512]{1,0:T(8,128)(2,1)S(1)}, bf16[512,512]{1,0:T(8,128)(2,1)}, u32[]{:S(2)}) copy-start(bf16[512,512]{1,0:T(8,128)(2,1)} %get-tuple-element.136) | copy-start | bytes 1572868
  45.4 3.9 %copy-start.13 = (bf16[512,512]{1,0:T(8,128)(2,1)S(1)}, bf16[512,512]{1,0:T(8,128)(2,1)}, u32[]{:S(2)}) copy-start(bf16[512,512]{1,0:T(8,128)(2,1)} %get-tuple-element.146) | copy-start | bytes 1572868
  47.3 13.8 %collective-permute-start.2 = (bf16[1024,256]{1,0:T(8,128)(2,1)S(1)}, bf16[1024,256]{1,0:T(8,128)(2,1)S(1)}, u32[]{:S(2)}, u32[]{:S(2)}) collective-permute-start(bf16[1024,256]{1,0:T(8,128)(2,1)S(1)} %fusion.24), channel_id=1, source_target_pairs={{0,32},{16,48},{32,0},{48,16},{64,96},{80,112},{96,64},{112,80},{1... | collective-permute-start | bytes 1572872 | tf_op jit(solution)/shard_map/ppermute | solution.py:16
  50.0 11.1 %copy-start.3 = (bf16[512,512]{1,0:T(8,128)(2,1)S(1)}, bf16[512,512]{1,0:T(8,128)(2,1)}, u32[]{:S(2)}) copy-start(bf16[512,512]{1,0:T(8,128)(2,1)} %get-tuple-element.134) | copy-start | bytes 1572868
  50.0 11.1 %copy-start.4 = (bf16[512,512]{1,0:T(8,128)(2,1)S(1)}, bf16[512,512]{1,0:T(8,128)(2,1)}, u32[]{:S(2)}) copy-start(bf16[512,512]{1,0:T(8,128)(2,1)} %get-tuple-element.145) | copy-start | bytes 1572868
  61.8 6.7 %copy-start.14 = (bf16[512,512]{1,0:T(8,128)(2,1)S(1)}, bf16[512,512]{1,0:T(8,128)(2,1)}, u32[]{:S(2)}) copy-start(bf16[512,512]{1,0:T(8,128)(2,1)} %get-tuple-element.131) | copy-start | bytes 1572868
  61.8 6.7 %copy-start.15 = (bf16[512,512]{1,0:T(8,128)(2,1)S(1)}, bf16[512,512]{1,0:T(8,128)(2,1)}, u32[]{:S(2)}) copy-start(bf16[512,512]{1,0:T(8,128)(2,1)} %get-tuple-element.132) | copy-start | bytes 1572868
  61.8 6.7 %copy-start.17 = (bf16[512,512]{1,0:T(8,128)(2,1)S(1)}, bf16[512,512]{1,0:T(8,128)(2,1)}, u32[]{:S(2)}) copy-start(bf16[512,512]{1,0:T(8,128)(2,1)} %get-tuple-element.144) | copy-start | bytes 1572868
  61.8 14.2 %collective-permute-start.3 = (bf16[1024,256]{1,0:T(8,128)(2,1)S(1)}, bf16[1024,256]{1,0:T(8,128)(2,1)S(1)}, u32[]{:S(2)}, u32[]{:S(2)}) collective-permute-start(bf16[1024,256]{1,0:T(8,128)(2,1)S(1)} %fusion.25), channel_id=1, source_target_pairs={{0,64},{16,80},{32,96},{48,112},{64,0},{80,16},{96,32},{112,48},{1... | collective-permute-start | bytes 1572872 | tf_op jit(solution)/shard_map/ppermute | solution.py:16
  67.8 27.4 %collective-permute-start.6 = (bf16[1024,256]{1,0:T(8,128)(2,1)}, bf16[1024,256]{1,0:T(8,128)(2,1)}, u32[]{:S(2)}, u32[]{:S(2)}) collective-permute-start(bf16[1024,256]{1,0:T(8,128)(2,1)} %fusion.27), channel_id=1, source_target_pairs={{0,32},{16,48},{32,0},{48,16},{64,96},{80,112},{96,64},{112,80},{1... | collective-permute-start | bytes 1572872 | tf_op jit(solution)/shard_map/ppermute | solution.py:16
  68.5 7.5 %copy-start.19 = (bf16[512,512]{1,0:T(8,128)(2,1)S(1)}, bf16[512,512]{1,0:T(8,128)(2,1)}, u32[]{:S(2)}) copy-start(bf16[512,512]{1,0:T(8,128)(2,1)} %get-tuple-element.129) | copy-start | bytes 1572868
  68.5 7.5 %copy-start.21 = (bf16[512,512]{1,0:T(8,128)(2,1)S(1)}, bf16[512,512]{1,0:T(8,128)(2,1)}, u32[]{:S(2)}) copy-start(bf16[512,512]{1,0:T(8,128)(2,1)} %get-tuple-element.130) | copy-start | bytes 1572868
  68.5 7.5 %copy-start.23 = (bf16[512,512]{1,0:T(8,128)(2,1)S(1)}, bf16[512,512]{1,0:T(8,128)(2,1)}, u32[]{:S(2)}) copy-start(bf16[512,512]{1,0:T(8,128)(2,1)} %get-tuple-element.143) | copy-start | bytes 1572868
  79.1 49.1 %all-to-all-start = ((bf16[128,8,640]{2,1,0:T(8,128)(2,1)}), bf16[128,8,640]{2,1,0:T(8,128)(2,1)S(1)}, u32[]{:S(2)}, u32[]{:S(2)}) async-start(bf16[128,8,640]{2,1,0:T(8,128)(2,1)} %fusion.14), calls=%async_computation | async-start | bytes 2621440 | tf_op jit(solution)/shard_map/all_to_all | solution.py:54
  95.2 5.6 %copy-start.16 = (bf16[512,512]{1,0:T(8,128)(2,1)S(1)}, bf16[512,512]{1,0:T(8,128)(2,1)}, u32[]{:S(2)}) copy-start(bf16[512,512]{1,0:T(8,128)(2,1)} %get-tuple-element.132) | copy-start | bytes 1572868
  95.2 5.6 %copy-start.18 = (bf16[512,512]{1,0:T(8,128)(2,1)S(1)}, bf16[512,512]{1,0:T(8,128)(2,1)}, u32[]{:S(2)}) copy-start(bf16[512,512]{1,0:T(8,128)(2,1)} %get-tuple-element.144) | copy-start | bytes 1572868
  97.4 28.1 %copy-start.20 = (bf16[512,512]{1,0:T(8,128)(2,1)S(1)}, bf16[512,512]{1,0:T(8,128)(2,1)}, u32[]{:S(2)}) copy-start(bf16[512,512]{1,0:T(8,128)(2,1)} %get-tuple-element.129) | copy-start | bytes 1572868
  97.4 28.1 %copy-start.22 = (bf16[512,512]{1,0:T(8,128)(2,1)S(1)}, bf16[512,512]{1,0:T(8,128)(2,1)}, u32[]{:S(2)}) copy-start(bf16[512,512]{1,0:T(8,128)(2,1)} %get-tuple-element.130) | copy-start | bytes 1572868
  97.4 28.1 %copy-start.24 = (bf16[512,512]{1,0:T(8,128)(2,1)S(1)}, bf16[512,512]{1,0:T(8,128)(2,1)}, u32[]{:S(2)}) copy-start(bf16[512,512]{1,0:T(8,128)(2,1)} %get-tuple-element.143) | copy-start | bytes 1572868
  97.4 28.1 %collective-permute-start.7 = (bf16[1024,256]{1,0:T(8,128)(2,1)S(1)}, bf16[1024,256]{1,0:T(8,128)(2,1)S(1)}, u32[]{:S(2)}, u32[]{:S(2)}) collective-permute-start(bf16[1024,256]{1,0:T(8,128)(2,1)S(1)} %fusion.28), channel_id=1, source_target_pairs={{0,64},{16,80},{32,96},{48,112},{64,0},{80,16},{96,32},{112,48},{1... | collective-permute-start | bytes 1572872 | tf_op jit(solution)/shard_map/ppermute | solution.py:16
  128.2 24.8 %all-to-all-start.1 = ((bf16[128,8,512]{2,1,0:T(8,128)(2,1)}), bf16[128,8,512]{2,1,0:T(8,128)(2,1)S(1)}, u32[]{:S(2)}, u32[]{:S(2)}) async-start(bf16[128,8,512]{2,1,0:T(8,128)(2,1)} %fusion.15), calls=%async_computation.1 | async-start | bytes 2097152 | tf_op jit(solution)/shard_map/all_to_all | solution.py:54
  (10 other events, 12.1 us)

commit v5 on v1

--- a/solution.py
+++ b/solution.py
@@ -50,14 +50,6 @@
     return jnp.sum((jnp.cumsum(onehot, axis=0) - 1) * onehot, axis=1)
 
 
-def route_rows(send, labels):
-    got = lax.all_to_all(send, ("sub", "rng"), split_axis=0, concat_axis=0, tiled=True)
-    table = lax.all_gather(labels.astype(jnp.float32), ("sub", "rng"), axis=0)
-    me = lax.axis_index("sub") * lax.axis_size("rng") + lax.axis_index("rng")
-    marks = lax.dynamic_index_in_dim(table, me, axis=1, keepdims=False).astype(jnp.int32)
-    return (got, marks)
-
-
 def on_device(echoes, chirp, offsets, weights, owners, targets):
     p_dev = echoes.shape[1]
     r_dev = echoes.shape[2]
@@ -73,6 +65,11 @@
     pieces = block_out.reshape(p_dev, 2, RBLK)
     image = pieces.transpose(1, 0, 2).reshape(2 * p_dev, r_dev)
     section_count = offsets.shape[0]
+    dest = owners.reshape(p_dev)
+    aim = targets.reshape(p_dev)
+    slot = dest * capacity + group_slots(dest, devices)
+    pick = jnp.arange(devices * capacity, dtype=jnp.int32)[:, None] == slot[None, :]
+    labels = jnp.sum(jnp.where(pick, aim[None, :] + 1, 0), axis=1) - 1
     for section in range(section_count):
         partner = from_partner(image, "sub", section)
         mine = merge_matrix(offsets[section, 0, 0], weights[section, 0, 0])
@@ -80,17 +77,17 @@
         merged = jnp.dot(mine, image, preferred_element_type=jnp.float32)
         merged = merged + jnp.dot(theirs, partner, preferred_element_type=jnp.float32)
         image = merged.astype(jnp.bfloat16)
+        if section == 0:
+            labels, image = lax.optimization_barrier((labels, image))
+            marks = lax.all_to_all(
+                labels.reshape(devices, capacity), ("sub", "rng"), split_axis=0, concat_axis=0, tiled=True
+            )
     rows = image.reshape(2, p_dev, r_dev).transpose(1, 0, 2).reshape(p_dev, 2 * r_dev)
-    dest = owners.reshape(p_dev)
-    aim = targets.reshape(p_dev)
-    slot = dest * capacity + group_slots(dest, devices)
-    pick = jnp.arange(devices * capacity, dtype=jnp.int32)[:, None] == slot[None, :]
     send = jnp.dot(pick.astype(jnp.bfloat16), rows, preferred_element_type=jnp.float32).astype(
         jnp.bfloat16
     )
-    labels = jnp.sum(jnp.where(pick, aim[None, :] + 1, 0), axis=1) - 1
-    got, marks = route_rows(
-        send.reshape(devices, capacity, 2 * r_dev), labels.reshape(devices, capacity)
+    got = lax.all_to_all(
+        send.reshape(devices, capacity, 2 * r_dev), ("sub", "rng"), split_axis=0, concat_axis=0, tiled=True
     )
     got_flat = got.reshape(devices * capacity, 2 * r_dev)
     mark_flat = marks.reshape(devices * capacity)

time: 185 us -> 144 us (0.78)
  blocking collectives: 71.8 us -> 0 us
  waiting for transfers between devices: 44.2 us -> 63.3 us
  starting transfers between devices: 21.4 us -> 31.3 us
  matrix products: 13.8 us -> 17.2 us
    all_gather x1 -> x0, blocking collectives: 71.8 us -> none  [route_rows(): table = lax.all_gather(labels.astype(jnp.float32), ('sub', 'rng'), axis=0)]
    all_to_all x1 -> x2, waiting for transfers between devices: 0.01 us -> 28.3 us  [the longest x1 28.3 us: on_device(): lax.all_to_all(send.reshape(devices, capacity, 2 * r_dev), ('sub', 'rng')...]
    ppermute x3, waiting for transfers between devices: 39.4 us -> 27 us  [from_partner(): lax.ppermute(value, axis, [(i, i ^ 1 << apart) for i in range(lax.axis_si...]
    all_to_all x1 -> x2, starting transfers between devices: 12.9 us -> 22.8 us  [the longest x1 12.8 us: on_device(): lax.all_to_all(send.reshape(devices, capacity, 2 * r_dev), ('sub', 'rng')...]
    ppermute x1, waiting for transfers between devices: 4.76 us -> 8 us  [shifted(): lax.ppermute(value, axis, [(source, source + steps) for source in range(f...]
    convert_element_type x2 -> x0, other arithmetic: 2.4 us -> none  [the longest x1 2.39 us: route_rows(): lax.dynamic_index_in_dim(table, me, axis=1, keepdims=False)]
    dot_general x3, matrix products: 3.73 us -> 5.93 us  [on_device(): jnp.dot(theirs, partner, preferred_element_type=jnp.float32)]
  transfers between devices with their start and end apart: 5 -> 6, of which waited for: 3 -> 4; matrix products, arithmetic and copies ran while one was open for 16% -> 24% of each run, Pallas kernels for 0% -> 0%
where the time goes in v5:
time: 144 us; the launch traced here: 143 us
  waiting for transfers between devices  63.3 us (44%)
  starting transfers between devices  31.3 us (22%)
  local copies, waits for them, and re-layouts  17.8 us (12%)
  matrix products  17.2 us (12%)
  other arithmetic  13.3 us (9%)
    all_to_all x1, waiting for transfers between devices, on_device(): lax.all_to_all(send.reshape(devices, capacity, 2 * r_dev), ('sub', 'rng')...  28.3 us
    ppermute x3, waiting for transfers between devices, from_partner(): lax.ppermute(value, axis, [(i, i ^ 1 << apart) for i in range(lax.axis_si...  27 us
    all_to_all x1, starting transfers between devices, on_device(): lax.all_to_all(send.reshape(devices, capacity, 2 * r_dev), ('sub', 'rng')...  12.8 us
    neg x6, other arithmetic, merge_matrix(): upper = jnp.concatenate([g_real, -g_imag], axis=1)  10.4 us
    all_to_all x1, starting transfers between devices, on_device(): lax.all_to_all(labels.reshape(devices, capacity), ('sub', 'rng'), split_a...  10 us
    ppermute x1, waiting for transfers between devices, shifted(): lax.ppermute(value, axis, [(source, source + steps) for source in range(f...  8 us
    ppermute x3, starting transfers between devices, from_partner(): lax.ppermute(value, axis, [(i, i ^ 1 << apart) for i in range(lax.axis_si...  7.02 us
    dot_general x3, matrix products, on_device(): jnp.dot(theirs, partner, preferred_element_type=jnp.float32)  5.93 us
  transfers between devices with their start and end apart: 6, of which 4 were waited for; matrix products, arithmetic and copies ran while one was open for 24% of the time, Pallas kernels for 0%

profile of v5, /device:TPU:1, one launch (start us, length us, event | category | flops | bytes accessed | tf_op | source)
XLA Modules:
  0.0 143.1 jit_solution(833513048283422886)
XLA Ops:
  0.0 1.4 collective-permute-start
  1.4 1.4 constant_dynamic-update-slice_fusion.1
  2.9 0.1 copy.20
  3.0 0.2 fusion.223
  3.3 0.2 fusion.222
  3.7 2.3 %tile.9 = bf16[524800]{0:T(1024)(128)(2,1)} reshape(bf16[512,1025]{1,0:T(8,128)(2,1)S(1)} %tile.8) | data formatting | bytes 2099200 | tf_op jit(solution)/shard_map/tile | solution.py:25
  6.0 1.2 slice-done
  7.2 1.3 reshape.106
  8.6 2.3 %tile.21 = bf16[524800]{0:T(1024)(128)(2,1)} reshape(bf16[512,1025]{1,0:T(8,128)(2,1)S(1)} %tile.20) | data formatting | bytes 2099200 | tf_op jit(solution)/shard_map/tile | solution.py:25
  10.9 1.2 slice-done.1
  12.1 1.3 reshape.107
  13.4 1.3 bitcast_negate_fusion
  14.7 0.3 select_reduce_fusion
  15.1 0.1 slice_reduce_fusion.71
  15.2 0.1 slice_reduce_fusion.39
  15.3 1.7 %fusion.233 = (bf16[512,512]{1,0:T(8,128)(2,1)S(1)}, bf16[512,512]{1,0:T(8,128)(2,1)S(1)}, bf16[512,512]{1,0:T(8,128)(2,1)S(1)}) fusion(bf16[512]{0:T(512)(128)(2,1)S(1)} %get-tuple-element.90, bf16[512]{0:T(512)(128)(2,1)S(1)} %get-tuple-element.91, bf16[512]{0:T(512)(128)(2,1)S(1)} %get-tuple-element.92, bf16[512]{0:T(512)(128)(2,1)S(1)} %get-tuple-element.93, ...), kind=kLoop, calls=%fused_computation.359 | loop fusion | flops 7340032 | bytes 1591296 | tf_op jit(solution)/shard_map/neg | solution.py:43
  17.1 1.7 %fusion.234 = (bf16[512,512]{1,0:T(8,128)(2,1)S(1)}, bf16[512,512]{1,0:T(8,128)(2,1)S(1)}, bf16[512,512]{1,0:T(8,128)(2,1)S(1)}) fusion(bf16[512]{0:T(512)(128)(2,1)S(1)} %get-tuple-element.74, bf16[512]{0:T(512)(128)(2,1)S(1)} %get-tuple-element.75, bf16[512]{0:T(512)(128)(2,1)S(1)} %get-tuple-element.76, bf16[512]{0:T(512)(128)(2,1)S(1)} %get-tuple-element.77, ...), kind=kLoop, calls=%fused_computation.360 | loop fusion | flops 7340032 | bytes 1591296 | tf_op jit(solution)/shard_map/neg | solution.py:43
  18.8 8.0 %collective-permute-done = bf16[2,512,512]{2,1,0:T(8,128)(2,1)} collective-permute-done((bf16[2,512,512]{2,1,0:T(8,128)(2,1)}, bf16[2,512,512]{2,1,0:T(8,128)(2,1)}, u32[]{:S(2)}, u32[]{:S(2)}) %collective-permute-start) | collective-permute-done | bytes 1048608 | tf_op jit(solution)/shard_map/ppermute | solution.py:12
  26.9 1.4 constant_dynamic-update-slice_fusion
  28.3 0.2 slice_bitcast_fusion.1
  28.4 1.0 copy-done
  29.5 0.3 copy-done.1
  29.8 2.4 %fusion.68 = bf16[512,1024]{1,0:T(8,128)(2,1)S(1)} fusion(bf16[1024,512]{0,1:T(8,128)(2,1)S(1)} %bitcast.82, bf16[1024,512]{0,1:T(8,128)(2,1)S(1)} %bitcast.81, bf16[1024,512]{0,1:T(8,128)(2,1)S(1)} %bitcast_negate_fusion, bf16[512,1024]{1,0:T(8,128)(2,1)S(1)} %get-tuple-element.108, bf16[512,1024]{1,0:T(8,128)(2,1)S(1)} %get-tuple-element.107), kind=kOutput, calls=%fused_computation.69 | convolution fusion | flops 2168979456 | bytes 6291456 | tf_op jit(solution)/shard_map/dot_general | solution.py:64
  32.2 1.7 %collective-permute-start.1 = (bf16[1024,512]{1,0:T(8,128)(2,1)S(1)}, bf16[1024,512]{1,0:T(8,128)(2,1)S(1)}, u32[]{:S(2)}, u32[]{:S(2)}) collective-permute-start(bf16[1024,512]{1,0:T(8,128)(2,1)S(1)} %bitcast.83), channel_id=1, source_target_pairs={{0,16},{16,0},{32,48},{48,32},{64,80},{80,64},{96,112},{112,96},{1... | collective-permute-start | bytes 3145736 | tf_op jit(solution)/shard_map/ppermute | solution.py:16
  34.0 1.7 %fusion.236 = (bf16[512,512]{1,0:T(8,128)(2,1)S(1)}, bf16[512,512]{1,0:T(8,128)(2,1)S(1)}, bf16[512,512]{1,0:T(8,128)(2,1)S(1)}) fusion(bf16[512]{0:T(512)(128)(2,1)S(1)} %get-tuple-element.58, bf16[512]{0:T(512)(128)(2,1)S(1)} %get-tuple-element.59, bf16[512]{0:T(512)(128)(2,1)S(1)} %get-tuple-element.60, bf16[512]{0:T(512)(128)(2,1)S(1)} %get-tuple-element.61, ...), kind=kLoop, calls=%fused_computation.362 | loop fusion | flops 7340032 | bytes 1591296 | tf_op jit(solution)/shard_map/neg | solution.py:43
  35.7 1.2 fusion.8
  36.9 1.2 add_convert_fusion.2
  38.2 2.1 %collective-permute-start.2 = (bf16[1024,512]{1,0:T(8,128)(2,1)S(1)}, bf16[1024,512]{1,0:T(8,128)(2,1)S(1)}, u32[]{:S(2)}, u32[]{:S(2)}) collective-permute-start(bf16[1024,512]{1,0:T(8,128)(2,1)S(1)} %add_convert_fusion.2), channel_id=1, source_target_pairs={{0,32},{16,48},{32,0},{48,16},{64,96},{80,112},{96,64},{112,80},{1... | collective-permute-start | bytes 3145736 | tf_op jit(solution)/shard_map/ppermute | solution.py:16
  40.5 1.7 %fusion.237 = (bf16[512,512]{1,0:T(8,128)(2,1)S(1)}, bf16[512,512]{1,0:T(8,128)(2,1)S(1)}, bf16[512,512]{1,0:T(8,128)(2,1)S(1)}) fusion(bf16[512]{0:T(512)(128)(2,1)S(1)} %get-tuple-element.42, bf16[512]{0:T(512)(128)(2,1)S(1)} %get-tuple-element.43, bf16[512]{0:T(512)(128)(2,1)S(1)} %get-tuple-element.44, bf16[512]{0:T(512)(128)(2,1)S(1)} %get-tuple-element.45, ...), kind=kLoop, calls=%fused_computation.363 | loop fusion | flops 7340032 | bytes 1591296 | tf_op jit(solution)/shard_map/neg | solution.py:43
  42.3 1.2 fusion.35
  43.5 20.3 %collective-permute-done.2 = bf16[1024,512]{1,0:T(8,128)(2,1)S(1)} collective-permute-done((bf16[1024,512]{1,0:T(8,128)(2,1)S(1)}, bf16[1024,512]{1,0:T(8,128)(2,1)S(1)}, u32[]{:S(2)}, u32[]{:S(2)}) %collective-permute-start.2) | collective-permute-done | bytes 1048608 | tf_op jit(solution)/shard_map/ppermute | solution.py:16
  63.8 2.2 %add_convert_fusion.1 = bf16[1024,512]{1,0:T(8,128)(2,1)} fusion(f32[1024,512]{1,0:T(8,128)S(1)} %fusion.35, bf16[1024,512]{1,0:T(8,128)(2,1)S(1)} %collective-permute-done.2, bf16[512,512]{1,0:T(8,128)(2,1)S(1)} %get-tuple-element.141, bf16[512,512]{1,0:T(8,128)(2,1)S(1)} %get-tuple-element.132, bf16[512,512]{1,0:T(8,128)(2,1)S(1)} %get-tuple-element.131), kind=kOutput, calls=%fused_computation.63 | convolution fusion | flops 1083179008 | bytes 5767168 | tf_op jit(solution)/shard_map/dot_general | solution.py:78
  66.0 3.2 %collective-permute-start.3 = (bf16[1024,512]{1,0:T(8,128)(2,1)}, bf16[1024,512]{1,0:T(8,128)(2,1)}, u32[]{:S(2)}, u32[]{:S(2)}) collective-permute-start(bf16[1024,512]{1,0:T(8,128)(2,1)} %add_convert_fusion.1), channel_id=1, source_target_pairs={{0,64},{16,80},{32,96},{48,112},{64,0},{80,16},{96,32},{112,48},{1... | collective-permute-start | bytes 3145736 | tf_op jit(solution)/shard_map/ppermute | solution.py:16
  69.2 1.7 %fusion.235 = (bf16[512,512]{1,0:T(8,128)(2,1)S(1)}, bf16[512,512]{1,0:T(8,128)(2,1)S(1)}, bf16[512,512]{1,0:T(8,128)(2,1)S(1)}) fusion(bf16[512]{0:T(512)(128)(2,1)S(1)} %get-tuple-element.26, bf16[512]{0:T(512)(128)(2,1)S(1)} %get-tuple-element.27, bf16[512]{0:T(512)(128)(2,1)S(1)} %get-tuple-element.28, bf16[512]{0:T(512)(128)(2,1)S(1)} %get-tuple-element.29, ...), kind=kLoop, calls=%fused_computation.361 | loop fusion | flops 7340032 | bytes 1591296 | tf_op jit(solution)/shard_map/neg | solution.py:43
  71.0 1.7 %fusion.238 = (bf16[512,512]{1,0:T(8,128)(2,1)S(1)}, bf16[512,512]{1,0:T(8,128)(2,1)S(1)}, bf16[512,512]{1,0:T(8,128)(2,1)S(1)}) fusion(bf16[512]{0:T(512)(128)(2,1)S(1)} %get-tuple-element.10, bf16[512]{0:T(512)(128)(2,1)S(1)} %get-tuple-element.11, bf16[512]{0:T(512)(128)(2,1)S(1)} %get-tuple-element.12, bf16[512]{0:T(512)(128)(2,1)S(1)} %get-tuple-element.13, ...), kind=kLoop, calls=%fused_computation.364 | loop fusion | flops 7340032 | bytes 1591296 | tf_op jit(solution)/shard_map/neg | solution.py:43
  72.7 0.7 all_to_all.9
  73.4 10.0 %all-to-all-start = ((s32[128,1,8]{2,1,0:T(1,128)}), s32[128,1,8]{2,1,0:T(1,128)S(1)}, u32[]{:S(2)}, u32[]{:S(2)}) async-start(s32[128,1,8]{2,1,0:T(1,128)} %bitcast.19), calls=%async_computation | async-start | bytes 131072 | tf_op jit(solution)/shard_map/all_to_all | solution.py:82
  83.4 2.5 %fusion.27 = f32[1024,512]{1,0:T(8,128)S(1)} fusion(bf16[1024,512]{1,0:T(8,128)(2,1)} %add_convert_fusion.1, bf16[512,512]{1,0:T(8,128)(2,1)S(1)} %get-tuple-element.140, bf16[512,512]{1,0:T(8,128)(2,1)S(1)} %get-tuple-element.130, bf16[512,512]{1,0:T(8,128)(2,1)S(1)} %get-tuple-element.129), kind=kOutput, calls=%fused_computation.27 | convolution fusion | flops 1082130432 | bytes 4718592 | tf_op jit(solution)/shard_map/dot_general | solution.py:77
  85.9 6.7 %collective-permute-done.3 = bf16[1024,512]{1,0:T(8,128)(2,1)} collective-permute-done((bf16[1024,512]{1,0:T(8,128)(2,1)}, bf16[1024,512]{1,0:T(8,128)(2,1)}, u32[]{:S(2)}, u32[]{:S(2)}) %collective-permute-start.3) | collective-permute-done | bytes 1048608 | tf_op jit(solution)/shard_map/ppermute | solution.py:16
  92.7 2.5 %add_convert_fusion = bf16[1024,512]{1,0:T(8,128)(2,1)S(1)} fusion(f32[1024,512]{1,0:T(8,128)S(1)} %fusion.27, bf16[1024,512]{1,0:T(8,128)(2,1)} %collective-permute-done.3, bf16[512,512]{1,0:T(8,128)(2,1)S(1)} %get-tuple-element.139, bf16[512,512]{1,0:T(8,128)(2,1)S(1)} %get-tuple-element.128, bf16[512,512]{1,0:T(8,128)(2,1)S(1)} %get-tuple-element.127), kind=kOutput, calls=%fused_computation.62 | convolution fusion | flops 1083179008 | bytes 5767168 | tf_op jit(solution)/shard_map/dot_general | solution.py:78
  95.1 0.5 copy.24
  95.7 2.6 %convert_bitcast_fusion = bf16[128,8,1024]{2,1,0:T(8,128)(2,1)} fusion(bf16[512,1024]{0,1:T(8,128)(2,1)S(1)} %bitcast.88, s32[512]{0:T(512)S(1)} %multiply_add_fusion), kind=kOutput, calls=%fused_computation.61 | convolution fusion | flops 1075314688 | bytes 3147776 | tf_op jit(solution)/shard_map/dot_general | solution.py:86
  98.3 12.8 %all-to-all-start.1 = ((bf16[128,8,1024]{2,1,0:T(8,128)(2,1)}), bf16[128,8,1024]{2,1,0:T(8,128)(2,1)S(1)}, u32[]{:S(2)}, u32[]{:S(2)}) async-start(bf16[128,8,1024]{2,1,0:T(8,128)(2,1)} %convert_bitcast_fusion), calls=%async_computation.1 | async-start | bytes 4194304 | tf_op jit(solution)/shard_map/all_to_all | solution.py:89
  111.2 0.5 broadcast.403
  111.7 0.8 reduce.199
  112.6 28.3 %all-to-all-done.1 = bf16[128,8,1024]{2,1,0:T(8,128)(2,1)S(1)} async-done(((bf16[128,8,1024]{2,1,0:T(8,128)(2,1)}), bf16[128,8,1024]{2,1,0:T(8,128)(2,1)S(1)}, u32[]{:S(2)}, u32[]{:S(2)}) %all-to-all-start.1) | async-done | bytes 2097184 | tf_op jit(solution)/shard_map/all_to_all | solution.py:89
  140.8 1.2 fusion.73
  142.1 1.0 copy.30
  (37 shorter events, 1.0 us)
Async XLA Ops:
  0.0 2.8 %copy-start.6 = (s32[1,1,512]{2,1,0:T(1,128)S(1)}, s32[1,1,512]{2,1,0:T(1,128)}, u32[]{:S(2)}) copy-start(s32[1,1,512]{2,1,0:T(1,128)} %param.11) | copy-start | bytes 6148
  0.0 2.8 %copy-start.3 = (s32[1,1,512,1]{2,3,1,0:T(1,128)S(1)}, s32[1,1,512,1]{2,3,1,0:T(1,128)}, u32[]{:S(2)}) copy-start(s32[1,1,512,1]{2,3,1,0:T(1,128)} %param.10) | copy-start | bytes 6148
  0.0 3.6 %copy-start.5 = (bf16[2,512]{1,0:T(2,128)(2,1)S(1)}, bf16[2,512]{1,0:T(2,128)(2,1)}, u32[]{:S(2)}) copy-start(bf16[2,512]{1,0:T(2,128)(2,1)} %param.7) | copy-start | bytes 6148
  0.0 26.8 %collective-permute-start = (bf16[2,512,512]{2,1,0:T(8,128)(2,1)}, bf16[2,512,512]{2,1,0:T(8,128)(2,1)}, u32[]{:S(2)}, u32[]{:S(2)}) collective-permute-start(bf16[2,512,512]{2,1,0:T(8,128)(2,1)} %param.6), channel_id=1, source_target_pairs={{1,0},{2,1},{3,2},{4,3},{5,4},{6,5},{7,6},{8,7},{9,8},{10,9},{11,1... | collective-permute-start | bytes 3145736 | tf_op jit(solution)/shard_map/ppermute | solution.py:12
  6.0 1.2 slice-start
  10.9 1.2 slice-start.1
  12.1 2.6 %copy-start.2 = (bf16[3,1,2,2,512,8]{4,5,3,2,1,0:T(8,128)(2,1)S(1)}, bf16[3,1,2,2,512,8]{4,5,3,2,1,0:T(8,128)(2,1)}, u32[]{:S(2)}) copy-start(bf16[3,1,2,2,512,8]{4,5,3,2,1,0:T(8,128)(2,1)} %param.9) | copy-start | bytes 294916
  12.1 3.2 %copy-start.4 = (s32[3,1,2,512]{3,2,1,0:T(2,128)S(1)}, s32[3,1,2,512]{3,2,1,0:T(2,128)}, u32[]{:S(2)}) copy-start(s32[3,1,2,512]{3,2,1,0:T(2,128)} %param.8) | copy-start | bytes 36868
  28.2 1.2 copy-start
  28.2 1.5 %copy-start.1 = (bf16[512,1024]{1,0:T(8,128)(2,1)S(1)}, bf16[512,1024]{1,0:T(8,128)(2,1)}, u32[]{:S(2)}) copy-start(bf16[512,1024]{1,0:T(8,128)(2,1)} %reshape.106) | copy-start | bytes 3145732
  32.2 4.7 %collective-permute-start.1 = (bf16[1024,512]{1,0:T(8,128)(2,1)S(1)}, bf16[1024,512]{1,0:T(8,128)(2,1)S(1)}, u32[]{:S(2)}, u32[]{:S(2)}) collective-permute-start(bf16[1024,512]{1,0:T(8,128)(2,1)S(1)} %bitcast.83), channel_id=1, source_target_pairs={{0,16},{16,0},{32,48},{48,32},{64,80},{80,64},{96,112},{112,96},{1... | collective-permute-start | bytes 3145736 | tf_op jit(solution)/shard_map/ppermute | solution.py:16
  38.2 25.6 %collective-permute-start.2 = (bf16[1024,512]{1,0:T(8,128)(2,1)S(1)}, bf16[1024,512]{1,0:T(8,128)(2,1)S(1)}, u32[]{:S(2)}, u32[]{:S(2)}) collective-permute-start(bf16[1024,512]{1,0:T(8,128)(2,1)S(1)} %add_convert_fusion.2), channel_id=1, source_target_pairs={{0,32},{16,48},{32,0},{48,16},{64,96},{80,112},{96,64},{112,80},{1... | collective-permute-start | bytes 3145736 | tf_op jit(solution)/shard_map/ppermute | solution.py:16
  66.0 26.6 %collective-permute-start.3 = (bf16[1024,512]{1,0:T(8,128)(2,1)}, bf16[1024,512]{1,0:T(8,128)(2,1)}, u32[]{:S(2)}, u32[]{:S(2)}) collective-permute-start(bf16[1024,512]{1,0:T(8,128)(2,1)} %add_convert_fusion.1), channel_id=1, source_target_pairs={{0,64},{16,80},{32,96},{48,112},{64,0},{80,16},{96,32},{112,48},{1... | collective-permute-start | bytes 3145736 | tf_op jit(solution)/shard_map/ppermute | solution.py:16
  73.4 24.9 %all-to-all-start = ((s32[128,1,8]{2,1,0:T(1,128)}), s32[128,1,8]{2,1,0:T(1,128)S(1)}, u32[]{:S(2)}, u32[]{:S(2)}) async-start(s32[128,1,8]{2,1,0:T(1,128)} %bitcast.19), calls=%async_computation | async-start | bytes 131072 | tf_op jit(solution)/shard_map/all_to_all | solution.py:82
  98.3 42.5 %all-to-all-start.1 = ((bf16[128,8,1024]{2,1,0:T(8,128)(2,1)}), bf16[128,8,1024]{2,1,0:T(8,128)(2,1)S(1)}, u32[]{:S(2)}, u32[]{:S(2)}) async-start(bf16[128,8,1024]{2,1,0:T(8,128)(2,1)} %convert_bitcast_fusion), calls=%async_computation.1 | async-start | bytes 4194304 | tf_op jit(solution)/shard_map/all_to_all | solution.py:89

commit v6 on v5

--- a/solution.py
+++ b/solution.py
@@ -65,12 +65,25 @@
     pieces = block_out.reshape(p_dev, 2, RBLK)
     image = pieces.transpose(1, 0, 2).reshape(2 * p_dev, r_dev)
     section_count = offsets.shape[0]
-    dest = owners.reshape(p_dev)
-    aim = targets.reshape(p_dev)
-    slot = dest * capacity + group_slots(dest, devices)
-    pick = jnp.arange(devices * capacity, dtype=jnp.int32)[:, None] == slot[None, :]
-    labels = jnp.sum(jnp.where(pick, aim[None, :] + 1, 0), axis=1) - 1
-    for section in range(section_count):
+    last = section_count - 1
+    bit = 1 << last
+    me_sub = lax.axis_index("sub")
+    far = lambda value: from_partner(value, "sub", last)
+    far_weights = far(weights[last, 0])
+    far_ints = far(jnp.concatenate([offsets[last, 0].reshape(-1), owners.reshape(-1), targets.reshape(-1)]))
+    far_offsets = far_ints[: 2 * p_dev].reshape(2, p_dev)
+    far_owners = far_ints[2 * p_dev : 3 * p_dev]
+    far_targets = far_ints[3 * p_dev :]
+    by_group = {0: (owners.reshape(p_dev), targets.reshape(p_dev)), bit: (far_owners, far_targets)}
+    picks = {}
+    codes = []
+    for m in (0, bit):
+        dest, aim = by_group[m]
+        slot = dest * capacity + group_slots(dest, devices)
+        picks[m] = jnp.arange(devices * capacity, dtype=jnp.int32)[:, None] == slot[None, :]
+        codes.append(jnp.sum(jnp.where(picks[m], aim[None, :] + 1, 0), axis=1).reshape(devices, capacity))
+    labels = jnp.stack(codes, axis=1) - 1
+    for section in range(last):
         partner = from_partner(image, "sub", section)
         mine = merge_matrix(offsets[section, 0, 0], weights[section, 0, 0])
         theirs = merge_matrix(offsets[section, 0, 1], weights[section, 0, 1])
@@ -79,21 +92,43 @@
         image = merged.astype(jnp.bfloat16)
         if section == 0:
             labels, image = lax.optimization_barrier((labels, image))
-            marks = lax.all_to_all(
-                labels.reshape(devices, capacity), ("sub", "rng"), split_axis=0, concat_axis=0, tiled=True
-            )
-    rows = image.reshape(2, p_dev, r_dev).transpose(1, 0, 2).reshape(p_dev, 2 * r_dev)
-    send = jnp.dot(pick.astype(jnp.bfloat16), rows, preferred_element_type=jnp.float32).astype(
-        jnp.bfloat16
-    )
-    got = lax.all_to_all(
-        send.reshape(devices, capacity, 2 * r_dev), ("sub", "rng"), split_axis=0, concat_axis=0, tiled=True
-    )
-    got_flat = got.reshape(devices * capacity, 2 * r_dev)
-    mark_flat = marks.reshape(devices * capacity)
-    place = (jnp.arange(p_dev, dtype=jnp.int32)[:, None] == mark_flat[None, :]).astype(jnp.bfloat16)
-    tile = jnp.dot(place, got_flat, preferred_element_type=jnp.float32).astype(jnp.bfloat16)
-    return tile.reshape(p_dev, 2, r_dev).transpose(1, 0, 2)
+            marks = lax.all_to_all(labels, ("sub", "rng"), split_axis=0, concat_axis=0, tiled=True)
+    half = r_dev // 2
+    keep_bit = (me_sub >> last) & 1
+    kept = lax.dynamic_slice_in_dim(image, keep_bit * half, half, axis=1)
+    sent = lax.dynamic_slice_in_dim(image, (1 - keep_bit) * half, half, axis=1)
+    old = {0: kept, bit: far(sent)}
+    bands = {
+        0: (offsets[last, 0], weights[last, 0]),
+        bit: (far_offsets, far_weights),
+    }
+    sends = []
+    for m in (0, bit):
+        starts, kernel = bands[m]
+        mine = merge_matrix(starts[0], kernel[0])
+        theirs = merge_matrix(starts[1], kernel[1])
+        merged = jnp.dot(mine, old[m], preferred_element_type=jnp.float32)
+        merged = merged + jnp.dot(theirs, old[m ^ bit], preferred_element_type=jnp.float32)
+        piece = merged.astype(jnp.bfloat16)
+        rows = piece.reshape(2, p_dev, half).transpose(1, 0, 2).reshape(p_dev, 2 * half)
+        send = jnp.dot(picks[m].astype(jnp.bfloat16), rows, preferred_element_type=jnp.float32)
+        sends.append(send.astype(jnp.bfloat16).reshape(devices, capacity, 2 * half))
+    payload = jnp.concatenate(sends, axis=1)
+    got = lax.all_to_all(payload, ("sub", "rng"), split_axis=0, concat_axis=0, tiled=True)
+    span = devices // 2
+    tiles = []
+    for h in range(2):
+        sources = [s for s in range(n_sub) if (s >> last) & 1 == h]
+        block_data = jnp.concatenate(
+            [got[s * n_rng : (s + 1) * n_rng] for s in sources], axis=0
+        ).reshape(span * 2 * capacity, 2 * half)
+        block_mark = jnp.concatenate(
+            [marks[s * n_rng : (s + 1) * n_rng] for s in sources], axis=0
+        ).reshape(span * 2 * capacity)
+        place = (jnp.arange(p_dev, dtype=jnp.int32)[:, None] == block_mark[None, :]).astype(jnp.bfloat16)
+        tile = jnp.dot(place, block_data, preferred_element_type=jnp.float32).astype(jnp.bfloat16)
+        tiles.append(tile.reshape(p_dev, 2, half))
+    return jnp.concatenate(tiles, axis=2).transpose(1, 0, 2)
 
 
 def solution(mesh):

time: 144 us -> 149 us (1.035)
  other arithmetic: 13.3 us -> 27.2 us
  waiting for transfers between devices: 63.3 us -> 49.9 us
  local copies, waits for them, and re-layouts: 17.8 us -> 20.1 us
  matrix products: 17.2 us -> 18.8 us
    neg x6 -> x8, other arithmetic: 10.4 us -> 21 us  [merge_matrix(): upper = jnp.concatenate([g_real, -g_imag], axis=1)]
    ppermute x1, waiting for transfers between devices: 8 us -> 0.01 us  [shifted(): lax.ppermute(value, axis, [(source, source + steps) for source in range(f...]
    ppermute x3 -> x5, waiting for transfers between devices: 27 us -> 20.5 us  [from_partner(): lax.ppermute(value, axis, [(i, i ^ 1 << apart) for i in range(lax.axis_si...]
    dot_general x2 -> x8, matrix products: 3.9 us -> 10.1 us  [the longest x2 3.59 us: on_device(): merged = jnp.dot(mine, old[m], preferred_element_type=jnp.float32)]
    ppermute x3 -> x5, starting transfers between devices: 7.02 us -> 10.2 us  [from_partner(): lax.ppermute(value, axis, [(i, i ^ 1 << apart) for i in range(lax.axis_si...]
    all_to_all x2, starting transfers between devices: 22.8 us -> 20.2 us  [the longest x1 10.5 us: on_device(): lax.all_to_all(labels, ('sub', 'rng'), split_axis=0, concat_axis=0, tiled...]
    dot_general x3 -> x2, matrix products: 4.95 us -> 2.48 us  [on_device(): merged = jnp.dot(mine, image, preferred_element_type=jnp.float32)]
    concatenate x0 -> x2, other arithmetic: none -> 2.38 us  [the longest x1 1.68 us: on_device(): payload = jnp.concatenate(sends, axis=1)]
  transfers between devices with their start and end apart: 6 -> 8, of which waited for: 4 -> 3; matrix products, arithmetic and copies ran while one was open for 24% -> 36% of each run, Pallas kernels for 0% -> 0%
where the time goes in v6:
time: 149 us
  waiting for transfers between devices  49.9 us (33%)
  starting transfers between devices  31.7 us (21%)
  other arithmetic  27.2 us (18%)
  local copies, waits for them, and re-layouts  20.1 us (13%)
  matrix products  18.8 us (13%)
    all_to_all x1, waiting for transfers between devices, on_device(): lax.all_to_all(payload, ('sub', 'rng'), split_axis=0, concat_axis=0, tile...  29.4 us
    neg x8, other arithmetic, merge_matrix(): upper = jnp.concatenate([g_real, -g_imag], axis=1)  21 us
    ppermute x5, waiting for transfers between devices, from_partner(): lax.ppermute(value, axis, [(i, i ^ 1 << apart) for i in range(lax.axis_si...  20.5 us
    all_to_all x1, starting transfers between devices, on_device(): lax.all_to_all(labels, ('sub', 'rng'), split_axis=0, concat_axis=0, tiled...  10.5 us
    ppermute x5, starting transfers between devices, from_partner(): lax.ppermute(value, axis, [(i, i ^ 1 << apart) for i in range(lax.axis_si...  10.2 us
    all_to_all x1, starting transfers between devices, on_device(): lax.all_to_all(payload, ('sub', 'rng'), split_axis=0, concat_axis=0, tile...  9.75 us
    unnamed x65, local copies, waits for them, and re-layouts  4.33 us
    another operation x4, local copies, waits for them, and re-layouts, replica_matrix(): jnp.tile(padded, block_len)[:block_len * width].reshape(block_len, width)  3.87 us
  transfers between devices with their start and end apart: 8, of which 3 were waited for; matrix products, arithmetic and copies ran while one was open for 36% of the time, Pallas kernels for 0%

profile of v6, /device:TPU:1, one launch (start us, length us, event | category | flops | bytes accessed | tf_op | source)
XLA Modules:
  0.0 148.5 jit_solution(15635710279439538870)
XLA Ops:
  0.0 1.3 collective-permute-start.1
  1.3 0.7 slice_bitcast_fusion.19
  2.0 0.7 pad_add_fusion
  2.7 4.4 %collective-permute-start = (s32[2048]{0:T(1024)S(1)}, s32[2048]{0:T(1024)S(1)}, u32[]{:S(2)}, u32[]{:S(2)}) collective-permute-start(s32[2048]{0:T(1024)S(1)} %pad_add_fusion), channel_id=1, source_target_pairs={{0,64},{16,80},{32,96},{48,112},{64,0},{80,16},{96,32},{112,48},{1... | collective-permute-start | bytes 24584 | tf_op jit(solution)/shard_map/ppermute | solution.py:16
  7.1 0.8 slice_bitcast_fusion.2
  7.9 0.9 slice_bitcast_fusion.7
  8.7 0.8 fusion.333
  9.5 0.8 slice_reduce_fusion.128
  10.4 1.3 tile.21
  12.4 1.1 bitcast_negate_fusion
  15.1 2.8 %fusion.323 = (bf16[512,512]{1,0:T(8,128)(2,1)}, bf16[512,512]{1,0:T(8,128)(2,1)}, bf16[512,512]{1,0:T(8,128)(2,1)}) fusion(bf16[512]{0:T(512)(128)(2,1)S(1)} %get-tuple-element.106, bf16[512]{0:T(512)(128)(2,1)S(1)} %get-tuple-element.107, bf16[512]{0:T(512)(128)(2,1)S(1)} %get-tuple-element.108, bf16[512]{0:T(512)(128)(2,1)S(1)} %get-tuple-element.109, ...), kind=kLoop, calls=%fused_computation.497 | loop fusion | flops 7340032 | bytes 1591296 | tf_op jit(solution)/shard_map/neg | solution.py:43
  17.9 2.8 %fusion.324 = (bf16[512,512]{1,0:T(8,128)(2,1)}, bf16[512,512]{1,0:T(8,128)(2,1)}, bf16[512,512]{1,0:T(8,128)(2,1)}) fusion(bf16[512]{0:T(512)(128)(2,1)S(1)} %get-tuple-element.90, bf16[512]{0:T(512)(128)(2,1)S(1)} %get-tuple-element.91, bf16[512]{0:T(512)(128)(2,1)S(1)} %get-tuple-element.92, bf16[512]{0:T(512)(128)(2,1)S(1)} %get-tuple-element.93, ...), kind=kLoop, calls=%fused_computation.498 | loop fusion | flops 7340032 | bytes 1591296 | tf_op jit(solution)/shard_map/neg | solution.py:43
  20.7 2.7 %fusion.326 = (bf16[512,512]{1,0:T(8,128)(2,1)}, bf16[512,512]{1,0:T(8,128)(2,1)}, bf16[512,512]{1,0:T(8,128)(2,1)}) fusion(bf16[512]{0:T(512)(128)(2,1)S(1)} %get-tuple-element.74, bf16[512]{0:T(512)(128)(2,1)S(1)} %get-tuple-element.75, bf16[512]{0:T(512)(128)(2,1)S(1)} %get-tuple-element.76, bf16[512]{0:T(512)(128)(2,1)S(1)} %get-tuple-element.77, ...), kind=kLoop, calls=%fused_computation.500 | loop fusion | flops 7340032 | bytes 1591296 | tf_op jit(solution)/shard_map/neg | solution.py:43
  23.4 2.8 %fusion.327 = (bf16[512,512]{1,0:T(8,128)(2,1)}, bf16[512,512]{1,0:T(8,128)(2,1)}, bf16[512,512]{1,0:T(8,128)(2,1)}) fusion(bf16[512]{0:T(512)(128)(2,1)S(1)} %get-tuple-element.58, bf16[512]{0:T(512)(128)(2,1)S(1)} %get-tuple-element.59, bf16[512]{0:T(512)(128)(2,1)S(1)} %get-tuple-element.60, bf16[512]{0:T(512)(128)(2,1)S(1)} %get-tuple-element.61, ...), kind=kLoop, calls=%fused_computation.501 | loop fusion | flops 7340032 | bytes 1591296 | tf_op jit(solution)/shard_map/neg | solution.py:43
  26.2 2.7 %fusion.325 = (bf16[512,512]{1,0:T(8,128)(2,1)}, bf16[512,512]{1,0:T(8,128)(2,1)}, bf16[512,512]{1,0:T(8,128)(2,1)}) fusion(bf16[512]{0:T(512)(128)(2,1)S(1)} %get-tuple-element.26, bf16[512]{0:T(512)(128)(2,1)S(1)} %get-tuple-element.27, bf16[512]{0:T(512)(128)(2,1)S(1)} %get-tuple-element.28, bf16[512]{0:T(512)(128)(2,1)S(1)} %get-tuple-element.29, ...), kind=kLoop, calls=%fused_computation.499 | loop fusion | flops 7340032 | bytes 1591296 | tf_op jit(solution)/shard_map/neg | solution.py:43
  28.9 2.8 %fusion.328 = (bf16[512,512]{1,0:T(8,128)(2,1)}, bf16[512,512]{1,0:T(8,128)(2,1)}, bf16[512,512]{1,0:T(8,128)(2,1)}) fusion(bf16[512]{0:T(512)(128)(2,1)S(1)} %get-tuple-element.10, bf16[512]{0:T(512)(128)(2,1)S(1)} %get-tuple-element.11, bf16[512]{0:T(512)(128)(2,1)S(1)} %get-tuple-element.12, bf16[512]{0:T(512)(128)(2,1)S(1)} %get-tuple-element.13, ...), kind=kLoop, calls=%fused_computation.502 | loop fusion | flops 7340032 | bytes 1591296 | tf_op jit(solution)/shard_map/neg | solution.py:43
  31.9 2.4 %tile.9 = bf16[524800]{0:T(1024)(128)(2,1)} reshape(bf16[512,1025]{1,0:T(8,128)(2,1)S(1)} %tile.8) | data formatting | bytes 2099200 | tf_op jit(solution)/shard_map/tile | solution.py:25
  34.3 1.2 slice-done
  35.5 1.3 reshape.168
  37.6 1.4 constant_dynamic-update-slice_fusion
  39.2 1.0 copy-done.1
  40.8 2.4 %fusion.83 = bf16[512,1024]{1,0:T(8,128)(2,1)S(1)} fusion(bf16[1024,512]{0,1:T(8,128)(2,1)S(1)} %bitcast.107, bf16[1024,512]{0,1:T(8,128)(2,1)S(1)} %bitcast.106, bf16[1024,512]{0,1:T(8,128)(2,1)S(1)} %copy-done.3, bf16[512,1024]{1,0:T(8,128)(2,1)S(1)} %get-tuple-element.142, bf16[512,1024]{1,0:T(8,128)(2,1)S(1)} %get-tuple-element.141), kind=kOutput, calls=%fused_computation.88 | convolution fusion | flops 2168979456 | bytes 6291456 | tf_op jit(solution)/shard_map/dot_general | solution.py:64
  43.3 1.2 collective-permute-start.2
  45.1 1.2 fusion.8
  47.0 2.6 %add_convert_fusion.1 = bf16[1024,512]{1,0:T(8,128)(2,1)S(1)} fusion(f32[1024,512]{1,0:T(8,128)S(1)} %fusion.8, bf16[1024,512]{1,0:T(8,128)(2,1)} %collective-permute-done.2, bf16[512,512]{1,0:T(8,128)(2,1)S(1)} %copy-done.22, bf16[512,512]{1,0:T(8,128)(2,1)S(1)} %copy-done.21, bf16[512,512]{1,0:T(8,128)(2,1)S(1)} %copy-done.20), kind=kOutput, calls=%fused_computation.78 | convolution fusion | flops 1083179008 | bytes 5767168 | tf_op jit(solution)/shard_map/dot_general | solution.py:91
  49.6 1.4 collective-permute-start.3
  51.2 1.7 %fusion.330 = (bf16[512,512]{1,0:T(8,128)(2,1)S(1)}, bf16[512,512]{1,0:T(8,128)(2,1)S(1)}, bf16[512,512]{1,0:T(8,128)(2,1)S(1)}) fusion(bf16[512]{0:T(512)(128)(2,1)S(1)} %get-tuple-element.122, bf16[512]{0:T(512)(128)(2,1)S(1)} %get-tuple-element.123, bf16[512]{0:T(512)(128)(2,1)S(1)} %get-tuple-element.124, bf16[512]{0:T(512)(128)(2,1)S(1)} %get-tuple-element.125, ...), kind=kLoop, calls=%fused_computation.504 | loop fusion | flops 7340032 | bytes 1591296 | tf_op jit(solution)/shard_map/neg | solution.py:43
  53.0 1.2 fusion.35
  54.2 19.8 %collective-permute-done.3 = bf16[1024,512]{1,0:T(8,128)(2,1)S(1)} collective-permute-done((bf16[1024,512]{1,0:T(8,128)(2,1)S(1)}, bf16[1024,512]{1,0:T(8,128)(2,1)S(1)}, u32[]{:S(2)}, u32[]{:S(2)}) %collective-permute-start.3) | collective-permute-done | bytes 1048608 | tf_op jit(solution)/shard_map/ppermute | solution.py:16
  74.0 1.2 add_convert_fusion
  75.3 1.0 copy-done.26
  76.3 0.8 constant_dynamic-slice_fusion
  77.1 3.2 %collective-permute-start.4 = (bf16[1024,256]{1,0:T(8,128)(2,1)}, bf16[1024,256]{1,0:T(8,128)(2,1)}, u32[]{:S(2)}, u32[]{:S(2)}) collective-permute-start(bf16[1024,256]{1,0:T(8,128)(2,1)} %constant_dynamic-slice_fusion), channel_id=1, source_target_pairs={{0,64},{16,80},{32,96},{48,112},{64,0},{80,16},{96,32},{112,48},{1... | collective-permute-start | bytes 1572872 | tf_op jit(solution)/shard_map/ppermute | solution.py:16
  80.3 2.7 %fusion.329 = (bf16[512,512]{1,0:T(8,128)(2,1)}, bf16[512,512]{1,0:T(8,128)(2,1)}, bf16[512,512]{1,0:T(8,128)(2,1)}) fusion(bf16[512]{0:T(512)(128)(2,1)S(1)} %get-tuple-element.42, bf16[512]{0:T(512)(128)(2,1)S(1)} %get-tuple-element.43, bf16[512]{0:T(512)(128)(2,1)S(1)} %get-tuple-element.44, bf16[512]{0:T(512)(128)(2,1)S(1)} %get-tuple-element.45, ...), kind=kLoop, calls=%fused_computation.503 | loop fusion | flops 7340032 | bytes 1591296 | tf_op jit(solution)/shard_map/neg | solution.py:43
  83.1 0.7 copy.38
  83.8 10.5 %all-to-all-start = ((s32[128,2,8]{2,1,0:T(2,128)}), s32[128,2,8]{2,1,0:T(2,128)S(1)}, u32[]{:S(2)}, u32[]{:S(2)}) async-start(s32[128,2,8]{2,1,0:T(2,128)} %copy.38), calls=%async_computation | async-start | bytes 262144 | tf_op jit(solution)/shard_map/all_to_all | solution.py:95
  94.3 1.8 %fusion.27 = f32[1024,256]{1,0:T(8,128)S(1)} fusion(bf16[512,512]{1,0:T(8,128)(2,1)S(1)} %copy-done.7, bf16[512,512]{1,0:T(8,128)(2,1)S(1)} %copy-done.6, bf16[512,512]{1,0:T(8,128)(2,1)S(1)} %copy-done.5, bf16[1024,512]{1,0:T(8,128)(2,1)} %copy-done.26, s32[]{:T(128)S(6)} %select_n.480), kind=kOutput, calls=%fused_computation.27 | convolution fusion | flops 545259520 | bytes 3145732 | tf_op jit(solution)/shard_map/dot_general | solution.py:110
  96.2 1.7 %fusion.67 = f32[1024,256]{1,0:T(8,128)} fusion(bf16[512,512]{1,0:T(8,128)(2,1)S(1)} %get-tuple-element.196, bf16[512,512]{1,0:T(8,128)(2,1)S(1)} %get-tuple-element.182, bf16[512,512]{1,0:T(8,128)(2,1)S(1)} %get-tuple-element.181, bf16[1024,512]{1,0:T(8,128)(2,1)S(1)} %copy-done.27, s32[]{:T(128)S(6)} %select_n.480), kind=kOutput, calls=%fused_computation.67 | convolution fusion | flops 545259520 | bytes 3145732 | tf_op jit(solution)/shard_map/dot_general | solution.py:111
  97.9 1.8 %fusion.100 = bf16[1024,256]{1,0:T(8,128)(2,1)S(1)} fusion(f32[1024,256]{1,0:T(8,128)S(1)} %fusion.27, bf16[1024,256]{1,0:T(8,128)(2,1)} %collective-permute-done.4, bf16[512,512]{1,0:T(8,128)(2,1)S(1)} %copy-done.10, bf16[512,512]{1,0:T(8,128)(2,1)S(1)} %copy-done.9, bf16[512,512]{1,0:T(8,128)(2,1)S(1)} %copy-done.8), kind=kOutput, calls=%fused_computation.97 | convolution fusion | flops 545783808 | bytes 3670016 | tf_op jit(solution)/shard_map/dot_general | solution.py:111
  99.9 0.8 fusion.91
  101.4 1.7 %fusion.103 = bf16[1024,256]{1,0:T(8,128)(2,1)S(1)} fusion(f32[1024,256]{1,0:T(8,128)S(1)} %copy-done.30, bf16[1024,256]{1,0:T(8,128)(2,1)} %collective-permute-done.4, bf16[512,512]{1,0:T(8,128)(2,1)S(1)} %copy-done.25, bf16[512,512]{1,0:T(8,128)(2,1)S(1)} %copy-done.24, bf16[512,512]{1,0:T(8,128)(2,1)S(1)} %copy-done.23), kind=kOutput, calls=%fused_computation.98 | convolution fusion | flops 545783808 | bytes 3670016 | tf_op jit(solution)/shard_map/dot_general | solution.py:110
  103.4 0.8 fusion.90
  104.2 1.7 %pad_maximum_fusion = bf16[128,16,512]{2,1,0:T(8,128)(2,1)} fusion(bf16[128,8,512]{2,1,0:T(8,128)(2,1)S(1)} %fusion.90, bf16[128,8,512]{2,1,0:T(8,128)(2,1)S(1)} %fusion.91), kind=kLoop, calls=%fused_computation.75 | loop fusion | flops 4194304 | bytes 4194304 | tf_op jit(solution)/shard_map/concatenate | solution.py:116
  105.8 9.8 %all-to-all-start.1 = ((bf16[128,16,512]{2,1,0:T(8,128)(2,1)}), bf16[128,16,512]{2,1,0:T(8,128)(2,1)S(1)}, u32[]{:S(2)}, u32[]{:S(2)}) async-start(bf16[128,16,512]{2,1,0:T(8,128)(2,1)} %pad_maximum_fusion), calls=%async_computation.1 | async-start | bytes 4194304 | tf_op jit(solution)/shard_map/all_to_all | solution.py:117
  115.9 29.4 %all-to-all-done.1 = bf16[128,16,512]{2,1,0:T(8,128)(2,1)S(1)} async-done(((bf16[128,16,512]{2,1,0:T(8,128)(2,1)}), bf16[128,16,512]{2,1,0:T(8,128)(2,1)S(1)}, u32[]{:S(2)}, u32[]{:S(2)}) %all-to-all-start.1) | async-done | bytes 2097184 | tf_op jit(solution)/shard_map/all_to_all | solution.py:117
  145.5 0.8 fusion.99
  146.5 0.8 fusion.98
  147.4 1.1 maximum_bitcast_fusion
  (119 shorter events, 7.5 us)
Async XLA Ops:
  0.0 37.6 %collective-permute-start.1 = (bf16[2,512,512]{2,1,0:T(8,128)(2,1)}, bf16[2,512,512]{2,1,0:T(8,128)(2,1)}, u32[]{:S(2)}, u32[]{:S(2)}) collective-permute-start(bf16[2,512,512]{2,1,0:T(8,128)(2,1)} %param.6), channel_id=1, source_target_pairs={{1,0},{2,1},{3,2},{4,3},{5,4},{6,5},{7,6},{8,7},{9,8},{10,9},{11,1... | collective-permute-start | bytes 3145736 | tf_op jit(solution)/shard_map/ppermute | solution.py:12
  2.7 34.2 %collective-permute-start = (s32[2048]{0:T(1024)S(1)}, s32[2048]{0:T(1024)S(1)}, u32[]{:S(2)}, u32[]{:S(2)}) collective-permute-start(s32[2048]{0:T(1024)S(1)} %pad_add_fusion), channel_id=1, source_target_pairs={{0,64},{16,80},{32,96},{48,112},{64,0},{80,16},{96,32},{112,48},{1... | collective-permute-start | bytes 24584 | tf_op jit(solution)/shard_map/ppermute | solution.py:16
  7.9 37.1 %collective-permute-start.5 = (bf16[2,2,512,8]{2,3,1,0:T(8,128)(2,1)S(1)}, bf16[2,2,512,8]{2,3,1,0:T(8,128)(2,1)S(1)}, u32[]{:S(2)}, u32[]{:S(2)}) collective-permute-start(bf16[2,2,512,8]{2,3,1,0:T(8,128)(2,1)S(1)} %slice_bitcast_fusion.2), channel_id=1, source_target_pairs={{0,64},{16,80},{32,96},{48,112},{64,0},{80,16},{96,32},{112,48},{1... | collective-permute-start | bytes 98312 | tf_op jit(solution)/shard_map/ppermute | solution.py:16
  11.8 1.7 %copy-start.28 = (s32[1,1,512,1]{2,3,1,0:T(1,128)S(1)}, s32[1,1,512,1]{2,3,1,0:T(1,128)}, u32[]{:S(2)}) copy-start(s32[1,1,512,1]{2,3,1,0:T(1,128)} %param.10) | copy-start | bytes 6148
  12.3 2.8 %copy-start = (bf16[512,1024]{1,0:T(8,128)(2,1)}, bf16[512,1024]{1,0:T(8,128)(2,1)S(1)}, u32[]{:S(2)}) copy-start(bf16[512,1024]{1,0:T(8,128)(2,1)S(1)} %reshape.169) | copy-start | bytes 3145732
  12.3 1.8 %copy-start.29 = (s32[1,1,512]{2,1,0:T(1,128)S(1)}, s32[1,1,512]{2,1,0:T(1,128)}, u32[]{:S(2)}) copy-start(s32[1,1,512]{2,1,0:T(1,128)} %param.11) | copy-start | bytes 6148
  23.4 8.3 %copy-start.2 = (bf16[2,512,512]{2,1,0:T(8,128)(2,1)S(1)}, bf16[2,512,512]{2,1,0:T(8,128)(2,1)}, u32[]{:S(2)}) copy-start(bf16[2,512,512]{2,1,0:T(8,128)(2,1)} %param.6) | copy-start | bytes 3145732
  34.3 1.2 slice-start
  39.0 1.2 copy-start.1
  39.0 1.5 %copy-start.3 = (bf16[1024,512]{0,1:T(8,128)(2,1)S(1)}, bf16[1024,512]{0,1:T(8,128)(2,1)}, u32[]{:S(2)}) copy-start(bf16[1024,512]{0,1:T(8,128)(2,1)} %bitcast_negate_fusion) | copy-start | bytes 3145732
  39.0 1.8 %copy-start.4 = (bf16[512,1024]{1,0:T(8,128)(2,1)S(1)}, bf16[512,1024]{1,0:T(8,128)(2,1)}, u32[]{:S(2)}) copy-start(bf16[512,1024]{1,0:T(8,128)(2,1)} %reshape.168) | copy-start | bytes 3145732
  43.2 1.8 %copy-start.17 = (bf16[512,512]{1,0:T(8,128)(2,1)S(1)}, bf16[512,512]{1,0:T(8,128)(2,1)}, u32[]{:S(2)}) copy-start(bf16[512,512]{1,0:T(8,128)(2,1)} %get-tuple-element.179) | copy-start | bytes 1572868
  43.2 1.8 %copy-start.18 = (bf16[512,512]{1,0:T(8,128)(2,1)S(1)}, bf16[512,512]{1,0:T(8,128)(2,1)}, u32[]{:S(2)}) copy-start(bf16[512,512]{1,0:T(8,128)(2,1)} %get-tuple-element.180) | copy-start | bytes 1572868
  43.3 1.8 %copy-start.19 = (bf16[512,512]{1,0:T(8,128)(2,1)S(1)}, bf16[512,512]{1,0:T(8,128)(2,1)}, u32[]{:S(2)}) copy-start(bf16[512,512]{1,0:T(8,128)(2,1)} %get-tuple-element.195) | copy-start | bytes 1572868
  43.3 3.6 %collective-permute-start.2 = (bf16[1024,512]{1,0:T(8,128)(2,1)S(1)}, bf16[1024,512]{1,0:T(8,128)(2,1)}, u32[]{:S(2)}, u32[]{:S(2)}) collective-permute-start(bf16[1024,512]{1,0:T(8,128)(2,1)S(1)} %bitcast.108), channel_id=1, source_target_pairs={{0,16},{16,0},{32,48},{48,32},{64,80},{80,64},{96,112},{112,96},{1... | collective-permute-start | bytes 3145736 | tf_op jit(solution)/shard_map/ppermute | solution.py:16
  45.0 2.0 %copy-start.20 = (bf16[512,512]{1,0:T(8,128)(2,1)S(1)}, bf16[512,512]{1,0:T(8,128)(2,1)}, u32[]{:S(2)}) copy-start(bf16[512,512]{1,0:T(8,128)(2,1)} %get-tuple-element.177) | copy-start | bytes 1572868
  45.0 1.9 %copy-start.21 = (bf16[512,512]{1,0:T(8,128)(2,1)S(1)}, bf16[512,512]{1,0:T(8,128)(2,1)}, u32[]{:S(2)}) copy-start(bf16[512,512]{1,0:T(8,128)(2,1)} %get-tuple-element.178) | copy-start | bytes 1572868
  45.0 1.9 %copy-start.22 = (bf16[512,512]{1,0:T(8,128)(2,1)S(1)}, bf16[512,512]{1,0:T(8,128)(2,1)}, u32[]{:S(2)}) copy-start(bf16[512,512]{1,0:T(8,128)(2,1)} %get-tuple-element.194) | copy-start | bytes 1572868
  47.0 5.9 %copy-start.11 = (bf16[512,512]{1,0:T(8,128)(2,1)S(1)}, bf16[512,512]{1,0:T(8,128)(2,1)}, u32[]{:S(2)}) copy-start(bf16[512,512]{1,0:T(8,128)(2,1)} %get-tuple-element.175) | copy-start | bytes 1572868
  47.0 5.9 %copy-start.12 = (bf16[512,512]{1,0:T(8,128)(2,1)S(1)}, bf16[512,512]{1,0:T(8,128)(2,1)}, u32[]{:S(2)}) copy-start(bf16[512,512]{1,0:T(8,128)(2,1)} %get-tuple-element.176) | copy-start | bytes 1572868
  47.0 5.9 %copy-start.13 = (bf16[512,512]{1,0:T(8,128)(2,1)S(1)}, bf16[512,512]{1,0:T(8,128)(2,1)}, u32[]{:S(2)}) copy-start(bf16[512,512]{1,0:T(8,128)(2,1)} %get-tuple-element.193) | copy-start | bytes 1572868
  49.6 24.4 %collective-permute-start.3 = (bf16[1024,512]{1,0:T(8,128)(2,1)S(1)}, bf16[1024,512]{1,0:T(8,128)(2,1)S(1)}, u32[]{:S(2)}, u32[]{:S(2)}) collective-permute-start(bf16[1024,512]{1,0:T(8,128)(2,1)S(1)} %add_convert_fusion.1), channel_id=1, source_target_pairs={{0,32},{16,48},{32,0},{48,16},{64,96},{80,112},{96,64},{112,80},{1... | collective-permute-start | bytes 3145736 | tf_op jit(solution)/shard_map/ppermute | solution.py:16
  52.9 21.1 %copy-start.14 = (bf16[512,512]{1,0:T(8,128)(2,1)S(1)}, bf16[512,512]{1,0:T(8,128)(2,1)}, u32[]{:S(2)}) copy-start(bf16[512,512]{1,0:T(8,128)(2,1)} %get-tuple-element.173) | copy-start | bytes 1572868
  52.9 21.1 %copy-start.15 = (bf16[512,512]{1,0:T(8,128)(2,1)S(1)}, bf16[512,512]{1,0:T(8,128)(2,1)}, u32[]{:S(2)}) copy-start(bf16[512,512]{1,0:T(8,128)(2,1)} %get-tuple-element.174) | copy-start | bytes 1572868
  53.0 21.1 %copy-start.16 = (bf16[512,512]{1,0:T(8,128)(2,1)S(1)}, bf16[512,512]{1,0:T(8,128)(2,1)}, u32[]{:S(2)}) copy-start(bf16[512,512]{1,0:T(8,128)(2,1)} %get-tuple-element.192) | copy-start | bytes 1572868
  75.3 1.0 copy-start.26
  76.2 18.0 %copy-start.5 = (bf16[512,512]{1,0:T(8,128)(2,1)S(1)}, bf16[512,512]{1,0:T(8,128)(2,1)}, u32[]{:S(2)}) copy-start(bf16[512,512]{1,0:T(8,128)(2,1)} %get-tuple-element.169) | copy-start | bytes 1572868
  76.3 18.0 %copy-start.6 = (bf16[512,512]{1,0:T(8,128)(2,1)S(1)}, bf16[512,512]{1,0:T(8,128)(2,1)}, u32[]{:S(2)}) copy-start(bf16[512,512]{1,0:T(8,128)(2,1)} %get-tuple-element.170) | copy-start | bytes 1572868
  76.3 18.0 %copy-start.7 = (bf16[512,512]{1,0:T(8,128)(2,1)S(1)}, bf16[512,512]{1,0:T(8,128)(2,1)}, u32[]{:S(2)}) copy-start(bf16[512,512]{1,0:T(8,128)(2,1)} %get-tuple-element.190) | copy-start | bytes 1572868
  77.1 20.8 %collective-permute-start.4 = (bf16[1024,256]{1,0:T(8,128)(2,1)}, bf16[1024,256]{1,0:T(8,128)(2,1)}, u32[]{:S(2)}, u32[]{:S(2)}) collective-permute-start(bf16[1024,256]{1,0:T(8,128)(2,1)} %constant_dynamic-slice_fusion), channel_id=1, source_target_pairs={{0,64},{16,80},{32,96},{48,112},{64,0},{80,16},{96,32},{112,48},{1... | collective-permute-start | bytes 1572872 | tf_op jit(solution)/shard_map/ppermute | solution.py:16
  83.8 22.0 %all-to-all-start = ((s32[128,2,8]{2,1,0:T(2,128)}), s32[128,2,8]{2,1,0:T(2,128)S(1)}, u32[]{:S(2)}, u32[]{:S(2)}) async-start(s32[128,2,8]{2,1,0:T(2,128)} %copy.38), calls=%async_computation | async-start | bytes 262144 | tf_op jit(solution)/shard_map/all_to_all | solution.py:95
  94.3 1.9 %copy-start.27 = (bf16[1024,512]{1,0:T(8,128)(2,1)S(1)}, bf16[1024,512]{1,0:T(8,128)(2,1)}, u32[]{:S(2)}) copy-start(bf16[1024,512]{1,0:T(8,128)(2,1)} %copy-done.26) | copy-start | bytes 3145732
  96.2 1.7 %copy-start.8 = (bf16[512,512]{1,0:T(8,128)(2,1)S(1)}, bf16[512,512]{1,0:T(8,128)(2,1)}, u32[]{:S(2)}) copy-start(bf16[512,512]{1,0:T(8,128)(2,1)} %get-tuple-element.167) | copy-start | bytes 1572868
  96.2 1.7 %copy-start.9 = (bf16[512,512]{1,0:T(8,128)(2,1)S(1)}, bf16[512,512]{1,0:T(8,128)(2,1)}, u32[]{:S(2)}) copy-start(bf16[512,512]{1,0:T(8,128)(2,1)} %get-tuple-element.168) | copy-start | bytes 1572868
  96.2 1.7 %copy-start.10 = (bf16[512,512]{1,0:T(8,128)(2,1)S(1)}, bf16[512,512]{1,0:T(8,128)(2,1)}, u32[]{:S(2)}) copy-start(bf16[512,512]{1,0:T(8,128)(2,1)} %get-tuple-element.189) | copy-start | bytes 1572868
  99.7 1.0 copy-start.23
  99.7 1.2 copy-start.24
  99.7 1.3 copy-start.25
  99.9 1.5 %copy-start.30 = (f32[1024,256]{1,0:T(8,128)S(1)}, f32[1024,256]{1,0:T(8,128)}, u32[]{:S(2)}) copy-start(f32[1024,256]{1,0:T(8,128)} %fusion.67) | copy-start | bytes 3145732
  105.8 39.4 %all-to-all-start.1 = ((bf16[128,16,512]{2,1,0:T(8,128)(2,1)}), bf16[128,16,512]{2,1,0:T(8,128)(2,1)S(1)}, u32[]{:S(2)}, u32[]{:S(2)}) async-start(bf16[128,16,512]{2,1,0:T(8,128)(2,1)} %pad_maximum_fusion), calls=%async_computation.1 | async-start | bytes 4194304 | tf_op jit(solution)/shard_map/all_to_all | solution.py:117

commit v7 on v6

--- a/solution.py
+++ b/solution.py
@@ -83,6 +83,11 @@
         picks[m] = jnp.arange(devices * capacity, dtype=jnp.int32)[:, None] == slot[None, :]
         codes.append(jnp.sum(jnp.where(picks[m], aim[None, :] + 1, 0), axis=1).reshape(devices, capacity))
     labels = jnp.stack(codes, axis=1) - 1
+    late = (offsets[1:], weights[1:], far_offsets, far_weights)
+    late, image = lax.optimization_barrier((late, image))
+    late_offsets, late_weights, far_offsets, far_weights = late
+    offsets = jnp.concatenate([offsets[:1], late_offsets], axis=0)
+    weights = jnp.concatenate([weights[:1], late_weights], axis=0)
     for section in range(last):
         partner = from_partner(image, "sub", section)
         mine = merge_matrix(offsets[section, 0, 0], weights[section, 0, 0])
@@ -93,6 +98,8 @@
         if section == 0:
             labels, image = lax.optimization_barrier((labels, image))
             marks = lax.all_to_all(labels, ("sub", "rng"), split_axis=0, concat_axis=0, tiled=True)
+        if section == 1:
+            marks, image = lax.optimization_barrier((marks, image))
     half = r_dev // 2
     keep_bit = (me_sub >> last) & 1
     kept = lax.dynamic_slice_in_dim(image, keep_bit * half, half, axis=1)

time: 149 us -> 149 us (level)
  starting transfers between devices: 31.7 us -> 34 us
  local copies, waits for them, and re-layouts: 20.1 us -> 18.2 us
  other arithmetic: 27.2 us -> 25.4 us
    ppermute x5, waiting for transfers between devices: 20.5 us -> 13.9 us  [from_partner(): lax.ppermute(value, axis, [(i, i ^ 1 << apart) for i in range(lax.axis_si...]
    ppermute x1, waiting for transfers between devices: 0.01 us -> 6.02 us  [shifted(): lax.ppermute(value, axis, [(source, source + steps) for source in range(f...]
    dot_general x2, matrix products: 2.48 us -> 4.79 us  [on_device(): merged = jnp.dot(mine, image, preferred_element_type=jnp.float32)]
    neg x8, other arithmetic: 21 us -> 19.1 us  [merge_matrix(): upper = jnp.concatenate([g_real, -g_imag], axis=1)]
    all_to_all x1, starting transfers between devices: 10.5 us -> 12.1 us  [on_device(): lax.all_to_all(labels, ('sub', 'rng'), split_axis=0, concat_axis=0, tiled...]
    all_to_all x1, starting transfers between devices: 9.75 us -> 11.3 us  [on_device(): lax.all_to_all(payload, ('sub', 'rng'), split_axis=0, concat_axis=0, tile...]
    unnamed x65 -> x57, local copies, waits for them, and re-layouts: 4.33 us -> 3.35 us
  transfers between devices with their start and end apart: 8 -> 8, of which waited for: 3 -> 5; matrix products, arithmetic and copies ran while one was open for 36% -> 31% of each run, Pallas kernels for 0% -> 0%
where the time goes in v7:
time: 149 us; the launch traced here: 148 us
  waiting for transfers between devices  50.5 us (34%)
  starting transfers between devices  34 us (23%)
  other arithmetic  25.4 us (17%)
  matrix products  19 us (13%)
  local copies, waits for them, and re-layouts  18.2 us (12%)
    all_to_all x1, waiting for transfers between devices, on_device(): lax.all_to_all(payload, ('sub', 'rng'), split_axis=0, concat_axis=0, tile...  29.4 us
    neg x8, other arithmetic, merge_matrix(): upper = jnp.concatenate([g_real, -g_imag], axis=1)  19.1 us
    ppermute x5, waiting for transfers between devices, from_partner(): lax.ppermute(value, axis, [(i, i ^ 1 << apart) for i in range(lax.axis_si...  13.9 us
    all_to_all x1, starting transfers between devices, on_device(): lax.all_to_all(labels, ('sub', 'rng'), split_axis=0, concat_axis=0, tiled...  12.1 us
    all_to_all x1, starting transfers between devices, on_device(): lax.all_to_all(payload, ('sub', 'rng'), split_axis=0, concat_axis=0, tile...  11.3 us
    ppermute x5, starting transfers between devices, from_partner(): lax.ppermute(value, axis, [(i, i ^ 1 << apart) for i in range(lax.axis_si...  9.36 us
    ppermute x1, waiting for transfers between devices, shifted(): lax.ppermute(value, axis, [(source, source + steps) for source in range(f...  6.02 us
    dot_general x2, matrix products, on_device(): merged = jnp.dot(mine, image, preferred_element_type=jnp.float32)  4.79 us
  transfers between devices with their start and end apart: 8, of which 5 were waited for; matrix products, arithmetic and copies ran while one was open for 31% of the time, Pallas kernels for 0%

profile of v7, /device:TPU:1, one launch (start us, length us, event | category | flops | bytes accessed | tf_op | source)
XLA Modules:
  0.0 147.9 jit_solution(756598592799845738)
XLA Ops:
  0.7 0.7 pad_add_fusion
  1.4 4.4 %collective-permute-start = (s32[2048]{0:T(1024)S(1)}, s32[2048]{0:T(1024)S(1)}, u32[]{:S(2)}, u32[]{:S(2)}) collective-permute-start(s32[2048]{0:T(1024)S(1)} %pad_add_fusion), channel_id=1, source_target_pairs={{0,64},{16,80},{32,96},{48,112},{64,0},{80,16},{96,32},{112,48},{1... | collective-permute-start | bytes 24584 | tf_op jit(solution)/shard_map/ppermute | solution.py:16
  5.8 0.8 slice_bitcast_fusion.2
  6.6 1.3 collective-permute-start.2
  7.9 0.8 slice_bitcast_fusion.17
  8.6 0.8 fusion.333
  9.4 0.8 slice_reduce_fusion.128
  10.3 1.3 tile.21
  12.2 1.2 bitcast_negate_fusion
  14.6 2.8 %fusion.324 = (bf16[512,512]{1,0:T(8,128)(2,1)}, bf16[512,512]{1,0:T(8,128)(2,1)}, bf16[512,512]{1,0:T(8,128)(2,1)}) fusion(bf16[512]{0:T(512)(128)(2,1)S(1)} %get-tuple-element.120, bf16[512]{0:T(512)(128)(2,1)S(1)} %get-tuple-element.121, bf16[512]{0:T(512)(128)(2,1)S(1)} %get-tuple-element.122, bf16[512]{0:T(512)(128)(2,1)S(1)} %get-tuple-element.123, ...), kind=kLoop, calls=%fused_computation.498 | loop fusion | flops 7340032 | bytes 1591296 | tf_op jit(solution)/shard_map/neg | solution.py:43
  17.4 2.8 %fusion.323 = (bf16[512,512]{1,0:T(8,128)(2,1)}, bf16[512,512]{1,0:T(8,128)(2,1)}, bf16[512,512]{1,0:T(8,128)(2,1)}) fusion(bf16[512]{0:T(512)(128)(2,1)S(1)} %get-tuple-element.104, bf16[512]{0:T(512)(128)(2,1)S(1)} %get-tuple-element.105, bf16[512]{0:T(512)(128)(2,1)S(1)} %get-tuple-element.106, bf16[512]{0:T(512)(128)(2,1)S(1)} %get-tuple-element.107, ...), kind=kLoop, calls=%fused_computation.497 | loop fusion | flops 7340032 | bytes 1591296 | tf_op jit(solution)/shard_map/neg | solution.py:43
  20.5 2.3 %tile.9 = bf16[524800]{0:T(1024)(128)(2,1)} reshape(bf16[512,1025]{1,0:T(8,128)(2,1)S(1)} %tile.8) | data formatting | bytes 2099200 | tf_op jit(solution)/shard_map/tile | solution.py:25
  22.8 1.2 slice-done
  24.0 1.3 reshape.172
  26.5 6.0 %collective-permute-done.2 = bf16[2,512,512]{2,1,0:T(8,128)(2,1)} collective-permute-done((bf16[2,512,512]{2,1,0:T(8,128)(2,1)}, bf16[2,512,512]{2,1,0:T(8,128)(2,1)}, u32[]{:S(2)}, u32[]{:S(2)}) %collective-permute-start.2) | collective-permute-done | bytes 1048608 | tf_op jit(solution)/shard_map/ppermute | solution.py:12
  32.5 1.4 constant_dynamic-update-slice_fusion
  34.1 1.0 copy-done.1
  35.8 2.4 %fusion.83 = bf16[512,1024]{1,0:T(8,128)(2,1)S(1)} fusion(bf16[1024,512]{0,1:T(8,128)(2,1)S(1)} %bitcast.111, bf16[1024,512]{0,1:T(8,128)(2,1)S(1)} %bitcast.108, bf16[1024,512]{0,1:T(8,128)(2,1)S(1)} %copy-done.3, bf16[512,1024]{1,0:T(8,128)(2,1)S(1)} %get-tuple-element.156, bf16[512,1024]{1,0:T(8,128)(2,1)S(1)} %get-tuple-element.155), kind=kOutput, calls=%fused_computation.88 | convolution fusion | flops 2168979456 | bytes 6291456 | tf_op jit(solution)/shard_map/dot_general | solution.py:64
  38.3 2.1 %collective-permute-start.3 = (bf16[1024,512]{1,0:T(8,128)(2,1)S(1)}, bf16[1024,512]{1,0:T(8,128)(2,1)S(1)}, u32[]{:S(2)}, u32[]{:S(2)}) collective-permute-start(bf16[1024,512]{1,0:T(8,128)(2,1)S(1)} %bitcast.109), channel_id=1, source_target_pairs={{0,16},{16,0},{32,48},{48,32},{64,80},{80,64},{96,112},{112,96},{1... | collective-permute-start | bytes 3145736 | tf_op jit(solution)/shard_map/ppermute | solution.py:16
  40.6 1.7 %fusion.330 = (bf16[512,512]{1,0:T(8,128)(2,1)S(1)}, bf16[512,512]{1,0:T(8,128)(2,1)S(1)}, bf16[512,512]{1,0:T(8,128)(2,1)S(1)}) fusion(bf16[512]{0:T(512)(128)(2,1)S(1)} %get-tuple-element.136, bf16[512]{0:T(512)(128)(2,1)S(1)} %get-tuple-element.137, bf16[512]{0:T(512)(128)(2,1)S(1)} %get-tuple-element.138, bf16[512]{0:T(512)(128)(2,1)S(1)} %get-tuple-element.139, ...), kind=kLoop, calls=%fused_computation.504 | loop fusion | flops 7340032 | bytes 1591296 | tf_op jit(solution)/shard_map/neg | solution.py:43
  42.4 1.7 %fusion.325 = (bf16[512,512]{1,0:T(8,128)(2,1)S(1)}, bf16[512,512]{1,0:T(8,128)(2,1)S(1)}, bf16[512,512]{1,0:T(8,128)(2,1)S(1)}) fusion(bf16[512]{0:T(512)(128)(2,1)S(1)} %get-tuple-element.88, bf16[512]{0:T(512)(128)(2,1)S(1)} %get-tuple-element.89, bf16[512]{0:T(512)(128)(2,1)S(1)} %get-tuple-element.90, bf16[512]{0:T(512)(128)(2,1)S(1)} %get-tuple-element.91, ...), kind=kLoop, calls=%fused_computation.499 | loop fusion | flops 7340032 | bytes 1591296 | tf_op jit(solution)/shard_map/neg | solution.py:43
  44.4 2.8 %fusion.326 = (bf16[512,512]{1,0:T(8,128)(2,1)}, bf16[512,512]{1,0:T(8,128)(2,1)}, bf16[512,512]{1,0:T(8,128)(2,1)}) fusion(bf16[512]{0:T(512)(128)(2,1)S(1)} %get-tuple-element.72, bf16[512]{0:T(512)(128)(2,1)S(1)} %get-tuple-element.73, bf16[512]{0:T(512)(128)(2,1)S(1)} %get-tuple-element.74, bf16[512]{0:T(512)(128)(2,1)S(1)} %get-tuple-element.75, ...), kind=kLoop, calls=%fused_computation.500 | loop fusion | flops 7340032 | bytes 1591296 | tf_op jit(solution)/shard_map/neg | solution.py:43
  47.2 2.8 %fusion.329 = (bf16[512,512]{1,0:T(8,128)(2,1)}, bf16[512,512]{1,0:T(8,128)(2,1)}, bf16[512,512]{1,0:T(8,128)(2,1)}) fusion(bf16[512]{0:T(512)(128)(2,1)S(1)} %get-tuple-element.56, bf16[512]{0:T(512)(128)(2,1)S(1)} %get-tuple-element.57, bf16[512]{0:T(512)(128)(2,1)S(1)} %get-tuple-element.58, bf16[512]{0:T(512)(128)(2,1)S(1)} %get-tuple-element.59, ...), kind=kLoop, calls=%fused_computation.503 | loop fusion | flops 7340032 | bytes 1591296 | tf_op jit(solution)/shard_map/neg | solution.py:43
  50.0 1.2 fusion.19
  51.3 2.2 %add_convert_fusion.1 = bf16[1024,512]{1,0:T(8,128)(2,1)} fusion(f32[1024,512]{1,0:T(8,128)S(1)} %fusion.19, bf16[1024,512]{1,0:T(8,128)(2,1)S(1)} %bitcast.110, bf16[512,512]{1,0:T(8,128)(2,1)S(1)} %copy-done.10, bf16[512,512]{1,0:T(8,128)(2,1)S(1)} %copy-done.9, bf16[512,512]{1,0:T(8,128)(2,1)S(1)} %copy-done.8), kind=kOutput, calls=%fused_computation.78 | convolution fusion | flops 1083179008 | bytes 5767168 | tf_op jit(solution)/shard_map/dot_general | solution.py:95
  53.6 1.0 collective-permute-start.4
  54.8 2.8 %fusion.327 = (bf16[512,512]{1,0:T(8,128)(2,1)}, bf16[512,512]{1,0:T(8,128)(2,1)}, bf16[512,512]{1,0:T(8,128)(2,1)}) fusion(bf16[512]{0:T(512)(128)(2,1)S(1)} %get-tuple-element.40, bf16[512]{0:T(512)(128)(2,1)S(1)} %get-tuple-element.41, bf16[512]{0:T(512)(128)(2,1)S(1)} %get-tuple-element.42, bf16[512]{0:T(512)(128)(2,1)S(1)} %get-tuple-element.43, ...), kind=kLoop, calls=%fused_computation.501 | loop fusion | flops 7340032 | bytes 1591296 | tf_op jit(solution)/shard_map/neg | solution.py:43
  57.6 0.8 copy.38
  58.3 12.1 %all-to-all-start = ((s32[128,2,8]{2,1,0:T(2,128)}), s32[128,2,8]{2,1,0:T(2,128)S(1)}, u32[]{:S(2)}, u32[]{:S(2)}) async-start(s32[128,2,8]{2,1,0:T(2,128)} %copy.38), calls=%async_computation | async-start | bytes 262144 | tf_op jit(solution)/shard_map/all_to_all | solution.py:100
  70.4 2.6 %fusion.27 = f32[1024,512]{1,0:T(8,128)S(1)} fusion(bf16[1024,512]{1,0:T(8,128)(2,1)} %add_convert_fusion.1, bf16[512,512]{1,0:T(8,128)(2,1)S(1)} %get-tuple-element.207, bf16[512,512]{1,0:T(8,128)(2,1)S(1)} %get-tuple-element.186, bf16[512,512]{1,0:T(8,128)(2,1)S(1)} %get-tuple-element.185), kind=kOutput, calls=%fused_computation.27 | convolution fusion | flops 1082130432 | bytes 4718592 | tf_op jit(solution)/shard_map/dot_general | solution.py:95
  73.0 6.5 %collective-permute-done.4 = bf16[1024,512]{1,0:T(8,128)(2,1)} collective-permute-done((bf16[1024,512]{1,0:T(8,128)(2,1)}, bf16[1024,512]{1,0:T(8,128)(2,1)}, u32[]{:S(2)}, u32[]{:S(2)}) %collective-permute-start.4) | collective-permute-done | bytes 1048608 | tf_op jit(solution)/shard_map/ppermute | solution.py:16
  79.5 2.5 %add_convert_fusion = bf16[1024,512]{1,0:T(8,128)(2,1)S(1)} fusion(f32[1024,512]{1,0:T(8,128)S(1)} %fusion.27, bf16[1024,512]{1,0:T(8,128)(2,1)} %collective-permute-done.4, bf16[512,512]{1,0:T(8,128)(2,1)S(1)} %copy-done.16, bf16[512,512]{1,0:T(8,128)(2,1)S(1)} %copy-done.15, bf16[512,512]{1,0:T(8,128)(2,1)S(1)} %copy-done.14), kind=kOutput, calls=%fused_computation.77 | convolution fusion | flops 1083179008 | bytes 5767168 | tf_op jit(solution)/shard_map/dot_general | solution.py:96
  82.0 1.2 all-to-all-done
  83.2 1.9 %collective-permute-start.5 = (bf16[1024,256]{1,0:T(8,128)(2,1)S(1)}, bf16[1024,256]{1,0:T(8,128)(2,1)S(1)}, u32[]{:S(2)}, u32[]{:S(2)}) collective-permute-start(bf16[1024,256]{1,0:T(8,128)(2,1)S(1)} %constant_dynamic-slice_fusion), channel_id=1, source_target_pairs={{0,64},{16,80},{32,96},{48,112},{64,0},{80,16},{96,32},{112,48},{1... | collective-permute-start | bytes 1572872 | tf_op jit(solution)/shard_map/ppermute | solution.py:16
  85.1 1.7 %fusion.328 = (bf16[512,512]{1,0:T(8,128)(2,1)S(1)}, bf16[512,512]{1,0:T(8,128)(2,1)S(1)}, bf16[512,512]{1,0:T(8,128)(2,1)S(1)}) fusion(bf16[512]{0:T(512)(128)(2,1)S(1)} %get-tuple-element.24, bf16[512]{0:T(512)(128)(2,1)S(1)} %get-tuple-element.25, bf16[512]{0:T(512)(128)(2,1)S(1)} %get-tuple-element.26, bf16[512]{0:T(512)(128)(2,1)S(1)} %get-tuple-element.27, ...), kind=kLoop, calls=%fused_computation.502 | loop fusion | flops 7340032 | bytes 1591296 | tf_op jit(solution)/shard_map/neg | solution.py:43
  86.8 1.9 %fusion.67 = f32[1024,256]{1,0:T(8,128)S(1)} fusion(bf16[512,512]{1,0:T(8,128)(2,1)S(1)} %get-tuple-element.210, bf16[512,512]{1,0:T(8,128)(2,1)S(1)} %get-tuple-element.192, bf16[512,512]{1,0:T(8,128)(2,1)S(1)} %get-tuple-element.191, bf16[1024,512]{1,0:T(8,128)(2,1)} %copy-done.20, s32[]{:T(128)S(6)} %select_n.480), kind=kOutput, calls=%fused_computation.67 | convolution fusion | flops 545259520 | bytes 3145732 | tf_op jit(solution)/shard_map/dot_general | solution.py:118
  88.8 1.7 %fusion.43 = f32[1024,256]{1,0:T(8,128)} fusion(bf16[512,512]{1,0:T(8,128)(2,1)S(1)} %copy-done.19, bf16[512,512]{1,0:T(8,128)(2,1)S(1)} %copy-done.18, bf16[512,512]{1,0:T(8,128)(2,1)S(1)} %copy-done.17, bf16[1024,512]{1,0:T(8,128)(2,1)S(1)} %copy-done.21, s32[]{:T(128)S(6)} %select_n.480), kind=kOutput, calls=%fused_computation.43 | convolution fusion | flops 545259520 | bytes 3145732 | tf_op jit(solution)/shard_map/dot_general | solution.py:117
  90.5 7.4 %collective-permute-done.5 = bf16[1024,256]{1,0:T(8,128)(2,1)S(1)} collective-permute-done((bf16[1024,256]{1,0:T(8,128)(2,1)S(1)}, bf16[1024,256]{1,0:T(8,128)(2,1)S(1)}, u32[]{:S(2)}, u32[]{:S(2)}) %collective-permute-start.5) | collective-permute-done | bytes 524320 | tf_op jit(solution)/shard_map/ppermute | solution.py:16
  97.9 0.7 fusion.103
  98.9 0.7 fusion.90
  100.3 0.7 fusion.100
  101.2 0.8 fusion.91
  102.0 1.7 %pad_maximum_fusion = bf16[128,16,512]{2,1,0:T(8,128)(2,1)} fusion(bf16[128,8,512]{2,1,0:T(8,128)(2,1)S(1)} %fusion.90, bf16[128,8,512]{2,1,0:T(8,128)(2,1)S(1)} %fusion.91), kind=kLoop, calls=%fused_computation.75 | loop fusion | flops 4194304 | bytes 4194304 | tf_op jit(solution)/shard_map/concatenate | solution.py:123
  103.7 11.3 %all-to-all-start.1 = ((bf16[128,16,512]{2,1,0:T(8,128)(2,1)}), bf16[128,16,512]{2,1,0:T(8,128)(2,1)S(1)}, u32[]{:S(2)}, u32[]{:S(2)}) async-start(bf16[128,16,512]{2,1,0:T(8,128)(2,1)} %pad_maximum_fusion), calls=%async_computation.1 | async-start | bytes 4194304 | tf_op jit(solution)/shard_map/all_to_all | solution.py:124
  115.2 29.4 %all-to-all-done.1 = bf16[128,16,512]{2,1,0:T(8,128)(2,1)S(1)} async-done(((bf16[128,16,512]{2,1,0:T(8,128)(2,1)}), bf16[128,16,512]{2,1,0:T(8,128)(2,1)S(1)}, u32[]{:S(2)}, u32[]{:S(2)}) %all-to-all-start.1) | async-done | bytes 2097184 | tf_op jit(solution)/shard_map/all_to_all | solution.py:124
  144.8 0.8 fusion.98
  145.8 0.8 fusion.99
  146.8 1.1 maximum_bitcast_fusion
  (120 shorter events, 7.6 us)
Async XLA Ops:
  1.4 24.0 %collective-permute-start = (s32[2048]{0:T(1024)S(1)}, s32[2048]{0:T(1024)S(1)}, u32[]{:S(2)}, u32[]{:S(2)}) collective-permute-start(s32[2048]{0:T(1024)S(1)} %pad_add_fusion), channel_id=1, source_target_pairs={{0,64},{16,80},{32,96},{48,112},{64,0},{80,16},{96,32},{112,48},{1... | collective-permute-start | bytes 24584 | tf_op jit(solution)/shard_map/ppermute | solution.py:16
  6.6 31.7 %collective-permute-start.1 = (bf16[2,2,512,8]{2,3,1,0:T(8,128)(2,1)S(1)}, bf16[2,2,512,8]{2,3,1,0:T(8,128)(2,1)S(1)}, u32[]{:S(2)}, u32[]{:S(2)}) collective-permute-start(bf16[2,2,512,8]{2,3,1,0:T(8,128)(2,1)S(1)} %slice_bitcast_fusion.2), channel_id=1, source_target_pairs={{0,64},{16,80},{32,96},{48,112},{64,0},{80,16},{96,32},{112,48},{1... | collective-permute-start | bytes 98312 | tf_op jit(solution)/shard_map/ppermute | solution.py:16
  6.6 26.0 %collective-permute-start.2 = (bf16[2,512,512]{2,1,0:T(8,128)(2,1)}, bf16[2,512,512]{2,1,0:T(8,128)(2,1)}, u32[]{:S(2)}, u32[]{:S(2)}) collective-permute-start(bf16[2,512,512]{2,1,0:T(8,128)(2,1)} %param.6), channel_id=1, source_target_pairs={{1,0},{2,1},{3,2},{4,3},{5,4},{6,5},{7,6},{8,7},{9,8},{10,9},{11,1... | collective-permute-start | bytes 3145736 | tf_op jit(solution)/shard_map/ppermute | solution.py:12
  11.7 1.7 %copy-start.22 = (s32[1,1,512,1]{2,3,1,0:T(1,128)S(1)}, s32[1,1,512,1]{2,3,1,0:T(1,128)}, u32[]{:S(2)}) copy-start(s32[1,1,512,1]{2,3,1,0:T(1,128)} %param.10) | copy-start | bytes 6148
  12.2 5.2 %copy-start = (bf16[512,1024]{1,0:T(8,128)(2,1)}, bf16[512,1024]{1,0:T(8,128)(2,1)S(1)}, u32[]{:S(2)}) copy-start(bf16[512,1024]{1,0:T(8,128)(2,1)S(1)} %reshape.173) | copy-start | bytes 3145732
  12.2 1.9 %copy-start.23 = (s32[1,1,512]{2,1,0:T(1,128)S(1)}, s32[1,1,512]{2,1,0:T(1,128)}, u32[]{:S(2)}) copy-start(s32[1,1,512]{2,1,0:T(1,128)} %param.11) | copy-start | bytes 6148
  13.8 6.4 %copy-start.2 = (bf16[2,512,512]{2,1,0:T(8,128)(2,1)S(1)}, bf16[2,512,512]{2,1,0:T(8,128)(2,1)}, u32[]{:S(2)}) copy-start(bf16[2,512,512]{2,1,0:T(8,128)(2,1)} %param.6) | copy-start | bytes 3145732
  22.8 1.2 slice-start
  33.9 1.2 copy-start.1
  33.9 1.5 %copy-start.3 = (bf16[1024,512]{0,1:T(8,128)(2,1)S(1)}, bf16[1024,512]{0,1:T(8,128)(2,1)}, u32[]{:S(2)}) copy-start(bf16[1024,512]{0,1:T(8,128)(2,1)} %bitcast_negate_fusion) | copy-start | bytes 3145732
  33.9 1.8 %copy-start.4 = (bf16[512,1024]{1,0:T(8,128)(2,1)S(1)}, bf16[512,1024]{1,0:T(8,128)(2,1)}, u32[]{:S(2)}) copy-start(bf16[512,1024]{1,0:T(8,128)(2,1)} %reshape.172) | copy-start | bytes 3145732
  38.2 2.2 %slice-start.1 = ((bf16[3,1,2,2,512,8]{4,5,3,2,1,0:T(8,128)(2,1)}), bf16[2,1,2,2,512,8]{4,5,3,2,1,0:T(8,128)(2,1)S(1)}, s32[]{:S(2)}) async-start(bf16[3,1,2,2,512,8]{4,5,3,2,1,0:T(8,128)(2,1)} %param.9), calls=%async_computation.3 | async-start | bytes 131072 | tf_op jit(solution)/shard_map/slice | solution.py:86
  38.2 2.2 %slice-start.2 = ((s32[3,1,2,512]{3,2,1,0:T(2,128)}), s32[2,1,2,512]{3,2,1,0:T(2,128)S(1)}, s32[]{:S(2)}) async-start(s32[3,1,2,512]{3,2,1,0:T(2,128)} %param.8), calls=%async_computation.4 | async-start | bytes 16384 | tf_op jit(solution)/shard_map/slice | solution.py:86
  38.3 11.6 %collective-permute-start.3 = (bf16[1024,512]{1,0:T(8,128)(2,1)S(1)}, bf16[1024,512]{1,0:T(8,128)(2,1)S(1)}, u32[]{:S(2)}, u32[]{:S(2)}) collective-permute-start(bf16[1024,512]{1,0:T(8,128)(2,1)S(1)} %bitcast.109), channel_id=1, source_target_pairs={{0,16},{16,0},{32,48},{48,32},{64,80},{80,64},{96,112},{112,96},{1... | collective-permute-start | bytes 3145736 | tf_op jit(solution)/shard_map/ppermute | solution.py:16
  42.4 7.6 %copy-start.5 = (bf16[512,512]{1,0:T(8,128)(2,1)S(1)}, bf16[512,512]{1,0:T(8,128)(2,1)}, u32[]{:S(2)}) copy-start(bf16[512,512]{1,0:T(8,128)(2,1)} %get-tuple-element.189) | copy-start | bytes 1572868
  42.4 7.6 %copy-start.6 = (bf16[512,512]{1,0:T(8,128)(2,1)S(1)}, bf16[512,512]{1,0:T(8,128)(2,1)}, u32[]{:S(2)}) copy-start(bf16[512,512]{1,0:T(8,128)(2,1)} %get-tuple-element.190) | copy-start | bytes 1572868
  42.4 7.6 %copy-start.7 = (bf16[512,512]{1,0:T(8,128)(2,1)S(1)}, bf16[512,512]{1,0:T(8,128)(2,1)}, u32[]{:S(2)}) copy-start(bf16[512,512]{1,0:T(8,128)(2,1)} %get-tuple-element.209) | copy-start | bytes 1572868
  50.0 1.3 copy-start.8
  50.0 1.3 copy-start.9
  50.0 1.3 copy-start.10
  53.6 25.9 %collective-permute-start.4 = (bf16[1024,512]{1,0:T(8,128)(2,1)}, bf16[1024,512]{1,0:T(8,128)(2,1)}, u32[]{:S(2)}, u32[]{:S(2)}) collective-permute-start(bf16[1024,512]{1,0:T(8,128)(2,1)} %add_convert_fusion.1), channel_id=1, source_target_pairs={{0,32},{16,48},{32,0},{48,16},{64,96},{80,112},{96,64},{112,80},{1... | collective-permute-start | bytes 3145736 | tf_op jit(solution)/shard_map/ppermute | solution.py:16
  58.3 24.9 %all-to-all-start = ((s32[128,2,8]{2,1,0:T(2,128)}), s32[128,2,8]{2,1,0:T(2,128)S(1)}, u32[]{:S(2)}, u32[]{:S(2)}) async-start(s32[128,2,8]{2,1,0:T(2,128)} %copy.38), calls=%async_computation | async-start | bytes 262144 | tf_op jit(solution)/shard_map/all_to_all | solution.py:100
  70.4 9.1 %copy-start.14 = (bf16[512,512]{1,0:T(8,128)(2,1)S(1)}, bf16[512,512]{1,0:T(8,128)(2,1)}, u32[]{:S(2)}) copy-start(bf16[512,512]{1,0:T(8,128)(2,1)} %get-tuple-element.183) | copy-start | bytes 1572868
  70.4 9.1 %copy-start.15 = (bf16[512,512]{1,0:T(8,128)(2,1)S(1)}, bf16[512,512]{1,0:T(8,128)(2,1)}, u32[]{:S(2)}) copy-start(bf16[512,512]{1,0:T(8,128)(2,1)} %get-tuple-element.184) | copy-start | bytes 1572868
  70.4 9.1 %copy-start.16 = (bf16[512,512]{1,0:T(8,128)(2,1)S(1)}, bf16[512,512]{1,0:T(8,128)(2,1)}, u32[]{:S(2)}) copy-start(bf16[512,512]{1,0:T(8,128)(2,1)} %get-tuple-element.206) | copy-start | bytes 1572868
  82.0 3.1 %copy-start.20 = (bf16[1024,512]{1,0:T(8,128)(2,1)}, bf16[1024,512]{1,0:T(8,128)(2,1)S(1)}, u32[]{:S(2)}) copy-start(bf16[1024,512]{1,0:T(8,128)(2,1)S(1)} %add_convert_fusion) | copy-start | bytes 3145732
  83.2 14.7 %collective-permute-start.5 = (bf16[1024,256]{1,0:T(8,128)(2,1)S(1)}, bf16[1024,256]{1,0:T(8,128)(2,1)S(1)}, u32[]{:S(2)}, u32[]{:S(2)}) collective-permute-start(bf16[1024,256]{1,0:T(8,128)(2,1)S(1)} %constant_dynamic-slice_fusion), channel_id=1, source_target_pairs={{0,64},{16,80},{32,96},{48,112},{64,0},{80,16},{96,32},{112,48},{1... | collective-permute-start | bytes 1572872 | tf_op jit(solution)/shard_map/ppermute | solution.py:16
  86.8 2.0 %copy-start.17 = (bf16[512,512]{1,0:T(8,128)(2,1)S(1)}, bf16[512,512]{1,0:T(8,128)(2,1)}, u32[]{:S(2)}) copy-start(bf16[512,512]{1,0:T(8,128)(2,1)} %get-tuple-element.179) | copy-start | bytes 1572868
  86.8 2.0 %copy-start.18 = (bf16[512,512]{1,0:T(8,128)(2,1)S(1)}, bf16[512,512]{1,0:T(8,128)(2,1)}, u32[]{:S(2)}) copy-start(bf16[512,512]{1,0:T(8,128)(2,1)} %get-tuple-element.180) | copy-start | bytes 1572868
  86.8 2.0 %copy-start.19 = (bf16[512,512]{1,0:T(8,128)(2,1)S(1)}, bf16[512,512]{1,0:T(8,128)(2,1)}, u32[]{:S(2)}) copy-start(bf16[512,512]{1,0:T(8,128)(2,1)} %get-tuple-element.204) | copy-start | bytes 1572868
  86.8 2.0 %copy-start.21 = (bf16[1024,512]{1,0:T(8,128)(2,1)S(1)}, bf16[1024,512]{1,0:T(8,128)(2,1)}, u32[]{:S(2)}) copy-start(bf16[1024,512]{1,0:T(8,128)(2,1)} %copy-done.20) | copy-start | bytes 3145732
  88.8 9.1 %copy-start.11 = (bf16[512,512]{1,0:T(8,128)(2,1)S(1)}, bf16[512,512]{1,0:T(8,128)(2,1)}, u32[]{:S(2)}) copy-start(bf16[512,512]{1,0:T(8,128)(2,1)} %get-tuple-element.181) | copy-start | bytes 1572868
  88.8 9.1 %copy-start.12 = (bf16[512,512]{1,0:T(8,128)(2,1)S(1)}, bf16[512,512]{1,0:T(8,128)(2,1)}, u32[]{:S(2)}) copy-start(bf16[512,512]{1,0:T(8,128)(2,1)} %get-tuple-element.182) | copy-start | bytes 1572868
  88.8 9.1 %copy-start.13 = (bf16[512,512]{1,0:T(8,128)(2,1)S(1)}, bf16[512,512]{1,0:T(8,128)(2,1)}, u32[]{:S(2)}) copy-start(bf16[512,512]{1,0:T(8,128)(2,1)} %get-tuple-element.205) | copy-start | bytes 1572868
  97.9 0.8 copy-start.24
  98.9 1.0 copy-start.25
  98.9 1.4 copy-start.26
  103.7 41.0 %all-to-all-start.1 = ((bf16[128,16,512]{2,1,0:T(8,128)(2,1)}), bf16[128,16,512]{2,1,0:T(8,128)(2,1)S(1)}, u32[]{:S(2)}, u32[]{:S(2)}) async-start(bf16[128,16,512]{2,1,0:T(8,128)(2,1)} %pad_maximum_fusion), calls=%async_computation.1 | async-start | bytes 4194304 | tf_op jit(solution)/shard_map/all_to_all | solution.py:124

commit v8 on v6

--- a/solution.py
+++ b/solution.py
@@ -69,20 +69,12 @@
     bit = 1 << last
     me_sub = lax.axis_index("sub")
     far = lambda value: from_partner(value, "sub", last)
-    far_weights = far(weights[last, 0])
-    far_ints = far(jnp.concatenate([offsets[last, 0].reshape(-1), owners.reshape(-1), targets.reshape(-1)]))
-    far_offsets = far_ints[: 2 * p_dev].reshape(2, p_dev)
-    far_owners = far_ints[2 * p_dev : 3 * p_dev]
-    far_targets = far_ints[3 * p_dev :]
-    by_group = {0: (owners.reshape(p_dev), targets.reshape(p_dev)), bit: (far_owners, far_targets)}
-    picks = {}
-    codes = []
-    for m in (0, bit):
-        dest, aim = by_group[m]
-        slot = dest * capacity + group_slots(dest, devices)
-        picks[m] = jnp.arange(devices * capacity, dtype=jnp.int32)[:, None] == slot[None, :]
-        codes.append(jnp.sum(jnp.where(picks[m], aim[None, :] + 1, 0), axis=1).reshape(devices, capacity))
-    labels = jnp.stack(codes, axis=1) - 1
+    dest = owners.reshape(p_dev)
+    aim = targets.reshape(p_dev)
+    slot = dest * capacity + group_slots(dest, devices)
+    pick = jnp.arange(devices * capacity, dtype=jnp.int32)[:, None] == slot[None, :]
+    labels = jnp.sum(jnp.where(pick, aim[None, :] + 1, 0), axis=1).reshape(devices, capacity) - 1
+    late = (offsets[last, 0], weights[last, 0], slot)
     for section in range(last):
         partner = from_partner(image, "sub", section)
         mine = merge_matrix(offsets[section, 0, 0], weights[section, 0, 0])
@@ -91,15 +83,29 @@
         merged = merged + jnp.dot(theirs, partner, preferred_element_type=jnp.float32)
         image = merged.astype(jnp.bfloat16)
         if section == 0:
-            labels, image = lax.optimization_barrier((labels, image))
+            (labels, late), image = lax.optimization_barrier(((labels, late), image))
             marks = lax.all_to_all(labels, ("sub", "rng"), split_axis=0, concat_axis=0, tiled=True)
+            own_offsets, own_weights, slot = late
+            far_weights = far(own_weights)
+            far_ints = far(jnp.concatenate([own_offsets.reshape(-1), slot]))
+            far_offsets = far_ints[: 2 * p_dev].reshape(2, p_dev)
+            far_slot = far_ints[2 * p_dev :]
+        if section == 1:
+            marks, image = lax.optimization_barrier((marks, image))
+    slots = jnp.arange(devices * capacity, dtype=jnp.int32)[:, None]
+    picks = {0: slots == slot[None, :], bit: slots == far_slot[None, :]}
+    grid = marks.reshape(n_sub, n_rng * capacity)
+    swapped = jnp.stack([grid[s ^ bit] for s in range(n_sub)], axis=0)
+    marks = jnp.stack(
+        [grid.reshape(devices, capacity), swapped.reshape(devices, capacity)], axis=1
+    ).reshape(devices, 2 * capacity)
     half = r_dev // 2
     keep_bit = (me_sub >> last) & 1
     kept = lax.dynamic_slice_in_dim(image, keep_bit * half, half, axis=1)
     sent = lax.dynamic_slice_in_dim(image, (1 - keep_bit) * half, half, axis=1)
     old = {0: kept, bit: far(sent)}
     bands = {
-        0: (offsets[last, 0], weights[last, 0]),
+        0: (own_offsets, own_weights),
         bit: (far_offsets, far_weights),
     }
     sends = []

time: 149 us -> 149 us (level)
  other arithmetic: 27.2 us -> 22.1 us
  starting transfers between devices: 31.7 us -> 34.9 us
  waiting for transfers between devices: 49.9 us -> 52.3 us
    ppermute x1, waiting for transfers between devices: 0.01 us -> 4.36 us  [shifted(): lax.ppermute(value, axis, [(source, source + steps) for source in range(f...]
    neg x8, other arithmetic: 21 us -> 17 us  [merge_matrix(): upper = jnp.concatenate([g_real, -g_imag], axis=1)]
    unnamed x65 -> x38, local copies, waits for them, and re-layouts: 4.33 us -> 3.39 us
  transfers between devices with their start and end apart: 8 -> 8, of which waited for: 3 -> 4; matrix products, arithmetic and copies ran while one was open for 36% -> 27% of each run, Pallas kernels for 0% -> 0%
where the time goes in v8:
time: 149 us
  waiting for transfers between devices  52.3 us (35%)
  starting transfers between devices  34.9 us (23%)
  other arithmetic  22.1 us (15%)
  local copies, waits for them, and re-layouts  20.1 us (13%)
  matrix products  18.8 us (13%)
    all_to_all x1, waiting for transfers between devices, on_device(): lax.all_to_all(payload, ('sub', 'rng'), split_axis=0, concat_axis=0, tile...  28.1 us
    ppermute x5, waiting for transfers between devices, from_partner(): lax.ppermute(value, axis, [(i, i ^ 1 << apart) for i in range(lax.axis_si...  19.9 us
    neg x8, other arithmetic, merge_matrix(): upper = jnp.concatenate([g_real, -g_imag], axis=1)  17 us
    all_to_all x1, starting transfers between devices, on_device(): lax.all_to_all(labels, ('sub', 'rng'), split_axis=0, concat_axis=0, tiled...  11.8 us
    ppermute x5, starting transfers between devices, from_partner(): lax.ppermute(value, axis, [(i, i ^ 1 << apart) for i in range(lax.axis_si...  11.3 us
    all_to_all x1, starting transfers between devices, on_device(): lax.all_to_all(payload, ('sub', 'rng'), split_axis=0, concat_axis=0, tile...  10.4 us
    another operation x4, local copies, waits for them, and re-layouts, replica_matrix(): jnp.tile(padded, block_len)[:block_len * width].reshape(block_len, width)  4.83 us
    dot_general x2, matrix products, on_device(): jnp.dot(theirs, partner, preferred_element_type=jnp.float32)  4.44 us
  transfers between devices with their start and end apart: 8, of which 4 were waited for; matrix products, arithmetic and copies ran while one was open for 27% of the time, Pallas kernels for 0%

profile of v8, /device:TPU:1, one launch (start us, length us, event | category | flops | bytes accessed | tf_op | source)
XLA Modules:
  0.0 148.7 jit_solution(2350758280201347524)
XLA Ops:
  0.0 1.4 collective-permute-start
  1.4 1.4 constant_dynamic-update-slice_fusion.1
  3.6 0.3 select_reduce_fusion
  3.9 0.7 sub.137
  4.7 2.3 %tile.9 = bf16[524800]{0:T(1024)(128)(2,1)} reshape(bf16[512,1025]{1,0:T(8,128)(2,1)S(1)} %tile.8) | data formatting | bytes 2099200 | tf_op jit(solution)/shard_map/tile | solution.py:25
  7.0 1.2 slice-done
  8.3 1.3 reshape.160
  9.6 2.3 %tile.21 = bf16[524800]{0:T(1024)(128)(2,1)} reshape(bf16[512,1025]{1,0:T(8,128)(2,1)S(1)} %tile.20) | data formatting | bytes 2099200 | tf_op jit(solution)/shard_map/tile | solution.py:25
  11.9 1.2 slice-done.1
  13.2 1.2 reshape.161
  14.4 1.3 bitcast_negate_fusion
  16.2 1.7 %fusion.334 = (bf16[512,512]{1,0:T(8,128)(2,1)S(1)}, bf16[512,512]{1,0:T(8,128)(2,1)S(1)}, bf16[512,512]{1,0:T(8,128)(2,1)S(1)}) fusion(bf16[512]{0:T(512)(128)(2,1)S(1)} %get-tuple-element.132, bf16[512]{0:T(512)(128)(2,1)S(1)} %get-tuple-element.133, bf16[512]{0:T(512)(128)(2,1)S(1)} %get-tuple-element.134, bf16[512]{0:T(512)(128)(2,1)S(1)} %get-tuple-element.135, ...), kind=kLoop, calls=%fused_computation.517 | loop fusion | flops 7340032 | bytes 1591296 | tf_op jit(solution)/shard_map/neg | solution.py:43
  18.0 1.7 %fusion.335 = (bf16[512,512]{1,0:T(8,128)(2,1)S(1)}, bf16[512,512]{1,0:T(8,128)(2,1)S(1)}, bf16[512,512]{1,0:T(8,128)(2,1)S(1)}) fusion(bf16[512]{0:T(512)(128)(2,1)S(1)} %get-tuple-element.116, bf16[512]{0:T(512)(128)(2,1)S(1)} %get-tuple-element.117, bf16[512]{0:T(512)(128)(2,1)S(1)} %get-tuple-element.118, bf16[512]{0:T(512)(128)(2,1)S(1)} %get-tuple-element.119, ...), kind=kLoop, calls=%fused_computation.518 | loop fusion | flops 7340032 | bytes 1591296 | tf_op jit(solution)/shard_map/neg | solution.py:43
  19.7 2.8 %fusion.336 = (bf16[512,512]{1,0:T(8,128)(2,1)}, bf16[512,512]{1,0:T(8,128)(2,1)}, bf16[512,512]{1,0:T(8,128)(2,1)}) fusion(bf16[512]{0:T(512)(128)(2,1)S(1)} %get-tuple-element.84, bf16[512]{0:T(512)(128)(2,1)S(1)} %get-tuple-element.85, bf16[512]{0:T(512)(128)(2,1)S(1)} %get-tuple-element.86, bf16[512]{0:T(512)(128)(2,1)S(1)} %get-tuple-element.87, ...), kind=kLoop, calls=%fused_computation.519 | loop fusion | flops 7340032 | bytes 1591296 | tf_op jit(solution)/shard_map/neg | solution.py:43
  22.5 4.4 %collective-permute-done = bf16[2,512,512]{2,1,0:T(8,128)(2,1)} collective-permute-done((bf16[2,512,512]{2,1,0:T(8,128)(2,1)}, bf16[2,512,512]{2,1,0:T(8,128)(2,1)}, u32[]{:S(2)}, u32[]{:S(2)}) %collective-permute-start) | collective-permute-done | bytes 1048608 | tf_op jit(solution)/shard_map/ppermute | solution.py:12
  26.9 1.4 constant_dynamic-update-slice_fusion
  28.4 1.0 copy-done
  29.5 0.3 copy-done.1
  29.8 2.4 %fusion.83 = bf16[512,1024]{1,0:T(8,128)(2,1)S(1)} fusion(bf16[1024,512]{0,1:T(8,128)(2,1)S(1)} %bitcast.119, bf16[1024,512]{0,1:T(8,128)(2,1)S(1)} %bitcast.118, bf16[1024,512]{0,1:T(8,128)(2,1)S(1)} %bitcast_negate_fusion, bf16[512,1024]{1,0:T(8,128)(2,1)S(1)} %get-tuple-element.152, bf16[512,1024]{1,0:T(8,128)(2,1)S(1)} %get-tuple-element.151), kind=kOutput, calls=%fused_computation.88 | convolution fusion | flops 2168979456 | bytes 6291456 | tf_op jit(solution)/shard_map/dot_general | solution.py:64
  32.2 1.7 %collective-permute-start.1 = (bf16[1024,512]{1,0:T(8,128)(2,1)S(1)}, bf16[1024,512]{1,0:T(8,128)(2,1)S(1)}, u32[]{:S(2)}, u32[]{:S(2)}) collective-permute-start(bf16[1024,512]{1,0:T(8,128)(2,1)S(1)} %bitcast.120), channel_id=1, source_target_pairs={{0,16},{16,0},{32,48},{48,32},{64,80},{80,64},{96,112},{112,96},{1... | collective-permute-start | bytes 3145736 | tf_op jit(solution)/shard_map/ppermute | solution.py:16
  34.0 1.7 %fusion.337 = (bf16[512,512]{1,0:T(8,128)(2,1)S(1)}, bf16[512,512]{1,0:T(8,128)(2,1)S(1)}, bf16[512,512]{1,0:T(8,128)(2,1)S(1)}) fusion(bf16[512]{0:T(512)(128)(2,1)S(1)} %get-tuple-element.68, bf16[512]{0:T(512)(128)(2,1)S(1)} %get-tuple-element.69, bf16[512]{0:T(512)(128)(2,1)S(1)} %get-tuple-element.70, bf16[512]{0:T(512)(128)(2,1)S(1)} %get-tuple-element.71, ...), kind=kLoop, calls=%fused_computation.520 | loop fusion | flops 7340032 | bytes 1591296 | tf_op jit(solution)/shard_map/neg | solution.py:43
  35.7 1.2 fusion.8
  37.0 2.2 %add_convert_fusion.1 = bf16[1024,512]{1,0:T(8,128)(2,1)} fusion(f32[1024,512]{1,0:T(8,128)S(1)} %fusion.8, bf16[1024,512]{1,0:T(8,128)(2,1)S(1)} %collective-permute-done.1, bf16[512,512]{1,0:T(8,128)(2,1)S(1)} %get-tuple-element.216, bf16[512,512]{1,0:T(8,128)(2,1)S(1)} %get-tuple-element.194, bf16[512,512]{1,0:T(8,128)(2,1)S(1)} %get-tuple-element.193), kind=kOutput, calls=%fused_computation.80 | convolution fusion | flops 1083179008 | bytes 5767168 | tf_op jit(solution)/shard_map/dot_general | solution.py:83
  39.2 3.8 %collective-permute-start.5 = (bf16[2,2,512,8]{2,3,1,0:T(8,128)(2,1)S(1)}, bf16[2,2,512,8]{2,3,1,0:T(8,128)(2,1)S(1)}, u32[]{:S(2)}, u32[]{:S(2)}) collective-permute-start(bf16[2,2,512,8]{2,3,1,0:T(8,128)(2,1)S(1)} %slice_bitcast_fusion.2), channel_id=1, source_target_pairs={{0,64},{16,80},{32,96},{48,112},{64,0},{80,16},{96,32},{112,48},{1... | collective-permute-start | bytes 98312 | tf_op jit(solution)/shard_map/ppermute | solution.py:16
  43.2 11.8 %all-to-all-start = ((s32[128,1,8]{2,1,0:T(1,128)}), s32[128,1,8]{2,1,0:T(1,128)S(1)}, u32[]{:S(2)}, u32[]{:S(2)}) async-start(s32[128,1,8]{2,1,0:T(1,128)} %bitcast.22), calls=%async_computation | async-start | bytes 131072 | tf_op jit(solution)/shard_map/all_to_all | solution.py:87
  55.0 1.7 %collective-permute-start.2 = (bf16[1024,512]{1,0:T(8,128)(2,1)}, bf16[1024,512]{1,0:T(8,128)(2,1)S(1)}, u32[]{:S(2)}, u32[]{:S(2)}) collective-permute-start(bf16[1024,512]{1,0:T(8,128)(2,1)} %add_convert_fusion.1), channel_id=1, source_target_pairs={{0,32},{16,48},{32,0},{48,16},{64,96},{80,112},{96,64},{112,80},{1... | collective-permute-start | bytes 3145736 | tf_op jit(solution)/shard_map/ppermute | solution.py:16
  57.0 2.5 %fusion.27 = f32[1024,512]{1,0:T(8,128)S(1)} fusion(bf16[1024,512]{1,0:T(8,128)(2,1)} %add_convert_fusion.1, bf16[512,512]{1,0:T(8,128)(2,1)S(1)} %copy-done.7, bf16[512,512]{1,0:T(8,128)(2,1)S(1)} %copy-done.6, bf16[512,512]{1,0:T(8,128)(2,1)S(1)} %copy-done.5), kind=kOutput, calls=%fused_computation.27 | convolution fusion | flops 1082130432 | bytes 4718592 | tf_op jit(solution)/shard_map/dot_general | solution.py:82
  59.5 1.7 %fusion.338 = (bf16[512,512]{1,0:T(8,128)(2,1)S(1)}, bf16[512,512]{1,0:T(8,128)(2,1)S(1)}, bf16[512,512]{1,0:T(8,128)(2,1)S(1)}) fusion(bf16[512]{0:T(512)(128)(2,1)S(1)} %get-tuple-element.36, bf16[512]{0:T(512)(128)(2,1)S(1)} %get-tuple-element.37, bf16[512]{0:T(512)(128)(2,1)S(1)} %get-tuple-element.38, bf16[512]{0:T(512)(128)(2,1)S(1)} %get-tuple-element.39, ...), kind=kLoop, calls=%fused_computation.521 | loop fusion | flops 7340032 | bytes 1591296 | tf_op jit(solution)/shard_map/neg | solution.py:43
  61.2 2.8 %fusion.339 = (bf16[512,512]{1,0:T(8,128)(2,1)}, bf16[512,512]{1,0:T(8,128)(2,1)}, bf16[512,512]{1,0:T(8,128)(2,1)}) fusion(bf16[512]{0:T(512)(128)(2,1)S(1)} %get-tuple-element.20, bf16[512]{0:T(512)(128)(2,1)S(1)} %get-tuple-element.21, bf16[512]{0:T(512)(128)(2,1)S(1)} %get-tuple-element.22, bf16[512]{0:T(512)(128)(2,1)S(1)} %get-tuple-element.23, ...), kind=kLoop, calls=%fused_computation.522 | loop fusion | flops 7340032 | bytes 1591296 | tf_op jit(solution)/shard_map/neg | solution.py:43
  64.2 2.8 %fusion.341 = (bf16[512,512]{1,0:T(8,128)(2,1)}, bf16[512,512]{1,0:T(8,128)(2,1)}, bf16[512,512]{1,0:T(8,128)(2,1)}) fusion(bf16[512]{0:T(512)(128)(2,1)S(1)} %get-tuple-element.100, bf16[512]{0:T(512)(128)(2,1)S(1)} %get-tuple-element.101, bf16[512]{0:T(512)(128)(2,1)S(1)} %get-tuple-element.102, bf16[512]{0:T(512)(128)(2,1)S(1)} %get-tuple-element.103, ...), kind=kLoop, calls=%fused_computation.524 | loop fusion | flops 7340032 | bytes 1591296 | tf_op jit(solution)/shard_map/neg | solution.py:43
  67.0 12.9 %collective-permute-done.2 = bf16[1024,512]{1,0:T(8,128)(2,1)S(1)} collective-permute-done((bf16[1024,512]{1,0:T(8,128)(2,1)}, bf16[1024,512]{1,0:T(8,128)(2,1)S(1)}, u32[]{:S(2)}, u32[]{:S(2)}) %collective-permute-start.2) | collective-permute-done | bytes 1048608 | tf_op jit(solution)/shard_map/ppermute | solution.py:16
  80.0 2.2 %add_convert_fusion = bf16[1024,512]{1,0:T(8,128)(2,1)} fusion(f32[1024,512]{1,0:T(8,128)S(1)} %fusion.27, bf16[1024,512]{1,0:T(8,128)(2,1)S(1)} %collective-permute-done.2, bf16[512,512]{1,0:T(8,128)(2,1)S(1)} %get-tuple-element.213, bf16[512,512]{1,0:T(8,128)(2,1)S(1)} %get-tuple-element.188, bf16[512,512]{1,0:T(8,128)(2,1)S(1)} %get-tuple-element.187), kind=kOutput, calls=%fused_computation.79 | convolution fusion | flops 1083179008 | bytes 5767168 | tf_op jit(solution)/shard_map/dot_general | solution.py:83
  82.2 1.2 constant_dynamic-slice_fusion
  83.4 3.9 %collective-permute-start.3 = (bf16[1024,256]{1,0:T(8,128)(2,1)S(1)}, bf16[1024,256]{1,0:T(8,128)(2,1)S(1)}, u32[]{:S(2)}, u32[]{:S(2)}) collective-permute-start(bf16[1024,256]{1,0:T(8,128)(2,1)S(1)} %constant_dynamic-slice_fusion), channel_id=1, source_target_pairs={{0,64},{16,80},{32,96},{48,112},{64,0},{80,16},{96,32},{112,48},{1... | collective-permute-start | bytes 1572872 | tf_op jit(solution)/shard_map/ppermute | solution.py:16
  87.3 1.7 %fusion.340 = (bf16[512,512]{1,0:T(8,128)(2,1)S(1)}, bf16[512,512]{1,0:T(8,128)(2,1)S(1)}, bf16[512,512]{1,0:T(8,128)(2,1)S(1)}) fusion(bf16[512]{0:T(512)(128)(2,1)S(1)} %get-tuple-element.52, bf16[512]{0:T(512)(128)(2,1)S(1)} %get-tuple-element.53, bf16[512]{0:T(512)(128)(2,1)S(1)} %get-tuple-element.54, bf16[512]{0:T(512)(128)(2,1)S(1)} %get-tuple-element.55, ...), kind=kLoop, calls=%fused_computation.523 | loop fusion | flops 7340032 | bytes 1591296 | tf_op jit(solution)/shard_map/neg | solution.py:43
  89.1 0.7 fusion.67
  89.8 1.7 %fusion.43 = f32[1024,256]{1,0:T(8,128)} fusion(bf16[512,512]{1,0:T(8,128)(2,1)S(1)} %get-tuple-element.211, bf16[512,512]{1,0:T(8,128)(2,1)S(1)} %get-tuple-element.184, bf16[512,512]{1,0:T(8,128)(2,1)S(1)} %get-tuple-element.183, bf16[1024,512]{1,0:T(8,128)(2,1)S(1)} %copy-done.11, s32[]{:T(128)S(6)} %select_n.476), kind=kOutput, calls=%fused_computation.43 | convolution fusion | flops 545259520 | bytes 3145732 | tf_op jit(solution)/shard_map/dot_general | solution.py:116
  91.5 6.9 %collective-permute-done.3 = bf16[1024,256]{1,0:T(8,128)(2,1)S(1)} collective-permute-done((bf16[1024,256]{1,0:T(8,128)(2,1)S(1)}, bf16[1024,256]{1,0:T(8,128)(2,1)S(1)}, u32[]{:S(2)}, u32[]{:S(2)}) %collective-permute-start.3) | collective-permute-done | bytes 524320 | tf_op jit(solution)/shard_map/ppermute | solution.py:16
  98.4 0.7 fusion.103
  100.0 2.1 %fusion.100 = bf16[1024,256]{1,0:T(8,128)(2,1)S(1)} fusion(f32[1024,256]{1,0:T(8,128)} %fusion.43, bf16[1024,256]{1,0:T(8,128)(2,1)} %copy-done.17, bf16[512,512]{1,0:T(8,128)(2,1)S(1)} %copy-done.4, bf16[512,512]{1,0:T(8,128)(2,1)S(1)} %copy-done.3, bf16[512,512]{1,0:T(8,128)(2,1)S(1)} %copy-done.2), kind=kOutput, calls=%fused_computation.97 | convolution fusion | flops 545783808 | bytes 3670016 | tf_op jit(solution)/shard_map/dot_general | solution.py:117
  102.3 0.8 fusion.90
  103.0 0.8 fusion.91
  103.8 1.7 %pad_maximum_fusion = bf16[128,16,512]{2,1,0:T(8,128)(2,1)} fusion(bf16[128,8,512]{2,1,0:T(8,128)(2,1)S(1)} %fusion.91, bf16[128,8,512]{2,1,0:T(8,128)(2,1)S(1)} %fusion.90), kind=kLoop, calls=%fused_computation.75 | loop fusion | flops 4194304 | bytes 4194304 | tf_op jit(solution)/shard_map/concatenate | solution.py:122
  105.5 10.4 %all-to-all-start.1 = ((bf16[128,16,512]{2,1,0:T(8,128)(2,1)}), bf16[128,16,512]{2,1,0:T(8,128)(2,1)S(1)}, u32[]{:S(2)}, u32[]{:S(2)}) async-start(bf16[128,16,512]{2,1,0:T(8,128)(2,1)} %pad_maximum_fusion), calls=%async_computation.1 | async-start | bytes 4194304 | tf_op jit(solution)/shard_map/all_to_all | solution.py:123
  117.4 28.1 %all-to-all-done.1 = bf16[128,16,512]{2,1,0:T(8,128)(2,1)S(1)} async-done(((bf16[128,16,512]{2,1,0:T(8,128)(2,1)}), bf16[128,16,512]{2,1,0:T(8,128)(2,1)S(1)}, u32[]{:S(2)}, u32[]{:S(2)}) %all-to-all-start.1) | async-done | bytes 2097184 | tf_op jit(solution)/shard_map/all_to_all | solution.py:123
  145.7 0.8 fusion.98
  146.7 0.8 fusion.99
  147.7 1.1 maximum_bitcast_fusion
  (106 shorter events, 5.3 us)
Async XLA Ops:
  0.0 2.8 %copy-start.16 = (s32[1,1,512]{2,1,0:T(1,128)S(1)}, s32[1,1,512]{2,1,0:T(1,128)}, u32[]{:S(2)}) copy-start(s32[1,1,512]{2,1,0:T(1,128)} %param.11) | copy-start | bytes 6148
  0.0 2.8 %copy-start.13 = (s32[1,1,512,1]{2,3,1,0:T(1,128)S(1)}, s32[1,1,512,1]{2,3,1,0:T(1,128)}, u32[]{:S(2)}) copy-start(s32[1,1,512,1]{2,3,1,0:T(1,128)} %param.10) | copy-start | bytes 6148
  0.0 4.6 %copy-start.15 = (bf16[2,512]{1,0:T(2,128)(2,1)S(1)}, bf16[2,512]{1,0:T(2,128)(2,1)}, u32[]{:S(2)}) copy-start(bf16[2,512]{1,0:T(2,128)(2,1)} %param.7) | copy-start | bytes 6148
  0.0 26.8 %collective-permute-start = (bf16[2,512,512]{2,1,0:T(8,128)(2,1)}, bf16[2,512,512]{2,1,0:T(8,128)(2,1)}, u32[]{:S(2)}, u32[]{:S(2)}) collective-permute-start(bf16[2,512,512]{2,1,0:T(8,128)(2,1)} %param.6), channel_id=1, source_target_pairs={{1,0},{2,1},{3,2},{4,3},{5,4},{6,5},{7,6},{8,7},{9,8},{10,9},{11,1... | collective-permute-start | bytes 3145736 | tf_op jit(solution)/shard_map/ppermute | solution.py:12
  7.0 1.2 slice-start
  11.9 1.2 slice-start.1
  13.2 2.5 %copy-start.12 = (bf16[3,1,2,2,512,8]{4,5,3,2,1,0:T(8,128)(2,1)S(1)}, bf16[3,1,2,2,512,8]{4,5,3,2,1,0:T(8,128)(2,1)}, u32[]{:S(2)}) copy-start(bf16[3,1,2,2,512,8]{4,5,3,2,1,0:T(8,128)(2,1)} %param.9) | copy-start | bytes 294916
  13.2 2.6 %copy-start.14 = (s32[3,1,2,512]{3,2,1,0:T(2,128)S(1)}, s32[3,1,2,512]{3,2,1,0:T(2,128)}, u32[]{:S(2)}) copy-start(s32[3,1,2,512]{3,2,1,0:T(2,128)} %param.8) | copy-start | bytes 36868
  28.2 1.2 copy-start
  28.2 1.5 %copy-start.1 = (bf16[512,1024]{1,0:T(8,128)(2,1)S(1)}, bf16[512,1024]{1,0:T(8,128)(2,1)}, u32[]{:S(2)}) copy-start(bf16[512,1024]{1,0:T(8,128)(2,1)} %reshape.160) | copy-start | bytes 3145732
  32.2 4.7 %collective-permute-start.1 = (bf16[1024,512]{1,0:T(8,128)(2,1)S(1)}, bf16[1024,512]{1,0:T(8,128)(2,1)S(1)}, u32[]{:S(2)}, u32[]{:S(2)}) collective-permute-start(bf16[1024,512]{1,0:T(8,128)(2,1)S(1)} %bitcast.120), channel_id=1, source_target_pairs={{0,16},{16,0},{32,48},{48,32},{64,80},{80,64},{96,112},{112,96},{1... | collective-permute-start | bytes 3145736 | tf_op jit(solution)/shard_map/ppermute | solution.py:16
  36.9 20.0 %copy-start.5 = (bf16[512,512]{1,0:T(8,128)(2,1)S(1)}, bf16[512,512]{1,0:T(8,128)(2,1)}, u32[]{:S(2)}) copy-start(bf16[512,512]{1,0:T(8,128)(2,1)} %get-tuple-element.189) | copy-start | bytes 1572868
  36.9 20.0 %copy-start.6 = (bf16[512,512]{1,0:T(8,128)(2,1)S(1)}, bf16[512,512]{1,0:T(8,128)(2,1)}, u32[]{:S(2)}) copy-start(bf16[512,512]{1,0:T(8,128)(2,1)} %get-tuple-element.190) | copy-start | bytes 1572868
  37.0 20.0 %copy-start.7 = (bf16[512,512]{1,0:T(8,128)(2,1)S(1)}, bf16[512,512]{1,0:T(8,128)(2,1)}, u32[]{:S(2)}) copy-start(bf16[512,512]{1,0:T(8,128)(2,1)} %get-tuple-element.214) | copy-start | bytes 1572868
  39.2 24.8 %collective-permute-start.5 = (bf16[2,2,512,8]{2,3,1,0:T(8,128)(2,1)S(1)}, bf16[2,2,512,8]{2,3,1,0:T(8,128)(2,1)S(1)}, u32[]{:S(2)}, u32[]{:S(2)}) collective-permute-start(bf16[2,2,512,8]{2,3,1,0:T(8,128)(2,1)S(1)} %slice_bitcast_fusion.2), channel_id=1, source_target_pairs={{0,64},{16,80},{32,96},{48,112},{64,0},{80,16},{96,32},{112,48},{1... | collective-permute-start | bytes 98312 | tf_op jit(solution)/shard_map/ppermute | solution.py:16
  43.1 20.9 %collective-permute-start.4 = (s32[1536]{0:T(1024)S(1)}, s32[1536]{0:T(1024)S(1)}, u32[]{:S(2)}, u32[]{:S(2)}) collective-permute-start(s32[1536]{0:T(1024)S(1)} %pad_add_fusion.2), channel_id=1, source_target_pairs={{0,64},{16,80},{32,96},{48,112},{64,0},{80,16},{96,32},{112,48},{1... | collective-permute-start | bytes 18440 | tf_op jit(solution)/shard_map/ppermute | solution.py:16
  43.2 39.0 %all-to-all-start = ((s32[128,1,8]{2,1,0:T(1,128)}), s32[128,1,8]{2,1,0:T(1,128)S(1)}, u32[]{:S(2)}, u32[]{:S(2)}) async-start(s32[128,1,8]{2,1,0:T(1,128)} %bitcast.22), calls=%async_computation | async-start | bytes 131072 | tf_op jit(solution)/shard_map/all_to_all | solution.py:87
  55.0 25.0 %collective-permute-start.2 = (bf16[1024,512]{1,0:T(8,128)(2,1)}, bf16[1024,512]{1,0:T(8,128)(2,1)S(1)}, u32[]{:S(2)}, u32[]{:S(2)}) collective-permute-start(bf16[1024,512]{1,0:T(8,128)(2,1)} %add_convert_fusion.1), channel_id=1, source_target_pairs={{0,32},{16,48},{32,0},{48,16},{64,96},{80,112},{96,64},{112,80},{1... | collective-permute-start | bytes 3145736 | tf_op jit(solution)/shard_map/ppermute | solution.py:16
  82.2 6.8 %copy-start.8 = (bf16[512,512]{1,0:T(8,128)(2,1)S(1)}, bf16[512,512]{1,0:T(8,128)(2,1)}, u32[]{:S(2)}) copy-start(bf16[512,512]{1,0:T(8,128)(2,1)} %get-tuple-element.191) | copy-start | bytes 1572868
  82.2 6.8 %copy-start.9 = (bf16[512,512]{1,0:T(8,128)(2,1)S(1)}, bf16[512,512]{1,0:T(8,128)(2,1)}, u32[]{:S(2)}) copy-start(bf16[512,512]{1,0:T(8,128)(2,1)} %get-tuple-element.192) | copy-start | bytes 1572868
  82.2 6.9 %copy-start.10 = (bf16[512,512]{1,0:T(8,128)(2,1)S(1)}, bf16[512,512]{1,0:T(8,128)(2,1)}, u32[]{:S(2)}) copy-start(bf16[512,512]{1,0:T(8,128)(2,1)} %get-tuple-element.215) | copy-start | bytes 1572868
  82.2 6.9 %copy-start.11 = (bf16[1024,512]{1,0:T(8,128)(2,1)S(1)}, bf16[1024,512]{1,0:T(8,128)(2,1)}, u32[]{:S(2)}) copy-start(bf16[1024,512]{1,0:T(8,128)(2,1)} %add_convert_fusion) | copy-start | bytes 3145732
  83.4 15.0 %collective-permute-start.3 = (bf16[1024,256]{1,0:T(8,128)(2,1)S(1)}, bf16[1024,256]{1,0:T(8,128)(2,1)S(1)}, u32[]{:S(2)}, u32[]{:S(2)}) collective-permute-start(bf16[1024,256]{1,0:T(8,128)(2,1)S(1)} %constant_dynamic-slice_fusion), channel_id=1, source_target_pairs={{0,64},{16,80},{32,96},{48,112},{64,0},{80,16},{96,32},{112,48},{1... | collective-permute-start | bytes 1572872 | tf_op jit(solution)/shard_map/ppermute | solution.py:16
  98.4 0.8 copy-start.17
  98.4 1.2 copy-start.2
  98.4 1.4 copy-start.3
  98.4 1.5 %copy-start.4 = (bf16[512,512]{1,0:T(8,128)(2,1)S(1)}, bf16[512,512]{1,0:T(8,128)(2,1)}, u32[]{:S(2)}) copy-start(bf16[512,512]{1,0:T(8,128)(2,1)} %get-tuple-element.210) | copy-start | bytes 1572868
  105.5 40.0 %all-to-all-start.1 = ((bf16[128,16,512]{2,1,0:T(8,128)(2,1)}), bf16[128,16,512]{2,1,0:T(8,128)(2,1)S(1)}, u32[]{:S(2)}, u32[]{:S(2)}) async-start(bf16[128,16,512]{2,1,0:T(8,128)(2,1)} %pad_maximum_fusion), calls=%async_computation.1 | async-start | bytes 4194304 | tf_op jit(solution)/shard_map/all_to_all | solution.py:123

commit v9 on v8

--- a/solution.py
+++ b/solution.py
@@ -80,16 +80,16 @@
         mine = merge_matrix(offsets[section, 0, 0], weights[section, 0, 0])
         theirs = merge_matrix(offsets[section, 0, 1], weights[section, 0, 1])
         merged = jnp.dot(mine, image, preferred_element_type=jnp.float32)
-        merged = merged + jnp.dot(theirs, partner, preferred_element_type=jnp.float32)
-        image = merged.astype(jnp.bfloat16)
-        if section == 0:
-            (labels, late), image = lax.optimization_barrier(((labels, late), image))
+        if section == 1:
+            (labels, late), merged = lax.optimization_barrier(((labels, late), merged))
             marks = lax.all_to_all(labels, ("sub", "rng"), split_axis=0, concat_axis=0, tiled=True)
             own_offsets, own_weights, slot = late
             far_weights = far(own_weights)
             far_ints = far(jnp.concatenate([own_offsets.reshape(-1), slot]))
             far_offsets = far_ints[: 2 * p_dev].reshape(2, p_dev)
             far_slot = far_ints[2 * p_dev :]
+        merged = merged + jnp.dot(theirs, partner, preferred_element_type=jnp.float32)
+        image = merged.astype(jnp.bfloat16)
         if section == 1:
             marks, image = lax.optimization_barrier((marks, image))
     slots = jnp.arange(devices * capacity, dtype=jnp.int32)[:, None]

time: 149 us -> 142 us (0.953)
  waiting for transfers between devices: 52.3 us -> 47.3 us
  starting transfers between devices: 34.9 us -> 30.6 us
  matrix products: 18.8 us -> 21.4 us
    ppermute x5, waiting for transfers between devices: 19.9 us -> 13.8 us  [from_partner(): lax.ppermute(value, axis, [(i, i ^ 1 << apart) for i in range(lax.axis_si...]
    ppermute x5, starting transfers between devices: 11.3 us -> 7.08 us  [from_partner(): lax.ppermute(value, axis, [(i, i ^ 1 << apart) for i in range(lax.axis_si...]
    unnamed x38 -> x34, local copies, waits for them, and re-layouts: 3.39 us -> 3.38 us
  transfers between devices with their start and end apart: 8 -> 8, of which waited for: 4 -> 4; matrix products, arithmetic and copies ran while one was open for 27% -> 29% of each run, Pallas kernels for 0% -> 0%
where the time goes in v9:
time: 142 us; the launch traced here: 141 us
  waiting for transfers between devices  47.3 us (33%)
  starting transfers between devices  30.6 us (22%)
  matrix products  21.4 us (15%)
  other arithmetic  21.1 us (15%)
  local copies, waits for them, and re-layouts  20 us (14%)
    all_to_all x1, waiting for transfers between devices, on_device(): lax.all_to_all(payload, ('sub', 'rng'), split_axis=0, concat_axis=0, tile...  28.1 us
    neg x8, other arithmetic, merge_matrix(): upper = jnp.concatenate([g_real, -g_imag], axis=1)  16 us
    ppermute x5, waiting for transfers between devices, from_partner(): lax.ppermute(value, axis, [(i, i ^ 1 << apart) for i in range(lax.axis_si...  13.8 us
    all_to_all x1, starting transfers between devices, on_device(): lax.all_to_all(labels, ('sub', 'rng'), split_axis=0, concat_axis=0, tiled...  11.9 us
    all_to_all x1, starting transfers between devices, on_device(): lax.all_to_all(payload, ('sub', 'rng'), split_axis=0, concat_axis=0, tile...  10.1 us
    ppermute x5, starting transfers between devices, from_partner(): lax.ppermute(value, axis, [(i, i ^ 1 << apart) for i in range(lax.axis_si...  7.08 us
    dot_general x2, matrix products, on_device(): jnp.dot(theirs, partner, preferred_element_type=jnp.float32)  5.65 us
    ppermute x1, waiting for transfers between devices, shifted(): lax.ppermute(value, axis, [(source, source + steps) for source in range(f...  5.43 us
  transfers between devices with their start and end apart: 8, of which 4 were waited for; matrix products, arithmetic and copies ran while one was open for 29% of the time, Pallas kernels for 0%

profile of v9, /device:TPU:1, one launch (start us, length us, event | category | flops | bytes accessed | tf_op | source)
XLA Modules:
  0.0 141.0 jit_solution(4989821022122178450)
XLA Ops:
  0.0 1.4 %collective-permute-start = (bf16[2,512,512]{2,1,0:T(8,128)(2,1)}, bf16[2,512,512]{2,1,0:T(8,128)(2,1)}, u32[]{:S(2)}, u32[]{:S(2)}) collective-permute-start(bf16[2,512,512]{2,1,0:T(8,128)(2,1)} %param.6), channel_id=1, source_target_pairs={{1,0},{2,1},{3,2},{4,3},{5,4},{6,5},{7,6},{8,7},{9,8},{10,9},{11,1... | collective-permute-start | bytes 3145736 | tf_op jit(solution)/shard_map/ppermute | solution.py:12
  1.4 1.4 constant_dynamic-update-slice_fusion.1
  3.3 0.2 fusion.304
  3.6 0.3 select_reduce_fusion
  3.9 0.7 sub.137
  4.7 2.3 %tile.9 = bf16[524800]{0:T(1024)(128)(2,1)} reshape(bf16[512,1025]{1,0:T(8,128)(2,1)S(1)} %tile.8) | data formatting | bytes 2099200 | tf_op jit(solution)/shard_map/tile | solution.py:25
  7.0 1.2 slice-done
  8.2 1.3 reshape.160
  9.6 2.3 %tile.21 = bf16[524800]{0:T(1024)(128)(2,1)} reshape(bf16[512,1025]{1,0:T(8,128)(2,1)S(1)} %tile.20) | data formatting | bytes 2099200 | tf_op jit(solution)/shard_map/tile | solution.py:25
  11.9 1.2 slice-done.1
  13.1 1.3 reshape.161
  14.4 1.3 bitcast_negate_fusion
  16.2 1.7 %fusion.335 = (bf16[512,512]{1,0:T(8,128)(2,1)S(1)}, bf16[512,512]{1,0:T(8,128)(2,1)S(1)}, bf16[512,512]{1,0:T(8,128)(2,1)S(1)}) fusion(bf16[512]{0:T(512)(128)(2,1)S(1)} %get-tuple-element.132, bf16[512]{0:T(512)(128)(2,1)S(1)} %get-tuple-element.133, bf16[512]{0:T(512)(128)(2,1)S(1)} %get-tuple-element.134, bf16[512]{0:T(512)(128)(2,1)S(1)} %get-tuple-element.135, ...), kind=kLoop, calls=%fused_computation.518 | loop fusion | flops 7340032 | bytes 1591296 | tf_op jit(solution)/shard_map/neg | solution.py:43
  17.9 1.7 %fusion.336 = (bf16[512,512]{1,0:T(8,128)(2,1)S(1)}, bf16[512,512]{1,0:T(8,128)(2,1)S(1)}, bf16[512,512]{1,0:T(8,128)(2,1)S(1)}) fusion(bf16[512]{0:T(512)(128)(2,1)S(1)} %get-tuple-element.116, bf16[512]{0:T(512)(128)(2,1)S(1)} %get-tuple-element.117, bf16[512]{0:T(512)(128)(2,1)S(1)} %get-tuple-element.118, bf16[512]{0:T(512)(128)(2,1)S(1)} %get-tuple-element.119, ...), kind=kLoop, calls=%fused_computation.519 | loop fusion | flops 7340032 | bytes 1591296 | tf_op jit(solution)/shard_map/neg | solution.py:43
  19.7 1.7 %fusion.334 = (bf16[512,512]{1,0:T(8,128)(2,1)S(1)}, bf16[512,512]{1,0:T(8,128)(2,1)S(1)}, bf16[512,512]{1,0:T(8,128)(2,1)S(1)}) fusion(bf16[512]{0:T(512)(128)(2,1)S(1)} %get-tuple-element.100, bf16[512]{0:T(512)(128)(2,1)S(1)} %get-tuple-element.101, bf16[512]{0:T(512)(128)(2,1)S(1)} %get-tuple-element.102, bf16[512]{0:T(512)(128)(2,1)S(1)} %get-tuple-element.103, ...), kind=kLoop, calls=%fused_computation.517 | loop fusion | flops 7340032 | bytes 1591296 | tf_op jit(solution)/shard_map/neg | solution.py:43
  21.4 5.4 %collective-permute-done = bf16[2,512,512]{2,1,0:T(8,128)(2,1)} collective-permute-done((bf16[2,512,512]{2,1,0:T(8,128)(2,1)}, bf16[2,512,512]{2,1,0:T(8,128)(2,1)}, u32[]{:S(2)}, u32[]{:S(2)}) %collective-permute-start) | collective-permute-done | bytes 1048608 | tf_op jit(solution)/shard_map/ppermute | solution.py:12
  26.9 1.4 constant_dynamic-update-slice_fusion
  28.4 1.0 copy-done
  29.5 0.3 copy-done.1
  29.8 2.4 %fusion.83 = bf16[512,1024]{1,0:T(8,128)(2,1)S(1)} fusion(bf16[1024,512]{0,1:T(8,128)(2,1)S(1)} %bitcast.119, bf16[1024,512]{0,1:T(8,128)(2,1)S(1)} %bitcast.118, bf16[1024,512]{0,1:T(8,128)(2,1)S(1)} %bitcast_negate_fusion, bf16[512,1024]{1,0:T(8,128)(2,1)S(1)} %get-tuple-element.152, bf16[512,1024]{1,0:T(8,128)(2,1)S(1)} %get-tuple-element.151), kind=kOutput, calls=%fused_computation.88 | convolution fusion | flops 2168979456 | bytes 6291456 | tf_op jit(solution)/shard_map/dot_general | solution.py:64
  32.2 1.7 %collective-permute-start.1 = (bf16[1024,512]{1,0:T(8,128)(2,1)S(1)}, bf16[1024,512]{1,0:T(8,128)(2,1)S(1)}, u32[]{:S(2)}, u32[]{:S(2)}) collective-permute-start(bf16[1024,512]{1,0:T(8,128)(2,1)S(1)} %bitcast.120), channel_id=1, source_target_pairs={{0,16},{16,0},{32,48},{48,32},{64,80},{80,64},{96,112},{112,96},{1... | collective-permute-start | bytes 3145736 | tf_op jit(solution)/shard_map/ppermute | solution.py:16
  34.0 1.7 %fusion.337 = (bf16[512,512]{1,0:T(8,128)(2,1)S(1)}, bf16[512,512]{1,0:T(8,128)(2,1)S(1)}, bf16[512,512]{1,0:T(8,128)(2,1)S(1)}) fusion(bf16[512]{0:T(512)(128)(2,1)S(1)} %get-tuple-element.68, bf16[512]{0:T(512)(128)(2,1)S(1)} %get-tuple-element.69, bf16[512]{0:T(512)(128)(2,1)S(1)} %get-tuple-element.70, bf16[512]{0:T(512)(128)(2,1)S(1)} %get-tuple-element.71, ...), kind=kLoop, calls=%fused_computation.520 | loop fusion | flops 7340032 | bytes 1591296 | tf_op jit(solution)/shard_map/neg | solution.py:43
  35.7 1.2 fusion.16
  36.9 2.2 %add_convert_fusion.1 = bf16[1024,512]{1,0:T(8,128)(2,1)} fusion(f32[1024,512]{1,0:T(8,128)S(1)} %fusion.16, bf16[1024,512]{1,0:T(8,128)(2,1)S(1)} %collective-permute-done.1, bf16[512,512]{1,0:T(8,128)(2,1)S(1)} %get-tuple-element.216, bf16[512,512]{1,0:T(8,128)(2,1)S(1)} %get-tuple-element.194, bf16[512,512]{1,0:T(8,128)(2,1)S(1)} %get-tuple-element.193), kind=kOutput, calls=%fused_computation.80 | convolution fusion | flops 1083179008 | bytes 5767168 | tf_op jit(solution)/shard_map/dot_general | solution.py:91
  39.2 1.9 %collective-permute-start.2 = (bf16[1024,512]{1,0:T(8,128)(2,1)}, bf16[1024,512]{1,0:T(8,128)(2,1)}, u32[]{:S(2)}, u32[]{:S(2)}) collective-permute-start(bf16[1024,512]{1,0:T(8,128)(2,1)} %add_convert_fusion.1), channel_id=1, source_target_pairs={{0,32},{16,48},{32,0},{48,16},{64,96},{80,112},{96,64},{112,80},{1... | collective-permute-start | bytes 3145736 | tf_op jit(solution)/shard_map/ppermute | solution.py:16
  41.0 3.9 %fusion.8 = f32[1024,512]{1,0:T(8,128)} fusion(bf16[1024,512]{1,0:T(8,128)(2,1)} %add_convert_fusion.1, bf16[512,512]{1,0:T(8,128)(2,1)S(1)} %get-tuple-element.215, bf16[512,512]{1,0:T(8,128)(2,1)S(1)} %get-tuple-element.192, bf16[512,512]{1,0:T(8,128)(2,1)S(1)} %get-tuple-element.191), kind=kOutput, calls=%fused_computation.8 | convolution fusion | flops 1082130432 | bytes 4718592 | tf_op jit(solution)/shard_map/dot_general | solution.py:82
  44.9 3.3 %collective-permute-start.5 = (bf16[2,2,512,8]{2,3,1,0:T(8,128)(2,1)S(1)}, bf16[2,2,512,8]{2,3,1,0:T(8,128)(2,1)S(1)}, u32[]{:S(2)}, u32[]{:S(2)}) collective-permute-start(bf16[2,2,512,8]{2,3,1,0:T(8,128)(2,1)S(1)} %slice_bitcast_fusion.2), channel_id=1, source_target_pairs={{0,64},{16,80},{32,96},{48,112},{64,0},{80,16},{96,32},{112,48},{1... | collective-permute-start | bytes 98312 | tf_op jit(solution)/shard_map/ppermute | solution.py:16
  48.3 11.9 %all-to-all-start = ((s32[128,1,8]{2,1,0:T(1,128)}), s32[128,1,8]{2,1,0:T(1,128)S(1)}, u32[]{:S(2)}, u32[]{:S(2)}) async-start(s32[128,1,8]{2,1,0:T(1,128)} %bitcast.25), calls=%async_computation | async-start | bytes 131072 | tf_op jit(solution)/shard_map/all_to_all | solution.py:85
  60.5 1.7 %fusion.338 = (bf16[512,512]{1,0:T(8,128)(2,1)S(1)}, bf16[512,512]{1,0:T(8,128)(2,1)S(1)}, bf16[512,512]{1,0:T(8,128)(2,1)S(1)}) fusion(bf16[512]{0:T(512)(128)(2,1)S(1)} %get-tuple-element.36, bf16[512]{0:T(512)(128)(2,1)S(1)} %get-tuple-element.37, bf16[512]{0:T(512)(128)(2,1)S(1)} %get-tuple-element.38, bf16[512]{0:T(512)(128)(2,1)S(1)} %get-tuple-element.39, ...), kind=kLoop, calls=%fused_computation.521 | loop fusion | flops 7340032 | bytes 1591296 | tf_op jit(solution)/shard_map/neg | solution.py:43
  62.3 2.8 %fusion.339 = (bf16[512,512]{1,0:T(8,128)(2,1)}, bf16[512,512]{1,0:T(8,128)(2,1)}, bf16[512,512]{1,0:T(8,128)(2,1)}) fusion(bf16[512]{0:T(512)(128)(2,1)S(1)} %get-tuple-element.20, bf16[512]{0:T(512)(128)(2,1)S(1)} %get-tuple-element.21, bf16[512]{0:T(512)(128)(2,1)S(1)} %get-tuple-element.22, bf16[512]{0:T(512)(128)(2,1)S(1)} %get-tuple-element.23, ...), kind=kLoop, calls=%fused_computation.522 | loop fusion | flops 7340032 | bytes 1591296 | tf_op jit(solution)/shard_map/neg | solution.py:43
  65.1 4.1 %collective-permute-done.4 = s32[1536]{0:T(1024)S(1)} collective-permute-done((s32[1536]{0:T(1024)S(1)}, s32[1536]{0:T(1024)S(1)}, u32[]{:S(2)}, u32[]{:S(2)}) %collective-permute-start.4) | collective-permute-done | bytes 6176 | tf_op jit(solution)/shard_map/ppermute | solution.py:16
  69.4 2.8 %fusion.341 = (bf16[512,512]{1,0:T(8,128)(2,1)}, bf16[512,512]{1,0:T(8,128)(2,1)}, bf16[512,512]{1,0:T(8,128)(2,1)}) fusion(bf16[512]{0:T(512)(128)(2,1)S(1)} %get-tuple-element.84, bf16[512]{0:T(512)(128)(2,1)S(1)} %get-tuple-element.85, bf16[512]{0:T(512)(128)(2,1)S(1)} %get-tuple-element.86, bf16[512]{0:T(512)(128)(2,1)S(1)} %get-tuple-element.87, ...), kind=kLoop, calls=%fused_computation.524 | loop fusion | flops 7340032 | bytes 1591296 | tf_op jit(solution)/shard_map/neg | solution.py:43
  72.2 3.4 %add_convert_fusion = bf16[1024,512]{1,0:T(8,128)(2,1)} fusion(f32[1024,512]{1,0:T(8,128)S(1)} %copy-done.15, bf16[1024,512]{1,0:T(8,128)(2,1)} %collective-permute-done.2, bf16[512,512]{1,0:T(8,128)(2,1)S(1)} %get-tuple-element.213, bf16[512,512]{1,0:T(8,128)(2,1)S(1)} %get-tuple-element.188, bf16[512,512]{1,0:T(8,128)(2,1)S(1)} %get-tuple-element.187), kind=kOutput, calls=%fused_computation.79 | convolution fusion | flops 1083179008 | bytes 5767168 | tf_op jit(solution)/shard_map/dot_general | solution.py:91
  75.7 1.2 constant_dynamic-slice_fusion
  77.0 1.7 %fusion.340 = (bf16[512,512]{1,0:T(8,128)(2,1)S(1)}, bf16[512,512]{1,0:T(8,128)(2,1)S(1)}, bf16[512,512]{1,0:T(8,128)(2,1)S(1)}) fusion(bf16[512]{0:T(512)(128)(2,1)S(1)} %get-tuple-element.52, bf16[512]{0:T(512)(128)(2,1)S(1)} %get-tuple-element.53, bf16[512]{0:T(512)(128)(2,1)S(1)} %get-tuple-element.54, bf16[512]{0:T(512)(128)(2,1)S(1)} %get-tuple-element.55, ...), kind=kLoop, calls=%fused_computation.523 | loop fusion | flops 7340032 | bytes 1591296 | tf_op jit(solution)/shard_map/neg | solution.py:43
  78.8 0.7 fusion.67
  79.5 1.7 %fusion.43 = f32[1024,256]{1,0:T(8,128)} fusion(bf16[512,512]{1,0:T(8,128)(2,1)S(1)} %get-tuple-element.211, bf16[512,512]{1,0:T(8,128)(2,1)S(1)} %get-tuple-element.184, bf16[512,512]{1,0:T(8,128)(2,1)S(1)} %get-tuple-element.183, bf16[1024,512]{1,0:T(8,128)(2,1)S(1)} %copy-done.8, s32[]{:T(128)S(6)} %select_n.476), kind=kOutput, calls=%fused_computation.43 | convolution fusion | flops 545259520 | bytes 3145732 | tf_op jit(solution)/shard_map/dot_general | solution.py:116
  81.2 9.7 %collective-permute-done.3 = bf16[1024,256]{1,0:T(8,128)(2,1)S(1)} collective-permute-done((bf16[1024,256]{1,0:T(8,128)(2,1)S(1)}, bf16[1024,256]{1,0:T(8,128)(2,1)S(1)}, u32[]{:S(2)}, u32[]{:S(2)}) %collective-permute-start.3) | collective-permute-done | bytes 524320 | tf_op jit(solution)/shard_map/ppermute | solution.py:16
  90.9 0.7 fusion.103
  92.5 2.1 %fusion.100 = bf16[1024,256]{1,0:T(8,128)(2,1)S(1)} fusion(f32[1024,256]{1,0:T(8,128)} %fusion.43, bf16[1024,256]{1,0:T(8,128)(2,1)} %copy-done.14, bf16[512,512]{1,0:T(8,128)(2,1)S(1)} %copy-done.4, bf16[512,512]{1,0:T(8,128)(2,1)S(1)} %copy-done.3, bf16[512,512]{1,0:T(8,128)(2,1)S(1)} %copy-done.2), kind=kOutput, calls=%fused_computation.97 | convolution fusion | flops 545783808 | bytes 3670016 | tf_op jit(solution)/shard_map/dot_general | solution.py:117
  94.8 0.7 fusion.90
  95.5 0.8 fusion.91
  96.3 1.7 %pad_maximum_fusion = bf16[128,16,512]{2,1,0:T(8,128)(2,1)} fusion(bf16[128,8,512]{2,1,0:T(8,128)(2,1)S(1)} %fusion.91, bf16[128,8,512]{2,1,0:T(8,128)(2,1)S(1)} %fusion.90), kind=kLoop, calls=%fused_computation.75 | loop fusion | flops 4194304 | bytes 4194304 | tf_op jit(solution)/shard_map/concatenate | solution.py:122
  98.0 10.1 %all-to-all-start.1 = ((bf16[128,16,512]{2,1,0:T(8,128)(2,1)}), bf16[128,16,512]{2,1,0:T(8,128)(2,1)S(1)}, u32[]{:S(2)}, u32[]{:S(2)}) async-start(bf16[128,16,512]{2,1,0:T(8,128)(2,1)} %pad_maximum_fusion), calls=%async_computation.1 | async-start | bytes 4194304 | tf_op jit(solution)/shard_map/all_to_all | solution.py:123
  109.7 28.1 %all-to-all-done.1 = bf16[128,16,512]{2,1,0:T(8,128)(2,1)S(1)} async-done(((bf16[128,16,512]{2,1,0:T(8,128)(2,1)}), bf16[128,16,512]{2,1,0:T(8,128)(2,1)S(1)}, u32[]{:S(2)}, u32[]{:S(2)}) %all-to-all-start.1) | async-done | bytes 2097184 | tf_op jit(solution)/shard_map/all_to_all | solution.py:123
  138.0 0.8 fusion.98
  139.0 0.8 fusion.99
  140.0 1.1 maximum_bitcast_fusion
  (102 shorter events, 5.2 us)
Async XLA Ops:
  0.0 2.8 %copy-start.13 = (s32[1,1,512]{2,1,0:T(1,128)S(1)}, s32[1,1,512]{2,1,0:T(1,128)}, u32[]{:S(2)}) copy-start(s32[1,1,512]{2,1,0:T(1,128)} %param.11) | copy-start | bytes 6148
  0.0 2.8 %copy-start.10 = (s32[1,1,512,1]{2,3,1,0:T(1,128)S(1)}, s32[1,1,512,1]{2,3,1,0:T(1,128)}, u32[]{:S(2)}) copy-start(s32[1,1,512,1]{2,3,1,0:T(1,128)} %param.10) | copy-start | bytes 6148
  0.0 4.6 %copy-start.12 = (bf16[2,512]{1,0:T(2,128)(2,1)S(1)}, bf16[2,512]{1,0:T(2,128)(2,1)}, u32[]{:S(2)}) copy-start(bf16[2,512]{1,0:T(2,128)(2,1)} %param.7) | copy-start | bytes 6148
  0.0 26.8 %collective-permute-start = (bf16[2,512,512]{2,1,0:T(8,128)(2,1)}, bf16[2,512,512]{2,1,0:T(8,128)(2,1)}, u32[]{:S(2)}, u32[]{:S(2)}) collective-permute-start(bf16[2,512,512]{2,1,0:T(8,128)(2,1)} %param.6), channel_id=1, source_target_pairs={{1,0},{2,1},{3,2},{4,3},{5,4},{6,5},{7,6},{8,7},{9,8},{10,9},{11,1... | collective-permute-start | bytes 3145736 | tf_op jit(solution)/shard_map/ppermute | solution.py:12
  7.0 1.2 slice-start
  11.9 1.2 slice-start.1
  13.1 2.6 %copy-start.9 = (bf16[3,1,2,2,512,8]{4,5,3,2,1,0:T(8,128)(2,1)S(1)}, bf16[3,1,2,2,512,8]{4,5,3,2,1,0:T(8,128)(2,1)}, u32[]{:S(2)}) copy-start(bf16[3,1,2,2,512,8]{4,5,3,2,1,0:T(8,128)(2,1)} %param.9) | copy-start | bytes 294916
  13.1 2.6 %copy-start.11 = (s32[3,1,2,512]{3,2,1,0:T(2,128)S(1)}, s32[3,1,2,512]{3,2,1,0:T(2,128)}, u32[]{:S(2)}) copy-start(s32[3,1,2,512]{3,2,1,0:T(2,128)} %param.8) | copy-start | bytes 36868
  28.2 1.2 copy-start
  28.2 1.5 %copy-start.1 = (bf16[512,1024]{1,0:T(8,128)(2,1)S(1)}, bf16[512,1024]{1,0:T(8,128)(2,1)}, u32[]{:S(2)}) copy-start(bf16[512,1024]{1,0:T(8,128)(2,1)} %reshape.160) | copy-start | bytes 3145732
  32.2 4.7 %collective-permute-start.1 = (bf16[1024,512]{1,0:T(8,128)(2,1)S(1)}, bf16[1024,512]{1,0:T(8,128)(2,1)S(1)}, u32[]{:S(2)}, u32[]{:S(2)}) collective-permute-start(bf16[1024,512]{1,0:T(8,128)(2,1)S(1)} %bitcast.120), channel_id=1, source_target_pairs={{0,16},{16,0},{32,48},{48,32},{64,80},{80,64},{96,112},{112,96},{1... | collective-permute-start | bytes 3145736 | tf_op jit(solution)/shard_map/ppermute | solution.py:16
  39.2 33.0 %collective-permute-start.2 = (bf16[1024,512]{1,0:T(8,128)(2,1)}, bf16[1024,512]{1,0:T(8,128)(2,1)}, u32[]{:S(2)}, u32[]{:S(2)}) collective-permute-start(bf16[1024,512]{1,0:T(8,128)(2,1)} %add_convert_fusion.1), channel_id=1, source_target_pairs={{0,32},{16,48},{32,0},{48,16},{64,96},{80,112},{96,64},{112,80},{1... | collective-permute-start | bytes 3145736 | tf_op jit(solution)/shard_map/ppermute | solution.py:16
  44.9 24.2 %collective-permute-start.5 = (bf16[2,2,512,8]{2,3,1,0:T(8,128)(2,1)S(1)}, bf16[2,2,512,8]{2,3,1,0:T(8,128)(2,1)S(1)}, u32[]{:S(2)}, u32[]{:S(2)}) collective-permute-start(bf16[2,2,512,8]{2,3,1,0:T(8,128)(2,1)S(1)} %slice_bitcast_fusion.2), channel_id=1, source_target_pairs={{0,64},{16,80},{32,96},{48,112},{64,0},{80,16},{96,32},{112,48},{1... | collective-permute-start | bytes 98312 | tf_op jit(solution)/shard_map/ppermute | solution.py:16
  48.2 20.9 %collective-permute-start.4 = (s32[1536]{0:T(1024)S(1)}, s32[1536]{0:T(1024)S(1)}, u32[]{:S(2)}, u32[]{:S(2)}) collective-permute-start(s32[1536]{0:T(1024)S(1)} %pad_add_fusion.2), channel_id=1, source_target_pairs={{0,64},{16,80},{32,96},{48,112},{64,0},{80,16},{96,32},{112,48},{1... | collective-permute-start | bytes 18440 | tf_op jit(solution)/shard_map/ppermute | solution.py:16
  48.3 27.3 %all-to-all-start = ((s32[128,1,8]{2,1,0:T(1,128)}), s32[128,1,8]{2,1,0:T(1,128)S(1)}, u32[]{:S(2)}, u32[]{:S(2)}) async-start(s32[128,1,8]{2,1,0:T(1,128)} %bitcast.25), calls=%async_computation | async-start | bytes 131072 | tf_op jit(solution)/shard_map/all_to_all | solution.py:85
  62.3 9.9 %copy-start.15 = (f32[1024,512]{1,0:T(8,128)S(1)}, f32[1024,512]{1,0:T(8,128)}, u32[]{:S(2)}) copy-start(f32[1024,512]{1,0:T(8,128)} %fusion.8) | copy-start | bytes 6291460
  75.6 3.1 %copy-start.5 = (bf16[512,512]{1,0:T(8,128)(2,1)S(1)}, bf16[512,512]{1,0:T(8,128)(2,1)}, u32[]{:S(2)}) copy-start(bf16[512,512]{1,0:T(8,128)(2,1)} %get-tuple-element.189) | copy-start | bytes 1572868
  75.6 3.1 %copy-start.6 = (bf16[512,512]{1,0:T(8,128)(2,1)S(1)}, bf16[512,512]{1,0:T(8,128)(2,1)}, u32[]{:S(2)}) copy-start(bf16[512,512]{1,0:T(8,128)(2,1)} %get-tuple-element.190) | copy-start | bytes 1572868
  75.7 3.1 %copy-start.7 = (bf16[512,512]{1,0:T(8,128)(2,1)S(1)}, bf16[512,512]{1,0:T(8,128)(2,1)}, u32[]{:S(2)}) copy-start(bf16[512,512]{1,0:T(8,128)(2,1)} %get-tuple-element.214) | copy-start | bytes 1572868
  75.7 3.1 %copy-start.8 = (bf16[1024,512]{1,0:T(8,128)(2,1)S(1)}, bf16[1024,512]{1,0:T(8,128)(2,1)}, u32[]{:S(2)}) copy-start(bf16[1024,512]{1,0:T(8,128)(2,1)} %add_convert_fusion) | copy-start | bytes 3145732
  76.9 14.0 %collective-permute-start.3 = (bf16[1024,256]{1,0:T(8,128)(2,1)S(1)}, bf16[1024,256]{1,0:T(8,128)(2,1)S(1)}, u32[]{:S(2)}, u32[]{:S(2)}) collective-permute-start(bf16[1024,256]{1,0:T(8,128)(2,1)S(1)} %constant_dynamic-slice_fusion), channel_id=1, source_target_pairs={{0,64},{16,80},{32,96},{48,112},{64,0},{80,16},{96,32},{112,48},{1... | collective-permute-start | bytes 1572872 | tf_op jit(solution)/shard_map/ppermute | solution.py:16
  90.9 0.8 copy-start.14
  90.9 1.2 copy-start.2
  90.9 1.4 copy-start.3
  90.9 1.5 %copy-start.4 = (bf16[512,512]{1,0:T(8,128)(2,1)S(1)}, bf16[512,512]{1,0:T(8,128)(2,1)}, u32[]{:S(2)}) copy-start(bf16[512,512]{1,0:T(8,128)(2,1)} %get-tuple-element.210) | copy-start | bytes 1572868
  98.0 39.8 %all-to-all-start.1 = ((bf16[128,16,512]{2,1,0:T(8,128)(2,1)}), bf16[128,16,512]{2,1,0:T(8,128)(2,1)S(1)}, u32[]{:S(2)}, u32[]{:S(2)}) async-start(bf16[128,16,512]{2,1,0:T(8,128)(2,1)} %pad_maximum_fusion), calls=%async_computation.1 | async-start | bytes 4194304 | tf_op jit(solution)/shard_map/all_to_all | solution.py:123

commit v10 on v9

--- a/solution.py
+++ b/solution.py
@@ -81,8 +81,7 @@
         theirs = merge_matrix(offsets[section, 0, 1], weights[section, 0, 1])
         merged = jnp.dot(mine, image, preferred_element_type=jnp.float32)
         if section == 1:
-            (labels, late), merged = lax.optimization_barrier(((labels, late), merged))
-            marks = lax.all_to_all(labels, ("sub", "rng"), split_axis=0, concat_axis=0, tiled=True)
+            late, merged = lax.optimization_barrier((late, merged))
             own_offsets, own_weights, slot = late
             far_weights = far(own_weights)
             far_ints = far(jnp.concatenate([own_offsets.reshape(-1), slot]))
@@ -90,15 +89,8 @@
             far_slot = far_ints[2 * p_dev :]
         merged = merged + jnp.dot(theirs, partner, preferred_element_type=jnp.float32)
         image = merged.astype(jnp.bfloat16)
-        if section == 1:
-            marks, image = lax.optimization_barrier((marks, image))
     slots = jnp.arange(devices * capacity, dtype=jnp.int32)[:, None]
     picks = {0: slots == slot[None, :], bit: slots == far_slot[None, :]}
-    grid = marks.reshape(n_sub, n_rng * capacity)
-    swapped = jnp.stack([grid[s ^ bit] for s in range(n_sub)], axis=0)
-    marks = jnp.stack(
-        [grid.reshape(devices, capacity), swapped.reshape(devices, capacity)], axis=1
-    ).reshape(devices, 2 * capacity)
     half = r_dev // 2
     keep_bit = (me_sub >> last) & 1
     kept = lax.dynamic_slice_in_dim(image, keep_bit * half, half, axis=1)
@@ -114,11 +106,19 @@
         mine = merge_matrix(starts[0], kernel[0])
         theirs = merge_matrix(starts[1], kernel[1])
         merged = jnp.dot(mine, old[m], preferred_element_type=jnp.float32)
+        if m == 0:
+            labels, merged = lax.optimization_barrier((labels, merged))
+            marks = lax.all_to_all(labels, ("sub", "rng"), split_axis=0, concat_axis=0, tiled=True)
         merged = merged + jnp.dot(theirs, old[m ^ bit], preferred_element_type=jnp.float32)
         piece = merged.astype(jnp.bfloat16)
         rows = piece.reshape(2, p_dev, half).transpose(1, 0, 2).reshape(p_dev, 2 * half)
         send = jnp.dot(picks[m].astype(jnp.bfloat16), rows, preferred_element_type=jnp.float32)
         sends.append(send.astype(jnp.bfloat16).reshape(devices, capacity, 2 * half))
+    grid = marks.reshape(n_sub, n_rng * capacity)
+    swapped = jnp.stack([grid[s ^ bit] for s in range(n_sub)], axis=0)
+    marks = jnp.stack(
+        [grid.reshape(devices, capacity), swapped.reshape(devices, capacity)], axis=1
+    ).reshape(devices, 2 * capacity)
     payload = jnp.concatenate(sends, axis=1)
     got = lax.all_to_all(payload, ("sub", "rng"), split_axis=0, concat_axis=0, tiled=True)
     span = devices // 2

time: 142 us -> 141 us (level)
  waiting for transfers between devices: 47.3 us -> 51.9 us
  matrix products: 21.4 us -> 17.8 us
    ppermute x5, waiting for transfers between devices: 13.8 us -> 18.4 us  [from_partner(): lax.ppermute(value, axis, [(i, i ^ 1 << apart) for i in range(lax.axis_si...]
    dot_general x2, matrix products: 5.65 us -> 2.49 us  [on_device(): jnp.dot(theirs, partner, preferred_element_type=jnp.float32)]
    dot_general x2, matrix products: 5.09 us -> 2.48 us  [on_device(): merged = jnp.dot(mine, image, preferred_element_type=jnp.float32)]
    unnamed x34 -> x24, local copies, waits for them, and re-layouts: 3.38 us -> 2.76 us
  transfers between devices with their start and end apart: 8 -> 8, of which waited for: 4 -> 4; matrix products, arithmetic and copies ran while one was open for 29% -> 30% of each run, Pallas kernels for 0% -> 0%
where the time goes in v10:
time: 141 us
  waiting for transfers between devices  51.9 us (37%)
  starting transfers between devices  30.9 us (22%)
  other arithmetic  20 us (14%)
  local copies, waits for them, and re-layouts  19.2 us (14%)
  matrix products  17.8 us (13%)
    all_to_all x1, waiting for transfers between devices, on_device(): lax.all_to_all(payload, ('sub', 'rng'), split_axis=0, concat_axis=0, tile...  28 us
    ppermute x5, waiting for transfers between devices, from_partner(): lax.ppermute(value, axis, [(i, i ^ 1 << apart) for i in range(lax.axis_si...  18.4 us
    neg x8, other arithmetic, merge_matrix(): upper = jnp.concatenate([g_real, -g_imag], axis=1)  14.9 us
    all_to_all x1, starting transfers between devices, on_device(): lax.all_to_all(labels, ('sub', 'rng'), split_axis=0, concat_axis=0, tiled...  12.5 us
    all_to_all x1, starting transfers between devices, on_device(): lax.all_to_all(payload, ('sub', 'rng'), split_axis=0, concat_axis=0, tile...  9.59 us
    ppermute x5, starting transfers between devices, from_partner(): lax.ppermute(value, axis, [(i, i ^ 1 << apart) for i in range(lax.axis_si...  7.37 us
    ppermute x1, waiting for transfers between devices, shifted(): lax.ppermute(value, axis, [(source, source + steps) for source in range(f...  5.41 us
    another operation x4, local copies, waits for them, and re-layouts, replica_matrix(): jnp.tile(padded, block_len)[:block_len * width].reshape(block_len, width)  4.78 us
  transfers between devices with their start and end apart: 8, of which 4 were waited for; matrix products, arithmetic and copies ran while one was open for 30% of the time, Pallas kernels for 0%

profile of v10, /device:TPU:1, one launch (start us, length us, event | category | flops | bytes accessed | tf_op | source)
XLA Modules:
  0.0 140.5 jit_solution(10288246044097621530)
XLA Ops:
  0.0 1.4 %collective-permute-start = (bf16[2,512,512]{2,1,0:T(8,128)(2,1)}, bf16[2,512,512]{2,1,0:T(8,128)(2,1)}, u32[]{:S(2)}, u32[]{:S(2)}) collective-permute-start(bf16[2,512,512]{2,1,0:T(8,128)(2,1)} %param.6), channel_id=1, source_target_pairs={{1,0},{2,1},{3,2},{4,3},{5,4},{6,5},{7,6},{8,7},{9,8},{10,9},{11,1... | collective-permute-start | bytes 3145736 | tf_op jit(solution)/shard_map/ppermute | solution.py:12
  1.4 1.4 constant_dynamic-update-slice_fusion.1
  3.3 0.2 fusion.304
  3.7 2.3 %tile.9 = bf16[524800]{0:T(1024)(128)(2,1)} reshape(bf16[512,1025]{1,0:T(8,128)(2,1)S(1)} %tile.8) | data formatting | bytes 2099200 | tf_op jit(solution)/shard_map/tile | solution.py:25
  6.0 1.2 slice-done
  7.2 1.3 reshape.177
  8.6 2.3 %tile.21 = bf16[524800]{0:T(1024)(128)(2,1)} reshape(bf16[512,1025]{1,0:T(8,128)(2,1)S(1)} %tile.20) | data formatting | bytes 2099200 | tf_op jit(solution)/shard_map/tile | solution.py:25
  10.9 1.2 slice-done.1
  12.1 1.3 reshape.178
  13.4 1.3 bitcast_negate_fusion
  14.7 0.3 select_reduce_fusion
  15.0 0.7 sub.137
  16.1 1.7 %fusion.336 = (bf16[512,512]{1,0:T(8,128)(2,1)S(1)}, bf16[512,512]{1,0:T(8,128)(2,1)S(1)}, bf16[512,512]{1,0:T(8,128)(2,1)S(1)}) fusion(bf16[512]{0:T(512)(128)(2,1)S(1)} %get-tuple-element.138, bf16[512]{0:T(512)(128)(2,1)S(1)} %get-tuple-element.139, bf16[512]{0:T(512)(128)(2,1)S(1)} %get-tuple-element.140, bf16[512]{0:T(512)(128)(2,1)S(1)} %get-tuple-element.141, ...), kind=kLoop, calls=%fused_computation.527 | loop fusion | flops 7340032 | bytes 1591296 | tf_op jit(solution)/shard_map/neg | solution.py:43
  17.9 1.7 %fusion.337 = (bf16[512,512]{1,0:T(8,128)(2,1)S(1)}, bf16[512,512]{1,0:T(8,128)(2,1)S(1)}, bf16[512,512]{1,0:T(8,128)(2,1)S(1)}) fusion(bf16[512]{0:T(512)(128)(2,1)S(1)} %get-tuple-element.122, bf16[512]{0:T(512)(128)(2,1)S(1)} %get-tuple-element.123, bf16[512]{0:T(512)(128)(2,1)S(1)} %get-tuple-element.124, bf16[512]{0:T(512)(128)(2,1)S(1)} %get-tuple-element.125, ...), kind=kLoop, calls=%fused_computation.528 | loop fusion | flops 7340032 | bytes 1591296 | tf_op jit(solution)/shard_map/neg | solution.py:43
  19.7 1.7 %fusion.335 = (bf16[512,512]{1,0:T(8,128)(2,1)S(1)}, bf16[512,512]{1,0:T(8,128)(2,1)S(1)}, bf16[512,512]{1,0:T(8,128)(2,1)S(1)}) fusion(bf16[512]{0:T(512)(128)(2,1)S(1)} %get-tuple-element.106, bf16[512]{0:T(512)(128)(2,1)S(1)} %get-tuple-element.107, bf16[512]{0:T(512)(128)(2,1)S(1)} %get-tuple-element.108, bf16[512]{0:T(512)(128)(2,1)S(1)} %get-tuple-element.109, ...), kind=kLoop, calls=%fused_computation.526 | loop fusion | flops 7340032 | bytes 1591296 | tf_op jit(solution)/shard_map/neg | solution.py:43
  21.4 5.4 %collective-permute-done = bf16[2,512,512]{2,1,0:T(8,128)(2,1)} collective-permute-done((bf16[2,512,512]{2,1,0:T(8,128)(2,1)}, bf16[2,512,512]{2,1,0:T(8,128)(2,1)}, u32[]{:S(2)}, u32[]{:S(2)}) %collective-permute-start) | collective-permute-done | bytes 1048608 | tf_op jit(solution)/shard_map/ppermute | solution.py:12
  26.8 1.4 constant_dynamic-update-slice_fusion
  28.4 1.0 copy-done
  29.4 0.3 copy-done.1
  29.8 2.4 %fusion.83 = bf16[512,1024]{1,0:T(8,128)(2,1)S(1)} fusion(bf16[1024,512]{0,1:T(8,128)(2,1)S(1)} %bitcast.117, bf16[1024,512]{0,1:T(8,128)(2,1)S(1)} %bitcast.116, bf16[1024,512]{0,1:T(8,128)(2,1)S(1)} %bitcast_negate_fusion, bf16[512,1024]{1,0:T(8,128)(2,1)S(1)} %get-tuple-element.158, bf16[512,1024]{1,0:T(8,128)(2,1)S(1)} %get-tuple-element.157), kind=kOutput, calls=%fused_computation.88 | convolution fusion | flops 2168979456 | bytes 6291456 | tf_op jit(solution)/shard_map/dot_general | solution.py:64
  32.2 1.7 %collective-permute-start.1 = (bf16[1024,512]{1,0:T(8,128)(2,1)S(1)}, bf16[1024,512]{1,0:T(8,128)(2,1)S(1)}, u32[]{:S(2)}, u32[]{:S(2)}) collective-permute-start(bf16[1024,512]{1,0:T(8,128)(2,1)S(1)} %bitcast.118), channel_id=1, source_target_pairs={{0,16},{16,0},{32,48},{48,32},{64,80},{80,64},{96,112},{112,96},{1... | collective-permute-start | bytes 3145736 | tf_op jit(solution)/shard_map/ppermute | solution.py:16
  34.0 1.7 %fusion.338 = (bf16[512,512]{1,0:T(8,128)(2,1)S(1)}, bf16[512,512]{1,0:T(8,128)(2,1)S(1)}, bf16[512,512]{1,0:T(8,128)(2,1)S(1)}) fusion(bf16[512]{0:T(512)(128)(2,1)S(1)} %get-tuple-element.74, bf16[512]{0:T(512)(128)(2,1)S(1)} %get-tuple-element.75, bf16[512]{0:T(512)(128)(2,1)S(1)} %get-tuple-element.76, bf16[512]{0:T(512)(128)(2,1)S(1)} %get-tuple-element.77, ...), kind=kLoop, calls=%fused_computation.529 | loop fusion | flops 7340032 | bytes 1591296 | tf_op jit(solution)/shard_map/neg | solution.py:43
  35.7 1.2 fusion.16
  36.9 1.2 add_convert_fusion.1
  38.2 2.0 %collective-permute-start.2 = (bf16[1024,512]{1,0:T(8,128)(2,1)S(1)}, bf16[1024,512]{1,0:T(8,128)(2,1)S(1)}, u32[]{:S(2)}, u32[]{:S(2)}) collective-permute-start(bf16[1024,512]{1,0:T(8,128)(2,1)S(1)} %add_convert_fusion.1), channel_id=1, source_target_pairs={{0,32},{16,48},{32,0},{48,16},{64,96},{80,112},{96,64},{112,80},{1... | collective-permute-start | bytes 3145736 | tf_op jit(solution)/shard_map/ppermute | solution.py:16
  40.1 1.2 fusion.8
  41.4 3.4 %collective-permute-start.5 = (bf16[2,2,512,8]{2,3,1,0:T(8,128)(2,1)S(1)}, bf16[2,2,512,8]{2,3,1,0:T(8,128)(2,1)S(1)}, u32[]{:S(2)}, u32[]{:S(2)}) collective-permute-start(bf16[2,2,512,8]{2,3,1,0:T(8,128)(2,1)S(1)} %slice_bitcast_fusion.2), channel_id=1, source_target_pairs={{0,64},{16,80},{32,96},{48,112},{64,0},{80,16},{96,32},{112,48},{1... | collective-permute-start | bytes 98312 | tf_op jit(solution)/shard_map/ppermute | solution.py:16
  44.8 0.3 collective-permute-start.4
  45.3 1.7 %fusion.334 = (bf16[512,512]{1,0:T(8,128)(2,1)S(1)}, bf16[512,512]{1,0:T(8,128)(2,1)S(1)}, bf16[512,512]{1,0:T(8,128)(2,1)S(1)}) fusion(bf16[512]{0:T(512)(128)(2,1)S(1)} %get-tuple-element.42, bf16[512]{0:T(512)(128)(2,1)S(1)} %get-tuple-element.43, bf16[512]{0:T(512)(128)(2,1)S(1)} %get-tuple-element.44, bf16[512]{0:T(512)(128)(2,1)S(1)} %get-tuple-element.45, ...), kind=kLoop, calls=%fused_computation.525 | loop fusion | flops 7340032 | bytes 1591296 | tf_op jit(solution)/shard_map/neg | solution.py:43
  47.1 1.7 %fusion.339 = (bf16[512,512]{1,0:T(8,128)(2,1)S(1)}, bf16[512,512]{1,0:T(8,128)(2,1)S(1)}, bf16[512,512]{1,0:T(8,128)(2,1)S(1)}) fusion(bf16[512]{0:T(512)(128)(2,1)S(1)} %get-tuple-element.26, bf16[512]{0:T(512)(128)(2,1)S(1)} %get-tuple-element.27, bf16[512]{0:T(512)(128)(2,1)S(1)} %get-tuple-element.28, bf16[512]{0:T(512)(128)(2,1)S(1)} %get-tuple-element.29, ...), kind=kLoop, calls=%fused_computation.530 | loop fusion | flops 7340032 | bytes 1591296 | tf_op jit(solution)/shard_map/neg | solution.py:43
  48.8 18.4 %collective-permute-done.4 = s32[1536]{0:T(1024)S(1)} collective-permute-done((s32[1536]{0:T(1024)S(1)}, s32[1536]{0:T(1024)S(1)}, u32[]{:S(2)}, u32[]{:S(2)}) %collective-permute-start.4) | collective-permute-done | bytes 6176 | tf_op jit(solution)/shard_map/ppermute | solution.py:16
  67.5 1.7 %fusion.341 = (bf16[512,512]{1,0:T(8,128)(2,1)S(1)}, bf16[512,512]{1,0:T(8,128)(2,1)S(1)}, bf16[512,512]{1,0:T(8,128)(2,1)S(1)}) fusion(bf16[512]{0:T(512)(128)(2,1)S(1)} %get-tuple-element.90, bf16[512]{0:T(512)(128)(2,1)S(1)} %get-tuple-element.91, bf16[512]{0:T(512)(128)(2,1)S(1)} %get-tuple-element.92, bf16[512]{0:T(512)(128)(2,1)S(1)} %get-tuple-element.93, ...), kind=kLoop, calls=%fused_computation.532 | loop fusion | flops 7340032 | bytes 1591296 | tf_op jit(solution)/shard_map/neg | solution.py:43
  69.2 1.2 add_convert_fusion
  70.5 0.9 constant_dynamic-slice_fusion
  71.4 2.7 %fusion.340 = (bf16[512,512]{1,0:T(8,128)(2,1)}, bf16[512,512]{1,0:T(8,128)(2,1)}, bf16[512,512]{1,0:T(8,128)(2,1)}) fusion(bf16[512]{0:T(512)(128)(2,1)S(1)} %get-tuple-element.58, bf16[512]{0:T(512)(128)(2,1)S(1)} %get-tuple-element.59, bf16[512]{0:T(512)(128)(2,1)S(1)} %get-tuple-element.60, bf16[512]{0:T(512)(128)(2,1)S(1)} %get-tuple-element.61, ...), kind=kLoop, calls=%fused_computation.531 | loop fusion | flops 7340032 | bytes 1591296 | tf_op jit(solution)/shard_map/neg | solution.py:43
  74.2 1.7 %fusion.35 = f32[1024,256]{1,0:T(8,128)} fusion(bf16[512,512]{1,0:T(8,128)(2,1)S(1)} %get-tuple-element.209, bf16[512,512]{1,0:T(8,128)(2,1)S(1)} %get-tuple-element.182, bf16[512,512]{1,0:T(8,128)(2,1)S(1)} %get-tuple-element.181, bf16[1024,512]{1,0:T(8,128)(2,1)S(1)} %add_convert_fusion, s32[]{:T(128)S(6)} %select_n.476), kind=kOutput, calls=%fused_computation.35 | convolution fusion | flops 545259520 | bytes 3145732 | tf_op jit(solution)/shard_map/dot_general | solution.py:108
  75.9 12.5 %all-to-all-start = ((s32[128,1,8]{2,1,0:T(1,128)}), s32[128,1,8]{2,1,0:T(1,128)S(1)}, u32[]{:S(2)}, u32[]{:S(2)}) async-start(s32[128,1,8]{2,1,0:T(1,128)} %bitcast.31), calls=%async_computation | async-start | bytes 131072 | tf_op jit(solution)/shard_map/all_to_all | solution.py:111
  88.4 1.9 %fusion.67 = f32[1024,256]{1,0:T(8,128)S(1)} fusion(bf16[512,512]{1,0:T(8,128)(2,1)S(1)} %get-tuple-element.212, bf16[512,512]{1,0:T(8,128)(2,1)S(1)} %get-tuple-element.188, bf16[512,512]{1,0:T(8,128)(2,1)S(1)} %get-tuple-element.187, bf16[1024,512]{1,0:T(8,128)(2,1)} %copy-done.5, s32[]{:T(128)S(6)} %select_n.476), kind=kOutput, calls=%fused_computation.67 | convolution fusion | flops 545259520 | bytes 3145732 | tf_op jit(solution)/shard_map/dot_general | solution.py:112
  90.3 1.7 %fusion.103 = bf16[1024,256]{1,0:T(8,128)(2,1)S(1)} fusion(f32[1024,256]{1,0:T(8,128)S(1)} %fusion.67, bf16[1024,256]{1,0:T(8,128)(2,1)} %collective-permute-done.3, bf16[512,512]{1,0:T(8,128)(2,1)S(1)} %copy-done.4, bf16[512,512]{1,0:T(8,128)(2,1)S(1)} %copy-done.3, bf16[512,512]{1,0:T(8,128)(2,1)S(1)} %copy-done.2), kind=kOutput, calls=%fused_computation.98 | convolution fusion | flops 545783808 | bytes 3670016 | tf_op jit(solution)/shard_map/dot_general | solution.py:108
  92.3 2.1 %fusion.100 = bf16[1024,256]{1,0:T(8,128)(2,1)S(1)} fusion(f32[1024,256]{1,0:T(8,128)} %fusion.35, bf16[1024,256]{1,0:T(8,128)(2,1)} %collective-permute-done.3, bf16[512,512]{1,0:T(8,128)(2,1)S(1)} %get-tuple-element.208, bf16[512,512]{1,0:T(8,128)(2,1)S(1)} %get-tuple-element.180, bf16[512,512]{1,0:T(8,128)(2,1)S(1)} %get-tuple-element.179), kind=kOutput, calls=%fused_computation.97 | convolution fusion | flops 545783808 | bytes 3670016 | tf_op jit(solution)/shard_map/dot_general | solution.py:112
  94.6 0.8 fusion.90
  95.4 0.8 fusion.91
  96.2 1.7 %pad_maximum_fusion = bf16[128,16,512]{2,1,0:T(8,128)(2,1)} fusion(bf16[128,8,512]{2,1,0:T(8,128)(2,1)S(1)} %fusion.91, bf16[128,8,512]{2,1,0:T(8,128)(2,1)S(1)} %fusion.90), kind=kLoop, calls=%fused_computation.75 | loop fusion | flops 4194304 | bytes 4194304 | tf_op jit(solution)/shard_map/concatenate | solution.py:122
  98.0 9.6 %all-to-all-start.1 = ((bf16[128,16,512]{2,1,0:T(8,128)(2,1)}), bf16[128,16,512]{2,1,0:T(8,128)(2,1)S(1)}, u32[]{:S(2)}, u32[]{:S(2)}) async-start(bf16[128,16,512]{2,1,0:T(8,128)(2,1)} %pad_maximum_fusion), calls=%async_computation.1 | async-start | bytes 4194304 | tf_op jit(solution)/shard_map/all_to_all | solution.py:123
  109.3 28.0 %all-to-all-done.1 = bf16[128,16,512]{2,1,0:T(8,128)(2,1)S(1)} async-done(((bf16[128,16,512]{2,1,0:T(8,128)(2,1)}), bf16[128,16,512]{2,1,0:T(8,128)(2,1)S(1)}, u32[]{:S(2)}, u32[]{:S(2)}) %all-to-all-start.1) | async-done | bytes 2097184 | tf_op jit(solution)/shard_map/all_to_all | solution.py:123
  137.5 0.8 fusion.98
  138.5 0.8 fusion.99
  139.5 1.1 maximum_bitcast_fusion
  (92 shorter events, 4.7 us)
Async XLA Ops:
  0.0 2.8 %copy-start.7 = (s32[1,1,512,1]{2,3,1,0:T(1,128)S(1)}, s32[1,1,512,1]{2,3,1,0:T(1,128)}, u32[]{:S(2)}) copy-start(s32[1,1,512,1]{2,3,1,0:T(1,128)} %param.10) | copy-start | bytes 6148
  0.0 3.5 %copy-start.9 = (bf16[2,512]{1,0:T(2,128)(2,1)S(1)}, bf16[2,512]{1,0:T(2,128)(2,1)}, u32[]{:S(2)}) copy-start(bf16[2,512]{1,0:T(2,128)(2,1)} %param.7) | copy-start | bytes 6148
  0.0 26.8 %collective-permute-start = (bf16[2,512,512]{2,1,0:T(8,128)(2,1)}, bf16[2,512,512]{2,1,0:T(8,128)(2,1)}, u32[]{:S(2)}, u32[]{:S(2)}) collective-permute-start(bf16[2,512,512]{2,1,0:T(8,128)(2,1)} %param.6), channel_id=1, source_target_pairs={{1,0},{2,1},{3,2},{4,3},{5,4},{6,5},{7,6},{8,7},{9,8},{10,9},{11,1... | collective-permute-start | bytes 3145736 | tf_op jit(solution)/shard_map/ppermute | solution.py:12
  6.0 1.2 slice-start
  10.9 1.2 slice-start.1
  12.1 2.6 %copy-start.6 = (bf16[3,1,2,2,512,8]{4,5,3,2,1,0:T(8,128)(2,1)S(1)}, bf16[3,1,2,2,512,8]{4,5,3,2,1,0:T(8,128)(2,1)}, u32[]{:S(2)}) copy-start(bf16[3,1,2,2,512,8]{4,5,3,2,1,0:T(8,128)(2,1)} %param.9) | copy-start | bytes 294916
  12.1 2.6 %copy-start.8 = (s32[3,1,2,512]{3,2,1,0:T(2,128)S(1)}, s32[3,1,2,512]{3,2,1,0:T(2,128)}, u32[]{:S(2)}) copy-start(s32[3,1,2,512]{3,2,1,0:T(2,128)} %param.8) | copy-start | bytes 36868
  12.1 2.6 %copy-start.10 = (s32[1,1,512]{2,1,0:T(1,128)S(1)}, s32[1,1,512]{2,1,0:T(1,128)}, u32[]{:S(2)}) copy-start(s32[1,1,512]{2,1,0:T(1,128)} %param.11) | copy-start | bytes 6148
  28.2 1.2 copy-start
  28.2 1.5 %copy-start.1 = (bf16[512,1024]{1,0:T(8,128)(2,1)S(1)}, bf16[512,1024]{1,0:T(8,128)(2,1)}, u32[]{:S(2)}) copy-start(bf16[512,1024]{1,0:T(8,128)(2,1)} %reshape.177) | copy-start | bytes 3145732
  32.2 4.7 %collective-permute-start.1 = (bf16[1024,512]{1,0:T(8,128)(2,1)S(1)}, bf16[1024,512]{1,0:T(8,128)(2,1)S(1)}, u32[]{:S(2)}, u32[]{:S(2)}) collective-permute-start(bf16[1024,512]{1,0:T(8,128)(2,1)S(1)} %bitcast.118), channel_id=1, source_target_pairs={{0,16},{16,0},{32,48},{48,32},{64,80},{80,64},{96,112},{112,96},{1... | collective-permute-start | bytes 3145736 | tf_op jit(solution)/shard_map/ppermute | solution.py:16
  38.2 31.0 %collective-permute-start.2 = (bf16[1024,512]{1,0:T(8,128)(2,1)S(1)}, bf16[1024,512]{1,0:T(8,128)(2,1)S(1)}, u32[]{:S(2)}, u32[]{:S(2)}) collective-permute-start(bf16[1024,512]{1,0:T(8,128)(2,1)S(1)} %add_convert_fusion.1), channel_id=1, source_target_pairs={{0,32},{16,48},{32,0},{48,16},{64,96},{80,112},{96,64},{112,80},{1... | collective-permute-start | bytes 3145736 | tf_op jit(solution)/shard_map/ppermute | solution.py:16
  41.4 25.8 %collective-permute-start.5 = (bf16[2,2,512,8]{2,3,1,0:T(8,128)(2,1)S(1)}, bf16[2,2,512,8]{2,3,1,0:T(8,128)(2,1)S(1)}, u32[]{:S(2)}, u32[]{:S(2)}) collective-permute-start(bf16[2,2,512,8]{2,3,1,0:T(8,128)(2,1)S(1)} %slice_bitcast_fusion.2), channel_id=1, source_target_pairs={{0,64},{16,80},{32,96},{48,112},{64,0},{80,16},{96,32},{112,48},{1... | collective-permute-start | bytes 98312 | tf_op jit(solution)/shard_map/ppermute | solution.py:16
  44.8 22.4 %collective-permute-start.4 = (s32[1536]{0:T(1024)S(1)}, s32[1536]{0:T(1024)S(1)}, u32[]{:S(2)}, u32[]{:S(2)}) collective-permute-start(s32[1536]{0:T(1024)S(1)} %pad_add_fusion.2), channel_id=1, source_target_pairs={{0,64},{16,80},{32,96},{48,112},{64,0},{80,16},{96,32},{112,48},{1... | collective-permute-start | bytes 18440 | tf_op jit(solution)/shard_map/ppermute | solution.py:16
  70.5 5.4 %copy-start.5 = (bf16[1024,512]{1,0:T(8,128)(2,1)}, bf16[1024,512]{1,0:T(8,128)(2,1)S(1)}, u32[]{:S(2)}) copy-start(bf16[1024,512]{1,0:T(8,128)(2,1)S(1)} %add_convert_fusion) | copy-start | bytes 3145732
  71.4 18.9 %collective-permute-start.3 = (bf16[1024,256]{1,0:T(8,128)(2,1)}, bf16[1024,256]{1,0:T(8,128)(2,1)}, u32[]{:S(2)}, u32[]{:S(2)}) collective-permute-start(bf16[1024,256]{1,0:T(8,128)(2,1)} %constant_dynamic-slice_fusion), channel_id=1, source_target_pairs={{0,64},{16,80},{32,96},{48,112},{64,0},{80,16},{96,32},{112,48},{1... | collective-permute-start | bytes 1572872 | tf_op jit(solution)/shard_map/ppermute | solution.py:16
  75.9 22.1 %all-to-all-start = ((s32[128,1,8]{2,1,0:T(1,128)}), s32[128,1,8]{2,1,0:T(1,128)S(1)}, u32[]{:S(2)}, u32[]{:S(2)}) async-start(s32[128,1,8]{2,1,0:T(1,128)} %bitcast.31), calls=%async_computation | async-start | bytes 131072 | tf_op jit(solution)/shard_map/all_to_all | solution.py:111
  88.4 1.9 %copy-start.2 = (bf16[512,512]{1,0:T(8,128)(2,1)S(1)}, bf16[512,512]{1,0:T(8,128)(2,1)}, u32[]{:S(2)}) copy-start(bf16[512,512]{1,0:T(8,128)(2,1)} %get-tuple-element.183) | copy-start | bytes 1572868
  88.4 1.9 %copy-start.3 = (bf16[512,512]{1,0:T(8,128)(2,1)S(1)}, bf16[512,512]{1,0:T(8,128)(2,1)}, u32[]{:S(2)}) copy-start(bf16[512,512]{1,0:T(8,128)(2,1)} %get-tuple-element.184) | copy-start | bytes 1572868
  88.4 1.9 %copy-start.4 = (bf16[512,512]{1,0:T(8,128)(2,1)S(1)}, bf16[512,512]{1,0:T(8,128)(2,1)}, u32[]{:S(2)}) copy-start(bf16[512,512]{1,0:T(8,128)(2,1)} %get-tuple-element.210) | copy-start | bytes 1572868
  98.0 39.3 %all-to-all-start.1 = ((bf16[128,16,512]{2,1,0:T(8,128)(2,1)}), bf16[128,16,512]{2,1,0:T(8,128)(2,1)S(1)}, u32[]{:S(2)}, u32[]{:S(2)}) async-start(bf16[128,16,512]{2,1,0:T(8,128)(2,1)} %pad_maximum_fusion), calls=%async_computation.1 | async-start | bytes 4194304 | tf_op jit(solution)/shard_map/all_to_all | solution.py:123

commit v11 on v10

--- a/solution.py
+++ b/solution.py
@@ -60,6 +60,8 @@
     tail = shifted(echoes, "rng", -1)
     extended = jnp.concatenate([echoes, tail], axis=2)
     matrix = replica_matrix(chirp, RBLK)
+    late = (offsets[-1, 0], weights[-1, 0], owners, targets)
+    late, matrix = lax.optimization_barrier((late, matrix))
     stacked = jnp.concatenate([extended[0], extended[1]], axis=1)
     block_out = jnp.dot(stacked, matrix, preferred_element_type=jnp.float32).astype(jnp.bfloat16)
     pieces = block_out.reshape(p_dev, 2, RBLK)
@@ -69,26 +71,28 @@
     bit = 1 << last
     me_sub = lax.axis_index("sub")
     far = lambda value: from_partner(value, "sub", last)
+    own_offsets, own_weights, owners, targets = late
     dest = owners.reshape(p_dev)
     aim = targets.reshape(p_dev)
     slot = dest * capacity + group_slots(dest, devices)
     pick = jnp.arange(devices * capacity, dtype=jnp.int32)[:, None] == slot[None, :]
     labels = jnp.sum(jnp.where(pick, aim[None, :] + 1, 0), axis=1).reshape(devices, capacity) - 1
-    late = (offsets[last, 0], weights[last, 0], slot)
+    far_weights = far(own_weights)
+    far_ints = far(jnp.concatenate([own_offsets.reshape(-1), slot]))
+    far_offsets = far_ints[: 2 * p_dev].reshape(2, p_dev)
+    far_slot = far_ints[2 * p_dev :]
     for section in range(last):
         partner = from_partner(image, "sub", section)
         mine = merge_matrix(offsets[section, 0, 0], weights[section, 0, 0])
         theirs = merge_matrix(offsets[section, 0, 1], weights[section, 0, 1])
         merged = jnp.dot(mine, image, preferred_element_type=jnp.float32)
         if section == 1:
-            late, merged = lax.optimization_barrier((late, merged))
-            own_offsets, own_weights, slot = late
-            far_weights = far(own_weights)
-            far_ints = far(jnp.concatenate([own_offsets.reshape(-1), slot]))
-            far_offsets = far_ints[: 2 * p_dev].reshape(2, p_dev)
-            far_slot = far_ints[2 * p_dev :]
+            labels, merged = lax.optimization_barrier((labels, merged))
+            marks = lax.all_to_all(labels, ("sub", "rng"), split_axis=0, concat_axis=0, tiled=True)
         merged = merged + jnp.dot(theirs, partner, preferred_element_type=jnp.float32)
         image = merged.astype(jnp.bfloat16)
+        if section == 1:
+            marks, image = lax.optimization_barrier((marks, image))
     slots = jnp.arange(devices * capacity, dtype=jnp.int32)[:, None]
     picks = {0: slots == slot[None, :], bit: slots == far_slot[None, :]}
     half = r_dev // 2
@@ -106,9 +110,6 @@
         mine = merge_matrix(starts[0], kernel[0])
         theirs = merge_matrix(starts[1], kernel[1])
         merged = jnp.dot(mine, old[m], preferred_element_type=jnp.float32)
-        if m == 0:
-            labels, merged = lax.optimization_barrier((labels, merged))
-            marks = lax.all_to_all(labels, ("sub", "rng"), split_axis=0, concat_axis=0, tiled=True)
         merged = merged + jnp.dot(theirs, old[m ^ bit], preferred_element_type=jnp.float32)
         piece = merged.astype(jnp.bfloat16)
         rows = piece.reshape(2, p_dev, half).transpose(1, 0, 2).reshape(p_dev, 2 * half)

time: 141 us -> 163 us (1.16)
  other arithmetic: 20 us -> 43.7 us
  waiting for transfers between devices: 51.9 us -> 40.6 us
  matrix products: 17.8 us -> 24.1 us
  starting transfers between devices: 30.9 us -> 36.9 us
  local copies, waits for them, and re-layouts: 19.2 us -> 16.7 us
    concatenate x0 -> x1, other arithmetic: none -> 18.9 us  [replica_matrix(): return jnp.concatenate([upper, lower], axis=0)]
    ppermute x5, waiting for transfers between devices: 18.4 us -> 12.4 us  [from_partner(): lax.ppermute(value, axis, [(i, i ^ 1 << apart) for i in range(lax.axis_si...]
    dot_general x2, matrix products: 2.49 us -> 7.99 us  [on_device(): jnp.dot(theirs, partner, preferred_element_type=jnp.float32)]
    ppermute x1, waiting for transfers between devices: 5.41 us -> 0.01 us  [shifted(): lax.ppermute(value, axis, [(source, source + steps) for source in range(f...]
    neg x8, other arithmetic: 14.9 us -> 19.9 us  [merge_matrix(): upper = jnp.concatenate([g_real, -g_imag], axis=1)]
    dot_general x2, matrix products: 2.48 us -> 6.78 us  [on_device(): merged = jnp.dot(mine, image, preferred_element_type=jnp.float32)]
    all_to_all x1, starting transfers between devices: 9.59 us -> 13.3 us  [on_device(): lax.all_to_all(payload, ('sub', 'rng'), split_axis=0, concat_axis=0, tile...]
    ppermute x5, starting transfers between devices: 7.37 us -> 10.5 us  [from_partner(): lax.ppermute(value, axis, [(i, i ^ 1 << apart) for i in range(lax.axis_si...]
  transfers between devices with their start and end apart: 8 -> 8, of which waited for: 4 -> 3; matrix products, arithmetic and copies ran while one was open for 30% -> 42% of each run, Pallas kernels for 0% -> 0%
where the time goes in v11:
time: 163 us
  other arithmetic  43.7 us (27%)
  waiting for transfers between devices  40.6 us (25%)
  starting transfers between devices  36.9 us (23%)
  matrix products  24.1 us (15%)
  local copies, waits for them, and re-layouts  16.7 us (10%)
    all_to_all x1, waiting for transfers between devices, on_device(): lax.all_to_all(payload, ('sub', 'rng'), split_axis=0, concat_axis=0, tile...  28.1 us
    neg x8, other arithmetic, merge_matrix(): upper = jnp.concatenate([g_real, -g_imag], axis=1)  19.9 us
    concatenate x1, other arithmetic, replica_matrix(): return jnp.concatenate([upper, lower], axis=0)  18.9 us
    all_to_all x1, starting transfers between devices, on_device(): lax.all_to_all(payload, ('sub', 'rng'), split_axis=0, concat_axis=0, tile...  13.3 us
    ppermute x5, waiting for transfers between devices, from_partner(): lax.ppermute(value, axis, [(i, i ^ 1 << apart) for i in range(lax.axis_si...  12.4 us
    all_to_all x1, starting transfers between devices, on_device(): lax.all_to_all(labels, ('sub', 'rng'), split_axis=0, concat_axis=0, tiled...  11.8 us
    ppermute x5, starting transfers between devices, from_partner(): lax.ppermute(value, axis, [(i, i ^ 1 << apart) for i in range(lax.axis_si...  10.5 us
    dot_general x2, matrix products, on_device(): jnp.dot(theirs, partner, preferred_element_type=jnp.float32)  7.99 us
  transfers between devices with their start and end apart: 8, of which 3 were waited for; matrix products, arithmetic and copies ran while one was open for 42% of the time, Pallas kernels for 0%

profile of v11, /device:TPU:1, one launch (start us, length us, event | category | flops | bytes accessed | tf_op | source)
XLA Modules:
  0.0 162.6 jit_solution(4300536059177255933)
XLA Ops:
  0.0 1.3 collective-permute-start
  1.3 0.8 slice_reduce_fusion.128
  2.2 1.3 tile.21
  3.6 0.5 reshape.158
  4.1 1.1 bitcast_negate_fusion
  5.3 1.3 tile.9
  6.6 1.0 slice.953
  7.7 1.5 reshape.157
  9.3 18.9 %maximum_maximum_fusion = bf16[2048,1024]{0,1:T(8,128)(2,1)} fusion(bf16[1024,512]{0,1:T(8,128)(2,1)S(1)} %bitcast.120, bf16[1024,512]{0,1:T(8,128)(2,1)S(1)} %bitcast.119, bf16[1024,512]{0,1:T(8,128)(2,1)S(1)} %copy-done.1), kind=kLoop, calls=%fused_computation | loop fusion | flops 16777216 | bytes 7340032 | tf_op jit(solution)/shard_map/concatenate | solution.py:30
  28.6 0.2 fusion.295
  28.9 4.7 %collective-permute-start.4 = (s32[1536]{0:T(1024)S(1)}, s32[1536]{0:T(1024)S(1)}, u32[]{:S(2)}, u32[]{:S(2)}) collective-permute-start(s32[1536]{0:T(1024)S(1)} %pad_add_fusion.2), channel_id=1, source_target_pairs={{0,64},{16,80},{32,96},{48,112},{64,0},{80,16},{96,32},{112,48},{1... | collective-permute-start | bytes 18440 | tf_op jit(solution)/shard_map/ppermute | solution.py:16
  33.8 0.3 select_reduce_fusion
  34.8 2.8 %fusion.326 = (bf16[512,512]{1,0:T(8,128)(2,1)}, bf16[512,512]{1,0:T(8,128)(2,1)}, bf16[512,512]{1,0:T(8,128)(2,1)}) fusion(bf16[512]{0:T(512)(128)(2,1)S(1)} %get-tuple-element.120, bf16[512]{0:T(512)(128)(2,1)S(1)} %get-tuple-element.121, bf16[512]{0:T(512)(128)(2,1)S(1)} %get-tuple-element.122, bf16[512]{0:T(512)(128)(2,1)S(1)} %get-tuple-element.123, ...), kind=kLoop, calls=%fused_computation.511 | loop fusion | flops 7340032 | bytes 1591296 | tf_op jit(solution)/shard_map/neg | solution.py:43
  37.5 2.7 %fusion.327 = (bf16[512,512]{1,0:T(8,128)(2,1)}, bf16[512,512]{1,0:T(8,128)(2,1)}, bf16[512,512]{1,0:T(8,128)(2,1)}) fusion(bf16[512]{0:T(512)(128)(2,1)S(1)} %get-tuple-element.104, bf16[512]{0:T(512)(128)(2,1)S(1)} %get-tuple-element.105, bf16[512]{0:T(512)(128)(2,1)S(1)} %get-tuple-element.106, bf16[512]{0:T(512)(128)(2,1)S(1)} %get-tuple-element.107, ...), kind=kLoop, calls=%fused_computation.512 | loop fusion | flops 7340032 | bytes 1591296 | tf_op jit(solution)/shard_map/neg | solution.py:43
  40.3 2.7 %fusion.325 = (bf16[512,512]{1,0:T(8,128)(2,1)S(1)}, bf16[512,512]{1,0:T(8,128)(2,1)}, bf16[512,512]{1,0:T(8,128)(2,1)}) fusion(bf16[512]{0:T(512)(128)(2,1)S(1)} %get-tuple-element.88, bf16[512]{0:T(512)(128)(2,1)S(1)} %get-tuple-element.89, bf16[512]{0:T(512)(128)(2,1)S(1)} %get-tuple-element.90, bf16[512]{0:T(512)(128)(2,1)S(1)} %get-tuple-element.91, ...), kind=kLoop, calls=%fused_computation.510 | loop fusion | flops 7340032 | bytes 1591296 | tf_op jit(solution)/shard_map/neg | solution.py:43
  42.9 2.8 %fusion.328 = (bf16[512,512]{1,0:T(8,128)(2,1)}, bf16[512,512]{1,0:T(8,128)(2,1)}, bf16[512,512]{1,0:T(8,128)(2,1)}) fusion(bf16[512]{0:T(512)(128)(2,1)S(1)} %get-tuple-element.72, bf16[512]{0:T(512)(128)(2,1)S(1)} %get-tuple-element.73, bf16[512]{0:T(512)(128)(2,1)S(1)} %get-tuple-element.74, bf16[512]{0:T(512)(128)(2,1)S(1)} %get-tuple-element.75, ...), kind=kLoop, calls=%fused_computation.513 | loop fusion | flops 7340032 | bytes 1591296 | tf_op jit(solution)/shard_map/neg | solution.py:43
  45.7 1.7 %fusion.330 = (bf16[512,512]{1,0:T(8,128)(2,1)S(1)}, bf16[512,512]{1,0:T(8,128)(2,1)S(1)}, bf16[512,512]{1,0:T(8,128)(2,1)S(1)}) fusion(bf16[512]{0:T(512)(128)(2,1)S(1)} %get-tuple-element.24, bf16[512]{0:T(512)(128)(2,1)S(1)} %get-tuple-element.25, bf16[512]{0:T(512)(128)(2,1)S(1)} %get-tuple-element.26, bf16[512]{0:T(512)(128)(2,1)S(1)} %get-tuple-element.27, ...), kind=kLoop, calls=%fused_computation.515 | loop fusion | flops 7340032 | bytes 1591296 | tf_op jit(solution)/shard_map/neg | solution.py:43
  47.4 2.8 %fusion.329 = (bf16[512,512]{1,0:T(8,128)(2,1)}, bf16[512,512]{1,0:T(8,128)(2,1)}, bf16[512,512]{1,0:T(8,128)(2,1)}) fusion(bf16[512]{0:T(512)(128)(2,1)S(1)} %get-tuple-element.40, bf16[512]{0:T(512)(128)(2,1)S(1)} %get-tuple-element.41, bf16[512]{0:T(512)(128)(2,1)S(1)} %get-tuple-element.42, bf16[512]{0:T(512)(128)(2,1)S(1)} %get-tuple-element.43, ...), kind=kLoop, calls=%fused_computation.514 | loop fusion | flops 7340032 | bytes 1591296 | tf_op jit(solution)/shard_map/neg | solution.py:43
  50.2 1.4 constant_dynamic-update-slice_fusion
  51.8 2.0 %copy-done = bf16[2048,1024]{0,1:T(8,128)(2,1)S(1)} copy-done((bf16[2048,1024]{0,1:T(8,128)(2,1)S(1)}, bf16[2048,1024]{0,1:T(8,128)(2,1)}, u32[]{:S(2)}) %copy-start) | copy-done | bytes 4194328
  53.8 2.4 %fusion.76 = bf16[512,1024]{1,0:T(8,128)(2,1)S(1)} fusion(bf16[2048,1024]{0,1:T(8,128)(2,1)S(1)} %copy-done, bf16[512,1024]{1,0:T(8,128)(2,1)S(1)} %get-tuple-element.156, bf16[512,1024]{1,0:T(8,128)(2,1)S(1)} %get-tuple-element.155), kind=kOutput, calls=%fused_computation.81 | convolution fusion | flops 2152202240 | bytes 7340032 | tf_op jit(solution)/shard_map/dot_general | solution.py:66
  56.2 1.0 collective-permute-start.1
  57.3 0.7 sub.137
  58.0 2.9 %fusion.8 = f32[1024,512]{1,0:T(8,128)S(1)} fusion(bf16[1024,512]{1,0:T(8,128)(2,1)S(1)} %bitcast.122, bf16[512,512]{1,0:T(8,128)(2,1)} %get-tuple-element.220, bf16[512,512]{1,0:T(8,128)(2,1)} %get-tuple-element.198, bf16[512,512]{1,0:T(8,128)(2,1)} %get-tuple-element.197), kind=kOutput, calls=%fused_computation.9 | convolution fusion | flops 1082130432 | bytes 4718592 | tf_op jit(solution)/shard_map/dot_general | solution.py:88
  61.0 3.5 %add_convert_fusion.1 = bf16[1024,512]{1,0:T(8,128)(2,1)} fusion(f32[1024,512]{1,0:T(8,128)S(1)} %fusion.8, bf16[1024,512]{1,0:T(8,128)(2,1)} %collective-permute-done.1, bf16[512,512]{1,0:T(8,128)(2,1)S(1)} %copy-done.12, bf16[512,512]{1,0:T(8,128)(2,1)S(1)} %copy-done.11, bf16[512,512]{1,0:T(8,128)(2,1)S(1)} %copy-done.10), kind=kOutput, calls=%fused_computation.73 | convolution fusion | flops 1083179008 | bytes 5767168 | tf_op jit(solution)/shard_map/dot_general | solution.py:92
  64.5 1.2 collective-permute-start.2
  65.9 2.8 %fusion.331 = (bf16[512,512]{1,0:T(8,128)(2,1)}, bf16[512,512]{1,0:T(8,128)(2,1)}, bf16[512,512]{1,0:T(8,128)(2,1)}) fusion(bf16[512]{0:T(512)(128)(2,1)S(1)} %get-tuple-element.56, bf16[512]{0:T(512)(128)(2,1)S(1)} %get-tuple-element.57, bf16[512]{0:T(512)(128)(2,1)S(1)} %get-tuple-element.58, bf16[512]{0:T(512)(128)(2,1)S(1)} %get-tuple-element.59, ...), kind=kLoop, calls=%fused_computation.516 | loop fusion | flops 7340032 | bytes 1591296 | tf_op jit(solution)/shard_map/neg | solution.py:43
  68.7 3.9 %fusion = f32[1024,512]{1,0:T(8,128)} fusion(bf16[1024,512]{1,0:T(8,128)(2,1)} %add_convert_fusion.1, bf16[512,512]{1,0:T(8,128)(2,1)S(1)} %copy-done.4, bf16[512,512]{1,0:T(8,128)(2,1)S(1)} %copy-done.3, bf16[512,512]{1,0:T(8,128)(2,1)S(1)} %get-tuple-element.193), kind=kOutput, calls=%fused_computation.1 | convolution fusion | flops 1082130432 | bytes 4718592 | tf_op jit(solution)/shard_map/dot_general | solution.py:88
  72.6 11.8 %all-to-all-start = ((s32[128,1,8]{2,1,0:T(1,128)}), s32[128,1,8]{2,1,0:T(1,128)S(1)}, u32[]{:S(2)}, u32[]{:S(2)}) async-start(s32[128,1,8]{2,1,0:T(1,128)} %bitcast.25), calls=%async_computation | async-start | bytes 131072 | tf_op jit(solution)/shard_map/all_to_all | solution.py:91
  84.4 5.3 %collective-permute-done.2 = bf16[1024,512]{1,0:T(8,128)(2,1)} collective-permute-done((bf16[1024,512]{1,0:T(8,128)(2,1)}, bf16[1024,512]{1,0:T(8,128)(2,1)}, u32[]{:S(2)}, u32[]{:S(2)}) %collective-permute-start.2) | collective-permute-done | bytes 1048608 | tf_op jit(solution)/shard_map/ppermute | solution.py:16
  89.8 4.5 %add_convert_fusion = bf16[1024,512]{1,0:T(8,128)(2,1)} fusion(f32[1024,512]{1,0:T(8,128)} %fusion, bf16[1024,512]{1,0:T(8,128)(2,1)} %collective-permute-done.2, bf16[512,512]{1,0:T(8,128)(2,1)} %get-tuple-element.217, bf16[512,512]{1,0:T(8,128)(2,1)S(1)} %copy-done.6, bf16[512,512]{1,0:T(8,128)(2,1)S(1)} %copy-done.5), kind=kOutput, calls=%fused_computation.72 | convolution fusion | flops 1083179008 | bytes 5767168 | tf_op jit(solution)/shard_map/dot_general | solution.py:92
  94.2 1.2 constant_dynamic-slice_fusion
  95.5 3.5 %collective-permute-start.3 = (bf16[1024,256]{1,0:T(8,128)(2,1)S(1)}, bf16[1024,256]{1,0:T(8,128)(2,1)S(1)}, u32[]{:S(2)}, u32[]{:S(2)}) collective-permute-start(bf16[1024,256]{1,0:T(8,128)(2,1)S(1)} %constant_dynamic-slice_fusion), channel_id=1, source_target_pairs={{0,64},{16,80},{32,96},{48,112},{64,0},{80,16},{96,32},{112,48},{1... | collective-permute-start | bytes 1572872 | tf_op jit(solution)/shard_map/ppermute | solution.py:16
  99.0 1.7 %fusion.332 = (bf16[512,512]{1,0:T(8,128)(2,1)S(1)}, bf16[512,512]{1,0:T(8,128)(2,1)S(1)}, bf16[512,512]{1,0:T(8,128)(2,1)S(1)}) fusion(bf16[512]{0:T(512)(128)(2,1)S(1)} %get-tuple-element.136, bf16[512]{0:T(512)(128)(2,1)S(1)} %get-tuple-element.137, bf16[512]{0:T(512)(128)(2,1)S(1)} %get-tuple-element.138, bf16[512]{0:T(512)(128)(2,1)S(1)} %get-tuple-element.139, ...), kind=kLoop, calls=%fused_computation.517 | loop fusion | flops 7340032 | bytes 1591296 | tf_op jit(solution)/shard_map/neg | solution.py:43
  100.8 0.7 fusion.36
  101.5 1.7 %fusion.60 = f32[1024,256]{1,0:T(8,128)} fusion(bf16[512,512]{1,0:T(8,128)(2,1)S(1)} %get-tuple-element.221, bf16[512,512]{1,0:T(8,128)(2,1)S(1)} %get-tuple-element.200, bf16[512,512]{1,0:T(8,128)(2,1)S(1)} %get-tuple-element.199, bf16[1024,512]{1,0:T(8,128)(2,1)S(1)} %copy-done.16, s32[]{:T(128)S(6)} %select_n.476), kind=kOutput, calls=%fused_computation.61 | convolution fusion | flops 545259520 | bytes 3145732 | tf_op jit(solution)/shard_map/dot_general | solution.py:113
  103.2 7.1 %collective-permute-done.3 = bf16[1024,256]{1,0:T(8,128)(2,1)S(1)} collective-permute-done((bf16[1024,256]{1,0:T(8,128)(2,1)S(1)}, bf16[1024,256]{1,0:T(8,128)(2,1)S(1)}, u32[]{:S(2)}, u32[]{:S(2)}) %collective-permute-start.3) | collective-permute-done | bytes 524320 | tf_op jit(solution)/shard_map/ppermute | solution.py:16
  110.3 0.7 fusion.91
  111.3 0.8 fusion.81
  112.6 0.3 copy-done.23
  113.0 0.7 fusion.94
  113.9 0.8 fusion.82
  114.7 1.7 %pad_maximum_fusion = bf16[128,16,512]{2,1,0:T(8,128)(2,1)} fusion(bf16[128,8,512]{2,1,0:T(8,128)(2,1)S(1)} %fusion.82, bf16[128,8,512]{2,1,0:T(8,128)(2,1)S(1)} %fusion.81), kind=kLoop, calls=%fused_computation.69 | loop fusion | flops 4194304 | bytes 4194304 | tf_op jit(solution)/shard_map/concatenate | solution.py:123
  116.4 13.3 %all-to-all-start.1 = ((bf16[128,16,512]{2,1,0:T(8,128)(2,1)}), bf16[128,16,512]{2,1,0:T(8,128)(2,1)S(1)}, u32[]{:S(2)}, u32[]{:S(2)}) async-start(bf16[128,16,512]{2,1,0:T(8,128)(2,1)} %pad_maximum_fusion), calls=%async_computation.1 | async-start | bytes 4194304 | tf_op jit(solution)/shard_map/all_to_all | solution.py:124
  131.2 28.1 %all-to-all-done.1 = bf16[128,16,512]{2,1,0:T(8,128)(2,1)S(1)} async-done(((bf16[128,16,512]{2,1,0:T(8,128)(2,1)}), bf16[128,16,512]{2,1,0:T(8,128)(2,1)S(1)}, u32[]{:S(2)}, u32[]{:S(2)}) %all-to-all-start.1) | async-done | bytes 2097184 | tf_op jit(solution)/shard_map/all_to_all | solution.py:124
  159.5 0.8 fusion.90
  160.5 0.8 fusion.89
  161.5 1.1 maximum_bitcast_fusion
  (113 shorter events, 5.3 us)
Async XLA Ops:
  0.0 50.2 %collective-permute-start = (bf16[2,512,512]{2,1,0:T(8,128)(2,1)}, bf16[2,512,512]{2,1,0:T(8,128)(2,1)}, u32[]{:S(2)}, u32[]{:S(2)}) collective-permute-start(bf16[2,512,512]{2,1,0:T(8,128)(2,1)} %param.6), channel_id=1, source_target_pairs={{1,0},{2,1},{3,2},{4,3},{5,4},{6,5},{7,6},{8,7},{9,8},{10,9},{11,1... | collective-permute-start | bytes 3145736 | tf_op jit(solution)/shard_map/ppermute | solution.py:12
  6.6 2.6 %copy-start.17 = (bf16[3,1,2,2,512,8]{4,5,3,2,1,0:T(8,128)(2,1)S(1)}, bf16[3,1,2,2,512,8]{4,5,3,2,1,0:T(8,128)(2,1)}, u32[]{:S(2)}) copy-start(bf16[3,1,2,2,512,8]{4,5,3,2,1,0:T(8,128)(2,1)} %param.9) | copy-start | bytes 294916
  6.6 2.6 %copy-start.19 = (s32[3,1,2,512]{3,2,1,0:T(2,128)S(1)}, s32[3,1,2,512]{3,2,1,0:T(2,128)}, u32[]{:S(2)}) copy-start(s32[3,1,2,512]{3,2,1,0:T(2,128)} %param.8) | copy-start | bytes 36868
  6.6 2.6 %copy-start.1 = (bf16[1024,512]{0,1:T(8,128)(2,1)S(1)}, bf16[1024,512]{0,1:T(8,128)(2,1)}, u32[]{:S(2)}) copy-start(bf16[1024,512]{0,1:T(8,128)(2,1)} %bitcast_negate_fusion) | copy-start | bytes 3145732
  9.2 18.9 %copy-start.18 = (s32[1,1,512,1]{2,3,1,0:T(1,128)S(1)}, s32[1,1,512,1]{2,3,1,0:T(1,128)}, u32[]{:S(2)}) copy-start(s32[1,1,512,1]{2,3,1,0:T(1,128)} %param.10) | copy-start | bytes 6148
  28.1 5.5 %copy-start.2 = (bf16[2,512,512]{2,1,0:T(8,128)(2,1)S(1)}, bf16[2,512,512]{2,1,0:T(8,128)(2,1)}, u32[]{:S(2)}) copy-start(bf16[2,512,512]{2,1,0:T(8,128)(2,1)} %param.6) | copy-start | bytes 3145732
  28.1 5.7 %copy-start.20 = (s32[1,1,512]{2,1,0:T(1,128)S(1)}, s32[1,1,512]{2,1,0:T(1,128)}, u32[]{:S(2)}) copy-start(s32[1,1,512]{2,1,0:T(1,128)} %param.11) | copy-start | bytes 6148
  28.9 29.1 %collective-permute-start.4 = (s32[1536]{0:T(1024)S(1)}, s32[1536]{0:T(1024)S(1)}, u32[]{:S(2)}, u32[]{:S(2)}) collective-permute-start(s32[1536]{0:T(1024)S(1)} %pad_add_fusion.2), channel_id=1, source_target_pairs={{0,64},{16,80},{32,96},{48,112},{64,0},{80,16},{96,32},{112,48},{1... | collective-permute-start | bytes 18440 | tf_op jit(solution)/shard_map/ppermute | solution.py:16
  33.5 24.5 %collective-permute-start.5 = (bf16[2,2,512,8]{2,3,1,0:T(8,128)(2,1)S(1)}, bf16[2,2,512,8]{2,3,1,0:T(8,128)(2,1)S(1)}, u32[]{:S(2)}, u32[]{:S(2)}) collective-permute-start(bf16[2,2,512,8]{2,3,1,0:T(8,128)(2,1)S(1)} %slice_bitcast_fusion.2), channel_id=1, source_target_pairs={{0,64},{16,80},{32,96},{48,112},{64,0},{80,16},{96,32},{112,48},{1... | collective-permute-start | bytes 98312 | tf_op jit(solution)/shard_map/ppermute | solution.py:16
  51.6 2.2 %copy-start = (bf16[2048,1024]{0,1:T(8,128)(2,1)S(1)}, bf16[2048,1024]{0,1:T(8,128)(2,1)}, u32[]{:S(2)}) copy-start(bf16[2048,1024]{0,1:T(8,128)(2,1)} %maximum_maximum_fusion) | copy-start | bytes 12582916
  56.2 4.7 %collective-permute-start.1 = (bf16[1024,512]{1,0:T(8,128)(2,1)S(1)}, bf16[1024,512]{1,0:T(8,128)(2,1)}, u32[]{:S(2)}, u32[]{:S(2)}) collective-permute-start(bf16[1024,512]{1,0:T(8,128)(2,1)S(1)} %bitcast.121), channel_id=1, source_target_pairs={{0,16},{16,0},{32,48},{48,32},{64,80},{80,64},{96,112},{112,96},{1... | collective-permute-start | bytes 3145736 | tf_op jit(solution)/shard_map/ppermute | solution.py:16
  58.0 2.9 %copy-start.10 = (bf16[512,512]{1,0:T(8,128)(2,1)S(1)}, bf16[512,512]{1,0:T(8,128)(2,1)}, u32[]{:S(2)}) copy-start(bf16[512,512]{1,0:T(8,128)(2,1)} %get-tuple-element.195) | copy-start | bytes 1572868
  58.0 2.9 %copy-start.11 = (bf16[512,512]{1,0:T(8,128)(2,1)S(1)}, bf16[512,512]{1,0:T(8,128)(2,1)}, u32[]{:S(2)}) copy-start(bf16[512,512]{1,0:T(8,128)(2,1)} %get-tuple-element.196) | copy-start | bytes 1572868
  58.0 2.9 %copy-start.12 = (bf16[512,512]{1,0:T(8,128)(2,1)S(1)}, bf16[512,512]{1,0:T(8,128)(2,1)}, u32[]{:S(2)}) copy-start(bf16[512,512]{1,0:T(8,128)(2,1)} %get-tuple-element.219) | copy-start | bytes 1572868
  61.0 7.7 %copy-start.3 = (bf16[512,512]{1,0:T(8,128)(2,1)S(1)}, bf16[512,512]{1,0:T(8,128)(2,1)}, u32[]{:S(2)}) copy-start(bf16[512,512]{1,0:T(8,128)(2,1)} %get-tuple-element.194) | copy-start | bytes 1572868
  61.0 7.7 %copy-start.4 = (bf16[512,512]{1,0:T(8,128)(2,1)S(1)}, bf16[512,512]{1,0:T(8,128)(2,1)}, u32[]{:S(2)}) copy-start(bf16[512,512]{1,0:T(8,128)(2,1)} %get-tuple-element.218) | copy-start | bytes 1572868
  64.5 25.3 %collective-permute-start.2 = (bf16[1024,512]{1,0:T(8,128)(2,1)}, bf16[1024,512]{1,0:T(8,128)(2,1)}, u32[]{:S(2)}, u32[]{:S(2)}) collective-permute-start(bf16[1024,512]{1,0:T(8,128)(2,1)} %add_convert_fusion.1), channel_id=1, source_target_pairs={{0,32},{16,48},{32,0},{48,16},{64,96},{80,112},{96,64},{112,80},{1... | collective-permute-start | bytes 3145736 | tf_op jit(solution)/shard_map/ppermute | solution.py:16
  68.7 21.1 %copy-start.5 = (bf16[512,512]{1,0:T(8,128)(2,1)S(1)}, bf16[512,512]{1,0:T(8,128)(2,1)}, u32[]{:S(2)}) copy-start(bf16[512,512]{1,0:T(8,128)(2,1)} %get-tuple-element.191) | copy-start | bytes 1572868
  68.7 21.1 %copy-start.6 = (bf16[512,512]{1,0:T(8,128)(2,1)S(1)}, bf16[512,512]{1,0:T(8,128)(2,1)}, u32[]{:S(2)}) copy-start(bf16[512,512]{1,0:T(8,128)(2,1)} %get-tuple-element.192) | copy-start | bytes 1572868
  72.6 21.6 %all-to-all-start = ((s32[128,1,8]{2,1,0:T(1,128)}), s32[128,1,8]{2,1,0:T(1,128)S(1)}, u32[]{:S(2)}, u32[]{:S(2)}) async-start(s32[128,1,8]{2,1,0:T(1,128)} %bitcast.25), calls=%async_computation | async-start | bytes 131072 | tf_op jit(solution)/shard_map/all_to_all | solution.py:91
  94.2 6.5 %copy-start.7 = (bf16[512,512]{1,0:T(8,128)(2,1)S(1)}, bf16[512,512]{1,0:T(8,128)(2,1)}, u32[]{:S(2)}) copy-start(bf16[512,512]{1,0:T(8,128)(2,1)} %get-tuple-element.187) | copy-start | bytes 1572868
  94.2 6.5 %copy-start.8 = (bf16[512,512]{1,0:T(8,128)(2,1)S(1)}, bf16[512,512]{1,0:T(8,128)(2,1)}, u32[]{:S(2)}) copy-start(bf16[512,512]{1,0:T(8,128)(2,1)} %get-tuple-element.188) | copy-start | bytes 1572868
  94.2 6.5 %copy-start.9 = (bf16[512,512]{1,0:T(8,128)(2,1)S(1)}, bf16[512,512]{1,0:T(8,128)(2,1)}, u32[]{:S(2)}) copy-start(bf16[512,512]{1,0:T(8,128)(2,1)} %get-tuple-element.215) | copy-start | bytes 1572868
  94.2 6.5 %copy-start.16 = (bf16[1024,512]{1,0:T(8,128)(2,1)S(1)}, bf16[1024,512]{1,0:T(8,128)(2,1)}, u32[]{:S(2)}) copy-start(bf16[1024,512]{1,0:T(8,128)(2,1)} %add_convert_fusion) | copy-start | bytes 3145732
  95.5 14.8 %collective-permute-start.3 = (bf16[1024,256]{1,0:T(8,128)(2,1)S(1)}, bf16[1024,256]{1,0:T(8,128)(2,1)S(1)}, u32[]{:S(2)}, u32[]{:S(2)}) collective-permute-start(bf16[1024,256]{1,0:T(8,128)(2,1)S(1)} %constant_dynamic-slice_fusion), channel_id=1, source_target_pairs={{0,64},{16,80},{32,96},{48,112},{64,0},{80,16},{96,32},{112,48},{1... | collective-permute-start | bytes 1572872 | tf_op jit(solution)/shard_map/ppermute | solution.py:16
  110.3 0.8 copy-start.21
  111.1 1.0 copy-start.13
  111.1 1.2 copy-start.14
  111.1 1.4 copy-start.15
  111.3 1.3 copy-start.22
  111.3 1.7 %copy-start.23 = (f32[1024,256]{1,0:T(8,128)S(1)}, f32[1024,256]{1,0:T(8,128)}, u32[]{:S(2)}) copy-start(f32[1024,256]{1,0:T(8,128)} %fusion.60) | copy-start | bytes 3145732
  116.4 43.0 %all-to-all-start.1 = ((bf16[128,16,512]{2,1,0:T(8,128)(2,1)}), bf16[128,16,512]{2,1,0:T(8,128)(2,1)S(1)}, u32[]{:S(2)}, u32[]{:S(2)}) async-start(bf16[128,16,512]{2,1,0:T(8,128)(2,1)} %pad_maximum_fusion), calls=%async_computation.1 | async-start | bytes 4194304 | tf_op jit(solution)/shard_map/all_to_all | solution.py:124

commit v12 on v11

--- a/solution.py
+++ b/solution.py
@@ -60,8 +60,6 @@
     tail = shifted(echoes, "rng", -1)
     extended = jnp.concatenate([echoes, tail], axis=2)
     matrix = replica_matrix(chirp, RBLK)
-    late = (offsets[-1, 0], weights[-1, 0], owners, targets)
-    late, matrix = lax.optimization_barrier((late, matrix))
     stacked = jnp.concatenate([extended[0], extended[1]], axis=1)
     block_out = jnp.dot(stacked, matrix, preferred_element_type=jnp.float32).astype(jnp.bfloat16)
     pieces = block_out.reshape(p_dev, 2, RBLK)
@@ -71,12 +69,14 @@
     bit = 1 << last
     me_sub = lax.axis_index("sub")
     far = lambda value: from_partner(value, "sub", last)
-    own_offsets, own_weights, owners, targets = late
     dest = owners.reshape(p_dev)
     aim = targets.reshape(p_dev)
     slot = dest * capacity + group_slots(dest, devices)
     pick = jnp.arange(devices * capacity, dtype=jnp.int32)[:, None] == slot[None, :]
     labels = jnp.sum(jnp.where(pick, aim[None, :] + 1, 0), axis=1).reshape(devices, capacity) - 1
+    late = (offsets[last, 0], weights[last, 0], slot)
+    late, labels = lax.optimization_barrier((late, labels))
+    own_offsets, own_weights, slot = late
     far_weights = far(own_weights)
     far_ints = far(jnp.concatenate([own_offsets.reshape(-1), slot]))
     far_offsets = far_ints[: 2 * p_dev].reshape(2, p_dev)

time: 163 us -> 154 us (0.945)
  other arithmetic: 43.7 us -> 30 us
  local copies, waits for them, and re-layouts: 16.7 us -> 23.7 us
  waiting for transfers between devices: 40.6 us -> 38.9 us
    concatenate x1 -> x0, other arithmetic: 18.9 us -> none  [replica_matrix(): return jnp.concatenate([upper, lower], axis=0)]
    ppermute x5, waiting for transfers between devices: 12.4 us -> 10.5 us  [from_partner(): lax.ppermute(value, axis, [(i, i ^ 1 << apart) for i in range(lax.axis_si...]
    another operation x4, local copies, waits for them, and re-layouts: 2.84 us -> 4.73 us  [replica_matrix(): jnp.tile(padded, block_len)[:block_len * width].reshape(block_len, width)]
    neg x8, other arithmetic: 19.9 us -> 21.8 us  [merge_matrix(): upper = jnp.concatenate([g_real, -g_imag], axis=1)]
    unnamed x50 -> x58, local copies, waits for them, and re-layouts: 3.22 us -> 3.49 us
  transfers between devices with their start and end apart: 8 -> 8, of which waited for: 3 -> 4; matrix products, arithmetic and copies ran while one was open for 42% -> 38% of each run, Pallas kernels for 0% -> 0%
where the time goes in v12:
time: 154 us; the launch traced here: 153 us
  waiting for transfers between devices  38.9 us (25%)
  starting transfers between devices  36.7 us (24%)
  other arithmetic  30 us (19%)
  local copies, waits for them, and re-layouts  23.7 us (15%)
  matrix products  23.6 us (15%)
    all_to_all x1, waiting for transfers between devices, on_device(): lax.all_to_all(payload, ('sub', 'rng'), split_axis=0, concat_axis=0, tile...  28.1 us
    neg x8, other arithmetic, merge_matrix(): upper = jnp.concatenate([g_real, -g_imag], axis=1)  21.8 us
    all_to_all x1, starting transfers between devices, on_device(): lax.all_to_all(payload, ('sub', 'rng'), split_axis=0, concat_axis=0, tile...  13.5 us
    all_to_all x1, starting transfers between devices, on_device(): lax.all_to_all(labels, ('sub', 'rng'), split_axis=0, concat_axis=0, tiled...  11.8 us
    ppermute x5, waiting for transfers between devices, from_partner(): lax.ppermute(value, axis, [(i, i ^ 1 << apart) for i in range(lax.axis_si...  10.5 us
    ppermute x5, starting transfers between devices, from_partner(): lax.ppermute(value, axis, [(i, i ^ 1 << apart) for i in range(lax.axis_si...  9.91 us
    dot_general x2, matrix products, on_device(): jnp.dot(theirs, partner, preferred_element_type=jnp.float32)  7.7 us
    dot_general x2, matrix products, on_device(): merged = jnp.dot(mine, image, preferred_element_type=jnp.float32)  6.69 us
  transfers between devices with their start and end apart: 8, of which 4 were waited for; matrix products, arithmetic and copies ran while one was open for 38% of the time, Pallas kernels for 0%

profile of v12, /device:TPU:1, one launch (start us, length us, event | category | flops | bytes accessed | tf_op | source)
XLA Modules:
  0.0 153.4 jit_solution(5051016770221465788)
XLA Ops:
  0.0 1.4 collective-permute-start
  1.4 0.8 copy.39
  2.6 0.9 fusion.304
  5.9 0.8 slice_bitcast_fusion.2
  7.3 4.4 %collective-permute-start.5 = (bf16[2,2,512,8]{2,3,1,0:T(8,128)(2,1)S(1)}, bf16[2,2,512,8]{2,3,1,0:T(8,128)(2,1)S(1)}, u32[]{:S(2)}, u32[]{:S(2)}) collective-permute-start(bf16[2,2,512,8]{2,3,1,0:T(8,128)(2,1)S(1)} %slice_bitcast_fusion.2), channel_id=1, source_target_pairs={{0,64},{16,80},{32,96},{48,112},{64,0},{80,16},{96,32},{112,48},{1... | collective-permute-start | bytes 98312 | tf_op jit(solution)/shard_map/ppermute | solution.py:16
  11.8 0.8 slice_bitcast_fusion.11
  12.6 0.8 fusion.344
  13.7 2.3 %tile.21 = bf16[524800]{0:T(1024)(128)(2,1)} reshape(bf16[512,1025]{1,0:T(8,128)(2,1)S(1)} %tile.20) | data formatting | bytes 2099200 | tf_op jit(solution)/shard_map/tile | solution.py:25
  16.0 1.2 slice-done
  17.2 1.3 reshape.161
  18.5 2.3 %bitcast_negate_fusion = bf16[1024,512]{0,1:T(8,128)(2,1)} fusion(bf16[512,1024]{1,0:T(8,128)(2,1)} %reshape.161), kind=kLoop, calls=%fused_computation.516 | loop fusion | flops 524288 | bytes 2097152 | tf_op jit(solution)/shard_map/neg | solution.py:28
  21.0 2.3 %tile.9 = bf16[524800]{0:T(1024)(128)(2,1)} reshape(bf16[512,1025]{1,0:T(8,128)(2,1)S(1)} %tile.8) | data formatting | bytes 2099200 | tf_op jit(solution)/shard_map/tile | solution.py:25
  23.2 1.2 slice-done.1
  24.5 1.3 reshape.160
  26.3 2.8 %fusion.335 = (bf16[512,512]{1,0:T(8,128)(2,1)}, bf16[512,512]{1,0:T(8,128)(2,1)}, bf16[512,512]{1,0:T(8,128)(2,1)}) fusion(bf16[512]{0:T(512)(128)(2,1)S(1)} %get-tuple-element.118, bf16[512]{0:T(512)(128)(2,1)S(1)} %get-tuple-element.119, bf16[512]{0:T(512)(128)(2,1)S(1)} %get-tuple-element.120, bf16[512]{0:T(512)(128)(2,1)S(1)} %get-tuple-element.121, ...), kind=kLoop, calls=%fused_computation.518 | loop fusion | flops 7340032 | bytes 1591296 | tf_op jit(solution)/shard_map/neg | solution.py:43
  29.1 2.7 %fusion.336 = (bf16[512,512]{1,0:T(8,128)(2,1)}, bf16[512,512]{1,0:T(8,128)(2,1)}, bf16[512,512]{1,0:T(8,128)(2,1)}) fusion(bf16[512]{0:T(512)(128)(2,1)S(1)} %get-tuple-element.102, bf16[512]{0:T(512)(128)(2,1)S(1)} %get-tuple-element.103, bf16[512]{0:T(512)(128)(2,1)S(1)} %get-tuple-element.104, bf16[512]{0:T(512)(128)(2,1)S(1)} %get-tuple-element.105, ...), kind=kLoop, calls=%fused_computation.519 | loop fusion | flops 7340032 | bytes 1591296 | tf_op jit(solution)/shard_map/neg | solution.py:43
  31.9 2.8 %fusion.334 = (bf16[512,512]{1,0:T(8,128)(2,1)}, bf16[512,512]{1,0:T(8,128)(2,1)}, bf16[512,512]{1,0:T(8,128)(2,1)}) fusion(bf16[512]{0:T(512)(128)(2,1)S(1)} %get-tuple-element.86, bf16[512]{0:T(512)(128)(2,1)S(1)} %get-tuple-element.87, bf16[512]{0:T(512)(128)(2,1)S(1)} %get-tuple-element.88, bf16[512]{0:T(512)(128)(2,1)S(1)} %get-tuple-element.89, ...), kind=kLoop, calls=%fused_computation.517 | loop fusion | flops 7340032 | bytes 1591296 | tf_op jit(solution)/shard_map/neg | solution.py:43
  34.6 2.8 %fusion.337 = (bf16[512,512]{1,0:T(8,128)(2,1)}, bf16[512,512]{1,0:T(8,128)(2,1)}, bf16[512,512]{1,0:T(8,128)(2,1)}) fusion(bf16[512]{0:T(512)(128)(2,1)S(1)} %get-tuple-element.70, bf16[512]{0:T(512)(128)(2,1)S(1)} %get-tuple-element.71, bf16[512]{0:T(512)(128)(2,1)S(1)} %get-tuple-element.72, bf16[512]{0:T(512)(128)(2,1)S(1)} %get-tuple-element.73, ...), kind=kLoop, calls=%fused_computation.520 | loop fusion | flops 7340032 | bytes 1591296 | tf_op jit(solution)/shard_map/neg | solution.py:43
  37.4 2.5 %fusion.338 = (bf16[512,512]{1,0:T(8,128)(2,1)S(1)}, bf16[512,512]{1,0:T(8,128)(2,1)S(1)}, bf16[512,512]{1,0:T(8,128)(2,1)}) fusion(bf16[512]{0:T(512)(128)(2,1)S(1)} %get-tuple-element.38, bf16[512]{0:T(512)(128)(2,1)S(1)} %get-tuple-element.39, bf16[512]{0:T(512)(128)(2,1)S(1)} %get-tuple-element.40, bf16[512]{0:T(512)(128)(2,1)S(1)} %get-tuple-element.41, ...), kind=kLoop, calls=%fused_computation.521 | loop fusion | flops 7340032 | bytes 1591296 | tf_op jit(solution)/shard_map/neg | solution.py:43
  40.0 1.4 constant_dynamic-update-slice_fusion
  41.6 1.0 copy-done
  43.2 2.4 %fusion.83 = bf16[512,1024]{1,0:T(8,128)(2,1)S(1)} fusion(bf16[1024,512]{0,1:T(8,128)(2,1)S(1)} %bitcast.119, bf16[1024,512]{0,1:T(8,128)(2,1)S(1)} %bitcast.118, bf16[1024,512]{0,1:T(8,128)(2,1)S(1)} %copy-done.2, bf16[512,1024]{1,0:T(8,128)(2,1)S(1)} %get-tuple-element.154, bf16[512,1024]{1,0:T(8,128)(2,1)S(1)} %get-tuple-element.153), kind=kOutput, calls=%fused_computation.88 | convolution fusion | flops 2168979456 | bytes 6291456 | tf_op jit(solution)/shard_map/dot_general | solution.py:64
  45.7 1.2 collective-permute-start.1
  46.9 2.6 %fusion.339 = (bf16[512,512]{1,0:T(8,128)(2,1)S(1)}, bf16[512,512]{1,0:T(8,128)(2,1)}, bf16[512,512]{1,0:T(8,128)(2,1)}) fusion(bf16[512]{0:T(512)(128)(2,1)S(1)} %get-tuple-element.22, bf16[512]{0:T(512)(128)(2,1)S(1)} %get-tuple-element.23, bf16[512]{0:T(512)(128)(2,1)S(1)} %get-tuple-element.24, bf16[512]{0:T(512)(128)(2,1)S(1)} %get-tuple-element.25, ...), kind=kLoop, calls=%fused_computation.522 | loop fusion | flops 7340032 | bytes 1591296 | tf_op jit(solution)/shard_map/neg | solution.py:43
  49.6 2.7 %fusion.16 = f32[1024,512]{1,0:T(8,128)S(1)} fusion(bf16[1024,512]{1,0:T(8,128)(2,1)S(1)} %bitcast.121, bf16[512,512]{1,0:T(8,128)(2,1)} %get-tuple-element.218, bf16[512,512]{1,0:T(8,128)(2,1)} %get-tuple-element.196, bf16[512,512]{1,0:T(8,128)(2,1)S(1)} %copy-done.13), kind=kOutput, calls=%fused_computation.16 | convolution fusion | flops 1082130432 | bytes 4718592 | tf_op jit(solution)/shard_map/dot_general | solution.py:88
  52.4 3.6 %add_convert_fusion.1 = bf16[1024,512]{1,0:T(8,128)(2,1)} fusion(f32[1024,512]{1,0:T(8,128)S(1)} %fusion.16, bf16[1024,512]{1,0:T(8,128)(2,1)} %collective-permute-done.1, bf16[512,512]{1,0:T(8,128)(2,1)S(1)} %copy-done.16, bf16[512,512]{1,0:T(8,128)(2,1)S(1)} %copy-done.15, bf16[512,512]{1,0:T(8,128)(2,1)S(1)} %copy-done.14), kind=kOutput, calls=%fused_computation.80 | convolution fusion | flops 1083179008 | bytes 5767168 | tf_op jit(solution)/shard_map/dot_general | solution.py:92
  55.9 1.2 collective-permute-start.2
  57.3 2.8 %fusion.341 = (bf16[512,512]{1,0:T(8,128)(2,1)}, bf16[512,512]{1,0:T(8,128)(2,1)}, bf16[512,512]{1,0:T(8,128)(2,1)}) fusion(bf16[512]{0:T(512)(128)(2,1)S(1)} %get-tuple-element.134, bf16[512]{0:T(512)(128)(2,1)S(1)} %get-tuple-element.135, bf16[512]{0:T(512)(128)(2,1)S(1)} %get-tuple-element.136, bf16[512]{0:T(512)(128)(2,1)S(1)} %get-tuple-element.137, ...), kind=kLoop, calls=%fused_computation.524 | loop fusion | flops 7340032 | bytes 1591296 | tf_op jit(solution)/shard_map/neg | solution.py:43
  60.2 4.0 %fusion.8 = f32[1024,512]{1,0:T(8,128)} fusion(bf16[1024,512]{1,0:T(8,128)(2,1)} %add_convert_fusion.1, bf16[512,512]{1,0:T(8,128)(2,1)S(1)} %copy-done.7, bf16[512,512]{1,0:T(8,128)(2,1)S(1)} %copy-done.6, bf16[512,512]{1,0:T(8,128)(2,1)S(1)} %copy-done.5), kind=kOutput, calls=%fused_computation.8 | convolution fusion | flops 1082130432 | bytes 4718592 | tf_op jit(solution)/shard_map/dot_general | solution.py:88
  64.1 11.8 %all-to-all-start = ((s32[128,1,8]{2,1,0:T(1,128)}), s32[128,1,8]{2,1,0:T(1,128)S(1)}, u32[]{:S(2)}, u32[]{:S(2)}) async-start(s32[128,1,8]{2,1,0:T(1,128)} %bitcast.25), calls=%async_computation | async-start | bytes 131072 | tf_op jit(solution)/shard_map/all_to_all | solution.py:91
  76.0 5.1 %collective-permute-done.2 = bf16[1024,512]{1,0:T(8,128)(2,1)} collective-permute-done((bf16[1024,512]{1,0:T(8,128)(2,1)}, bf16[1024,512]{1,0:T(8,128)(2,1)}, u32[]{:S(2)}, u32[]{:S(2)}) %collective-permute-start.2) | collective-permute-done | bytes 1048608 | tf_op jit(solution)/shard_map/ppermute | solution.py:16
  81.2 4.1 %add_convert_fusion = bf16[1024,512]{1,0:T(8,128)(2,1)} fusion(f32[1024,512]{1,0:T(8,128)} %fusion.8, bf16[1024,512]{1,0:T(8,128)(2,1)} %collective-permute-done.2, bf16[512,512]{1,0:T(8,128)(2,1)S(1)} %copy-done.10, bf16[512,512]{1,0:T(8,128)(2,1)S(1)} %copy-done.9, bf16[512,512]{1,0:T(8,128)(2,1)S(1)} %copy-done.8), kind=kOutput, calls=%fused_computation.79 | convolution fusion | flops 1083179008 | bytes 5767168 | tf_op jit(solution)/shard_map/dot_general | solution.py:92
  85.6 1.2 constant_dynamic-slice_fusion
  86.8 3.0 %collective-permute-start.3 = (bf16[1024,256]{1,0:T(8,128)(2,1)S(1)}, bf16[1024,256]{1,0:T(8,128)(2,1)S(1)}, u32[]{:S(2)}, u32[]{:S(2)}) collective-permute-start(bf16[1024,256]{1,0:T(8,128)(2,1)S(1)} %constant_dynamic-slice_fusion), channel_id=1, source_target_pairs={{0,64},{16,80},{32,96},{48,112},{64,0},{80,16},{96,32},{112,48},{1... | collective-permute-start | bytes 1572872 | tf_op jit(solution)/shard_map/ppermute | solution.py:16
  89.8 2.8 %fusion.340 = (bf16[512,512]{1,0:T(8,128)(2,1)}, bf16[512,512]{1,0:T(8,128)(2,1)}, bf16[512,512]{1,0:T(8,128)(2,1)}) fusion(bf16[512]{0:T(512)(128)(2,1)S(1)} %get-tuple-element.54, bf16[512]{0:T(512)(128)(2,1)S(1)} %get-tuple-element.55, bf16[512]{0:T(512)(128)(2,1)S(1)} %get-tuple-element.56, bf16[512]{0:T(512)(128)(2,1)S(1)} %get-tuple-element.57, ...), kind=kLoop, calls=%fused_computation.523 | loop fusion | flops 7340032 | bytes 1591296 | tf_op jit(solution)/shard_map/neg | solution.py:43
  92.6 0.7 fusion.43
  93.9 1.7 %fusion.67 = f32[1024,256]{1,0:T(8,128)} fusion(bf16[512,512]{1,0:T(8,128)(2,1)S(1)} %copy-done.19, bf16[512,512]{1,0:T(8,128)(2,1)S(1)} %copy-done.18, bf16[512,512]{1,0:T(8,128)(2,1)S(1)} %copy-done.17, bf16[1024,512]{1,0:T(8,128)(2,1)S(1)} %copy-done.23, s32[]{:T(128)S(6)} %select_n.476), kind=kOutput, calls=%fused_computation.67 | convolution fusion | flops 545259520 | bytes 3145732 | tf_op jit(solution)/shard_map/dot_general | solution.py:113
  95.6 5.3 %collective-permute-done.3 = bf16[1024,256]{1,0:T(8,128)(2,1)S(1)} collective-permute-done((bf16[1024,256]{1,0:T(8,128)(2,1)S(1)}, bf16[1024,256]{1,0:T(8,128)(2,1)S(1)}, u32[]{:S(2)}, u32[]{:S(2)}) %collective-permute-start.3) | collective-permute-done | bytes 524320 | tf_op jit(solution)/shard_map/ppermute | solution.py:16
  100.9 0.7 fusion.100
  101.9 0.7 fusion.90
  103.6 0.7 fusion.103
  104.5 0.8 fusion.91
  105.3 1.7 %pad_maximum_fusion = bf16[128,16,512]{2,1,0:T(8,128)(2,1)} fusion(bf16[128,8,512]{2,1,0:T(8,128)(2,1)S(1)} %fusion.91, bf16[128,8,512]{2,1,0:T(8,128)(2,1)S(1)} %fusion.90), kind=kLoop, calls=%fused_computation.75 | loop fusion | flops 4194304 | bytes 4194304 | tf_op jit(solution)/shard_map/concatenate | solution.py:123
  107.0 13.5 %all-to-all-start.1 = ((bf16[128,16,512]{2,1,0:T(8,128)(2,1)}), bf16[128,16,512]{2,1,0:T(8,128)(2,1)S(1)}, u32[]{:S(2)}, u32[]{:S(2)}) async-start(bf16[128,16,512]{2,1,0:T(8,128)(2,1)} %pad_maximum_fusion), calls=%async_computation.1 | async-start | bytes 4194304 | tf_op jit(solution)/shard_map/all_to_all | solution.py:124
  122.0 28.1 %all-to-all-done.1 = bf16[128,16,512]{2,1,0:T(8,128)(2,1)S(1)} async-done(((bf16[128,16,512]{2,1,0:T(8,128)(2,1)}), bf16[128,16,512]{2,1,0:T(8,128)(2,1)S(1)}, u32[]{:S(2)}, u32[]{:S(2)}) %all-to-all-start.1) | async-done | bytes 2097184 | tf_op jit(solution)/shard_map/all_to_all | solution.py:124
  150.3 0.8 fusion.99
  151.3 0.8 fusion.98
  152.3 1.1 maximum_bitcast_fusion
  (122 shorter events, 10.1 us)
Async XLA Ops:
  0.0 13.4 %copy-start.1 = (bf16[2,512,512]{2,1,0:T(8,128)(2,1)S(1)}, bf16[2,512,512]{2,1,0:T(8,128)(2,1)}, u32[]{:S(2)}) copy-start(bf16[2,512,512]{2,1,0:T(8,128)(2,1)} %param.6) | copy-start | bytes 3145732
  0.0 40.0 %collective-permute-start = (bf16[2,512,512]{2,1,0:T(8,128)(2,1)}, bf16[2,512,512]{2,1,0:T(8,128)(2,1)}, u32[]{:S(2)}, u32[]{:S(2)}) collective-permute-start(bf16[2,512,512]{2,1,0:T(8,128)(2,1)} %param.6), channel_id=1, source_target_pairs={{1,0},{2,1},{3,2},{4,3},{5,4},{6,5},{7,6},{8,7},{9,8},{10,9},{11,1... | collective-permute-start | bytes 3145736 | tf_op jit(solution)/shard_map/ppermute | solution.py:12
  2.2 11.4 %copy-start.24 = (bf16[2,512]{1,0:T(2,128)(2,1)S(1)}, bf16[2,512]{1,0:T(2,128)(2,1)}, u32[]{:S(2)}) copy-start(bf16[2,512]{1,0:T(2,128)(2,1)} %param.7) | copy-start | bytes 6148
  7.3 42.2 %collective-permute-start.5 = (bf16[2,2,512,8]{2,3,1,0:T(8,128)(2,1)S(1)}, bf16[2,2,512,8]{2,3,1,0:T(8,128)(2,1)S(1)}, u32[]{:S(2)}, u32[]{:S(2)}) collective-permute-start(bf16[2,2,512,8]{2,3,1,0:T(8,128)(2,1)S(1)} %slice_bitcast_fusion.2), channel_id=1, source_target_pairs={{0,64},{16,80},{32,96},{48,112},{64,0},{80,16},{96,32},{112,48},{1... | collective-permute-start | bytes 98312 | tf_op jit(solution)/shard_map/ppermute | solution.py:16
  11.7 37.8 %collective-permute-start.4 = (s32[1536]{0:T(1024)S(1)}, s32[1536]{0:T(1024)S(1)}, u32[]{:S(2)}, u32[]{:S(2)}) collective-permute-start(s32[1536]{0:T(1024)S(1)} %pad_add_fusion.2), channel_id=1, source_target_pairs={{0,64},{16,80},{32,96},{48,112},{64,0},{80,16},{96,32},{112,48},{1... | collective-permute-start | bytes 18440 | tf_op jit(solution)/shard_map/ppermute | solution.py:16
  16.0 1.2 slice-start
  23.2 1.2 slice-start.1
  41.3 1.2 copy-start
  41.4 1.5 %copy-start.2 = (bf16[1024,512]{0,1:T(8,128)(2,1)S(1)}, bf16[1024,512]{0,1:T(8,128)(2,1)}, u32[]{:S(2)}) copy-start(bf16[1024,512]{0,1:T(8,128)(2,1)} %bitcast_negate_fusion) | copy-start | bytes 3145732
  41.4 1.8 %copy-start.3 = (bf16[512,1024]{1,0:T(8,128)(2,1)S(1)}, bf16[512,1024]{1,0:T(8,128)(2,1)}, u32[]{:S(2)}) copy-start(bf16[512,1024]{1,0:T(8,128)(2,1)} %reshape.160) | copy-start | bytes 3145732
  45.6 4.0 %copy-start.13 = (bf16[512,512]{1,0:T(8,128)(2,1)S(1)}, bf16[512,512]{1,0:T(8,128)(2,1)}, u32[]{:S(2)}) copy-start(bf16[512,512]{1,0:T(8,128)(2,1)} %get-tuple-element.195) | copy-start | bytes 1572868
  45.7 6.6 %collective-permute-start.1 = (bf16[1024,512]{1,0:T(8,128)(2,1)S(1)}, bf16[1024,512]{1,0:T(8,128)(2,1)}, u32[]{:S(2)}, u32[]{:S(2)}) collective-permute-start(bf16[1024,512]{1,0:T(8,128)(2,1)S(1)} %bitcast.120), channel_id=1, source_target_pairs={{0,16},{16,0},{32,48},{48,32},{64,80},{80,64},{96,112},{112,96},{1... | collective-permute-start | bytes 3145736 | tf_op jit(solution)/shard_map/ppermute | solution.py:16
  49.6 2.8 %copy-start.14 = (bf16[512,512]{1,0:T(8,128)(2,1)S(1)}, bf16[512,512]{1,0:T(8,128)(2,1)}, u32[]{:S(2)}) copy-start(bf16[512,512]{1,0:T(8,128)(2,1)} %get-tuple-element.193) | copy-start | bytes 1572868
  49.6 2.8 %copy-start.15 = (bf16[512,512]{1,0:T(8,128)(2,1)S(1)}, bf16[512,512]{1,0:T(8,128)(2,1)}, u32[]{:S(2)}) copy-start(bf16[512,512]{1,0:T(8,128)(2,1)} %get-tuple-element.194) | copy-start | bytes 1572868
  49.6 2.8 %copy-start.16 = (bf16[512,512]{1,0:T(8,128)(2,1)S(1)}, bf16[512,512]{1,0:T(8,128)(2,1)}, u32[]{:S(2)}) copy-start(bf16[512,512]{1,0:T(8,128)(2,1)} %get-tuple-element.217) | copy-start | bytes 1572868
  52.4 7.8 %copy-start.5 = (bf16[512,512]{1,0:T(8,128)(2,1)S(1)}, bf16[512,512]{1,0:T(8,128)(2,1)}, u32[]{:S(2)}) copy-start(bf16[512,512]{1,0:T(8,128)(2,1)} %get-tuple-element.191) | copy-start | bytes 1572868
  52.4 7.8 %copy-start.6 = (bf16[512,512]{1,0:T(8,128)(2,1)S(1)}, bf16[512,512]{1,0:T(8,128)(2,1)}, u32[]{:S(2)}) copy-start(bf16[512,512]{1,0:T(8,128)(2,1)} %get-tuple-element.192) | copy-start | bytes 1572868
  52.4 7.8 %copy-start.7 = (bf16[512,512]{1,0:T(8,128)(2,1)S(1)}, bf16[512,512]{1,0:T(8,128)(2,1)}, u32[]{:S(2)}) copy-start(bf16[512,512]{1,0:T(8,128)(2,1)} %get-tuple-element.216) | copy-start | bytes 1572868
  55.9 25.2 %collective-permute-start.2 = (bf16[1024,512]{1,0:T(8,128)(2,1)}, bf16[1024,512]{1,0:T(8,128)(2,1)}, u32[]{:S(2)}, u32[]{:S(2)}) collective-permute-start(bf16[1024,512]{1,0:T(8,128)(2,1)} %add_convert_fusion.1), channel_id=1, source_target_pairs={{0,32},{16,48},{32,0},{48,16},{64,96},{80,112},{96,64},{112,80},{1... | collective-permute-start | bytes 3145736 | tf_op jit(solution)/shard_map/ppermute | solution.py:16
  60.1 21.0 %copy-start.8 = (bf16[512,512]{1,0:T(8,128)(2,1)S(1)}, bf16[512,512]{1,0:T(8,128)(2,1)}, u32[]{:S(2)}) copy-start(bf16[512,512]{1,0:T(8,128)(2,1)} %get-tuple-element.189) | copy-start | bytes 1572868
  60.1 21.0 %copy-start.9 = (bf16[512,512]{1,0:T(8,128)(2,1)S(1)}, bf16[512,512]{1,0:T(8,128)(2,1)}, u32[]{:S(2)}) copy-start(bf16[512,512]{1,0:T(8,128)(2,1)} %get-tuple-element.190) | copy-start | bytes 1572868
  60.2 21.0 %copy-start.10 = (bf16[512,512]{1,0:T(8,128)(2,1)S(1)}, bf16[512,512]{1,0:T(8,128)(2,1)}, u32[]{:S(2)}) copy-start(bf16[512,512]{1,0:T(8,128)(2,1)} %get-tuple-element.215) | copy-start | bytes 1572868
  64.1 21.5 %all-to-all-start = ((s32[128,1,8]{2,1,0:T(1,128)}), s32[128,1,8]{2,1,0:T(1,128)S(1)}, u32[]{:S(2)}, u32[]{:S(2)}) async-start(s32[128,1,8]{2,1,0:T(1,128)} %bitcast.25), calls=%async_computation | async-start | bytes 131072 | tf_op jit(solution)/shard_map/all_to_all | solution.py:91
  85.3 7.3 %copy-start.4 = (bf16[512,512]{1,0:T(8,128)(2,1)S(1)}, bf16[512,512]{1,0:T(8,128)(2,1)}, u32[]{:S(2)}) copy-start(bf16[512,512]{1,0:T(8,128)(2,1)} %get-tuple-element.213) | copy-start | bytes 1572868
  85.6 6.9 %copy-start.23 = (bf16[1024,512]{1,0:T(8,128)(2,1)S(1)}, bf16[1024,512]{1,0:T(8,128)(2,1)}, u32[]{:S(2)}) copy-start(bf16[1024,512]{1,0:T(8,128)(2,1)} %add_convert_fusion) | copy-start | bytes 3145732
  86.8 14.1 %collective-permute-start.3 = (bf16[1024,256]{1,0:T(8,128)(2,1)S(1)}, bf16[1024,256]{1,0:T(8,128)(2,1)S(1)}, u32[]{:S(2)}, u32[]{:S(2)}) collective-permute-start(bf16[1024,256]{1,0:T(8,128)(2,1)S(1)} %constant_dynamic-slice_fusion), channel_id=1, source_target_pairs={{0,64},{16,80},{32,96},{48,112},{64,0},{80,16},{96,32},{112,48},{1... | collective-permute-start | bytes 1572872 | tf_op jit(solution)/shard_map/ppermute | solution.py:16
  92.5 1.0 copy-start.17
  92.6 1.2 copy-start.18
  92.6 1.3 copy-start.19
  93.9 7.0 %copy-start.11 = (bf16[512,512]{1,0:T(8,128)(2,1)S(1)}, bf16[512,512]{1,0:T(8,128)(2,1)}, u32[]{:S(2)}) copy-start(bf16[512,512]{1,0:T(8,128)(2,1)} %get-tuple-element.184) | copy-start | bytes 1572868
  93.9 7.0 %copy-start.12 = (bf16[512,512]{1,0:T(8,128)(2,1)S(1)}, bf16[512,512]{1,0:T(8,128)(2,1)}, u32[]{:S(2)}) copy-start(bf16[512,512]{1,0:T(8,128)(2,1)} %get-tuple-element.212) | copy-start | bytes 1572868
  100.9 0.8 copy-start.25
  101.7 1.0 copy-start.20
  101.7 1.2 copy-start.21
  101.7 1.4 copy-start.22
  101.9 1.3 copy-start.26
  101.9 1.7 %copy-start.27 = (f32[1024,256]{1,0:T(8,128)S(1)}, f32[1024,256]{1,0:T(8,128)}, u32[]{:S(2)}) copy-start(f32[1024,256]{1,0:T(8,128)} %fusion.67) | copy-start | bytes 3145732
  107.0 43.2 %all-to-all-start.1 = ((bf16[128,16,512]{2,1,0:T(8,128)(2,1)}), bf16[128,16,512]{2,1,0:T(8,128)(2,1)S(1)}, u32[]{:S(2)}, u32[]{:S(2)}) async-start(bf16[128,16,512]{2,1,0:T(8,128)(2,1)} %pad_maximum_fusion), calls=%async_computation.1 | async-start | bytes 4194304 | tf_op jit(solution)/shard_map/all_to_all | solution.py:124

commit v13 on v12

--- a/solution.py
+++ b/solution.py
@@ -83,8 +83,13 @@
     far_slot = far_ints[2 * p_dev :]
     for section in range(last):
         partner = from_partner(image, "sub", section)
-        mine = merge_matrix(offsets[section, 0, 0], weights[section, 0, 0])
-        theirs = merge_matrix(offsets[section, 0, 1], weights[section, 0, 1])
+        band_in = (offsets[section, 0], weights[section, 0])
+        if section == 1:
+            (band_in, own_offsets, own_weights), image = lax.optimization_barrier(
+                ((band_in, own_offsets, own_weights), image)
+            )
+        mine = merge_matrix(band_in[0][0], band_in[1][0])
+        theirs = merge_matrix(band_in[0][1], band_in[1][1])
         merged = jnp.dot(mine, image, preferred_element_type=jnp.float32)
         if section == 1:
             labels, merged = lax.optimization_barrier((labels, merged))
@@ -92,7 +97,9 @@
         merged = merged + jnp.dot(theirs, partner, preferred_element_type=jnp.float32)
         image = merged.astype(jnp.bfloat16)
         if section == 1:
-            marks, image = lax.optimization_barrier((marks, image))
+            (marks, far_offsets, far_weights), image = lax.optimization_barrier(
+                ((marks, far_offsets, far_weights), image)
+            )
     slots = jnp.arange(devices * capacity, dtype=jnp.int32)[:, None]
     picks = {0: slots == slot[None, :], bit: slots == far_slot[None, :]}
     half = r_dev // 2

time: 154 us -> 145 us (0.942)
  other arithmetic: 30 us -> 20.7 us
  waiting for transfers between devices: 38.9 us -> 43.8 us
  local copies, waits for them, and re-layouts: 23.7 us -> 19.2 us
    ppermute x1, waiting for transfers between devices: 0.01 us -> 7.5 us  [shifted(): lax.ppermute(value, axis, [(source, source + steps) for source in range(f...]
    neg x8, other arithmetic: 21.8 us -> 14.8 us  [merge_matrix(): upper = jnp.concatenate([g_real, -g_imag], axis=1)]
    slice x4 -> x2, local copies, waits for them, and re-layouts: 2.45 us -> 0.14 us  [replica_matrix(): jnp.tile(padded, block_len)[:block_len * width].reshape(block_len, width)]
    ppermute x5, waiting for transfers between devices: 10.5 us -> 8.15 us  [from_partner(): lax.ppermute(value, axis, [(i, i ^ 1 << apart) for i in range(lax.axis_si...]
    neg x1, other arithmetic: 2.32 us -> 0.07 us  [replica_matrix(): upper = jnp.concatenate([h_real, -h_imag], axis=1)]
    unnamed x58 -> x22, local copies, waits for them, and re-layouts: 3.49 us -> 1.28 us
    another operation x4, local copies, waits for them, and re-layouts: 4.73 us -> 2.84 us  [replica_matrix(): jnp.tile(padded, block_len)[:block_len * width].reshape(block_len, width)]
    reshape x2, local copies, waits for them, and re-layouts: 0.42 us -> 2.27 us  [on_device(): piece.reshape(2, p_dev, half).transpose(1, 0, 2).reshape(p_dev, 2 * half)]
  transfers between devices with their start and end apart: 8 -> 8, of which waited for: 4 -> 4; matrix products, arithmetic and copies ran while one was open for 38% -> 33% of each run, Pallas kernels for 0% -> 0%
where the time goes in v13:
time: 145 us; the launch traced here: 144 us
  waiting for transfers between devices  43.8 us (30%)
  starting transfers between devices  37.3 us (26%)
  matrix products  22.2 us (15%)
  other arithmetic  20.7 us (14%)
  local copies, waits for them, and re-layouts  19.2 us (13%)
    all_to_all x1, waiting for transfers between devices, on_device(): lax.all_to_all(payload, ('sub', 'rng'), split_axis=0, concat_axis=0, tile...  28.1 us
    neg x8, other arithmetic, merge_matrix(): upper = jnp.concatenate([g_real, -g_imag], axis=1)  14.8 us
    all_to_all x1, starting transfers between devices, on_device(): lax.all_to_all(payload, ('sub', 'rng'), split_axis=0, concat_axis=0, tile...  12.9 us
    all_to_all x1, starting transfers between devices, on_device(): lax.all_to_all(labels, ('sub', 'rng'), split_axis=0, concat_axis=0, tiled...  11.7 us
    ppermute x5, starting transfers between devices, from_partner(): lax.ppermute(value, axis, [(i, i ^ 1 << apart) for i in range(lax.axis_si...  11.4 us
    ppermute x5, waiting for transfers between devices, from_partner(): lax.ppermute(value, axis, [(i, i ^ 1 << apart) for i in range(lax.axis_si...  8.15 us
    ppermute x1, waiting for transfers between devices, shifted(): lax.ppermute(value, axis, [(source, source + steps) for source in range(f...  7.5 us
    dot_general x2, matrix products, on_device(): jnp.dot(theirs, partner, preferred_element_type=jnp.float32)  6.88 us
  transfers between devices with their start and end apart: 8, of which 4 were waited for; matrix products, arithmetic and copies ran while one was open for 33% of the time, Pallas kernels for 0%

profile of v13, /device:TPU:1, one launch (start us, length us, event | category | flops | bytes accessed | tf_op | source)
XLA Modules:
  0.0 143.7 jit_solution(2703347457472388770)
XLA Ops:
  0.0 1.3 collective-permute-start
  1.3 0.7 slice_bitcast_fusion.20
  2.0 0.8 slice_bitcast_fusion.2
  2.8 0.8 copy.39
  3.9 0.9 fusion.304
  7.2 4.4 %collective-permute-start.2 = (s32[1536]{0:T(1024)S(1)}, s32[1536]{0:T(1024)S(1)}, u32[]{:S(2)}, u32[]{:S(2)}) collective-permute-start(s32[1536]{0:T(1024)S(1)} %pad_add_fusion.1), channel_id=1, source_target_pairs={{0,64},{16,80},{32,96},{48,112},{64,0},{80,16},{96,32},{112,48},{1... | collective-permute-start | bytes 18440 | tf_op jit(solution)/shard_map/ppermute | solution.py:16
  11.7 0.8 slice_reduce_fusion.128
  12.6 1.3 tile.9
  14.0 1.3 reshape.172
  15.4 1.3 tile.21
  17.3 0.8 slice_bitcast_fusion.16
  18.3 0.8 fusion.344
  19.2 7.5 %collective-permute-done = bf16[2,512,512]{2,1,0:T(8,128)(2,1)} collective-permute-done((bf16[2,512,512]{2,1,0:T(8,128)(2,1)}, bf16[2,512,512]{2,1,0:T(8,128)(2,1)}, u32[]{:S(2)}, u32[]{:S(2)}) %collective-permute-start) | collective-permute-done | bytes 1048608 | tf_op jit(solution)/shard_map/ppermute | solution.py:12
  26.7 1.4 constant_dynamic-update-slice_fusion
  28.3 1.0 copy-done.1
  29.3 2.4 %fusion.83 = bf16[512,1024]{1,0:T(8,128)(2,1)S(1)} fusion(bf16[1024,512]{0,1:T(8,128)(2,1)S(1)} %bitcast.127, bf16[1024,512]{0,1:T(8,128)(2,1)S(1)} %bitcast.124, bf16[1024,512]{0,1:T(8,128)(2,1)S(1)} %bitcast_negate_fusion, bf16[512,1024]{1,0:T(8,128)(2,1)S(1)} %get-tuple-element.168, bf16[512,1024]{1,0:T(8,128)(2,1)S(1)} %get-tuple-element.167), kind=kOutput, calls=%fused_computation.88 | convolution fusion | flops 2168979456 | bytes 6291456 | tf_op jit(solution)/shard_map/dot_general | solution.py:64
  31.8 1.7 %collective-permute-start.1 = (bf16[1024,512]{1,0:T(8,128)(2,1)S(1)}, bf16[1024,512]{1,0:T(8,128)(2,1)}, u32[]{:S(2)}, u32[]{:S(2)}) collective-permute-start(bf16[1024,512]{1,0:T(8,128)(2,1)S(1)} %bitcast.125), channel_id=1, source_target_pairs={{0,16},{16,0},{32,48},{48,32},{64,80},{80,64},{96,112},{112,96},{1... | collective-permute-start | bytes 3145736 | tf_op jit(solution)/shard_map/ppermute | solution.py:16
  33.5 1.7 %fusion.335 = (bf16[512,512]{1,0:T(8,128)(2,1)S(1)}, bf16[512,512]{1,0:T(8,128)(2,1)S(1)}, bf16[512,512]{1,0:T(8,128)(2,1)S(1)}) fusion(bf16[512]{0:T(512)(128)(2,1)S(1)} %get-tuple-element.148, bf16[512]{0:T(512)(128)(2,1)S(1)} %get-tuple-element.149, bf16[512]{0:T(512)(128)(2,1)S(1)} %get-tuple-element.150, bf16[512]{0:T(512)(128)(2,1)S(1)} %get-tuple-element.151, ...), kind=kLoop, calls=%fused_computation.520 | loop fusion | flops 7340032 | bytes 1591296 | tf_op jit(solution)/shard_map/neg | solution.py:43
  35.3 2.7 %fusion.336 = (bf16[512,512]{1,0:T(8,128)(2,1)S(1)}, bf16[512,512]{1,0:T(8,128)(2,1)}, bf16[512,512]{1,0:T(8,128)(2,1)}) fusion(bf16[512]{0:T(512)(128)(2,1)S(1)} %get-tuple-element.132, bf16[512]{0:T(512)(128)(2,1)S(1)} %get-tuple-element.133, bf16[512]{0:T(512)(128)(2,1)S(1)} %get-tuple-element.134, bf16[512]{0:T(512)(128)(2,1)S(1)} %get-tuple-element.135, ...), kind=kLoop, calls=%fused_computation.521 | loop fusion | flops 7340032 | bytes 1591296 | tf_op jit(solution)/shard_map/neg | solution.py:43
  38.0 1.2 fusion.8
  39.3 3.4 %add_convert_fusion.1 = bf16[1024,512]{1,0:T(8,128)(2,1)} fusion(f32[1024,512]{1,0:T(8,128)S(1)} %fusion.8, bf16[1024,512]{1,0:T(8,128)(2,1)} %collective-permute-done.1, bf16[512,512]{1,0:T(8,128)(2,1)S(1)} %copy-done.3, bf16[512,512]{1,0:T(8,128)(2,1)S(1)} %copy-done.2, bf16[512,512]{1,0:T(8,128)(2,1)S(1)} %get-tuple-element.211), kind=kOutput, calls=%fused_computation.80 | convolution fusion | flops 1083179008 | bytes 5767168 | tf_op jit(solution)/shard_map/dot_general | solution.py:97
  42.8 1.9 %collective-permute-start.4 = (bf16[1024,512]{1,0:T(8,128)(2,1)}, bf16[1024,512]{1,0:T(8,128)(2,1)}, u32[]{:S(2)}, u32[]{:S(2)}) collective-permute-start(bf16[1024,512]{1,0:T(8,128)(2,1)} %add_convert_fusion.1), channel_id=1, source_target_pairs={{0,32},{16,48},{32,0},{48,16},{64,96},{80,112},{96,64},{112,80},{1... | collective-permute-start | bytes 3145736 | tf_op jit(solution)/shard_map/ppermute | solution.py:16
  44.8 1.7 %fusion.334 = (bf16[512,512]{1,0:T(8,128)(2,1)S(1)}, bf16[512,512]{1,0:T(8,128)(2,1)S(1)}, bf16[512,512]{1,0:T(8,128)(2,1)S(1)}) fusion(bf16[512]{0:T(512)(128)(2,1)S(1)} %get-tuple-element.116, bf16[512]{0:T(512)(128)(2,1)S(1)} %get-tuple-element.117, bf16[512]{0:T(512)(128)(2,1)S(1)} %get-tuple-element.118, bf16[512]{0:T(512)(128)(2,1)S(1)} %get-tuple-element.119, ...), kind=kLoop, calls=%fused_computation.519 | loop fusion | flops 7340032 | bytes 1591296 | tf_op jit(solution)/shard_map/neg | solution.py:43
  46.5 3.8 %fusion.27 = f32[1024,512]{1,0:T(8,128)} fusion(bf16[1024,512]{1,0:T(8,128)(2,1)} %add_convert_fusion.1, bf16[512,512]{1,0:T(8,128)(2,1)S(1)} %get-tuple-element.234, bf16[512,512]{1,0:T(8,128)(2,1)S(1)} %get-tuple-element.210, bf16[512,512]{1,0:T(8,128)(2,1)S(1)} %get-tuple-element.209), kind=kOutput, calls=%fused_computation.27 | convolution fusion | flops 1082130432 | bytes 4718592 | tf_op jit(solution)/shard_map/dot_general | solution.py:93
  50.4 11.7 %all-to-all-start = ((s32[128,1,8]{2,1,0:T(1,128)}), s32[128,1,8]{2,1,0:T(1,128)S(1)}, u32[]{:S(2)}, u32[]{:S(2)}) async-start(s32[128,1,8]{2,1,0:T(1,128)} %bitcast.27), calls=%async_computation | async-start | bytes 131072 | tf_op jit(solution)/shard_map/all_to_all | solution.py:96
  62.5 1.7 %fusion.337 = (bf16[512,512]{1,0:T(8,128)(2,1)S(1)}, bf16[512,512]{1,0:T(8,128)(2,1)S(1)}, bf16[512,512]{1,0:T(8,128)(2,1)S(1)}) fusion(bf16[512]{0:T(512)(128)(2,1)S(1)} %get-tuple-element.100, bf16[512]{0:T(512)(128)(2,1)S(1)} %get-tuple-element.101, bf16[512]{0:T(512)(128)(2,1)S(1)} %get-tuple-element.102, bf16[512]{0:T(512)(128)(2,1)S(1)} %get-tuple-element.103, ...), kind=kLoop, calls=%fused_computation.522 | loop fusion | flops 7340032 | bytes 1591296 | tf_op jit(solution)/shard_map/neg | solution.py:43
  64.2 1.7 %fusion.339 = (bf16[512,512]{1,0:T(8,128)(2,1)S(1)}, bf16[512,512]{1,0:T(8,128)(2,1)S(1)}, bf16[512,512]{1,0:T(8,128)(2,1)S(1)}) fusion(bf16[512]{0:T(512)(128)(2,1)S(1)} %get-tuple-element.52, bf16[512]{0:T(512)(128)(2,1)S(1)} %get-tuple-element.53, bf16[512]{0:T(512)(128)(2,1)S(1)} %get-tuple-element.54, bf16[512]{0:T(512)(128)(2,1)S(1)} %get-tuple-element.55, ...), kind=kLoop, calls=%fused_computation.524 | loop fusion | flops 7340032 | bytes 1591296 | tf_op jit(solution)/shard_map/neg | solution.py:43
  66.0 1.7 %fusion.338 = (bf16[512,512]{1,0:T(8,128)(2,1)S(1)}, bf16[512,512]{1,0:T(8,128)(2,1)S(1)}, bf16[512,512]{1,0:T(8,128)(2,1)S(1)}) fusion(bf16[512]{0:T(512)(128)(2,1)S(1)} %get-tuple-element.36, bf16[512]{0:T(512)(128)(2,1)S(1)} %get-tuple-element.37, bf16[512]{0:T(512)(128)(2,1)S(1)} %get-tuple-element.38, bf16[512]{0:T(512)(128)(2,1)S(1)} %get-tuple-element.39, ...), kind=kLoop, calls=%fused_computation.523 | loop fusion | flops 7340032 | bytes 1591296 | tf_op jit(solution)/shard_map/neg | solution.py:43
  67.7 1.2 collective-permute-done.4
  68.9 3.4 %add_convert_fusion = bf16[1024,512]{1,0:T(8,128)(2,1)} fusion(f32[1024,512]{1,0:T(8,128)S(1)} %copy-done.9, bf16[1024,512]{1,0:T(8,128)(2,1)} %collective-permute-done.4, bf16[512,512]{1,0:T(8,128)(2,1)S(1)} %get-tuple-element.233, bf16[512,512]{1,0:T(8,128)(2,1)S(1)} %get-tuple-element.208, bf16[512,512]{1,0:T(8,128)(2,1)S(1)} %get-tuple-element.207), kind=kOutput, calls=%fused_computation.79 | convolution fusion | flops 1083179008 | bytes 5767168 | tf_op jit(solution)/shard_map/dot_general | solution.py:97
  72.5 1.2 constant_dynamic-slice_fusion
  73.7 3.3 %collective-permute-start.5 = (bf16[1024,256]{1,0:T(8,128)(2,1)S(1)}, bf16[1024,256]{1,0:T(8,128)(2,1)S(1)}, u32[]{:S(2)}, u32[]{:S(2)}) collective-permute-start(bf16[1024,256]{1,0:T(8,128)(2,1)S(1)} %constant_dynamic-slice_fusion), channel_id=1, source_target_pairs={{0,64},{16,80},{32,96},{48,112},{64,0},{80,16},{96,32},{112,48},{1... | collective-permute-start | bytes 1572872 | tf_op jit(solution)/shard_map/ppermute | solution.py:16
  77.0 1.7 %fusion.341 = (bf16[512,512]{1,0:T(8,128)(2,1)S(1)}, bf16[512,512]{1,0:T(8,128)(2,1)S(1)}, bf16[512,512]{1,0:T(8,128)(2,1)S(1)}) fusion(bf16[512]{0:T(512)(128)(2,1)S(1)} %get-tuple-element.84, bf16[512]{0:T(512)(128)(2,1)S(1)} %get-tuple-element.85, bf16[512]{0:T(512)(128)(2,1)S(1)} %get-tuple-element.86, bf16[512]{0:T(512)(128)(2,1)S(1)} %get-tuple-element.87, ...), kind=kLoop, calls=%fused_computation.526 | loop fusion | flops 7340032 | bytes 1591296 | tf_op jit(solution)/shard_map/neg | solution.py:43
  78.8 0.7 fusion.67
  79.6 1.7 %fusion.340 = (bf16[512,512]{1,0:T(8,128)(2,1)S(1)}, bf16[512,512]{1,0:T(8,128)(2,1)S(1)}, bf16[512,512]{1,0:T(8,128)(2,1)S(1)}) fusion(bf16[512]{0:T(512)(128)(2,1)S(1)} %get-tuple-element.68, bf16[512]{0:T(512)(128)(2,1)S(1)} %get-tuple-element.69, bf16[512]{0:T(512)(128)(2,1)S(1)} %get-tuple-element.70, bf16[512]{0:T(512)(128)(2,1)S(1)} %get-tuple-element.71, ...), kind=kLoop, calls=%fused_computation.525 | loop fusion | flops 7340032 | bytes 1591296 | tf_op jit(solution)/shard_map/neg | solution.py:43
  81.3 6.9 %collective-permute-done.5 = bf16[1024,256]{1,0:T(8,128)(2,1)S(1)} collective-permute-done((bf16[1024,256]{1,0:T(8,128)(2,1)S(1)}, bf16[1024,256]{1,0:T(8,128)(2,1)S(1)}, u32[]{:S(2)}, u32[]{:S(2)}) %collective-permute-start.5) | collective-permute-done | bytes 524320 | tf_op jit(solution)/shard_map/ppermute | solution.py:16
  88.3 1.5 %fusion.103 = bf16[1024,256]{1,0:T(8,128)(2,1)} fusion(f32[1024,256]{1,0:T(8,128)S(1)} %fusion.67, bf16[1024,256]{1,0:T(8,128)(2,1)S(1)} %collective-permute-done.5, bf16[512,512]{1,0:T(8,128)(2,1)S(1)} %get-tuple-element.231, bf16[512,512]{1,0:T(8,128)(2,1)S(1)} %get-tuple-element.204, bf16[512,512]{1,0:T(8,128)(2,1)S(1)} %get-tuple-element.203), kind=kOutput, calls=%fused_computation.98 | convolution fusion | flops 545783808 | bytes 3670016 | tf_op jit(solution)/shard_map/dot_general | solution.py:119
  89.8 2.1 %copy.47 = bf16[2,512,256]{1,2,0:T(8,128)(2,1)} copy(bf16[2,512,256]{2,1,0:T(8,128)(2,1)} %bitcast.135) | data formatting | bytes 1048576 | tf_op jit(solution)/shard_map/reshape | solution.py:122
  91.9 1.8 %fusion.51 = f32[1024,256]{1,0:T(8,128)S(1)} fusion(bf16[1024,256]{1,0:T(8,128)(2,1)} %copy-done.8, bf16[512,512]{1,0:T(8,128)(2,1)S(1)} %get-tuple-element.230, bf16[512,512]{1,0:T(8,128)(2,1)S(1)} %get-tuple-element.202, bf16[512,512]{1,0:T(8,128)(2,1)S(1)} %get-tuple-element.201), kind=kOutput, calls=%fused_computation.51 | convolution fusion | flops 545259520 | bytes 3145728 | tf_op jit(solution)/shard_map/dot_general | solution.py:120
  93.7 0.7 fusion.100
  94.7 0.7 fusion.90
  95.5 0.7 fusion.91
  96.2 1.7 %pad_maximum_fusion = bf16[128,16,512]{2,1,0:T(8,128)(2,1)} fusion(bf16[128,8,512]{2,1,0:T(8,128)(2,1)S(1)} %fusion.91, bf16[128,8,512]{2,1,0:T(8,128)(2,1)S(1)} %fusion.90), kind=kLoop, calls=%fused_computation.75 | loop fusion | flops 4194304 | bytes 4194304 | tf_op jit(solution)/shard_map/concatenate | solution.py:130
  97.9 12.9 %all-to-all-start.1 = ((bf16[128,16,512]{2,1,0:T(8,128)(2,1)}), bf16[128,16,512]{2,1,0:T(8,128)(2,1)S(1)}, u32[]{:S(2)}, u32[]{:S(2)}) async-start(bf16[128,16,512]{2,1,0:T(8,128)(2,1)} %pad_maximum_fusion), calls=%async_computation.1 | async-start | bytes 4194304 | tf_op jit(solution)/shard_map/all_to_all | solution.py:131
  112.4 28.1 %all-to-all-done.1 = bf16[128,16,512]{2,1,0:T(8,128)(2,1)S(1)} async-done(((bf16[128,16,512]{2,1,0:T(8,128)(2,1)}), bf16[128,16,512]{2,1,0:T(8,128)(2,1)S(1)}, u32[]{:S(2)}, u32[]{:S(2)}) %all-to-all-start.1) | async-done | bytes 2097184 | tf_op jit(solution)/shard_map/all_to_all | solution.py:131
  140.7 0.8 fusion.98
  141.7 0.8 fusion.99
  142.7 1.1 maximum_bitcast_fusion
  (96 shorter events, 7.4 us)
Async XLA Ops:
  0.0 26.7 %collective-permute-start = (bf16[2,512,512]{2,1,0:T(8,128)(2,1)}, bf16[2,512,512]{2,1,0:T(8,128)(2,1)}, u32[]{:S(2)}, u32[]{:S(2)}) collective-permute-start(bf16[2,512,512]{2,1,0:T(8,128)(2,1)} %param.6), channel_id=1, source_target_pairs={{1,0},{2,1},{3,2},{4,3},{5,4},{6,5},{7,6},{8,7},{9,8},{10,9},{11,1... | collective-permute-start | bytes 3145736 | tf_op jit(solution)/shard_map/ppermute | solution.py:12
  7.2 30.8 %collective-permute-start.2 = (s32[1536]{0:T(1024)S(1)}, s32[1536]{0:T(1024)S(1)}, u32[]{:S(2)}, u32[]{:S(2)}) collective-permute-start(s32[1536]{0:T(1024)S(1)} %pad_add_fusion.1), channel_id=1, source_target_pairs={{0,64},{16,80},{32,96},{48,112},{64,0},{80,16},{96,32},{112,48},{1... | collective-permute-start | bytes 18440 | tf_op jit(solution)/shard_map/ppermute | solution.py:16
  11.6 60.7 %collective-permute-start.3 = (bf16[2,2,512,8]{2,3,1,0:T(8,128)(2,1)S(1)}, bf16[2,2,512,8]{2,3,1,0:T(8,128)(2,1)S(1)}, u32[]{:S(2)}, u32[]{:S(2)}) collective-permute-start(bf16[2,2,512,8]{2,3,1,0:T(8,128)(2,1)S(1)} %get-tuple-element.31), channel_id=1, source_target_pairs={{0,64},{16,80},{32,96},{48,112},{64,0},{80,16},{96,32},{112,48},{1... | collective-permute-start | bytes 98312 | tf_op jit(solution)/shard_map/ppermute | solution.py:16
  16.8 1.4 copy-start
  28.1 1.2 copy-start.1
  31.8 7.5 %collective-permute-start.1 = (bf16[1024,512]{1,0:T(8,128)(2,1)S(1)}, bf16[1024,512]{1,0:T(8,128)(2,1)}, u32[]{:S(2)}, u32[]{:S(2)}) collective-permute-start(bf16[1024,512]{1,0:T(8,128)(2,1)S(1)} %bitcast.125), channel_id=1, source_target_pairs={{0,16},{16,0},{32,48},{48,32},{64,80},{80,64},{96,112},{112,96},{1... | collective-permute-start | bytes 3145736 | tf_op jit(solution)/shard_map/ppermute | solution.py:16
  38.0 1.3 copy-start.7
  38.0 1.3 copy-start.2
  38.0 1.3 copy-start.3
  42.8 26.2 %collective-permute-start.4 = (bf16[1024,512]{1,0:T(8,128)(2,1)}, bf16[1024,512]{1,0:T(8,128)(2,1)}, u32[]{:S(2)}, u32[]{:S(2)}) collective-permute-start(bf16[1024,512]{1,0:T(8,128)(2,1)} %add_convert_fusion.1), channel_id=1, source_target_pairs={{0,32},{16,48},{32,0},{48,16},{64,96},{80,112},{96,64},{112,80},{1... | collective-permute-start | bytes 3145736 | tf_op jit(solution)/shard_map/ppermute | solution.py:16
  50.4 22.0 %all-to-all-start = ((s32[128,1,8]{2,1,0:T(1,128)}), s32[128,1,8]{2,1,0:T(1,128)S(1)}, u32[]{:S(2)}, u32[]{:S(2)}) async-start(s32[128,1,8]{2,1,0:T(1,128)} %bitcast.27), calls=%async_computation | async-start | bytes 131072 | tf_op jit(solution)/shard_map/all_to_all | solution.py:96
  62.5 6.5 %copy-start.9 = (f32[1024,512]{1,0:T(8,128)S(1)}, f32[1024,512]{1,0:T(8,128)}, u32[]{:S(2)}) copy-start(f32[1024,512]{1,0:T(8,128)} %fusion.27) | copy-start | bytes 6291460
  72.4 6.4 %copy-start.5 = (bf16[1024,512]{1,0:T(8,128)(2,1)S(1)}, bf16[1024,512]{1,0:T(8,128)(2,1)}, u32[]{:S(2)}) copy-start(bf16[1024,512]{1,0:T(8,128)(2,1)} %add_convert_fusion) | copy-start | bytes 3145732
  73.7 14.6 %collective-permute-start.5 = (bf16[1024,256]{1,0:T(8,128)(2,1)S(1)}, bf16[1024,256]{1,0:T(8,128)(2,1)S(1)}, u32[]{:S(2)}, u32[]{:S(2)}) collective-permute-start(bf16[1024,256]{1,0:T(8,128)(2,1)S(1)} %constant_dynamic-slice_fusion), channel_id=1, source_target_pairs={{0,64},{16,80},{32,96},{48,112},{64,0},{80,16},{96,32},{112,48},{1... | collective-permute-start | bytes 1572872 | tf_op jit(solution)/shard_map/ppermute | solution.py:16
  88.3 1.5 %copy-start.8 = (bf16[1024,256]{1,0:T(8,128)(2,1)}, bf16[1024,256]{1,0:T(8,128)(2,1)S(1)}, u32[]{:S(2)}) copy-start(bf16[1024,256]{1,0:T(8,128)(2,1)S(1)} %collective-permute-done.5) | copy-start | bytes 1572868
  91.9 1.8 %copy-start.6 = (bf16[1024,512]{1,0:T(8,128)(2,1)S(1)}, bf16[1024,512]{1,0:T(8,128)(2,1)}, u32[]{:S(2)}) copy-start(bf16[1024,512]{1,0:T(8,128)(2,1)} %add_convert_fusion) | copy-start | bytes 3145732
  94.4 1.0 copy-start.4
  94.4 1.0 slice-start
  97.9 42.6 %all-to-all-start.1 = ((bf16[128,16,512]{2,1,0:T(8,128)(2,1)}), bf16[128,16,512]{2,1,0:T(8,128)(2,1)S(1)}, u32[]{:S(2)}, u32[]{:S(2)}) async-start(bf16[128,16,512]{2,1,0:T(8,128)(2,1)} %pad_maximum_fusion), calls=%async_computation.1 | async-start | bytes 4194304 | tf_op jit(solution)/shard_map/all_to_all | solution.py:131

commit v14 on v10

--- a/solution.py
+++ b/solution.py
@@ -58,10 +58,17 @@
     devices = n_sub * n_rng
     capacity = max(2, 2 * p_dev // devices)
     tail = shifted(echoes, "rng", -1)
-    extended = jnp.concatenate([echoes, tail], axis=2)
     matrix = replica_matrix(chirp, RBLK)
-    stacked = jnp.concatenate([extended[0], extended[1]], axis=1)
-    block_out = jnp.dot(stacked, matrix, preferred_element_type=jnp.float32).astype(jnp.bfloat16)
+    span = matrix.shape[0] // 2
+    m_local = jnp.concatenate([matrix[:r_dev], matrix[span : span + r_dev]], axis=0)
+    m_tail = jnp.concatenate([matrix[r_dev:span], matrix[span + r_dev :]], axis=0)
+    local = jnp.dot(
+        jnp.concatenate([echoes[0], echoes[1]], axis=1), m_local, preferred_element_type=jnp.float32
+    )
+    far_part = jnp.dot(
+        jnp.concatenate([tail[0], tail[1]], axis=1), m_tail, preferred_element_type=jnp.float32
+    )
+    block_out = (local + far_part).astype(jnp.bfloat16)
     pieces = block_out.reshape(p_dev, 2, RBLK)
     image = pieces.transpose(1, 0, 2).reshape(2 * p_dev, r_dev)
     section_count = offsets.shape[0]

time: 141 us -> 138 us (0.979)
  local copies, waits for them, and re-layouts: 19.2 us -> 14.7 us
  matrix products: 17.8 us -> 19.9 us
  waiting for transfers between devices: 51.9 us -> 50.4 us
    squeeze x1 -> x2, local copies, waits for them, and re-layouts: 0.17 us -> 3.5 us  [the longest x1 2.23 us: on_device(): echoes[0]]
    unnamed x24 -> x25, local copies, waits for them, and re-layouts: 2.76 us -> 0.05 us
    dot_general x1 -> x2, matrix products: 2.38 us -> 4.42 us  [the longest x1 3.14 us: on_device(): jnp.dot(jnp.concatenate([echoes[0], echoes[1]], axis=1), m_local, preferr...]
    another operation x4, local copies, waits for them, and re-layouts: 4.78 us -> 2.84 us  [replica_matrix(): jnp.tile(padded, block_len)[:block_len * width].reshape(block_len, width)]
    concatenate x0 -> x1, other arithmetic: none -> 1.51 us  [replica_matrix(): upper = jnp.concatenate([h_real, -h_imag], axis=1)]
    ppermute x1, waiting for transfers between devices: 5.41 us -> 3.91 us  [shifted(): lax.ppermute(value, axis, [(source, source + steps) for source in range(f...]
  transfers between devices with their start and end apart: 8 -> 8, of which waited for: 4 -> 4; matrix products, arithmetic and copies ran while one was open for 30% -> 34% of each run, Pallas kernels for 0% -> 0%
where the time goes in v14:
time: 138 us
  waiting for transfers between devices  50.4 us (37%)
  starting transfers between devices  30.9 us (22%)
  other arithmetic  21.3 us (15%)
  matrix products  19.9 us (14%)
  local copies, waits for them, and re-layouts  14.7 us (11%)
    all_to_all x1, waiting for transfers between devices, on_device(): lax.all_to_all(payload, ('sub', 'rng'), split_axis=0, concat_axis=0, tile...  28 us
    ppermute x5, waiting for transfers between devices, from_partner(): lax.ppermute(value, axis, [(i, i ^ 1 << apart) for i in range(lax.axis_si...  18.4 us
    neg x8, other arithmetic, merge_matrix(): upper = jnp.concatenate([g_real, -g_imag], axis=1)  15.9 us
    all_to_all x1, starting transfers between devices, on_device(): lax.all_to_all(labels, ('sub', 'rng'), split_axis=0, concat_axis=0, tiled...  12.6 us
    all_to_all x1, starting transfers between devices, on_device(): lax.all_to_all(payload, ('sub', 'rng'), split_axis=0, concat_axis=0, tile...  9.6 us
    ppermute x5, starting transfers between devices, from_partner(): lax.ppermute(value, axis, [(i, i ^ 1 << apart) for i in range(lax.axis_si...  7.36 us
    dot_general x2, matrix products, on_device(): jnp.dot(theirs, old[m ^ bit], preferred_element_type=jnp.float32)  3.96 us
    ppermute x1, waiting for transfers between devices, shifted(): lax.ppermute(value, axis, [(source, source + steps) for source in range(f...  3.91 us
  transfers between devices with their start and end apart: 8, of which 4 were waited for; matrix products, arithmetic and copies ran while one was open for 34% of the time, Pallas kernels for 0%

profile of v14, /device:TPU:1, one launch (start us, length us, event | category | flops | bytes accessed | tf_op | source)
XLA Modules:
  0.0 137.8 jit_solution(18226028557640969726)
XLA Ops:
  0.0 1.4 %collective-permute-start = (bf16[2,512,512]{2,1,0:T(8,128)(2,1)}, bf16[2,512,512]{2,1,0:T(8,128)(2,1)}, u32[]{:S(2)}, u32[]{:S(2)}) collective-permute-start(bf16[2,512,512]{2,1,0:T(8,128)(2,1)} %param.6), channel_id=1, source_target_pairs={{1,0},{2,1},{3,2},{4,3},{5,4},{6,5},{7,6},{8,7},{9,8},{10,9},{11,1... | collective-permute-start | bytes 3145736 | tf_op jit(solution)/shard_map/ppermute | solution.py:12
  1.4 2.2 %slice_bitcast_fusion.3 = (bf16[512,512]{1,0:T(8,128)(2,1)}, bf16[512,512]{1,0:T(8,128)(2,1)}) fusion(bf16[2,512,512]{2,1,0:T(8,128)(2,1)} %param.6), kind=kLoop, calls=%fused_computation.323 | loop fusion | bytes 2097152 | tf_op jit(solution)/shard_map/squeeze | solution.py:66
  4.2 0.2 fusion.312
  4.5 1.3 tile.9
  6.0 0.5 reshape.177
  6.6 1.3 tile.21
  7.9 1.0 slice.1019
  9.0 1.5 %reshape.178 = bf16[512,1024]{1,0:T(8,128)(2,1)S(1)} reshape(bf16[524288]{0:T(1024)(128)(2,1)} %slice.1019) | data formatting | bytes 2097152 | tf_op jit(solution)/shard_map/reshape | solution.py:25
  10.6 0.3 select_reduce_fusion
  11.3 1.5 %fusion.105 = (bf16[512,1024]{0,1:T(8,128)(2,1)}, bf16[512,1024]{0,1:T(8,128)(2,1)}) fusion(bf16[1024,512]{0,1:T(8,128)(2,1)S(1)} %bitcast.122, bf16[1024,512]{0,1:T(8,128)(2,1)S(1)} %bitcast_negate_fusion, bf16[1024,512]{0,1:T(8,128)(2,1)S(1)} %bitcast.120), kind=kLoop, calls=%fused_computation.105 | loop fusion | flops 4194304 | bytes 5242880 | tf_op jit(solution)/shard_map/concatenate | solution.py:28
  12.8 2.7 %fusion.346 = (bf16[512,512]{1,0:T(8,128)(2,1)}, bf16[512,512]{1,0:T(8,128)(2,1)}, bf16[512,512]{1,0:T(8,128)(2,1)}) fusion(bf16[512]{0:T(512)(128)(2,1)S(1)} %get-tuple-element.138, bf16[512]{0:T(512)(128)(2,1)S(1)} %get-tuple-element.139, bf16[512]{0:T(512)(128)(2,1)S(1)} %get-tuple-element.140, bf16[512]{0:T(512)(128)(2,1)S(1)} %get-tuple-element.141, ...), kind=kLoop, calls=%fused_computation.544 | loop fusion | flops 7340032 | bytes 1591296 | tf_op jit(solution)/shard_map/neg | solution.py:43
  15.6 0.7 sub.137
  16.3 3.1 %fusion.25 = f32[512,1024]{1,0:T(8,128)S(1)} fusion(bf16[512,1024]{0,1:T(8,128)(2,1)} %get-tuple-element.162, bf16[512,1024]{0,1:T(8,128)(2,1)} %get-tuple-element.161, bf16[512,512]{1,0:T(8,128)(2,1)} %get-tuple-element.160, bf16[512,512]{1,0:T(8,128)(2,1)} %get-tuple-element.159), kind=kOutput, calls=%fused_computation.29 | convolution fusion | flops 1080033280 | bytes 5242880 | tf_op jit(solution)/shard_map/dot_general | solution.py:65
  19.4 1.7 %fusion.347 = (bf16[512,512]{1,0:T(8,128)(2,1)S(1)}, bf16[512,512]{1,0:T(8,128)(2,1)S(1)}, bf16[512,512]{1,0:T(8,128)(2,1)S(1)}) fusion(bf16[512]{0:T(512)(128)(2,1)S(1)} %get-tuple-element.122, bf16[512]{0:T(512)(128)(2,1)S(1)} %get-tuple-element.123, bf16[512]{0:T(512)(128)(2,1)S(1)} %get-tuple-element.124, bf16[512]{0:T(512)(128)(2,1)S(1)} %get-tuple-element.125, ...), kind=kLoop, calls=%fused_computation.545 | loop fusion | flops 7340032 | bytes 1591296 | tf_op jit(solution)/shard_map/neg | solution.py:43
  21.2 1.7 %fusion.345 = (bf16[512,512]{1,0:T(8,128)(2,1)S(1)}, bf16[512,512]{1,0:T(8,128)(2,1)S(1)}, bf16[512,512]{1,0:T(8,128)(2,1)S(1)}) fusion(bf16[512]{0:T(512)(128)(2,1)S(1)} %get-tuple-element.106, bf16[512]{0:T(512)(128)(2,1)S(1)} %get-tuple-element.107, bf16[512]{0:T(512)(128)(2,1)S(1)} %get-tuple-element.108, bf16[512]{0:T(512)(128)(2,1)S(1)} %get-tuple-element.109, ...), kind=kLoop, calls=%fused_computation.543 | loop fusion | flops 7340032 | bytes 1591296 | tf_op jit(solution)/shard_map/neg | solution.py:43
  22.9 3.9 %collective-permute-done = bf16[2,512,512]{2,1,0:T(8,128)(2,1)} collective-permute-done((bf16[2,512,512]{2,1,0:T(8,128)(2,1)}, bf16[2,512,512]{2,1,0:T(8,128)(2,1)}, u32[]{:S(2)}, u32[]{:S(2)}) %collective-permute-start) | collective-permute-done | bytes 1048608 | tf_op jit(solution)/shard_map/ppermute | solution.py:12
  26.9 1.3 slice_bitcast_fusion.1
  28.1 1.3 add_convert_fusion.2
  29.5 1.7 %collective-permute-start.1 = (bf16[1024,512]{1,0:T(8,128)(2,1)S(1)}, bf16[1024,512]{1,0:T(8,128)(2,1)S(1)}, u32[]{:S(2)}, u32[]{:S(2)}) collective-permute-start(bf16[1024,512]{1,0:T(8,128)(2,1)S(1)} %bitcast.124), channel_id=1, source_target_pairs={{0,16},{16,0},{32,48},{48,32},{64,80},{80,64},{96,112},{112,96},{1... | collective-permute-start | bytes 3145736 | tf_op jit(solution)/shard_map/ppermute | solution.py:16
  31.3 1.7 %fusion.348 = (bf16[512,512]{1,0:T(8,128)(2,1)S(1)}, bf16[512,512]{1,0:T(8,128)(2,1)S(1)}, bf16[512,512]{1,0:T(8,128)(2,1)S(1)}) fusion(bf16[512]{0:T(512)(128)(2,1)S(1)} %get-tuple-element.74, bf16[512]{0:T(512)(128)(2,1)S(1)} %get-tuple-element.75, bf16[512]{0:T(512)(128)(2,1)S(1)} %get-tuple-element.76, bf16[512]{0:T(512)(128)(2,1)S(1)} %get-tuple-element.77, ...), kind=kLoop, calls=%fused_computation.546 | loop fusion | flops 7340032 | bytes 1591296 | tf_op jit(solution)/shard_map/neg | solution.py:43
  33.0 1.2 fusion.17
  34.3 1.2 add_convert_fusion.1
  35.5 2.0 %collective-permute-start.2 = (bf16[1024,512]{1,0:T(8,128)(2,1)S(1)}, bf16[1024,512]{1,0:T(8,128)(2,1)S(1)}, u32[]{:S(2)}, u32[]{:S(2)}) collective-permute-start(bf16[1024,512]{1,0:T(8,128)(2,1)S(1)} %add_convert_fusion.1), channel_id=1, source_target_pairs={{0,32},{16,48},{32,0},{48,16},{64,96},{80,112},{96,64},{112,80},{1... | collective-permute-start | bytes 3145736 | tf_op jit(solution)/shard_map/ppermute | solution.py:16
  37.5 1.2 fusion.9
  38.7 3.4 %collective-permute-start.5 = (bf16[2,2,512,8]{2,3,1,0:T(8,128)(2,1)S(1)}, bf16[2,2,512,8]{2,3,1,0:T(8,128)(2,1)S(1)}, u32[]{:S(2)}, u32[]{:S(2)}) collective-permute-start(bf16[2,2,512,8]{2,3,1,0:T(8,128)(2,1)S(1)} %slice_bitcast_fusion.4), channel_id=1, source_target_pairs={{0,64},{16,80},{32,96},{48,112},{64,0},{80,16},{96,32},{112,48},{1... | collective-permute-start | bytes 98312 | tf_op jit(solution)/shard_map/ppermute | solution.py:16
  42.1 0.3 collective-permute-start.4
  42.6 1.7 %fusion.344 = (bf16[512,512]{1,0:T(8,128)(2,1)S(1)}, bf16[512,512]{1,0:T(8,128)(2,1)S(1)}, bf16[512,512]{1,0:T(8,128)(2,1)S(1)}) fusion(bf16[512]{0:T(512)(128)(2,1)S(1)} %get-tuple-element.42, bf16[512]{0:T(512)(128)(2,1)S(1)} %get-tuple-element.43, bf16[512]{0:T(512)(128)(2,1)S(1)} %get-tuple-element.44, bf16[512]{0:T(512)(128)(2,1)S(1)} %get-tuple-element.45, ...), kind=kLoop, calls=%fused_computation.542 | loop fusion | flops 7340032 | bytes 1591296 | tf_op jit(solution)/shard_map/neg | solution.py:43
  44.4 1.7 %fusion.349 = (bf16[512,512]{1,0:T(8,128)(2,1)S(1)}, bf16[512,512]{1,0:T(8,128)(2,1)S(1)}, bf16[512,512]{1,0:T(8,128)(2,1)S(1)}) fusion(bf16[512]{0:T(512)(128)(2,1)S(1)} %get-tuple-element.26, bf16[512]{0:T(512)(128)(2,1)S(1)} %get-tuple-element.27, bf16[512]{0:T(512)(128)(2,1)S(1)} %get-tuple-element.28, bf16[512]{0:T(512)(128)(2,1)S(1)} %get-tuple-element.29, ...), kind=kLoop, calls=%fused_computation.547 | loop fusion | flops 7340032 | bytes 1591296 | tf_op jit(solution)/shard_map/neg | solution.py:43
  46.1 18.4 %collective-permute-done.4 = s32[1536]{0:T(1024)S(1)} collective-permute-done((s32[1536]{0:T(1024)S(1)}, s32[1536]{0:T(1024)S(1)}, u32[]{:S(2)}, u32[]{:S(2)}) %collective-permute-start.4) | collective-permute-done | bytes 6176 | tf_op jit(solution)/shard_map/ppermute | solution.py:16
  64.8 1.7 %fusion.351 = (bf16[512,512]{1,0:T(8,128)(2,1)S(1)}, bf16[512,512]{1,0:T(8,128)(2,1)S(1)}, bf16[512,512]{1,0:T(8,128)(2,1)S(1)}) fusion(bf16[512]{0:T(512)(128)(2,1)S(1)} %get-tuple-element.90, bf16[512]{0:T(512)(128)(2,1)S(1)} %get-tuple-element.91, bf16[512]{0:T(512)(128)(2,1)S(1)} %get-tuple-element.92, bf16[512]{0:T(512)(128)(2,1)S(1)} %get-tuple-element.93, ...), kind=kLoop, calls=%fused_computation.549 | loop fusion | flops 7340032 | bytes 1591296 | tf_op jit(solution)/shard_map/neg | solution.py:43
  66.5 1.2 add_convert_fusion
  67.8 0.9 constant_dynamic-slice_fusion
  68.7 2.7 %fusion.350 = (bf16[512,512]{1,0:T(8,128)(2,1)}, bf16[512,512]{1,0:T(8,128)(2,1)}, bf16[512,512]{1,0:T(8,128)(2,1)}) fusion(bf16[512]{0:T(512)(128)(2,1)S(1)} %get-tuple-element.58, bf16[512]{0:T(512)(128)(2,1)S(1)} %get-tuple-element.59, bf16[512]{0:T(512)(128)(2,1)S(1)} %get-tuple-element.60, bf16[512]{0:T(512)(128)(2,1)S(1)} %get-tuple-element.61, ...), kind=kLoop, calls=%fused_computation.548 | loop fusion | flops 7340032 | bytes 1591296 | tf_op jit(solution)/shard_map/neg | solution.py:43
  71.4 1.7 %fusion.37 = f32[1024,256]{1,0:T(8,128)} fusion(bf16[512,512]{1,0:T(8,128)(2,1)S(1)} %get-tuple-element.213, bf16[512,512]{1,0:T(8,128)(2,1)S(1)} %get-tuple-element.186, bf16[512,512]{1,0:T(8,128)(2,1)S(1)} %get-tuple-element.185, bf16[1024,512]{1,0:T(8,128)(2,1)S(1)} %add_convert_fusion, s32[]{:T(128)S(6)} %select_n.476), kind=kOutput, calls=%fused_computation.41 | convolution fusion | flops 545259520 | bytes 3145732 | tf_op jit(solution)/shard_map/dot_general | solution.py:115
  73.2 12.6 %all-to-all-start = ((s32[128,1,8]{2,1,0:T(1,128)}), s32[128,1,8]{2,1,0:T(1,128)S(1)}, u32[]{:S(2)}, u32[]{:S(2)}) async-start(s32[128,1,8]{2,1,0:T(1,128)} %bitcast.33), calls=%async_computation | async-start | bytes 131072 | tf_op jit(solution)/shard_map/all_to_all | solution.py:118
  85.7 1.9 %fusion.69 = f32[1024,256]{1,0:T(8,128)S(1)} fusion(bf16[512,512]{1,0:T(8,128)(2,1)S(1)} %get-tuple-element.216, bf16[512,512]{1,0:T(8,128)(2,1)S(1)} %get-tuple-element.192, bf16[512,512]{1,0:T(8,128)(2,1)S(1)} %get-tuple-element.191, bf16[1024,512]{1,0:T(8,128)(2,1)} %copy-done.6, s32[]{:T(128)S(6)} %select_n.476), kind=kOutput, calls=%fused_computation.73 | convolution fusion | flops 545259520 | bytes 3145732 | tf_op jit(solution)/shard_map/dot_general | solution.py:119
  87.7 1.7 %fusion.102 = bf16[1024,256]{1,0:T(8,128)(2,1)S(1)} fusion(f32[1024,256]{1,0:T(8,128)S(1)} %fusion.69, bf16[1024,256]{1,0:T(8,128)(2,1)} %collective-permute-done.3, bf16[512,512]{1,0:T(8,128)(2,1)S(1)} %copy-done.5, bf16[512,512]{1,0:T(8,128)(2,1)S(1)} %copy-done.4, bf16[512,512]{1,0:T(8,128)(2,1)S(1)} %copy-done.3), kind=kOutput, calls=%fused_computation.104 | convolution fusion | flops 545783808 | bytes 3670016 | tf_op jit(solution)/shard_map/dot_general | solution.py:115
  89.4 0.2 copy.47
  89.6 2.1 %fusion.99 = bf16[1024,256]{1,0:T(8,128)(2,1)S(1)} fusion(f32[1024,256]{1,0:T(8,128)} %fusion.37, bf16[1024,256]{1,0:T(8,128)(2,1)} %collective-permute-done.3, bf16[512,512]{1,0:T(8,128)(2,1)S(1)} %get-tuple-element.212, bf16[512,512]{1,0:T(8,128)(2,1)S(1)} %get-tuple-element.184, bf16[512,512]{1,0:T(8,128)(2,1)S(1)} %get-tuple-element.183), kind=kOutput, calls=%fused_computation.103 | convolution fusion | flops 545783808 | bytes 3670016 | tf_op jit(solution)/shard_map/dot_general | solution.py:119
  91.7 0.2 copy.46
  91.9 0.7 fusion.89
  92.7 0.8 fusion.90
  93.5 1.7 %pad_maximum_fusion.2 = bf16[128,16,512]{2,1,0:T(8,128)(2,1)} fusion(bf16[128,8,512]{2,1,0:T(8,128)(2,1)S(1)} %fusion.90, bf16[128,8,512]{2,1,0:T(8,128)(2,1)S(1)} %fusion.89), kind=kLoop, calls=%fused_computation.81 | loop fusion | flops 4194304 | bytes 4194304 | tf_op jit(solution)/shard_map/concatenate | solution.py:129
  95.3 9.6 %all-to-all-start.1 = ((bf16[128,16,512]{2,1,0:T(8,128)(2,1)}), bf16[128,16,512]{2,1,0:T(8,128)(2,1)S(1)}, u32[]{:S(2)}, u32[]{:S(2)}) async-start(bf16[128,16,512]{2,1,0:T(8,128)(2,1)} %pad_maximum_fusion.2), calls=%async_computation.1 | async-start | bytes 4194304 | tf_op jit(solution)/shard_map/all_to_all | solution.py:130
  106.6 28.0 %all-to-all-done.1 = bf16[128,16,512]{2,1,0:T(8,128)(2,1)S(1)} async-done(((bf16[128,16,512]{2,1,0:T(8,128)(2,1)}), bf16[128,16,512]{2,1,0:T(8,128)(2,1)S(1)}, u32[]{:S(2)}, u32[]{:S(2)}) %all-to-all-start.1) | async-done | bytes 2097184 | tf_op jit(solution)/shard_map/all_to_all | solution.py:130
  134.8 0.8 fusion.97
  135.8 0.8 fusion.98
  136.8 1.1 maximum_bitcast_fusion
  (93 shorter events, 4.3 us)
Async XLA Ops:
  0.0 3.7 %copy-start.7 = (bf16[3,1,2,2,512,8]{4,5,3,2,1,0:T(8,128)(2,1)S(1)}, bf16[3,1,2,2,512,8]{4,5,3,2,1,0:T(8,128)(2,1)}, u32[]{:S(2)}) copy-start(bf16[3,1,2,2,512,8]{4,5,3,2,1,0:T(8,128)(2,1)} %param.9) | copy-start | bytes 294916
  0.0 3.7 %copy-start.8 = (s32[1,1,512,1]{2,3,1,0:T(1,128)S(1)}, s32[1,1,512,1]{2,3,1,0:T(1,128)}, u32[]{:S(2)}) copy-start(s32[1,1,512,1]{2,3,1,0:T(1,128)} %param.10) | copy-start | bytes 6148
  0.0 4.4 %copy-start.10 = (bf16[2,512]{1,0:T(2,128)(2,1)S(1)}, bf16[2,512]{1,0:T(2,128)(2,1)}, u32[]{:S(2)}) copy-start(bf16[2,512]{1,0:T(2,128)(2,1)} %param.7) | copy-start | bytes 6148
  0.0 26.8 %collective-permute-start = (bf16[2,512,512]{2,1,0:T(8,128)(2,1)}, bf16[2,512,512]{2,1,0:T(8,128)(2,1)}, u32[]{:S(2)}, u32[]{:S(2)}) collective-permute-start(bf16[2,512,512]{2,1,0:T(8,128)(2,1)} %param.6), channel_id=1, source_target_pairs={{1,0},{2,1},{3,2},{4,3},{5,4},{6,5},{7,6},{8,7},{9,8},{10,9},{11,1... | collective-permute-start | bytes 3145736 | tf_op jit(solution)/shard_map/ppermute | solution.py:12
  9.0 1.6 %copy-start.9 = (s32[3,1,2,512]{3,2,1,0:T(2,128)S(1)}, s32[3,1,2,512]{3,2,1,0:T(2,128)}, u32[]{:S(2)}) copy-start(s32[3,1,2,512]{3,2,1,0:T(2,128)} %param.8) | copy-start | bytes 36868
  9.0 1.7 %copy-start.11 = (s32[1,1,512]{2,1,0:T(1,128)S(1)}, s32[1,1,512]{2,1,0:T(1,128)}, u32[]{:S(2)}) copy-start(s32[1,1,512]{2,1,0:T(1,128)} %param.11) | copy-start | bytes 6148
  29.4 3.6 %copy-start = (bf16[512,512]{1,0:T(8,128)(2,1)S(1)}, bf16[512,512]{1,0:T(8,128)(2,1)}, u32[]{:S(2)}) copy-start(bf16[512,512]{1,0:T(8,128)(2,1)} %get-tuple-element.197) | copy-start | bytes 1572868
  29.4 3.6 %copy-start.1 = (bf16[512,512]{1,0:T(8,128)(2,1)S(1)}, bf16[512,512]{1,0:T(8,128)(2,1)}, u32[]{:S(2)}) copy-start(bf16[512,512]{1,0:T(8,128)(2,1)} %get-tuple-element.198) | copy-start | bytes 1572868
  29.4 3.6 %copy-start.2 = (bf16[512,512]{1,0:T(8,128)(2,1)S(1)}, bf16[512,512]{1,0:T(8,128)(2,1)}, u32[]{:S(2)}) copy-start(bf16[512,512]{1,0:T(8,128)(2,1)} %get-tuple-element.219) | copy-start | bytes 1572868
  29.5 4.7 %collective-permute-start.1 = (bf16[1024,512]{1,0:T(8,128)(2,1)S(1)}, bf16[1024,512]{1,0:T(8,128)(2,1)S(1)}, u32[]{:S(2)}, u32[]{:S(2)}) collective-permute-start(bf16[1024,512]{1,0:T(8,128)(2,1)S(1)} %bitcast.124), channel_id=1, source_target_pairs={{0,16},{16,0},{32,48},{48,32},{64,80},{80,64},{96,112},{112,96},{1... | collective-permute-start | bytes 3145736 | tf_op jit(solution)/shard_map/ppermute | solution.py:16
  35.5 31.0 %collective-permute-start.2 = (bf16[1024,512]{1,0:T(8,128)(2,1)S(1)}, bf16[1024,512]{1,0:T(8,128)(2,1)S(1)}, u32[]{:S(2)}, u32[]{:S(2)}) collective-permute-start(bf16[1024,512]{1,0:T(8,128)(2,1)S(1)} %add_convert_fusion.1), channel_id=1, source_target_pairs={{0,32},{16,48},{32,0},{48,16},{64,96},{80,112},{96,64},{112,80},{1... | collective-permute-start | bytes 3145736 | tf_op jit(solution)/shard_map/ppermute | solution.py:16
  38.7 25.8 %collective-permute-start.5 = (bf16[2,2,512,8]{2,3,1,0:T(8,128)(2,1)S(1)}, bf16[2,2,512,8]{2,3,1,0:T(8,128)(2,1)S(1)}, u32[]{:S(2)}, u32[]{:S(2)}) collective-permute-start(bf16[2,2,512,8]{2,3,1,0:T(8,128)(2,1)S(1)} %slice_bitcast_fusion.4), channel_id=1, source_target_pairs={{0,64},{16,80},{32,96},{48,112},{64,0},{80,16},{96,32},{112,48},{1... | collective-permute-start | bytes 98312 | tf_op jit(solution)/shard_map/ppermute | solution.py:16
  42.1 22.4 %collective-permute-start.4 = (s32[1536]{0:T(1024)S(1)}, s32[1536]{0:T(1024)S(1)}, u32[]{:S(2)}, u32[]{:S(2)}) collective-permute-start(s32[1536]{0:T(1024)S(1)} %pad_add_fusion.2), channel_id=1, source_target_pairs={{0,64},{16,80},{32,96},{48,112},{64,0},{80,16},{96,32},{112,48},{1... | collective-permute-start | bytes 18440 | tf_op jit(solution)/shard_map/ppermute | solution.py:16
  67.8 5.4 %copy-start.6 = (bf16[1024,512]{1,0:T(8,128)(2,1)}, bf16[1024,512]{1,0:T(8,128)(2,1)S(1)}, u32[]{:S(2)}) copy-start(bf16[1024,512]{1,0:T(8,128)(2,1)S(1)} %add_convert_fusion) | copy-start | bytes 3145732
  68.7 18.9 %collective-permute-start.3 = (bf16[1024,256]{1,0:T(8,128)(2,1)}, bf16[1024,256]{1,0:T(8,128)(2,1)}, u32[]{:S(2)}, u32[]{:S(2)}) collective-permute-start(bf16[1024,256]{1,0:T(8,128)(2,1)} %constant_dynamic-slice_fusion), channel_id=1, source_target_pairs={{0,64},{16,80},{32,96},{48,112},{64,0},{80,16},{96,32},{112,48},{1... | collective-permute-start | bytes 1572872 | tf_op jit(solution)/shard_map/ppermute | solution.py:16
  73.2 22.2 %all-to-all-start = ((s32[128,1,8]{2,1,0:T(1,128)}), s32[128,1,8]{2,1,0:T(1,128)S(1)}, u32[]{:S(2)}, u32[]{:S(2)}) async-start(s32[128,1,8]{2,1,0:T(1,128)} %bitcast.33), calls=%async_computation | async-start | bytes 131072 | tf_op jit(solution)/shard_map/all_to_all | solution.py:118
  85.7 1.9 %copy-start.3 = (bf16[512,512]{1,0:T(8,128)(2,1)S(1)}, bf16[512,512]{1,0:T(8,128)(2,1)}, u32[]{:S(2)}) copy-start(bf16[512,512]{1,0:T(8,128)(2,1)} %get-tuple-element.187) | copy-start | bytes 1572868
  85.7 1.9 %copy-start.4 = (bf16[512,512]{1,0:T(8,128)(2,1)S(1)}, bf16[512,512]{1,0:T(8,128)(2,1)}, u32[]{:S(2)}) copy-start(bf16[512,512]{1,0:T(8,128)(2,1)} %get-tuple-element.188) | copy-start | bytes 1572868
  85.7 1.9 %copy-start.5 = (bf16[512,512]{1,0:T(8,128)(2,1)S(1)}, bf16[512,512]{1,0:T(8,128)(2,1)}, u32[]{:S(2)}) copy-start(bf16[512,512]{1,0:T(8,128)(2,1)} %get-tuple-element.214) | copy-start | bytes 1572868
  95.3 39.3 %all-to-all-start.1 = ((bf16[128,16,512]{2,1,0:T(8,128)(2,1)}), bf16[128,16,512]{2,1,0:T(8,128)(2,1)S(1)}, u32[]{:S(2)}, u32[]{:S(2)}) async-start(bf16[128,16,512]{2,1,0:T(8,128)(2,1)} %pad_maximum_fusion.2), calls=%async_computation.1 | async-start | bytes 4194304 | tf_op jit(solution)/shard_map/all_to_all | solution.py:130

commit v15 on v10

--- a/solution.py
+++ b/solution.py
@@ -58,10 +58,18 @@
     devices = n_sub * n_rng
     capacity = max(2, 2 * p_dev // devices)
     tail = shifted(echoes, "rng", -1)
-    extended = jnp.concatenate([echoes, tail], axis=2)
     matrix = replica_matrix(chirp, RBLK)
-    stacked = jnp.concatenate([extended[0], extended[1]], axis=1)
-    block_out = jnp.dot(stacked, matrix, preferred_element_type=jnp.float32).astype(jnp.bfloat16)
+    span = matrix.shape[0] // 2
+
+    def corr(block, start):
+        real = jnp.dot(block[0], matrix[start : start + r_dev], preferred_element_type=jnp.float32)
+        imag = jnp.dot(
+            block[1], matrix[span + start : span + start + r_dev], preferred_element_type=jnp.float32
+        )
+        return real + imag
+
+    local = corr(echoes, 0)
+    block_out = (local + corr(tail, r_dev)).astype(jnp.bfloat16)
     pieces = block_out.reshape(p_dev, 2, RBLK)
     image = pieces.transpose(1, 0, 2).reshape(2 * p_dev, r_dev)
     section_count = offsets.shape[0]

time: 141 us -> 142 us (level)
  matrix products: 17.8 us -> 24.7 us
  waiting for transfers between devices: 51.9 us -> 46.5 us
  other arithmetic: 20 us -> 24 us
  local copies, waits for them, and re-layouts: 19.2 us -> 15.3 us
    dot_general x1 -> x4, matrix products: 2.38 us -> 7.89 us  [the longest x2 3.97 us: corr(): jnp.dot(block[1], matrix[span + start:span + start + r_dev], preferred_el...]
    ppermute x1, waiting for transfers between devices: 5.41 us -> 0.01 us  [shifted(): lax.ppermute(value, axis, [(source, source + steps) for source in range(f...]
    neg x8, other arithmetic: 14.9 us -> 18.8 us  [merge_matrix(): upper = jnp.concatenate([g_real, -g_imag], axis=1)]
    another operation x4, local copies, waits for them, and re-layouts: 4.78 us -> 2.84 us  [replica_matrix(): jnp.tile(padded, block_len)[:block_len * width].reshape(block_len, width)]
  transfers between devices with their start and end apart: 8 -> 8, of which waited for: 4 -> 3; matrix products, arithmetic and copies ran while one was open for 30% -> 36% of each run, Pallas kernels for 0% -> 0%
where the time goes in v15:
time: 142 us
  waiting for transfers between devices  46.5 us (33%)
  starting transfers between devices  30.5 us (21%)
  matrix products  24.7 us (17%)
  other arithmetic  24 us (17%)
  local copies, waits for them, and re-layouts  15.3 us (11%)
    all_to_all x1, waiting for transfers between devices, on_device(): lax.all_to_all(payload, ('sub', 'rng'), split_axis=0, concat_axis=0, tile...  28 us
    neg x8, other arithmetic, merge_matrix(): upper = jnp.concatenate([g_real, -g_imag], axis=1)  18.8 us
    ppermute x5, waiting for transfers between devices, from_partner(): lax.ppermute(value, axis, [(i, i ^ 1 << apart) for i in range(lax.axis_si...  18.4 us
    all_to_all x1, starting transfers between devices, on_device(): lax.all_to_all(labels, ('sub', 'rng'), split_axis=0, concat_axis=0, tiled...  12.7 us
    all_to_all x1, starting transfers between devices, on_device(): lax.all_to_all(payload, ('sub', 'rng'), split_axis=0, concat_axis=0, tile...  9.59 us
    ppermute x5, starting transfers between devices, from_partner(): lax.ppermute(value, axis, [(i, i ^ 1 << apart) for i in range(lax.axis_si...  6.97 us
    dot_general x2, matrix products, corr(): jnp.dot(block[1], matrix[span + start:span + start + r_dev], preferred_el...  3.97 us
    dot_general x2, matrix products, on_device(): jnp.dot(theirs, old[m ^ bit], preferred_element_type=jnp.float32)  3.96 us
  transfers between devices with their start and end apart: 8, of which 3 were waited for; matrix products, arithmetic and copies ran while one was open for 36% of the time, Pallas kernels for 0%

profile of v15, /device:TPU:1, one launch (start us, length us, event | category | flops | bytes accessed | tf_op | source)
XLA Modules:
  0.0 141.6 jit_solution(15546400949968057610)
XLA Ops:
  0.0 1.3 collective-permute-start
  1.3 0.8 copy.39
  2.4 0.9 fusion.301
  3.3 0.7 multiply_add_fusion
  4.0 0.8 slice_reduce_fusion.136
  4.9 1.3 tile.9
  6.3 0.5 reshape.177
  7.0 1.3 tile.21
  8.3 1.0 slice.1019
  9.3 1.5 %reshape.178 = bf16[512,1024]{1,0:T(8,128)(2,1)S(1)} reshape(bf16[524288]{0:T(1024)(128)(2,1)} %slice.1019) | data formatting | bytes 2097152 | tf_op jit(solution)/shard_map/reshape | solution.py:25
  10.9 1.1 copy-done.2
  12.1 2.1 %fusion.94 = f32[1024,512]{1,0:T(8,128)} fusion(bf16[1024,512]{0,1:T(8,128)(2,1)S(1)} %bitcast.123, bf16[1024,512]{0,1:T(8,128)(2,1)S(1)} %bitcast_negate_fusion, bf16[2,512,512]{2,1,0:T(8,128)(2,1)S(1)} %copy-done.2), kind=kOutput, calls=%fused_computation.95 | convolution fusion | flops 538968064 | bytes 4718592 | tf_op jit(solution)/shard_map/dot_general | solution.py:65
  14.2 2.0 %fusion.91 = f32[1024,512]{1,0:T(8,128)} fusion(bf16[1024,512]{0,1:T(8,128)(2,1)S(1)} %bitcast.127, bf16[1024,512]{0,1:T(8,128)(2,1)S(1)} %bitcast.124, bf16[2,512,512]{2,1,0:T(8,128)(2,1)S(1)} %copy-done.2), kind=kOutput, calls=%fused_computation.93 | convolution fusion | flops 538968064 | bytes 4718592 | tf_op jit(solution)/shard_map/dot_general | solution.py:66
  16.6 0.7 sub.137
  17.3 0.7 slice_reduce_fusion.111
  18.3 3.6 %fusion.336 = (bf16[512,512]{1,0:T(8,128)(2,1)}, bf16[512,512]{1,0:T(8,128)(2,1)}, bf16[512,512]{1,0:T(8,128)(2,1)}) fusion(bf16[512]{0:T(512)(128)(2,1)S(1)} %get-tuple-element.138, bf16[512]{0:T(512)(128)(2,1)S(1)} %get-tuple-element.139, bf16[512]{0:T(512)(128)(2,1)S(1)} %get-tuple-element.140, bf16[512]{0:T(512)(128)(2,1)S(1)} %get-tuple-element.141, ...), kind=kLoop, calls=%fused_computation.533 | loop fusion | flops 7340032 | bytes 1591296 | tf_op jit(solution)/shard_map/neg | solution.py:43
  21.8 2.8 %fusion.337 = (bf16[512,512]{1,0:T(8,128)(2,1)}, bf16[512,512]{1,0:T(8,128)(2,1)}, bf16[512,512]{1,0:T(8,128)(2,1)}) fusion(bf16[512]{0:T(512)(128)(2,1)S(1)} %get-tuple-element.122, bf16[512]{0:T(512)(128)(2,1)S(1)} %get-tuple-element.123, bf16[512]{0:T(512)(128)(2,1)S(1)} %get-tuple-element.124, bf16[512]{0:T(512)(128)(2,1)S(1)} %get-tuple-element.125, ...), kind=kLoop, calls=%fused_computation.534 | loop fusion | flops 7340032 | bytes 1591296 | tf_op jit(solution)/shard_map/neg | solution.py:43
  24.6 2.8 %fusion.335 = (bf16[512,512]{1,0:T(8,128)(2,1)}, bf16[512,512]{1,0:T(8,128)(2,1)}, bf16[512,512]{1,0:T(8,128)(2,1)}) fusion(bf16[512]{0:T(512)(128)(2,1)S(1)} %get-tuple-element.106, bf16[512]{0:T(512)(128)(2,1)S(1)} %get-tuple-element.107, bf16[512]{0:T(512)(128)(2,1)S(1)} %get-tuple-element.108, bf16[512]{0:T(512)(128)(2,1)S(1)} %get-tuple-element.109, ...), kind=kLoop, calls=%fused_computation.532 | loop fusion | flops 7340032 | bytes 1591296 | tf_op jit(solution)/shard_map/neg | solution.py:43
  27.4 1.9 %fusion.96 = f32[1024,512]{1,0:T(8,128)S(1)} fusion(bf16[1024,512]{0,1:T(8,128)(2,1)S(1)} %bitcast.125, bf16[1024,512]{0,1:T(8,128)(2,1)S(1)} %bitcast.128, bf16[2,512,512]{2,1,0:T(8,128)(2,1)} %collective-permute-done), kind=kOutput, calls=%fused_computation.97 | convolution fusion | flops 538968064 | bytes 4718592 | tf_op jit(solution)/shard_map/dot_general | solution.py:66
  29.8 1.8 %add_convert_fusion.2 = bf16[1024,512]{1,0:T(8,128)(2,1)S(1)} fusion(f32[1024,512]{1,0:T(8,128)S(1)} %fusion.96, f32[1024,512]{1,0:T(8,128)S(1)} %copy-done, f32[1024,512]{1,0:T(8,128)S(1)} %copy-done.1, bf16[1024,512]{0,1:T(8,128)(2,1)S(1)} %bitcast_negate_fusion, bf16[1024,512]{0,1:T(8,128)(2,1)S(1)} %bitcast.126, ...), kind=kOutput, calls=%fused_computation.74 | convolution fusion | flops 541065216 | bytes 9961472 | tf_op jit(solution)/shard_map/dot_general | solution.py:65
  31.6 0.5 copy.41
  32.2 1.5 %collective-permute-start.1 = (bf16[1024,512]{1,0:T(8,128)(2,1)S(1)}, bf16[1024,512]{1,0:T(8,128)(2,1)S(1)}, u32[]{:S(2)}, u32[]{:S(2)}) collective-permute-start(bf16[1024,512]{1,0:T(8,128)(2,1)S(1)} %bitcast.130), channel_id=1, source_target_pairs={{0,16},{16,0},{32,48},{48,32},{64,80},{80,64},{96,112},{112,96},{1... | collective-permute-start | bytes 3145736 | tf_op jit(solution)/shard_map/ppermute | solution.py:16
  33.7 1.7 %fusion.338 = (bf16[512,512]{1,0:T(8,128)(2,1)S(1)}, bf16[512,512]{1,0:T(8,128)(2,1)S(1)}, bf16[512,512]{1,0:T(8,128)(2,1)S(1)}) fusion(bf16[512]{0:T(512)(128)(2,1)S(1)} %get-tuple-element.74, bf16[512]{0:T(512)(128)(2,1)S(1)} %get-tuple-element.75, bf16[512]{0:T(512)(128)(2,1)S(1)} %get-tuple-element.76, bf16[512]{0:T(512)(128)(2,1)S(1)} %get-tuple-element.77, ...), kind=kLoop, calls=%fused_computation.535 | loop fusion | flops 7340032 | bytes 1591296 | tf_op jit(solution)/shard_map/neg | solution.py:43
  35.4 2.6 %fusion.8 = f32[1024,512]{1,0:T(8,128)S(1)} fusion(bf16[1024,512]{1,0:T(8,128)(2,1)S(1)} %bitcast.131, bf16[512,512]{1,0:T(8,128)(2,1)} %get-tuple-element.213, bf16[512,512]{1,0:T(8,128)(2,1)S(1)} %copy-done.4, bf16[512,512]{1,0:T(8,128)(2,1)S(1)} %copy-done.3), kind=kOutput, calls=%fused_computation.8 | convolution fusion | flops 1082130432 | bytes 4718592 | tf_op jit(solution)/shard_map/dot_general | solution.py:90
  38.0 1.2 add_convert_fusion.1
  39.3 1.8 %collective-permute-start.2 = (bf16[1024,512]{1,0:T(8,128)(2,1)S(1)}, bf16[1024,512]{1,0:T(8,128)(2,1)S(1)}, u32[]{:S(2)}, u32[]{:S(2)}) collective-permute-start(bf16[1024,512]{1,0:T(8,128)(2,1)S(1)} %add_convert_fusion.1), channel_id=1, source_target_pairs={{0,32},{16,48},{32,0},{48,16},{64,96},{80,112},{96,64},{112,80},{1... | collective-permute-start | bytes 3145736 | tf_op jit(solution)/shard_map/ppermute | solution.py:16
  41.1 1.2 fusion
  42.4 3.6 %collective-permute-start.5 = (bf16[2,2,512,8]{2,3,1,0:T(8,128)(2,1)S(1)}, bf16[2,2,512,8]{2,3,1,0:T(8,128)(2,1)S(1)}, u32[]{:S(2)}, u32[]{:S(2)}) collective-permute-start(bf16[2,2,512,8]{2,3,1,0:T(8,128)(2,1)S(1)} %slice_bitcast_fusion.4), channel_id=1, source_target_pairs={{0,64},{16,80},{32,96},{48,112},{64,0},{80,16},{96,32},{112,48},{1... | collective-permute-start | bytes 98312 | tf_op jit(solution)/shard_map/ppermute | solution.py:16
  46.3 1.7 %fusion.334 = (bf16[512,512]{1,0:T(8,128)(2,1)S(1)}, bf16[512,512]{1,0:T(8,128)(2,1)S(1)}, bf16[512,512]{1,0:T(8,128)(2,1)S(1)}) fusion(bf16[512]{0:T(512)(128)(2,1)S(1)} %get-tuple-element.42, bf16[512]{0:T(512)(128)(2,1)S(1)} %get-tuple-element.43, bf16[512]{0:T(512)(128)(2,1)S(1)} %get-tuple-element.44, bf16[512]{0:T(512)(128)(2,1)S(1)} %get-tuple-element.45, ...), kind=kLoop, calls=%fused_computation.531 | loop fusion | flops 7340032 | bytes 1591296 | tf_op jit(solution)/shard_map/neg | solution.py:43
  48.1 1.7 %fusion.339 = (bf16[512,512]{1,0:T(8,128)(2,1)S(1)}, bf16[512,512]{1,0:T(8,128)(2,1)S(1)}, bf16[512,512]{1,0:T(8,128)(2,1)S(1)}) fusion(bf16[512]{0:T(512)(128)(2,1)S(1)} %get-tuple-element.26, bf16[512]{0:T(512)(128)(2,1)S(1)} %get-tuple-element.27, bf16[512]{0:T(512)(128)(2,1)S(1)} %get-tuple-element.28, bf16[512]{0:T(512)(128)(2,1)S(1)} %get-tuple-element.29, ...), kind=kLoop, calls=%fused_computation.536 | loop fusion | flops 7340032 | bytes 1591296 | tf_op jit(solution)/shard_map/neg | solution.py:43
  49.8 18.4 %collective-permute-done.4 = s32[1536]{0:T(1024)S(1)} collective-permute-done((s32[1536]{0:T(1024)S(1)}, s32[1536]{0:T(1024)S(1)}, u32[]{:S(2)}, u32[]{:S(2)}) %collective-permute-start.4) | collective-permute-done | bytes 6176 | tf_op jit(solution)/shard_map/ppermute | solution.py:16
  68.4 1.7 %fusion.341 = (bf16[512,512]{1,0:T(8,128)(2,1)S(1)}, bf16[512,512]{1,0:T(8,128)(2,1)S(1)}, bf16[512,512]{1,0:T(8,128)(2,1)S(1)}) fusion(bf16[512]{0:T(512)(128)(2,1)S(1)} %get-tuple-element.90, bf16[512]{0:T(512)(128)(2,1)S(1)} %get-tuple-element.91, bf16[512]{0:T(512)(128)(2,1)S(1)} %get-tuple-element.92, bf16[512]{0:T(512)(128)(2,1)S(1)} %get-tuple-element.93, ...), kind=kLoop, calls=%fused_computation.538 | loop fusion | flops 7340032 | bytes 1591296 | tf_op jit(solution)/shard_map/neg | solution.py:43
  70.2 1.2 add_convert_fusion
  71.5 0.9 constant_dynamic-slice_fusion
  72.4 2.7 %fusion.340 = (bf16[512,512]{1,0:T(8,128)(2,1)}, bf16[512,512]{1,0:T(8,128)(2,1)}, bf16[512,512]{1,0:T(8,128)(2,1)}) fusion(bf16[512]{0:T(512)(128)(2,1)S(1)} %get-tuple-element.58, bf16[512]{0:T(512)(128)(2,1)S(1)} %get-tuple-element.59, bf16[512]{0:T(512)(128)(2,1)S(1)} %get-tuple-element.60, bf16[512]{0:T(512)(128)(2,1)S(1)} %get-tuple-element.61, ...), kind=kLoop, calls=%fused_computation.537 | loop fusion | flops 7340032 | bytes 1591296 | tf_op jit(solution)/shard_map/neg | solution.py:43
  75.1 1.7 %fusion.24 = f32[1024,256]{1,0:T(8,128)} fusion(bf16[512,512]{1,0:T(8,128)(2,1)S(1)} %get-tuple-element.207, bf16[512,512]{1,0:T(8,128)(2,1)S(1)} %get-tuple-element.180, bf16[512,512]{1,0:T(8,128)(2,1)S(1)} %get-tuple-element.179, bf16[1024,512]{1,0:T(8,128)(2,1)S(1)} %add_convert_fusion, s32[]{:T(128)S(6)} %select_n.476), kind=kOutput, calls=%fused_computation.28 | convolution fusion | flops 545259520 | bytes 3145732 | tf_op jit(solution)/shard_map/dot_general | solution.py:116
  76.8 12.7 %all-to-all-start = ((s32[128,1,8]{2,1,0:T(1,128)}), s32[128,1,8]{2,1,0:T(1,128)S(1)}, u32[]{:S(2)}, u32[]{:S(2)}) async-start(s32[128,1,8]{2,1,0:T(1,128)} %bitcast.35), calls=%async_computation | async-start | bytes 131072 | tf_op jit(solution)/shard_map/all_to_all | solution.py:119
  89.5 1.9 %fusion.56 = f32[1024,256]{1,0:T(8,128)S(1)} fusion(bf16[512,512]{1,0:T(8,128)(2,1)S(1)} %get-tuple-element.210, bf16[512,512]{1,0:T(8,128)(2,1)S(1)} %get-tuple-element.186, bf16[512,512]{1,0:T(8,128)(2,1)S(1)} %get-tuple-element.185, bf16[1024,512]{1,0:T(8,128)(2,1)} %copy-done.14, s32[]{:T(128)S(6)} %select_n.476), kind=kOutput, calls=%fused_computation.60 | convolution fusion | flops 545259520 | bytes 3145732 | tf_op jit(solution)/shard_map/dot_general | solution.py:120
  91.4 1.7 %fusion.87 = bf16[1024,256]{1,0:T(8,128)(2,1)S(1)} fusion(f32[1024,256]{1,0:T(8,128)S(1)} %fusion.56, bf16[1024,256]{1,0:T(8,128)(2,1)} %collective-permute-done.3, bf16[512,512]{1,0:T(8,128)(2,1)S(1)} %copy-done.13, bf16[512,512]{1,0:T(8,128)(2,1)S(1)} %copy-done.12, bf16[512,512]{1,0:T(8,128)(2,1)S(1)} %copy-done.11), kind=kOutput, calls=%fused_computation.91 | convolution fusion | flops 545783808 | bytes 3670016 | tf_op jit(solution)/shard_map/dot_general | solution.py:116
  93.4 2.1 %fusion.84 = bf16[1024,256]{1,0:T(8,128)(2,1)S(1)} fusion(f32[1024,256]{1,0:T(8,128)} %fusion.24, bf16[1024,256]{1,0:T(8,128)(2,1)} %collective-permute-done.3, bf16[512,512]{1,0:T(8,128)(2,1)S(1)} %get-tuple-element.206, bf16[512,512]{1,0:T(8,128)(2,1)S(1)} %get-tuple-element.178, bf16[512,512]{1,0:T(8,128)(2,1)S(1)} %get-tuple-element.177), kind=kOutput, calls=%fused_computation.90 | convolution fusion | flops 545783808 | bytes 3670016 | tf_op jit(solution)/shard_map/dot_general | solution.py:120
  95.7 0.8 fusion.74
  96.5 0.8 fusion.75
  97.3 1.7 %pad_maximum_fusion = bf16[128,16,512]{2,1,0:T(8,128)(2,1)} fusion(bf16[128,8,512]{2,1,0:T(8,128)(2,1)S(1)} %fusion.75, bf16[128,8,512]{2,1,0:T(8,128)(2,1)S(1)} %fusion.74), kind=kLoop, calls=%fused_computation.68 | loop fusion | flops 4194304 | bytes 4194304 | tf_op jit(solution)/shard_map/concatenate | solution.py:130
  99.1 9.6 %all-to-all-start.1 = ((bf16[128,16,512]{2,1,0:T(8,128)(2,1)}), bf16[128,16,512]{2,1,0:T(8,128)(2,1)S(1)}, u32[]{:S(2)}, u32[]{:S(2)}) async-start(bf16[128,16,512]{2,1,0:T(8,128)(2,1)} %pad_maximum_fusion), calls=%async_computation.1 | async-start | bytes 4194304 | tf_op jit(solution)/shard_map/all_to_all | solution.py:131
  110.4 28.0 %all-to-all-done.1 = bf16[128,16,512]{2,1,0:T(8,128)(2,1)S(1)} async-done(((bf16[128,16,512]{2,1,0:T(8,128)(2,1)}), bf16[128,16,512]{2,1,0:T(8,128)(2,1)S(1)}, u32[]{:S(2)}, u32[]{:S(2)}) %all-to-all-start.1) | async-done | bytes 2097184 | tf_op jit(solution)/shard_map/all_to_all | solution.py:131
  138.6 0.8 fusion.82
  139.6 0.8 fusion.83
  140.6 1.1 maximum_bitcast_fusion
  (104 shorter events, 5.2 us)
Async XLA Ops:
  0.0 27.4 %collective-permute-start = (bf16[2,512,512]{2,1,0:T(8,128)(2,1)}, bf16[2,512,512]{2,1,0:T(8,128)(2,1)}, u32[]{:S(2)}, u32[]{:S(2)}) collective-permute-start(bf16[2,512,512]{2,1,0:T(8,128)(2,1)} %param.6), channel_id=1, source_target_pairs={{1,0},{2,1},{3,2},{4,3},{5,4},{6,5},{7,6},{8,7},{9,8},{10,9},{11,1... | collective-permute-start | bytes 3145736 | tf_op jit(solution)/shard_map/ppermute | solution.py:12
  10.8 1.2 copy-start.2
  14.2 2.0 %copy-start.15 = (bf16[3,1,2,2,512,8]{4,5,3,2,1,0:T(8,128)(2,1)S(1)}, bf16[3,1,2,2,512,8]{4,5,3,2,1,0:T(8,128)(2,1)}, u32[]{:S(2)}) copy-start(bf16[3,1,2,2,512,8]{4,5,3,2,1,0:T(8,128)(2,1)} %param.9) | copy-start | bytes 294916
  14.2 2.1 %copy-start.16 = (s32[3,1,2,512]{3,2,1,0:T(2,128)S(1)}, s32[3,1,2,512]{3,2,1,0:T(2,128)}, u32[]{:S(2)}) copy-start(s32[3,1,2,512]{3,2,1,0:T(2,128)} %param.8) | copy-start | bytes 36868
  14.2 2.1 %copy-start.17 = (s32[1,1,512]{2,1,0:T(1,128)S(1)}, s32[1,1,512]{2,1,0:T(1,128)}, u32[]{:S(2)}) copy-start(s32[1,1,512]{2,1,0:T(1,128)} %param.11) | copy-start | bytes 6148
  27.4 1.9 %copy-start = (f32[1024,512]{1,0:T(8,128)S(1)}, f32[1024,512]{1,0:T(8,128)}, u32[]{:S(2)}) copy-start(f32[1024,512]{1,0:T(8,128)} %fusion.94) | copy-start | bytes 6291460
  27.4 2.4 %copy-start.1 = (f32[1024,512]{1,0:T(8,128)S(1)}, f32[1024,512]{1,0:T(8,128)}, u32[]{:S(2)}) copy-start(f32[1024,512]{1,0:T(8,128)} %fusion.91) | copy-start | bytes 6291460
  31.6 3.7 %copy-start.3 = (bf16[512,512]{1,0:T(8,128)(2,1)S(1)}, bf16[512,512]{1,0:T(8,128)(2,1)}, u32[]{:S(2)}) copy-start(bf16[512,512]{1,0:T(8,128)(2,1)} %get-tuple-element.191) | copy-start | bytes 1572868
  31.6 3.7 %copy-start.4 = (bf16[512,512]{1,0:T(8,128)(2,1)S(1)}, bf16[512,512]{1,0:T(8,128)(2,1)}, u32[]{:S(2)}) copy-start(bf16[512,512]{1,0:T(8,128)(2,1)} %get-tuple-element.192) | copy-start | bytes 1572868
  32.2 5.8 %collective-permute-start.1 = (bf16[1024,512]{1,0:T(8,128)(2,1)S(1)}, bf16[1024,512]{1,0:T(8,128)(2,1)S(1)}, u32[]{:S(2)}, u32[]{:S(2)}) collective-permute-start(bf16[1024,512]{1,0:T(8,128)(2,1)S(1)} %bitcast.130), channel_id=1, source_target_pairs={{0,16},{16,0},{32,48},{48,32},{64,80},{80,64},{96,112},{112,96},{1... | collective-permute-start | bytes 3145736 | tf_op jit(solution)/shard_map/ppermute | solution.py:16
  35.4 2.6 %copy-start.5 = (bf16[512,512]{1,0:T(8,128)(2,1)S(1)}, bf16[512,512]{1,0:T(8,128)(2,1)}, u32[]{:S(2)}) copy-start(bf16[512,512]{1,0:T(8,128)(2,1)} %get-tuple-element.189) | copy-start | bytes 1572868
  35.4 2.6 %copy-start.6 = (bf16[512,512]{1,0:T(8,128)(2,1)S(1)}, bf16[512,512]{1,0:T(8,128)(2,1)}, u32[]{:S(2)}) copy-start(bf16[512,512]{1,0:T(8,128)(2,1)} %get-tuple-element.190) | copy-start | bytes 1572868
  35.4 2.6 %copy-start.7 = (bf16[512,512]{1,0:T(8,128)(2,1)S(1)}, bf16[512,512]{1,0:T(8,128)(2,1)}, u32[]{:S(2)}) copy-start(bf16[512,512]{1,0:T(8,128)(2,1)} %get-tuple-element.212) | copy-start | bytes 1572868
  38.0 3.1 %copy-start.8 = (bf16[512,512]{1,0:T(8,128)(2,1)S(1)}, bf16[512,512]{1,0:T(8,128)(2,1)}, u32[]{:S(2)}) copy-start(bf16[512,512]{1,0:T(8,128)(2,1)} %get-tuple-element.187) | copy-start | bytes 1572868
  38.0 3.1 %copy-start.9 = (bf16[512,512]{1,0:T(8,128)(2,1)S(1)}, bf16[512,512]{1,0:T(8,128)(2,1)}, u32[]{:S(2)}) copy-start(bf16[512,512]{1,0:T(8,128)(2,1)} %get-tuple-element.188) | copy-start | bytes 1572868
  38.0 3.1 %copy-start.10 = (bf16[512,512]{1,0:T(8,128)(2,1)S(1)}, bf16[512,512]{1,0:T(8,128)(2,1)}, u32[]{:S(2)}) copy-start(bf16[512,512]{1,0:T(8,128)(2,1)} %get-tuple-element.211) | copy-start | bytes 1572868
  39.3 30.9 %collective-permute-start.2 = (bf16[1024,512]{1,0:T(8,128)(2,1)S(1)}, bf16[1024,512]{1,0:T(8,128)(2,1)S(1)}, u32[]{:S(2)}, u32[]{:S(2)}) collective-permute-start(bf16[1024,512]{1,0:T(8,128)(2,1)S(1)} %add_convert_fusion.1), channel_id=1, source_target_pairs={{0,32},{16,48},{32,0},{48,16},{64,96},{80,112},{96,64},{112,80},{1... | collective-permute-start | bytes 3145736 | tf_op jit(solution)/shard_map/ppermute | solution.py:16
  42.4 25.8 %collective-permute-start.5 = (bf16[2,2,512,8]{2,3,1,0:T(8,128)(2,1)S(1)}, bf16[2,2,512,8]{2,3,1,0:T(8,128)(2,1)S(1)}, u32[]{:S(2)}, u32[]{:S(2)}) collective-permute-start(bf16[2,2,512,8]{2,3,1,0:T(8,128)(2,1)S(1)} %slice_bitcast_fusion.4), channel_id=1, source_target_pairs={{0,64},{16,80},{32,96},{48,112},{64,0},{80,16},{96,32},{112,48},{1... | collective-permute-start | bytes 98312 | tf_op jit(solution)/shard_map/ppermute | solution.py:16
  46.0 22.2 %collective-permute-start.4 = (s32[1536]{0:T(1024)S(1)}, s32[1536]{0:T(1024)S(1)}, u32[]{:S(2)}, u32[]{:S(2)}) collective-permute-start(s32[1536]{0:T(1024)S(1)} %pad_add_fusion.2), channel_id=1, source_target_pairs={{0,64},{16,80},{32,96},{48,112},{64,0},{80,16},{96,32},{112,48},{1... | collective-permute-start | bytes 18440 | tf_op jit(solution)/shard_map/ppermute | solution.py:16
  71.5 5.4 %copy-start.14 = (bf16[1024,512]{1,0:T(8,128)(2,1)}, bf16[1024,512]{1,0:T(8,128)(2,1)S(1)}, u32[]{:S(2)}) copy-start(bf16[1024,512]{1,0:T(8,128)(2,1)S(1)} %add_convert_fusion) | copy-start | bytes 3145732
  72.4 19.0 %collective-permute-start.3 = (bf16[1024,256]{1,0:T(8,128)(2,1)}, bf16[1024,256]{1,0:T(8,128)(2,1)}, u32[]{:S(2)}, u32[]{:S(2)}) collective-permute-start(bf16[1024,256]{1,0:T(8,128)(2,1)} %constant_dynamic-slice_fusion), channel_id=1, source_target_pairs={{0,64},{16,80},{32,96},{48,112},{64,0},{80,16},{96,32},{112,48},{1... | collective-permute-start | bytes 1572872 | tf_op jit(solution)/shard_map/ppermute | solution.py:16
  76.8 22.3 %all-to-all-start = ((s32[128,1,8]{2,1,0:T(1,128)}), s32[128,1,8]{2,1,0:T(1,128)S(1)}, u32[]{:S(2)}, u32[]{:S(2)}) async-start(s32[128,1,8]{2,1,0:T(1,128)} %bitcast.35), calls=%async_computation | async-start | bytes 131072 | tf_op jit(solution)/shard_map/all_to_all | solution.py:119
  89.5 1.9 %copy-start.11 = (bf16[512,512]{1,0:T(8,128)(2,1)S(1)}, bf16[512,512]{1,0:T(8,128)(2,1)}, u32[]{:S(2)}) copy-start(bf16[512,512]{1,0:T(8,128)(2,1)} %get-tuple-element.181) | copy-start | bytes 1572868
  89.5 1.9 %copy-start.12 = (bf16[512,512]{1,0:T(8,128)(2,1)S(1)}, bf16[512,512]{1,0:T(8,128)(2,1)}, u32[]{:S(2)}) copy-start(bf16[512,512]{1,0:T(8,128)(2,1)} %get-tuple-element.182) | copy-start | bytes 1572868
  89.5 1.9 %copy-start.13 = (bf16[512,512]{1,0:T(8,128)(2,1)S(1)}, bf16[512,512]{1,0:T(8,128)(2,1)}, u32[]{:S(2)}) copy-start(bf16[512,512]{1,0:T(8,128)(2,1)} %get-tuple-element.208) | copy-start | bytes 1572868
  99.1 39.3 %all-to-all-start.1 = ((bf16[128,16,512]{2,1,0:T(8,128)(2,1)}), bf16[128,16,512]{2,1,0:T(8,128)(2,1)S(1)}, u32[]{:S(2)}, u32[]{:S(2)}) async-start(bf16[128,16,512]{2,1,0:T(8,128)(2,1)} %pad_maximum_fusion), calls=%async_computation.1 | async-start | bytes 4194304 | tf_op jit(solution)/shard_map/all_to_all | solution.py:131

commit v16 on v14

--- a/solution.py
+++ b/solution.py
@@ -97,7 +97,12 @@
         merged = merged + jnp.dot(theirs, partner, preferred_element_type=jnp.float32)
         image = merged.astype(jnp.bfloat16)
     slots = jnp.arange(devices * capacity, dtype=jnp.int32)[:, None]
-    picks = {0: slots == slot[None, :], bit: slots == far_slot[None, :]}
+    rows_at = jnp.concatenate(
+        [(s // capacity) * (2 * capacity) + i * capacity + s % capacity for i, s in enumerate((slot, far_slot))]
+    )
+    pick_both = (
+        jnp.arange(2 * devices * capacity, dtype=jnp.int32)[:, None] == rows_at[None, :]
+    ).astype(jnp.bfloat16)
     half = r_dev // 2
     keep_bit = (me_sub >> last) & 1
     kept = lax.dynamic_slice_in_dim(image, keep_bit * half, half, axis=1)
@@ -119,14 +124,14 @@
         merged = merged + jnp.dot(theirs, old[m ^ bit], preferred_element_type=jnp.float32)
         piece = merged.astype(jnp.bfloat16)
         rows = piece.reshape(2, p_dev, half).transpose(1, 0, 2).reshape(p_dev, 2 * half)
-        send = jnp.dot(picks[m].astype(jnp.bfloat16), rows, preferred_element_type=jnp.float32)
-        sends.append(send.astype(jnp.bfloat16).reshape(devices, capacity, 2 * half))
+        sends.append(rows)
     grid = marks.reshape(n_sub, n_rng * capacity)
     swapped = jnp.stack([grid[s ^ bit] for s in range(n_sub)], axis=0)
     marks = jnp.stack(
         [grid.reshape(devices, capacity), swapped.reshape(devices, capacity)], axis=1
     ).reshape(devices, 2 * capacity)
-    payload = jnp.concatenate(sends, axis=1)
+    payload = jnp.dot(pick_both, jnp.concatenate(sends, axis=0), preferred_element_type=jnp.float32)
+    payload = payload.astype(jnp.bfloat16).reshape(devices, 2 * capacity, 2 * half)
     got = lax.all_to_all(payload, ("sub", "rng"), split_axis=0, concat_axis=0, tiled=True)
     span = devices // 2
     tiles = []

time: 138 us -> 139 us (level)
  matrix products: 19.9 us -> 22.1 us
  other arithmetic: 21.3 us -> 19.6 us
    dot_general x2 -> x1, matrix products: 1.5 us -> 3.72 us  [on_device(): jnp.dot(pick_both, jnp.concatenate(sends, axis=0), preferred_element_type...]
    concatenate x1, other arithmetic: 1.68 us -> 0.01 us  [on_device(): jnp.concatenate([s // capacity * (2 * capacity) + i * capacity + s % capa...]
  transfers between devices with their start and end apart: 8 -> 8, of which waited for: 4 -> 3; matrix products, arithmetic and copies ran while one was open for 34% -> 34% of each run, Pallas kernels for 0% -> 0%
where the time goes in v16:
time: 139 us; the launch traced here: 138 us
  waiting for transfers between devices  50.2 us (36%)
  starting transfers between devices  31.1 us (22%)
  matrix products  22.1 us (16%)
  other arithmetic  19.6 us (14%)
  local copies, waits for them, and re-layouts  14.7 us (11%)
    all_to_all x1, waiting for transfers between devices, on_device(): lax.all_to_all(payload, ('sub', 'rng'), split_axis=0, concat_axis=0, tile...  27.9 us
    ppermute x5, waiting for transfers between devices, from_partner(): lax.ppermute(value, axis, [(i, i ^ 1 << apart) for i in range(lax.axis_si...  18.4 us
    neg x8, other arithmetic, merge_matrix(): upper = jnp.concatenate([g_real, -g_imag], axis=1)  15.9 us
    all_to_all x1, starting transfers between devices, on_device(): lax.all_to_all(labels, ('sub', 'rng'), split_axis=0, concat_axis=0, tiled...  12.6 us
    all_to_all x1, starting transfers between devices, on_device(): lax.all_to_all(payload, ('sub', 'rng'), split_axis=0, concat_axis=0, tile...  9.77 us
    ppermute x5, starting transfers between devices, from_partner(): lax.ppermute(value, axis, [(i, i ^ 1 << apart) for i in range(lax.axis_si...  7.36 us
    dot_general x2, matrix products, on_device(): jnp.dot(theirs, old[m ^ bit], preferred_element_type=jnp.float32)  3.96 us
    ppermute x1, waiting for transfers between devices, shifted(): lax.ppermute(value, axis, [(source, source + steps) for source in range(f...  3.91 us
  transfers between devices with their start and end apart: 8, of which 3 were waited for; matrix products, arithmetic and copies ran while one was open for 34% of the time, Pallas kernels for 0%

profile of v16, /device:TPU:1, one launch (start us, length us, event | category | flops | bytes accessed | tf_op | source)
XLA Modules:
  0.0 138.4 jit_solution(6802434224840463209)
XLA Ops:
  0.0 1.4 %collective-permute-start = (bf16[2,512,512]{2,1,0:T(8,128)(2,1)}, bf16[2,512,512]{2,1,0:T(8,128)(2,1)}, u32[]{:S(2)}, u32[]{:S(2)}) collective-permute-start(bf16[2,512,512]{2,1,0:T(8,128)(2,1)} %param.6), channel_id=1, source_target_pairs={{1,0},{2,1},{3,2},{4,3},{5,4},{6,5},{7,6},{8,7},{9,8},{10,9},{11,1... | collective-permute-start | bytes 3145736 | tf_op jit(solution)/shard_map/ppermute | solution.py:12
  1.4 2.2 %slice_bitcast_fusion.3 = (bf16[512,512]{1,0:T(8,128)(2,1)}, bf16[512,512]{1,0:T(8,128)(2,1)}) fusion(bf16[2,512,512]{2,1,0:T(8,128)(2,1)} %param.6), kind=kLoop, calls=%fused_computation.319 | loop fusion | bytes 2097152 | tf_op jit(solution)/shard_map/squeeze | solution.py:66
  4.2 0.2 fusion.310
  4.5 1.3 tile.9
  6.0 0.5 reshape.173
  6.6 1.3 tile.21
  7.9 1.0 slice.1019
  9.0 1.5 %reshape.174 = bf16[512,1024]{1,0:T(8,128)(2,1)S(1)} reshape(bf16[524288]{0:T(1024)(128)(2,1)} %slice.1019) | data formatting | bytes 2097152 | tf_op jit(solution)/shard_map/reshape | solution.py:25
  10.6 0.3 select_reduce_fusion
  11.3 1.5 %fusion.102 = (bf16[512,1024]{0,1:T(8,128)(2,1)}, bf16[512,1024]{0,1:T(8,128)(2,1)}) fusion(bf16[1024,512]{0,1:T(8,128)(2,1)S(1)} %bitcast.117, bf16[1024,512]{0,1:T(8,128)(2,1)S(1)} %bitcast_negate_fusion, bf16[1024,512]{0,1:T(8,128)(2,1)S(1)} %bitcast.115), kind=kLoop, calls=%fused_computation.100 | loop fusion | flops 4194304 | bytes 5242880 | tf_op jit(solution)/shard_map/concatenate | solution.py:28
  12.8 2.7 %fusion.354 = (bf16[512,512]{1,0:T(8,128)(2,1)}, bf16[512,512]{1,0:T(8,128)(2,1)}, bf16[512,512]{1,0:T(8,128)(2,1)}) fusion(bf16[512]{0:T(512)(128)(2,1)S(1)} %get-tuple-element.138, bf16[512]{0:T(512)(128)(2,1)S(1)} %get-tuple-element.139, bf16[512]{0:T(512)(128)(2,1)S(1)} %get-tuple-element.140, bf16[512]{0:T(512)(128)(2,1)S(1)} %get-tuple-element.141, ...), kind=kLoop, calls=%fused_computation.563 | loop fusion | flops 7340032 | bytes 1591296 | tf_op jit(solution)/shard_map/neg | solution.py:43
  15.6 0.7 sub.147
  16.3 3.1 %fusion.28 = f32[512,1024]{1,0:T(8,128)S(1)} fusion(bf16[512,1024]{0,1:T(8,128)(2,1)} %get-tuple-element.162, bf16[512,1024]{0,1:T(8,128)(2,1)} %get-tuple-element.161, bf16[512,512]{1,0:T(8,128)(2,1)} %get-tuple-element.160, bf16[512,512]{1,0:T(8,128)(2,1)} %get-tuple-element.159), kind=kOutput, calls=%fused_computation.33 | convolution fusion | flops 1080033280 | bytes 5242880 | tf_op jit(solution)/shard_map/dot_general | solution.py:65
  19.4 1.7 %fusion.355 = (bf16[512,512]{1,0:T(8,128)(2,1)S(1)}, bf16[512,512]{1,0:T(8,128)(2,1)S(1)}, bf16[512,512]{1,0:T(8,128)(2,1)S(1)}) fusion(bf16[512]{0:T(512)(128)(2,1)S(1)} %get-tuple-element.122, bf16[512]{0:T(512)(128)(2,1)S(1)} %get-tuple-element.123, bf16[512]{0:T(512)(128)(2,1)S(1)} %get-tuple-element.124, bf16[512]{0:T(512)(128)(2,1)S(1)} %get-tuple-element.125, ...), kind=kLoop, calls=%fused_computation.564 | loop fusion | flops 7340032 | bytes 1591296 | tf_op jit(solution)/shard_map/neg | solution.py:43
  21.2 1.7 %fusion.353 = (bf16[512,512]{1,0:T(8,128)(2,1)S(1)}, bf16[512,512]{1,0:T(8,128)(2,1)S(1)}, bf16[512,512]{1,0:T(8,128)(2,1)S(1)}) fusion(bf16[512]{0:T(512)(128)(2,1)S(1)} %get-tuple-element.106, bf16[512]{0:T(512)(128)(2,1)S(1)} %get-tuple-element.107, bf16[512]{0:T(512)(128)(2,1)S(1)} %get-tuple-element.108, bf16[512]{0:T(512)(128)(2,1)S(1)} %get-tuple-element.109, ...), kind=kLoop, calls=%fused_computation.562 | loop fusion | flops 7340032 | bytes 1591296 | tf_op jit(solution)/shard_map/neg | solution.py:43
  22.9 3.9 %collective-permute-done = bf16[2,512,512]{2,1,0:T(8,128)(2,1)} collective-permute-done((bf16[2,512,512]{2,1,0:T(8,128)(2,1)}, bf16[2,512,512]{2,1,0:T(8,128)(2,1)}, u32[]{:S(2)}, u32[]{:S(2)}) %collective-permute-start) | collective-permute-done | bytes 1048608 | tf_op jit(solution)/shard_map/ppermute | solution.py:12
  26.9 1.3 slice_bitcast_fusion.1
  28.1 1.3 add_convert_fusion.2
  29.5 1.7 %collective-permute-start.1 = (bf16[1024,512]{1,0:T(8,128)(2,1)S(1)}, bf16[1024,512]{1,0:T(8,128)(2,1)S(1)}, u32[]{:S(2)}, u32[]{:S(2)}) collective-permute-start(bf16[1024,512]{1,0:T(8,128)(2,1)S(1)} %bitcast.120), channel_id=1, source_target_pairs={{0,16},{16,0},{32,48},{48,32},{64,80},{80,64},{96,112},{112,96},{1... | collective-permute-start | bytes 3145736 | tf_op jit(solution)/shard_map/ppermute | solution.py:16
  31.3 1.7 %fusion.356 = (bf16[512,512]{1,0:T(8,128)(2,1)S(1)}, bf16[512,512]{1,0:T(8,128)(2,1)S(1)}, bf16[512,512]{1,0:T(8,128)(2,1)S(1)}) fusion(bf16[512]{0:T(512)(128)(2,1)S(1)} %get-tuple-element.74, bf16[512]{0:T(512)(128)(2,1)S(1)} %get-tuple-element.75, bf16[512]{0:T(512)(128)(2,1)S(1)} %get-tuple-element.76, bf16[512]{0:T(512)(128)(2,1)S(1)} %get-tuple-element.77, ...), kind=kLoop, calls=%fused_computation.565 | loop fusion | flops 7340032 | bytes 1591296 | tf_op jit(solution)/shard_map/neg | solution.py:43
  33.0 1.2 fusion.20
  34.3 1.2 add_convert_fusion.1
  35.5 2.0 %collective-permute-start.2 = (bf16[1024,512]{1,0:T(8,128)(2,1)S(1)}, bf16[1024,512]{1,0:T(8,128)(2,1)S(1)}, u32[]{:S(2)}, u32[]{:S(2)}) collective-permute-start(bf16[1024,512]{1,0:T(8,128)(2,1)S(1)} %add_convert_fusion.1), channel_id=1, source_target_pairs={{0,32},{16,48},{32,0},{48,16},{64,96},{80,112},{96,64},{112,80},{1... | collective-permute-start | bytes 3145736 | tf_op jit(solution)/shard_map/ppermute | solution.py:16
  37.5 1.2 fusion.12
  38.7 3.4 %collective-permute-start.5 = (bf16[2,2,512,8]{2,3,1,0:T(8,128)(2,1)S(1)}, bf16[2,2,512,8]{2,3,1,0:T(8,128)(2,1)S(1)}, u32[]{:S(2)}, u32[]{:S(2)}) collective-permute-start(bf16[2,2,512,8]{2,3,1,0:T(8,128)(2,1)S(1)} %slice_bitcast_fusion.4), channel_id=1, source_target_pairs={{0,64},{16,80},{32,96},{48,112},{64,0},{80,16},{96,32},{112,48},{1... | collective-permute-start | bytes 98312 | tf_op jit(solution)/shard_map/ppermute | solution.py:16
  42.1 0.3 collective-permute-start.3
  42.6 1.7 %fusion.352 = (bf16[512,512]{1,0:T(8,128)(2,1)S(1)}, bf16[512,512]{1,0:T(8,128)(2,1)S(1)}, bf16[512,512]{1,0:T(8,128)(2,1)S(1)}) fusion(bf16[512]{0:T(512)(128)(2,1)S(1)} %get-tuple-element.42, bf16[512]{0:T(512)(128)(2,1)S(1)} %get-tuple-element.43, bf16[512]{0:T(512)(128)(2,1)S(1)} %get-tuple-element.44, bf16[512]{0:T(512)(128)(2,1)S(1)} %get-tuple-element.45, ...), kind=kLoop, calls=%fused_computation.561 | loop fusion | flops 7340032 | bytes 1591296 | tf_op jit(solution)/shard_map/neg | solution.py:43
  44.4 1.7 %fusion.357 = (bf16[512,512]{1,0:T(8,128)(2,1)S(1)}, bf16[512,512]{1,0:T(8,128)(2,1)S(1)}, bf16[512,512]{1,0:T(8,128)(2,1)S(1)}) fusion(bf16[512]{0:T(512)(128)(2,1)S(1)} %get-tuple-element.26, bf16[512]{0:T(512)(128)(2,1)S(1)} %get-tuple-element.27, bf16[512]{0:T(512)(128)(2,1)S(1)} %get-tuple-element.28, bf16[512]{0:T(512)(128)(2,1)S(1)} %get-tuple-element.29, ...), kind=kLoop, calls=%fused_computation.566 | loop fusion | flops 7340032 | bytes 1591296 | tf_op jit(solution)/shard_map/neg | solution.py:43
  46.2 18.4 %collective-permute-done.3 = s32[1536]{0:T(1024)S(1)} collective-permute-done((s32[1536]{0:T(1024)S(1)}, s32[1536]{0:T(1024)S(1)}, u32[]{:S(2)}, u32[]{:S(2)}) %collective-permute-start.3) | collective-permute-done | bytes 6176 | tf_op jit(solution)/shard_map/ppermute | solution.py:16
  64.8 1.7 %fusion.359 = (bf16[512,512]{1,0:T(8,128)(2,1)S(1)}, bf16[512,512]{1,0:T(8,128)(2,1)S(1)}, bf16[512,512]{1,0:T(8,128)(2,1)S(1)}) fusion(bf16[512]{0:T(512)(128)(2,1)S(1)} %get-tuple-element.90, bf16[512]{0:T(512)(128)(2,1)S(1)} %get-tuple-element.91, bf16[512]{0:T(512)(128)(2,1)S(1)} %get-tuple-element.92, bf16[512]{0:T(512)(128)(2,1)S(1)} %get-tuple-element.93, ...), kind=kLoop, calls=%fused_computation.568 | loop fusion | flops 7340032 | bytes 1591296 | tf_op jit(solution)/shard_map/neg | solution.py:43
  66.6 1.2 add_convert_fusion
  67.8 0.9 constant_dynamic-slice_fusion
  68.7 2.7 %fusion.358 = (bf16[512,512]{1,0:T(8,128)(2,1)}, bf16[512,512]{1,0:T(8,128)(2,1)}, bf16[512,512]{1,0:T(8,128)(2,1)}) fusion(bf16[512]{0:T(512)(128)(2,1)S(1)} %get-tuple-element.58, bf16[512]{0:T(512)(128)(2,1)S(1)} %get-tuple-element.59, bf16[512]{0:T(512)(128)(2,1)S(1)} %get-tuple-element.60, bf16[512]{0:T(512)(128)(2,1)S(1)} %get-tuple-element.61, ...), kind=kLoop, calls=%fused_computation.567 | loop fusion | flops 7340032 | bytes 1591296 | tf_op jit(solution)/shard_map/neg | solution.py:43
  71.5 1.7 %fusion.40 = f32[1024,256]{1,0:T(8,128)} fusion(bf16[512,512]{1,0:T(8,128)(2,1)S(1)} %get-tuple-element.213, bf16[512,512]{1,0:T(8,128)(2,1)S(1)} %get-tuple-element.186, bf16[512,512]{1,0:T(8,128)(2,1)S(1)} %get-tuple-element.185, bf16[1024,512]{1,0:T(8,128)(2,1)S(1)} %add_convert_fusion, s32[]{:T(128)S(6)} %select_n.495), kind=kOutput, calls=%fused_computation.45 | convolution fusion | flops 545259520 | bytes 3145732 | tf_op jit(solution)/shard_map/dot_general | solution.py:120
  73.2 12.6 %all-to-all-start = ((s32[128,1,8]{2,1,0:T(1,128)}), s32[128,1,8]{2,1,0:T(1,128)S(1)}, u32[]{:S(2)}, u32[]{:S(2)}) async-start(s32[128,1,8]{2,1,0:T(1,128)} %bitcast.33), calls=%async_computation | async-start | bytes 131072 | tf_op jit(solution)/shard_map/all_to_all | solution.py:123
  85.8 1.9 %fusion.72 = f32[1024,256]{1,0:T(8,128)S(1)} fusion(bf16[512,512]{1,0:T(8,128)(2,1)S(1)} %get-tuple-element.216, bf16[512,512]{1,0:T(8,128)(2,1)S(1)} %get-tuple-element.192, bf16[512,512]{1,0:T(8,128)(2,1)S(1)} %get-tuple-element.191, bf16[1024,512]{1,0:T(8,128)(2,1)} %copy-done.6, s32[]{:T(128)S(6)} %select_n.495), kind=kOutput, calls=%fused_computation.77 | convolution fusion | flops 545259520 | bytes 3145732 | tf_op jit(solution)/shard_map/dot_general | solution.py:124
  87.7 1.7 %fusion.99 = bf16[1024,256]{1,0:T(8,128)(2,1)S(1)} fusion(f32[1024,256]{1,0:T(8,128)S(1)} %fusion.72, bf16[1024,256]{1,0:T(8,128)(2,1)} %collective-permute-done.4, bf16[512,512]{1,0:T(8,128)(2,1)S(1)} %copy-done.5, bf16[512,512]{1,0:T(8,128)(2,1)S(1)} %copy-done.4, bf16[512,512]{1,0:T(8,128)(2,1)S(1)} %copy-done.3), kind=kOutput, calls=%fused_computation.99 | convolution fusion | flops 545783808 | bytes 3670016 | tf_op jit(solution)/shard_map/dot_general | solution.py:120
  89.4 0.2 copy.47
  89.7 2.1 %fusion.96 = bf16[1024,256]{1,0:T(8,128)(2,1)S(1)} fusion(f32[1024,256]{1,0:T(8,128)} %fusion.40, bf16[1024,256]{1,0:T(8,128)(2,1)} %collective-permute-done.4, bf16[512,512]{1,0:T(8,128)(2,1)S(1)} %get-tuple-element.212, bf16[512,512]{1,0:T(8,128)(2,1)S(1)} %get-tuple-element.184, bf16[512,512]{1,0:T(8,128)(2,1)S(1)} %get-tuple-element.183), kind=kOutput, calls=%fused_computation.98 | convolution fusion | flops 545783808 | bytes 3670016 | tf_op jit(solution)/shard_map/dot_general | solution.py:124
  91.8 0.2 copy.46
  92.0 3.7 %fusion.4 = bf16[2048,512]{1,0:T(8,128)(2,1)} fusion(s32[1024]{0:T(1024)S(1)} %pad_add_fusion.4, bf16[512,512]{0,1:T(8,128)(2,1)S(1)} %bitcast.125, bf16[512,512]{0,1:T(8,128)(2,1)S(1)} %bitcast.128), kind=kOutput, calls=%fused_computation.6 | convolution fusion | flops 2152726528 | bytes 3149824 | tf_op jit(solution)/shard_map/dot_general | solution.py:133
  95.7 9.8 %all-to-all-start.1 = ((bf16[128,16,512]{2,1,0:T(8,128)(2,1)}), bf16[128,16,512]{2,1,0:T(8,128)(2,1)S(1)}, u32[]{:S(2)}, u32[]{:S(2)}) async-start(bf16[128,16,512]{2,1,0:T(8,128)(2,1)} %bitcast.119), calls=%async_computation.1 | async-start | bytes 4194304 | tf_op jit(solution)/shard_map/all_to_all | solution.py:135
  107.2 27.9 %all-to-all-done.1 = bf16[128,16,512]{2,1,0:T(8,128)(2,1)S(1)} async-done(((bf16[128,16,512]{2,1,0:T(8,128)(2,1)}), bf16[128,16,512]{2,1,0:T(8,128)(2,1)S(1)}, u32[]{:S(2)}, u32[]{:S(2)}) %all-to-all-start.1) | async-done | bytes 2097184 | tf_op jit(solution)/shard_map/all_to_all | solution.py:135
  135.3 0.8 fusion.94
  136.1 0.2 copy.50
  136.3 0.8 fusion.95
  137.1 0.2 copy.49
  137.3 1.1 maximum_bitcast_fusion
  (93 shorter events, 3.7 us)
Async XLA Ops:
  0.0 3.7 %copy-start.7 = (bf16[3,1,2,2,512,8]{4,5,3,2,1,0:T(8,128)(2,1)S(1)}, bf16[3,1,2,2,512,8]{4,5,3,2,1,0:T(8,128)(2,1)}, u32[]{:S(2)}) copy-start(bf16[3,1,2,2,512,8]{4,5,3,2,1,0:T(8,128)(2,1)} %param.9) | copy-start | bytes 294916
  0.0 3.7 %copy-start.8 = (s32[1,1,512,1]{2,3,1,0:T(1,128)S(1)}, s32[1,1,512,1]{2,3,1,0:T(1,128)}, u32[]{:S(2)}) copy-start(s32[1,1,512,1]{2,3,1,0:T(1,128)} %param.10) | copy-start | bytes 6148
  0.0 4.4 %copy-start.10 = (bf16[2,512]{1,0:T(2,128)(2,1)S(1)}, bf16[2,512]{1,0:T(2,128)(2,1)}, u32[]{:S(2)}) copy-start(bf16[2,512]{1,0:T(2,128)(2,1)} %param.7) | copy-start | bytes 6148
  0.0 26.8 %collective-permute-start = (bf16[2,512,512]{2,1,0:T(8,128)(2,1)}, bf16[2,512,512]{2,1,0:T(8,128)(2,1)}, u32[]{:S(2)}, u32[]{:S(2)}) collective-permute-start(bf16[2,512,512]{2,1,0:T(8,128)(2,1)} %param.6), channel_id=1, source_target_pairs={{1,0},{2,1},{3,2},{4,3},{5,4},{6,5},{7,6},{8,7},{9,8},{10,9},{11,1... | collective-permute-start | bytes 3145736 | tf_op jit(solution)/shard_map/ppermute | solution.py:12
  9.0 1.6 %copy-start.9 = (s32[3,1,2,512]{3,2,1,0:T(2,128)S(1)}, s32[3,1,2,512]{3,2,1,0:T(2,128)}, u32[]{:S(2)}) copy-start(s32[3,1,2,512]{3,2,1,0:T(2,128)} %param.8) | copy-start | bytes 36868
  9.0 1.7 %copy-start.11 = (s32[1,1,512]{2,1,0:T(1,128)S(1)}, s32[1,1,512]{2,1,0:T(1,128)}, u32[]{:S(2)}) copy-start(s32[1,1,512]{2,1,0:T(1,128)} %param.11) | copy-start | bytes 6148
  29.4 3.6 %copy-start = (bf16[512,512]{1,0:T(8,128)(2,1)S(1)}, bf16[512,512]{1,0:T(8,128)(2,1)}, u32[]{:S(2)}) copy-start(bf16[512,512]{1,0:T(8,128)(2,1)} %get-tuple-element.197) | copy-start | bytes 1572868
  29.4 3.6 %copy-start.1 = (bf16[512,512]{1,0:T(8,128)(2,1)S(1)}, bf16[512,512]{1,0:T(8,128)(2,1)}, u32[]{:S(2)}) copy-start(bf16[512,512]{1,0:T(8,128)(2,1)} %get-tuple-element.198) | copy-start | bytes 1572868
  29.4 3.6 %copy-start.2 = (bf16[512,512]{1,0:T(8,128)(2,1)S(1)}, bf16[512,512]{1,0:T(8,128)(2,1)}, u32[]{:S(2)}) copy-start(bf16[512,512]{1,0:T(8,128)(2,1)} %get-tuple-element.219) | copy-start | bytes 1572868
  29.5 4.7 %collective-permute-start.1 = (bf16[1024,512]{1,0:T(8,128)(2,1)S(1)}, bf16[1024,512]{1,0:T(8,128)(2,1)S(1)}, u32[]{:S(2)}, u32[]{:S(2)}) collective-permute-start(bf16[1024,512]{1,0:T(8,128)(2,1)S(1)} %bitcast.120), channel_id=1, source_target_pairs={{0,16},{16,0},{32,48},{48,32},{64,80},{80,64},{96,112},{112,96},{1... | collective-permute-start | bytes 3145736 | tf_op jit(solution)/shard_map/ppermute | solution.py:16
  35.5 31.1 %collective-permute-start.2 = (bf16[1024,512]{1,0:T(8,128)(2,1)S(1)}, bf16[1024,512]{1,0:T(8,128)(2,1)S(1)}, u32[]{:S(2)}, u32[]{:S(2)}) collective-permute-start(bf16[1024,512]{1,0:T(8,128)(2,1)S(1)} %add_convert_fusion.1), channel_id=1, source_target_pairs={{0,32},{16,48},{32,0},{48,16},{64,96},{80,112},{96,64},{112,80},{1... | collective-permute-start | bytes 3145736 | tf_op jit(solution)/shard_map/ppermute | solution.py:16
  38.7 25.9 %collective-permute-start.5 = (bf16[2,2,512,8]{2,3,1,0:T(8,128)(2,1)S(1)}, bf16[2,2,512,8]{2,3,1,0:T(8,128)(2,1)S(1)}, u32[]{:S(2)}, u32[]{:S(2)}) collective-permute-start(bf16[2,2,512,8]{2,3,1,0:T(8,128)(2,1)S(1)} %slice_bitcast_fusion.4), channel_id=1, source_target_pairs={{0,64},{16,80},{32,96},{48,112},{64,0},{80,16},{96,32},{112,48},{1... | collective-permute-start | bytes 98312 | tf_op jit(solution)/shard_map/ppermute | solution.py:16
  42.1 22.4 %collective-permute-start.3 = (s32[1536]{0:T(1024)S(1)}, s32[1536]{0:T(1024)S(1)}, u32[]{:S(2)}, u32[]{:S(2)}) collective-permute-start(s32[1536]{0:T(1024)S(1)} %pad_add_fusion.2), channel_id=1, source_target_pairs={{0,64},{16,80},{32,96},{48,112},{64,0},{80,16},{96,32},{112,48},{1... | collective-permute-start | bytes 18440 | tf_op jit(solution)/shard_map/ppermute | solution.py:16
  67.8 5.4 %copy-start.6 = (bf16[1024,512]{1,0:T(8,128)(2,1)}, bf16[1024,512]{1,0:T(8,128)(2,1)S(1)}, u32[]{:S(2)}) copy-start(bf16[1024,512]{1,0:T(8,128)(2,1)S(1)} %add_convert_fusion) | copy-start | bytes 3145732
  68.7 18.9 %collective-permute-start.4 = (bf16[1024,256]{1,0:T(8,128)(2,1)}, bf16[1024,256]{1,0:T(8,128)(2,1)}, u32[]{:S(2)}, u32[]{:S(2)}) collective-permute-start(bf16[1024,256]{1,0:T(8,128)(2,1)} %constant_dynamic-slice_fusion), channel_id=1, source_target_pairs={{0,64},{16,80},{32,96},{48,112},{64,0},{80,16},{96,32},{112,48},{1... | collective-permute-start | bytes 1572872 | tf_op jit(solution)/shard_map/ppermute | solution.py:16
  73.2 22.5 %all-to-all-start = ((s32[128,1,8]{2,1,0:T(1,128)}), s32[128,1,8]{2,1,0:T(1,128)S(1)}, u32[]{:S(2)}, u32[]{:S(2)}) async-start(s32[128,1,8]{2,1,0:T(1,128)} %bitcast.33), calls=%async_computation | async-start | bytes 131072 | tf_op jit(solution)/shard_map/all_to_all | solution.py:123
  85.7 1.9 %copy-start.3 = (bf16[512,512]{1,0:T(8,128)(2,1)S(1)}, bf16[512,512]{1,0:T(8,128)(2,1)}, u32[]{:S(2)}) copy-start(bf16[512,512]{1,0:T(8,128)(2,1)} %get-tuple-element.187) | copy-start | bytes 1572868
  85.8 1.9 %copy-start.4 = (bf16[512,512]{1,0:T(8,128)(2,1)S(1)}, bf16[512,512]{1,0:T(8,128)(2,1)}, u32[]{:S(2)}) copy-start(bf16[512,512]{1,0:T(8,128)(2,1)} %get-tuple-element.188) | copy-start | bytes 1572868
  85.8 1.9 %copy-start.5 = (bf16[512,512]{1,0:T(8,128)(2,1)S(1)}, bf16[512,512]{1,0:T(8,128)(2,1)}, u32[]{:S(2)}) copy-start(bf16[512,512]{1,0:T(8,128)(2,1)} %get-tuple-element.214) | copy-start | bytes 1572868
  95.7 39.5 %all-to-all-start.1 = ((bf16[128,16,512]{2,1,0:T(8,128)(2,1)}), bf16[128,16,512]{2,1,0:T(8,128)(2,1)S(1)}, u32[]{:S(2)}, u32[]{:S(2)}) async-start(bf16[128,16,512]{2,1,0:T(8,128)(2,1)} %bitcast.119), calls=%async_computation.1 | async-start | bytes 4194304 | tf_op jit(solution)/shard_map/all_to_all | solution.py:135

commit v17 on v14

--- a/solution.py
+++ b/solution.py
@@ -88,7 +88,8 @@
         theirs = merge_matrix(offsets[section, 0, 1], weights[section, 0, 1])
         merged = jnp.dot(mine, image, preferred_element_type=jnp.float32)
         if section == 1:
-            late, merged = lax.optimization_barrier((late, merged))
+            (labels, late), merged = lax.optimization_barrier(((labels, late), merged))
+            marks = lax.all_to_all(labels, ("sub", "rng"), split_axis=0, concat_axis=0, tiled=True)
             own_offsets, own_weights, slot = late
             far_weights = far(own_weights)
             far_ints = far(jnp.concatenate([own_offsets.reshape(-1), slot]))
@@ -96,6 +97,8 @@
             far_slot = far_ints[2 * p_dev :]
         merged = merged + jnp.dot(theirs, partner, preferred_element_type=jnp.float32)
         image = merged.astype(jnp.bfloat16)
+        if section == 1:
+            marks, image = lax.optimization_barrier((marks, image))
     slots = jnp.arange(devices * capacity, dtype=jnp.int32)[:, None]
     picks = {0: slots == slot[None, :], bit: slots == far_slot[None, :]}
     half = r_dev // 2
@@ -113,9 +116,6 @@
         mine = merge_matrix(starts[0], kernel[0])
         theirs = merge_matrix(starts[1], kernel[1])
         merged = jnp.dot(mine, old[m], preferred_element_type=jnp.float32)
-        if m == 0:
-            labels, merged = lax.optimization_barrier((labels, merged))
-            marks = lax.all_to_all(labels, ("sub", "rng"), split_axis=0, concat_axis=0, tiled=True)
         merged = merged + jnp.dot(theirs, old[m ^ bit], preferred_element_type=jnp.float32)
         piece = merged.astype(jnp.bfloat16)
         rows = piece.reshape(2, p_dev, half).transpose(1, 0, 2).reshape(p_dev, 2 * half)

time: 138 us -> 139 us (level)
  waiting for transfers between devices: 50.4 us -> 45.7 us
  matrix products: 19.9 us -> 23.5 us
    ppermute x5, waiting for transfers between devices: 18.4 us -> 13.7 us  [from_partner(): lax.ppermute(value, axis, [(i, i ^ 1 << apart) for i in range(lax.axis_si...]
    dot_general x2, matrix products: 2.49 us -> 5.66 us  [on_device(): jnp.dot(theirs, partner, preferred_element_type=jnp.float32)]
    dot_general x2, matrix products: 2.48 us -> 5.09 us  [on_device(): merged = jnp.dot(mine, image, preferred_element_type=jnp.float32)]
  transfers between devices with their start and end apart: 8 -> 8, of which waited for: 4 -> 4; matrix products, arithmetic and copies ran while one was open for 34% -> 33% of each run, Pallas kernels for 0% -> 0%
where the time goes in v17:
time: 139 us; the launch traced here: 138 us
  waiting for transfers between devices  45.7 us (33%)
  starting transfers between devices  30.7 us (22%)
  matrix products  23.5 us (17%)
  other arithmetic  22.4 us (16%)
  local copies, waits for them, and re-layouts  15.5 us (11%)
    all_to_all x1, waiting for transfers between devices, on_device(): lax.all_to_all(payload, ('sub', 'rng'), split_axis=0, concat_axis=0, tile...  28.1 us
    neg x8, other arithmetic, merge_matrix(): upper = jnp.concatenate([g_real, -g_imag], axis=1)  17 us
    ppermute x5, waiting for transfers between devices, from_partner(): lax.ppermute(value, axis, [(i, i ^ 1 << apart) for i in range(lax.axis_si...  13.7 us
    all_to_all x1, starting transfers between devices, on_device(): lax.all_to_all(labels, ('sub', 'rng'), split_axis=0, concat_axis=0, tiled...  11.9 us
    all_to_all x1, starting transfers between devices, on_device(): lax.all_to_all(payload, ('sub', 'rng'), split_axis=0, concat_axis=0, tile...  10.1 us
    ppermute x5, starting transfers between devices, from_partner(): lax.ppermute(value, axis, [(i, i ^ 1 << apart) for i in range(lax.axis_si...  7.27 us
    dot_general x2, matrix products, on_device(): jnp.dot(theirs, partner, preferred_element_type=jnp.float32)  5.66 us
    dot_general x2, matrix products, on_device(): merged = jnp.dot(mine, image, preferred_element_type=jnp.float32)  5.09 us
  transfers between devices with their start and end apart: 8, of which 4 were waited for; matrix products, arithmetic and copies ran while one was open for 33% of the time, Pallas kernels for 0%

profile of v17, /device:TPU:1, one launch (start us, length us, event | category | flops | bytes accessed | tf_op | source)
XLA Modules:
  0.0 138.3 jit_solution(12968049422746835691)
XLA Ops:
  0.0 1.4 %collective-permute-start = (bf16[2,512,512]{2,1,0:T(8,128)(2,1)}, bf16[2,512,512]{2,1,0:T(8,128)(2,1)}, u32[]{:S(2)}, u32[]{:S(2)}) collective-permute-start(bf16[2,512,512]{2,1,0:T(8,128)(2,1)} %param.6), channel_id=1, source_target_pairs={{1,0},{2,1},{3,2},{4,3},{5,4},{6,5},{7,6},{8,7},{9,8},{10,9},{11,1... | collective-permute-start | bytes 3145736 | tf_op jit(solution)/shard_map/ppermute | solution.py:12
  1.5 2.2 %slice_bitcast_fusion.3 = (bf16[512,512]{1,0:T(8,128)(2,1)}, bf16[512,512]{1,0:T(8,128)(2,1)}) fusion(bf16[2,512,512]{2,1,0:T(8,128)(2,1)} %param.6), kind=kLoop, calls=%fused_computation.323 | loop fusion | bytes 2097152 | tf_op jit(solution)/shard_map/squeeze | solution.py:66
  4.2 0.2 fusion.312
  4.4 0.3 select_reduce_fusion
  4.9 1.3 tile.9
  6.3 0.5 reshape.160
  6.9 1.3 tile.21
  8.3 1.0 slice.1011
  9.3 1.5 %reshape.161 = bf16[512,1024]{1,0:T(8,128)(2,1)S(1)} reshape(bf16[524288]{0:T(1024)(128)(2,1)} %slice.1011) | data formatting | bytes 2097152 | tf_op jit(solution)/shard_map/reshape | solution.py:25
  11.2 1.5 %fusion.105 = (bf16[512,1024]{0,1:T(8,128)(2,1)}, bf16[512,1024]{0,1:T(8,128)(2,1)}) fusion(bf16[1024,512]{0,1:T(8,128)(2,1)S(1)} %bitcast.124, bf16[1024,512]{0,1:T(8,128)(2,1)S(1)} %bitcast_negate_fusion, bf16[1024,512]{0,1:T(8,128)(2,1)S(1)} %bitcast.122), kind=kLoop, calls=%fused_computation.105 | loop fusion | flops 4194304 | bytes 5242880 | tf_op jit(solution)/shard_map/concatenate | solution.py:28
  12.8 2.7 %fusion.345 = (bf16[512,512]{1,0:T(8,128)(2,1)}, bf16[512,512]{1,0:T(8,128)(2,1)}, bf16[512,512]{1,0:T(8,128)(2,1)}) fusion(bf16[512]{0:T(512)(128)(2,1)S(1)} %get-tuple-element.132, bf16[512]{0:T(512)(128)(2,1)S(1)} %get-tuple-element.133, bf16[512]{0:T(512)(128)(2,1)S(1)} %get-tuple-element.134, bf16[512]{0:T(512)(128)(2,1)S(1)} %get-tuple-element.135, ...), kind=kLoop, calls=%fused_computation.535 | loop fusion | flops 7340032 | bytes 1591296 | tf_op jit(solution)/shard_map/neg | solution.py:43
  15.6 0.7 sub.137
  16.3 3.1 %fusion.25 = f32[512,1024]{1,0:T(8,128)S(1)} fusion(bf16[512,1024]{0,1:T(8,128)(2,1)} %get-tuple-element.156, bf16[512,1024]{0,1:T(8,128)(2,1)} %get-tuple-element.155, bf16[512,512]{1,0:T(8,128)(2,1)} %get-tuple-element.154, bf16[512,512]{1,0:T(8,128)(2,1)} %get-tuple-element.153), kind=kOutput, calls=%fused_computation.29 | convolution fusion | flops 1080033280 | bytes 5242880 | tf_op jit(solution)/shard_map/dot_general | solution.py:65
  19.4 1.7 %fusion.346 = (bf16[512,512]{1,0:T(8,128)(2,1)S(1)}, bf16[512,512]{1,0:T(8,128)(2,1)S(1)}, bf16[512,512]{1,0:T(8,128)(2,1)S(1)}) fusion(bf16[512]{0:T(512)(128)(2,1)S(1)} %get-tuple-element.116, bf16[512]{0:T(512)(128)(2,1)S(1)} %get-tuple-element.117, bf16[512]{0:T(512)(128)(2,1)S(1)} %get-tuple-element.118, bf16[512]{0:T(512)(128)(2,1)S(1)} %get-tuple-element.119, ...), kind=kLoop, calls=%fused_computation.536 | loop fusion | flops 7340032 | bytes 1591296 | tf_op jit(solution)/shard_map/neg | solution.py:43
  21.2 1.7 %fusion.344 = (bf16[512,512]{1,0:T(8,128)(2,1)S(1)}, bf16[512,512]{1,0:T(8,128)(2,1)S(1)}, bf16[512,512]{1,0:T(8,128)(2,1)S(1)}) fusion(bf16[512]{0:T(512)(128)(2,1)S(1)} %get-tuple-element.100, bf16[512]{0:T(512)(128)(2,1)S(1)} %get-tuple-element.101, bf16[512]{0:T(512)(128)(2,1)S(1)} %get-tuple-element.102, bf16[512]{0:T(512)(128)(2,1)S(1)} %get-tuple-element.103, ...), kind=kLoop, calls=%fused_computation.534 | loop fusion | flops 7340032 | bytes 1591296 | tf_op jit(solution)/shard_map/neg | solution.py:43
  22.9 3.9 %collective-permute-done = bf16[2,512,512]{2,1,0:T(8,128)(2,1)} collective-permute-done((bf16[2,512,512]{2,1,0:T(8,128)(2,1)}, bf16[2,512,512]{2,1,0:T(8,128)(2,1)}, u32[]{:S(2)}, u32[]{:S(2)}) %collective-permute-start) | collective-permute-done | bytes 1048608 | tf_op jit(solution)/shard_map/ppermute | solution.py:12
  26.9 1.3 slice_bitcast_fusion.1
  28.1 1.3 add_convert_fusion.2
  29.5 1.7 %collective-permute-start.1 = (bf16[1024,512]{1,0:T(8,128)(2,1)S(1)}, bf16[1024,512]{1,0:T(8,128)(2,1)S(1)}, u32[]{:S(2)}, u32[]{:S(2)}) collective-permute-start(bf16[1024,512]{1,0:T(8,128)(2,1)S(1)} %bitcast.126), channel_id=1, source_target_pairs={{0,16},{16,0},{32,48},{48,32},{64,80},{80,64},{96,112},{112,96},{1... | collective-permute-start | bytes 3145736 | tf_op jit(solution)/shard_map/ppermute | solution.py:16
  31.3 1.7 %fusion.347 = (bf16[512,512]{1,0:T(8,128)(2,1)S(1)}, bf16[512,512]{1,0:T(8,128)(2,1)S(1)}, bf16[512,512]{1,0:T(8,128)(2,1)S(1)}) fusion(bf16[512]{0:T(512)(128)(2,1)S(1)} %get-tuple-element.68, bf16[512]{0:T(512)(128)(2,1)S(1)} %get-tuple-element.69, bf16[512]{0:T(512)(128)(2,1)S(1)} %get-tuple-element.70, bf16[512]{0:T(512)(128)(2,1)S(1)} %get-tuple-element.71, ...), kind=kLoop, calls=%fused_computation.537 | loop fusion | flops 7340032 | bytes 1591296 | tf_op jit(solution)/shard_map/neg | solution.py:43
  33.0 1.2 fusion.17
  34.3 2.2 %add_convert_fusion.1 = bf16[1024,512]{1,0:T(8,128)(2,1)} fusion(f32[1024,512]{1,0:T(8,128)S(1)} %fusion.17, bf16[1024,512]{1,0:T(8,128)(2,1)S(1)} %collective-permute-done.1, bf16[512,512]{1,0:T(8,128)(2,1)S(1)} %get-tuple-element.220, bf16[512,512]{1,0:T(8,128)(2,1)S(1)} %get-tuple-element.198, bf16[512,512]{1,0:T(8,128)(2,1)S(1)} %get-tuple-element.197), kind=kOutput, calls=%fused_computation.86 | convolution fusion | flops 1083179008 | bytes 5767168 | tf_op jit(solution)/shard_map/dot_general | solution.py:98
  36.5 1.9 %collective-permute-start.2 = (bf16[1024,512]{1,0:T(8,128)(2,1)}, bf16[1024,512]{1,0:T(8,128)(2,1)}, u32[]{:S(2)}, u32[]{:S(2)}) collective-permute-start(bf16[1024,512]{1,0:T(8,128)(2,1)} %add_convert_fusion.1), channel_id=1, source_target_pairs={{0,32},{16,48},{32,0},{48,16},{64,96},{80,112},{96,64},{112,80},{1... | collective-permute-start | bytes 3145736 | tf_op jit(solution)/shard_map/ppermute | solution.py:16
  38.4 3.9 %fusion.9 = f32[1024,512]{1,0:T(8,128)} fusion(bf16[1024,512]{1,0:T(8,128)(2,1)} %add_convert_fusion.1, bf16[512,512]{1,0:T(8,128)(2,1)S(1)} %get-tuple-element.219, bf16[512,512]{1,0:T(8,128)(2,1)S(1)} %get-tuple-element.196, bf16[512,512]{1,0:T(8,128)(2,1)S(1)} %get-tuple-element.195), kind=kOutput, calls=%fused_computation.11 | convolution fusion | flops 1082130432 | bytes 4718592 | tf_op jit(solution)/shard_map/dot_general | solution.py:89
  42.2 3.3 %collective-permute-start.5 = (bf16[2,2,512,8]{2,3,1,0:T(8,128)(2,1)S(1)}, bf16[2,2,512,8]{2,3,1,0:T(8,128)(2,1)S(1)}, u32[]{:S(2)}, u32[]{:S(2)}) collective-permute-start(bf16[2,2,512,8]{2,3,1,0:T(8,128)(2,1)S(1)} %slice_bitcast_fusion.4), channel_id=1, source_target_pairs={{0,64},{16,80},{32,96},{48,112},{64,0},{80,16},{96,32},{112,48},{1... | collective-permute-start | bytes 98312 | tf_op jit(solution)/shard_map/ppermute | solution.py:16
  45.6 0.3 collective-permute-start.4
  45.8 11.9 %all-to-all-start = ((s32[128,1,8]{2,1,0:T(1,128)}), s32[128,1,8]{2,1,0:T(1,128)S(1)}, u32[]{:S(2)}, u32[]{:S(2)}) async-start(s32[128,1,8]{2,1,0:T(1,128)} %bitcast.27), calls=%async_computation | async-start | bytes 131072 | tf_op jit(solution)/shard_map/all_to_all | solution.py:92
  58.0 1.7 %fusion.348 = (bf16[512,512]{1,0:T(8,128)(2,1)S(1)}, bf16[512,512]{1,0:T(8,128)(2,1)S(1)}, bf16[512,512]{1,0:T(8,128)(2,1)S(1)}) fusion(bf16[512]{0:T(512)(128)(2,1)S(1)} %get-tuple-element.36, bf16[512]{0:T(512)(128)(2,1)S(1)} %get-tuple-element.37, bf16[512]{0:T(512)(128)(2,1)S(1)} %get-tuple-element.38, bf16[512]{0:T(512)(128)(2,1)S(1)} %get-tuple-element.39, ...), kind=kLoop, calls=%fused_computation.538 | loop fusion | flops 7340032 | bytes 1591296 | tf_op jit(solution)/shard_map/neg | solution.py:43
  59.8 2.8 %fusion.349 = (bf16[512,512]{1,0:T(8,128)(2,1)}, bf16[512,512]{1,0:T(8,128)(2,1)}, bf16[512,512]{1,0:T(8,128)(2,1)}) fusion(bf16[512]{0:T(512)(128)(2,1)S(1)} %get-tuple-element.20, bf16[512]{0:T(512)(128)(2,1)S(1)} %get-tuple-element.21, bf16[512]{0:T(512)(128)(2,1)S(1)} %get-tuple-element.22, bf16[512]{0:T(512)(128)(2,1)S(1)} %get-tuple-element.23, ...), kind=kLoop, calls=%fused_computation.539 | loop fusion | flops 7340032 | bytes 1591296 | tf_op jit(solution)/shard_map/neg | solution.py:43
  62.6 3.9 %collective-permute-done.4 = s32[1536]{0:T(1024)S(1)} collective-permute-done((s32[1536]{0:T(1024)S(1)}, s32[1536]{0:T(1024)S(1)}, u32[]{:S(2)}, u32[]{:S(2)}) %collective-permute-start.4) | collective-permute-done | bytes 6176 | tf_op jit(solution)/shard_map/ppermute | solution.py:16
  66.7 2.8 %fusion.351 = (bf16[512,512]{1,0:T(8,128)(2,1)}, bf16[512,512]{1,0:T(8,128)(2,1)}, bf16[512,512]{1,0:T(8,128)(2,1)}) fusion(bf16[512]{0:T(512)(128)(2,1)S(1)} %get-tuple-element.84, bf16[512]{0:T(512)(128)(2,1)S(1)} %get-tuple-element.85, bf16[512]{0:T(512)(128)(2,1)S(1)} %get-tuple-element.86, bf16[512]{0:T(512)(128)(2,1)S(1)} %get-tuple-element.87, ...), kind=kLoop, calls=%fused_computation.541 | loop fusion | flops 7340032 | bytes 1591296 | tf_op jit(solution)/shard_map/neg | solution.py:43
  69.5 3.4 %add_convert_fusion = bf16[1024,512]{1,0:T(8,128)(2,1)} fusion(f32[1024,512]{1,0:T(8,128)S(1)} %copy-done.16, bf16[1024,512]{1,0:T(8,128)(2,1)} %collective-permute-done.2, bf16[512,512]{1,0:T(8,128)(2,1)S(1)} %get-tuple-element.217, bf16[512,512]{1,0:T(8,128)(2,1)S(1)} %get-tuple-element.192, bf16[512,512]{1,0:T(8,128)(2,1)S(1)} %get-tuple-element.191), kind=kOutput, calls=%fused_computation.85 | convolution fusion | flops 1083179008 | bytes 5767168 | tf_op jit(solution)/shard_map/dot_general | solution.py:98
  73.0 1.2 constant_dynamic-slice_fusion
  74.3 1.7 %fusion.350 = (bf16[512,512]{1,0:T(8,128)(2,1)S(1)}, bf16[512,512]{1,0:T(8,128)(2,1)S(1)}, bf16[512,512]{1,0:T(8,128)(2,1)S(1)}) fusion(bf16[512]{0:T(512)(128)(2,1)S(1)} %get-tuple-element.52, bf16[512]{0:T(512)(128)(2,1)S(1)} %get-tuple-element.53, bf16[512]{0:T(512)(128)(2,1)S(1)} %get-tuple-element.54, bf16[512]{0:T(512)(128)(2,1)S(1)} %get-tuple-element.55, ...), kind=kLoop, calls=%fused_computation.540 | loop fusion | flops 7340032 | bytes 1591296 | tf_op jit(solution)/shard_map/neg | solution.py:43
  76.1 0.7 fusion.69
  76.9 1.7 %fusion.45 = f32[1024,256]{1,0:T(8,128)} fusion(bf16[512,512]{1,0:T(8,128)(2,1)S(1)} %get-tuple-element.215, bf16[512,512]{1,0:T(8,128)(2,1)S(1)} %get-tuple-element.188, bf16[512,512]{1,0:T(8,128)(2,1)S(1)} %get-tuple-element.187, bf16[1024,512]{1,0:T(8,128)(2,1)S(1)} %copy-done.9, s32[]{:T(128)S(6)} %select_n.476), kind=kOutput, calls=%fused_computation.49 | convolution fusion | flops 545259520 | bytes 3145732 | tf_op jit(solution)/shard_map/dot_general | solution.py:118
  78.5 9.7 %collective-permute-done.3 = bf16[1024,256]{1,0:T(8,128)(2,1)S(1)} collective-permute-done((bf16[1024,256]{1,0:T(8,128)(2,1)S(1)}, bf16[1024,256]{1,0:T(8,128)(2,1)S(1)}, u32[]{:S(2)}, u32[]{:S(2)}) %collective-permute-start.3) | collective-permute-done | bytes 524320 | tf_op jit(solution)/shard_map/ppermute | solution.py:16
  88.3 0.7 fusion.102
  89.3 0.2 copy-done.3
  89.8 2.1 %fusion.99 = bf16[1024,256]{1,0:T(8,128)(2,1)S(1)} fusion(f32[1024,256]{1,0:T(8,128)} %fusion.45, bf16[1024,256]{1,0:T(8,128)(2,1)} %copy-done.15, bf16[512,512]{1,0:T(8,128)(2,1)S(1)} %copy-done.5, bf16[512,512]{1,0:T(8,128)(2,1)S(1)} %copy-done.4, bf16[512,512]{1,0:T(8,128)(2,1)S(1)} %copy-done.3), kind=kOutput, calls=%fused_computation.103 | convolution fusion | flops 545783808 | bytes 3670016 | tf_op jit(solution)/shard_map/dot_general | solution.py:119
  92.1 0.7 fusion.89
  92.9 0.7 fusion.90
  93.7 1.7 %pad_maximum_fusion.2 = bf16[128,16,512]{2,1,0:T(8,128)(2,1)} fusion(bf16[128,8,512]{2,1,0:T(8,128)(2,1)S(1)} %fusion.90, bf16[128,8,512]{2,1,0:T(8,128)(2,1)S(1)} %fusion.89), kind=kLoop, calls=%fused_computation.81 | loop fusion | flops 4194304 | bytes 4194304 | tf_op jit(solution)/shard_map/concatenate | solution.py:129
  95.3 10.1 %all-to-all-start.1 = ((bf16[128,16,512]{2,1,0:T(8,128)(2,1)}), bf16[128,16,512]{2,1,0:T(8,128)(2,1)S(1)}, u32[]{:S(2)}, u32[]{:S(2)}) async-start(bf16[128,16,512]{2,1,0:T(8,128)(2,1)} %pad_maximum_fusion.2), calls=%async_computation.1 | async-start | bytes 4194304 | tf_op jit(solution)/shard_map/all_to_all | solution.py:130
  107.0 28.1 %all-to-all-done.1 = bf16[128,16,512]{2,1,0:T(8,128)(2,1)S(1)} async-done(((bf16[128,16,512]{2,1,0:T(8,128)(2,1)}), bf16[128,16,512]{2,1,0:T(8,128)(2,1)S(1)}, u32[]{:S(2)}, u32[]{:S(2)}) %all-to-all-start.1) | async-done | bytes 2097184 | tf_op jit(solution)/shard_map/all_to_all | solution.py:130
  135.3 0.8 fusion.97
  136.3 0.8 fusion.98
  137.3 1.1 maximum_bitcast_fusion
  (103 shorter events, 4.8 us)
Async XLA Ops:
  0.0 3.7 %copy-start.10 = (bf16[3,1,2,2,512,8]{4,5,3,2,1,0:T(8,128)(2,1)S(1)}, bf16[3,1,2,2,512,8]{4,5,3,2,1,0:T(8,128)(2,1)}, u32[]{:S(2)}) copy-start(bf16[3,1,2,2,512,8]{4,5,3,2,1,0:T(8,128)(2,1)} %param.9) | copy-start | bytes 294916
  0.0 3.7 %copy-start.14 = (s32[1,1,512]{2,1,0:T(1,128)S(1)}, s32[1,1,512]{2,1,0:T(1,128)}, u32[]{:S(2)}) copy-start(s32[1,1,512]{2,1,0:T(1,128)} %param.11) | copy-start | bytes 6148
  0.0 3.7 %copy-start.11 = (s32[1,1,512,1]{2,3,1,0:T(1,128)S(1)}, s32[1,1,512,1]{2,3,1,0:T(1,128)}, u32[]{:S(2)}) copy-start(s32[1,1,512,1]{2,3,1,0:T(1,128)} %param.10) | copy-start | bytes 6148
  0.0 4.7 %copy-start.13 = (bf16[2,512]{1,0:T(2,128)(2,1)S(1)}, bf16[2,512]{1,0:T(2,128)(2,1)}, u32[]{:S(2)}) copy-start(bf16[2,512]{1,0:T(2,128)(2,1)} %param.7) | copy-start | bytes 6148
  0.0 26.8 %collective-permute-start = (bf16[2,512,512]{2,1,0:T(8,128)(2,1)}, bf16[2,512,512]{2,1,0:T(8,128)(2,1)}, u32[]{:S(2)}, u32[]{:S(2)}) collective-permute-start(bf16[2,512,512]{2,1,0:T(8,128)(2,1)} %param.6), channel_id=1, source_target_pairs={{1,0},{2,1},{3,2},{4,3},{5,4},{6,5},{7,6},{8,7},{9,8},{10,9},{11,1... | collective-permute-start | bytes 3145736 | tf_op jit(solution)/shard_map/ppermute | solution.py:12
  9.3 1.6 %copy-start.12 = (s32[3,1,2,512]{3,2,1,0:T(2,128)S(1)}, s32[3,1,2,512]{3,2,1,0:T(2,128)}, u32[]{:S(2)}) copy-start(s32[3,1,2,512]{3,2,1,0:T(2,128)} %param.8) | copy-start | bytes 36868
  29.4 3.6 %copy-start = (bf16[512,512]{1,0:T(8,128)(2,1)S(1)}, bf16[512,512]{1,0:T(8,128)(2,1)}, u32[]{:S(2)}) copy-start(bf16[512,512]{1,0:T(8,128)(2,1)} %get-tuple-element.199) | copy-start | bytes 1572868
  29.4 3.6 %copy-start.1 = (bf16[512,512]{1,0:T(8,128)(2,1)S(1)}, bf16[512,512]{1,0:T(8,128)(2,1)}, u32[]{:S(2)}) copy-start(bf16[512,512]{1,0:T(8,128)(2,1)} %get-tuple-element.200) | copy-start | bytes 1572868
  29.4 3.6 %copy-start.2 = (bf16[512,512]{1,0:T(8,128)(2,1)S(1)}, bf16[512,512]{1,0:T(8,128)(2,1)}, u32[]{:S(2)}) copy-start(bf16[512,512]{1,0:T(8,128)(2,1)} %get-tuple-element.221) | copy-start | bytes 1572868
  29.5 4.7 %collective-permute-start.1 = (bf16[1024,512]{1,0:T(8,128)(2,1)S(1)}, bf16[1024,512]{1,0:T(8,128)(2,1)S(1)}, u32[]{:S(2)}, u32[]{:S(2)}) collective-permute-start(bf16[1024,512]{1,0:T(8,128)(2,1)S(1)} %bitcast.126), channel_id=1, source_target_pairs={{0,16},{16,0},{32,48},{48,32},{64,80},{80,64},{96,112},{112,96},{1... | collective-permute-start | bytes 3145736 | tf_op jit(solution)/shard_map/ppermute | solution.py:16
  36.5 33.0 %collective-permute-start.2 = (bf16[1024,512]{1,0:T(8,128)(2,1)}, bf16[1024,512]{1,0:T(8,128)(2,1)}, u32[]{:S(2)}, u32[]{:S(2)}) collective-permute-start(bf16[1024,512]{1,0:T(8,128)(2,1)} %add_convert_fusion.1), channel_id=1, source_target_pairs={{0,32},{16,48},{32,0},{48,16},{64,96},{80,112},{96,64},{112,80},{1... | collective-permute-start | bytes 3145736 | tf_op jit(solution)/shard_map/ppermute | solution.py:16
  42.2 24.3 %collective-permute-start.5 = (bf16[2,2,512,8]{2,3,1,0:T(8,128)(2,1)S(1)}, bf16[2,2,512,8]{2,3,1,0:T(8,128)(2,1)S(1)}, u32[]{:S(2)}, u32[]{:S(2)}) collective-permute-start(bf16[2,2,512,8]{2,3,1,0:T(8,128)(2,1)S(1)} %slice_bitcast_fusion.4), channel_id=1, source_target_pairs={{0,64},{16,80},{32,96},{48,112},{64,0},{80,16},{96,32},{112,48},{1... | collective-permute-start | bytes 98312 | tf_op jit(solution)/shard_map/ppermute | solution.py:16
  45.6 20.9 %collective-permute-start.4 = (s32[1536]{0:T(1024)S(1)}, s32[1536]{0:T(1024)S(1)}, u32[]{:S(2)}, u32[]{:S(2)}) collective-permute-start(s32[1536]{0:T(1024)S(1)} %pad_add_fusion.2), channel_id=1, source_target_pairs={{0,64},{16,80},{32,96},{48,112},{64,0},{80,16},{96,32},{112,48},{1... | collective-permute-start | bytes 18440 | tf_op jit(solution)/shard_map/ppermute | solution.py:16
  45.8 27.2 %all-to-all-start = ((s32[128,1,8]{2,1,0:T(1,128)}), s32[128,1,8]{2,1,0:T(1,128)S(1)}, u32[]{:S(2)}, u32[]{:S(2)}) async-start(s32[128,1,8]{2,1,0:T(1,128)} %bitcast.27), calls=%async_computation | async-start | bytes 131072 | tf_op jit(solution)/shard_map/all_to_all | solution.py:92
  59.8 9.8 %copy-start.16 = (f32[1024,512]{1,0:T(8,128)S(1)}, f32[1024,512]{1,0:T(8,128)}, u32[]{:S(2)}) copy-start(f32[1024,512]{1,0:T(8,128)} %fusion.9) | copy-start | bytes 6291460
  73.0 3.1 %copy-start.6 = (bf16[512,512]{1,0:T(8,128)(2,1)S(1)}, bf16[512,512]{1,0:T(8,128)(2,1)}, u32[]{:S(2)}) copy-start(bf16[512,512]{1,0:T(8,128)(2,1)} %get-tuple-element.193) | copy-start | bytes 1572868
  73.0 3.1 %copy-start.7 = (bf16[512,512]{1,0:T(8,128)(2,1)S(1)}, bf16[512,512]{1,0:T(8,128)(2,1)}, u32[]{:S(2)}) copy-start(bf16[512,512]{1,0:T(8,128)(2,1)} %get-tuple-element.194) | copy-start | bytes 1572868
  73.0 3.1 %copy-start.8 = (bf16[512,512]{1,0:T(8,128)(2,1)S(1)}, bf16[512,512]{1,0:T(8,128)(2,1)}, u32[]{:S(2)}) copy-start(bf16[512,512]{1,0:T(8,128)(2,1)} %get-tuple-element.218) | copy-start | bytes 1572868
  73.0 3.1 %copy-start.9 = (bf16[1024,512]{1,0:T(8,128)(2,1)S(1)}, bf16[1024,512]{1,0:T(8,128)(2,1)}, u32[]{:S(2)}) copy-start(bf16[1024,512]{1,0:T(8,128)(2,1)} %add_convert_fusion) | copy-start | bytes 3145732
  74.2 14.0 %collective-permute-start.3 = (bf16[1024,256]{1,0:T(8,128)(2,1)S(1)}, bf16[1024,256]{1,0:T(8,128)(2,1)S(1)}, u32[]{:S(2)}, u32[]{:S(2)}) collective-permute-start(bf16[1024,256]{1,0:T(8,128)(2,1)S(1)} %constant_dynamic-slice_fusion), channel_id=1, source_target_pairs={{0,64},{16,80},{32,96},{48,112},{64,0},{80,16},{96,32},{112,48},{1... | collective-permute-start | bytes 1572872 | tf_op jit(solution)/shard_map/ppermute | solution.py:16
  88.3 0.8 copy-start.15
  88.3 1.2 copy-start.3
  88.3 1.4 %copy-start.4 = (bf16[512,512]{1,0:T(8,128)(2,1)S(1)}, bf16[512,512]{1,0:T(8,128)(2,1)}, u32[]{:S(2)}) copy-start(bf16[512,512]{1,0:T(8,128)(2,1)} %get-tuple-element.186) | copy-start | bytes 1572868
  88.3 1.5 %copy-start.5 = (bf16[512,512]{1,0:T(8,128)(2,1)S(1)}, bf16[512,512]{1,0:T(8,128)(2,1)}, u32[]{:S(2)}) copy-start(bf16[512,512]{1,0:T(8,128)(2,1)} %get-tuple-element.214) | copy-start | bytes 1572868
  95.3 39.8 %all-to-all-start.1 = ((bf16[128,16,512]{2,1,0:T(8,128)(2,1)}), bf16[128,16,512]{2,1,0:T(8,128)(2,1)S(1)}, u32[]{:S(2)}, u32[]{:S(2)}) async-start(bf16[128,16,512]{2,1,0:T(8,128)(2,1)} %pad_maximum_fusion.2), calls=%async_computation.1 | async-start | bytes 4194304 | tf_op jit(solution)/shard_map/all_to_all | solution.py:130

commit v18 on v14

--- a/solution.py
+++ b/solution.py
@@ -87,15 +87,15 @@
         mine = merge_matrix(offsets[section, 0, 0], weights[section, 0, 0])
         theirs = merge_matrix(offsets[section, 0, 1], weights[section, 0, 1])
         merged = jnp.dot(mine, image, preferred_element_type=jnp.float32)
-        if section == 1:
-            late, merged = lax.optimization_barrier((late, merged))
+        merged = merged + jnp.dot(theirs, partner, preferred_element_type=jnp.float32)
+        image = merged.astype(jnp.bfloat16)
+        if section == 0:
+            late, image = lax.optimization_barrier((late, image))
             own_offsets, own_weights, slot = late
             far_weights = far(own_weights)
             far_ints = far(jnp.concatenate([own_offsets.reshape(-1), slot]))
             far_offsets = far_ints[: 2 * p_dev].reshape(2, p_dev)
             far_slot = far_ints[2 * p_dev :]
-        merged = merged + jnp.dot(theirs, partner, preferred_element_type=jnp.float32)
-        image = merged.astype(jnp.bfloat16)
     slots = jnp.arange(devices * capacity, dtype=jnp.int32)[:, None]
     picks = {0: slots == slot[None, :], bit: slots == far_slot[None, :]}
     half = r_dev // 2

time: 138 us -> 136 us (0.986)
  waiting for transfers between devices: 50.4 us -> 48.8 us
    all_to_all x1, starting transfers between devices: 12.6 us -> 10.4 us  [on_device(): lax.all_to_all(labels, ('sub', 'rng'), split_axis=0, concat_axis=0, tiled...]
    ppermute x5, starting transfers between devices: 7.36 us -> 9.17 us  [from_partner(): lax.ppermute(value, axis, [(i, i ^ 1 << apart) for i in range(lax.axis_si...]
    ppermute x5, waiting for transfers between devices: 18.4 us -> 16.8 us  [from_partner(): lax.ppermute(value, axis, [(i, i ^ 1 << apart) for i in range(lax.axis_si...]
where the time goes in v18:
time: 136 us
  waiting for transfers between devices  48.8 us (36%)
  starting transfers between devices  30.6 us (22%)
  other arithmetic  21.3 us (16%)
  matrix products  19.9 us (15%)
  local copies, waits for them, and re-layouts  14.7 us (11%)
    all_to_all x1, waiting for transfers between devices, on_device(): lax.all_to_all(payload, ('sub', 'rng'), split_axis=0, concat_axis=0, tile...  27.9 us
    ppermute x5, waiting for transfers between devices, from_partner(): lax.ppermute(value, axis, [(i, i ^ 1 << apart) for i in range(lax.axis_si...  16.8 us
    neg x8, other arithmetic, merge_matrix(): upper = jnp.concatenate([g_real, -g_imag], axis=1)  15.9 us
    all_to_all x1, starting transfers between devices, on_device(): lax.all_to_all(labels, ('sub', 'rng'), split_axis=0, concat_axis=0, tiled...  10.4 us
    all_to_all x1, starting transfers between devices, on_device(): lax.all_to_all(payload, ('sub', 'rng'), split_axis=0, concat_axis=0, tile...  9.61 us
    ppermute x5, starting transfers between devices, from_partner(): lax.ppermute(value, axis, [(i, i ^ 1 << apart) for i in range(lax.axis_si...  9.17 us
    dot_general x2, matrix products, on_device(): jnp.dot(theirs, old[m ^ bit], preferred_element_type=jnp.float32)  3.96 us
    ppermute x1, waiting for transfers between devices, shifted(): lax.ppermute(value, axis, [(source, source + steps) for source in range(f...  3.91 us
  transfers between devices with their start and end apart: 8, of which 4 were waited for; matrix products, arithmetic and copies ran while one was open for 34% of the time, Pallas kernels for 0%

profile of v18, /device:TPU:1, one launch (start us, length us, event | category | flops | bytes accessed | tf_op | source)
XLA Modules:
  0.0 135.9 jit_solution(3041578421673370749)
XLA Ops:
  0.0 1.4 %collective-permute-start = (bf16[2,512,512]{2,1,0:T(8,128)(2,1)}, bf16[2,512,512]{2,1,0:T(8,128)(2,1)}, u32[]{:S(2)}, u32[]{:S(2)}) collective-permute-start(bf16[2,512,512]{2,1,0:T(8,128)(2,1)} %param.6), channel_id=1, source_target_pairs={{1,0},{2,1},{3,2},{4,3},{5,4},{6,5},{7,6},{8,7},{9,8},{10,9},{11,1... | collective-permute-start | bytes 3145736 | tf_op jit(solution)/shard_map/ppermute | solution.py:12
  1.4 2.2 %slice_bitcast_fusion.3 = (bf16[512,512]{1,0:T(8,128)(2,1)}, bf16[512,512]{1,0:T(8,128)(2,1)}) fusion(bf16[2,512,512]{2,1,0:T(8,128)(2,1)} %param.6), kind=kLoop, calls=%fused_computation.323 | loop fusion | bytes 2097152 | tf_op jit(solution)/shard_map/squeeze | solution.py:66
  4.2 0.2 fusion.312
  4.5 1.3 tile.9
  6.0 0.5 reshape.177
  6.6 1.3 tile.21
  7.9 1.0 slice.1003
  9.0 1.5 %reshape.178 = bf16[512,1024]{1,0:T(8,128)(2,1)S(1)} reshape(bf16[524288]{0:T(1024)(128)(2,1)} %slice.1003) | data formatting | bytes 2097152 | tf_op jit(solution)/shard_map/reshape | solution.py:25
  10.6 0.3 select_reduce_fusion
  11.3 1.5 %fusion.105 = (bf16[512,1024]{0,1:T(8,128)(2,1)}, bf16[512,1024]{0,1:T(8,128)(2,1)}) fusion(bf16[1024,512]{0,1:T(8,128)(2,1)S(1)} %bitcast.122, bf16[1024,512]{0,1:T(8,128)(2,1)S(1)} %bitcast_negate_fusion, bf16[1024,512]{0,1:T(8,128)(2,1)S(1)} %bitcast.120), kind=kLoop, calls=%fused_computation.105 | loop fusion | flops 4194304 | bytes 5242880 | tf_op jit(solution)/shard_map/concatenate | solution.py:28
  12.8 2.7 %fusion.345 = (bf16[512,512]{1,0:T(8,128)(2,1)}, bf16[512,512]{1,0:T(8,128)(2,1)}, bf16[512,512]{1,0:T(8,128)(2,1)}) fusion(bf16[512]{0:T(512)(128)(2,1)S(1)} %get-tuple-element.138, bf16[512]{0:T(512)(128)(2,1)S(1)} %get-tuple-element.139, bf16[512]{0:T(512)(128)(2,1)S(1)} %get-tuple-element.140, bf16[512]{0:T(512)(128)(2,1)S(1)} %get-tuple-element.141, ...), kind=kLoop, calls=%fused_computation.543 | loop fusion | flops 7340032 | bytes 1591296 | tf_op jit(solution)/shard_map/neg | solution.py:43
  15.6 0.7 sub.137
  16.3 3.1 %fusion.17 = f32[512,1024]{1,0:T(8,128)S(1)} fusion(bf16[512,1024]{0,1:T(8,128)(2,1)} %get-tuple-element.162, bf16[512,1024]{0,1:T(8,128)(2,1)} %get-tuple-element.161, bf16[512,512]{1,0:T(8,128)(2,1)} %get-tuple-element.160, bf16[512,512]{1,0:T(8,128)(2,1)} %get-tuple-element.159), kind=kOutput, calls=%fused_computation.21 | convolution fusion | flops 1080033280 | bytes 5242880 | tf_op jit(solution)/shard_map/dot_general | solution.py:65
  19.4 1.7 %fusion.346 = (bf16[512,512]{1,0:T(8,128)(2,1)S(1)}, bf16[512,512]{1,0:T(8,128)(2,1)S(1)}, bf16[512,512]{1,0:T(8,128)(2,1)S(1)}) fusion(bf16[512]{0:T(512)(128)(2,1)S(1)} %get-tuple-element.122, bf16[512]{0:T(512)(128)(2,1)S(1)} %get-tuple-element.123, bf16[512]{0:T(512)(128)(2,1)S(1)} %get-tuple-element.124, bf16[512]{0:T(512)(128)(2,1)S(1)} %get-tuple-element.125, ...), kind=kLoop, calls=%fused_computation.544 | loop fusion | flops 7340032 | bytes 1591296 | tf_op jit(solution)/shard_map/neg | solution.py:43
  21.2 1.7 %fusion.347 = (bf16[512,512]{1,0:T(8,128)(2,1)S(1)}, bf16[512,512]{1,0:T(8,128)(2,1)S(1)}, bf16[512,512]{1,0:T(8,128)(2,1)S(1)}) fusion(bf16[512]{0:T(512)(128)(2,1)S(1)} %get-tuple-element.90, bf16[512]{0:T(512)(128)(2,1)S(1)} %get-tuple-element.91, bf16[512]{0:T(512)(128)(2,1)S(1)} %get-tuple-element.92, bf16[512]{0:T(512)(128)(2,1)S(1)} %get-tuple-element.93, ...), kind=kLoop, calls=%fused_computation.545 | loop fusion | flops 7340032 | bytes 1591296 | tf_op jit(solution)/shard_map/neg | solution.py:43
  22.9 3.9 %collective-permute-done = bf16[2,512,512]{2,1,0:T(8,128)(2,1)} collective-permute-done((bf16[2,512,512]{2,1,0:T(8,128)(2,1)}, bf16[2,512,512]{2,1,0:T(8,128)(2,1)}, u32[]{:S(2)}, u32[]{:S(2)}) %collective-permute-start) | collective-permute-done | bytes 1048608 | tf_op jit(solution)/shard_map/ppermute | solution.py:12
  26.9 1.3 slice_bitcast_fusion.1
  28.1 1.3 add_convert_fusion.2
  29.5 1.7 %collective-permute-start.1 = (bf16[1024,512]{1,0:T(8,128)(2,1)S(1)}, bf16[1024,512]{1,0:T(8,128)(2,1)S(1)}, u32[]{:S(2)}, u32[]{:S(2)}) collective-permute-start(bf16[1024,512]{1,0:T(8,128)(2,1)S(1)} %bitcast.124), channel_id=1, source_target_pairs={{0,16},{16,0},{32,48},{48,32},{64,80},{80,64},{96,112},{112,96},{1... | collective-permute-start | bytes 3145736 | tf_op jit(solution)/shard_map/ppermute | solution.py:16
  31.3 1.7 %fusion.348 = (bf16[512,512]{1,0:T(8,128)(2,1)S(1)}, bf16[512,512]{1,0:T(8,128)(2,1)S(1)}, bf16[512,512]{1,0:T(8,128)(2,1)S(1)}) fusion(bf16[512]{0:T(512)(128)(2,1)S(1)} %get-tuple-element.74, bf16[512]{0:T(512)(128)(2,1)S(1)} %get-tuple-element.75, bf16[512]{0:T(512)(128)(2,1)S(1)} %get-tuple-element.76, bf16[512]{0:T(512)(128)(2,1)S(1)} %get-tuple-element.77, ...), kind=kLoop, calls=%fused_computation.546 | loop fusion | flops 7340032 | bytes 1591296 | tf_op jit(solution)/shard_map/neg | solution.py:43
  33.0 1.2 fusion.9
  34.3 1.2 add_convert_fusion.1
  35.5 3.9 %collective-permute-start.5 = (bf16[2,2,512,8]{2,3,1,0:T(8,128)(2,1)S(1)}, bf16[2,2,512,8]{2,3,1,0:T(8,128)(2,1)S(1)}, u32[]{:S(2)}, u32[]{:S(2)}) collective-permute-start(bf16[2,2,512,8]{2,3,1,0:T(8,128)(2,1)S(1)} %slice_bitcast_fusion.4), channel_id=1, source_target_pairs={{0,64},{16,80},{32,96},{48,112},{64,0},{80,16},{96,32},{112,48},{1... | collective-permute-start | bytes 98312 | tf_op jit(solution)/shard_map/ppermute | solution.py:16
  39.6 1.0 collective-permute-start.2
  40.8 1.2 fusion.37
  42.0 1.7 %fusion.344 = (bf16[512,512]{1,0:T(8,128)(2,1)S(1)}, bf16[512,512]{1,0:T(8,128)(2,1)S(1)}, bf16[512,512]{1,0:T(8,128)(2,1)S(1)}) fusion(bf16[512]{0:T(512)(128)(2,1)S(1)} %get-tuple-element.42, bf16[512]{0:T(512)(128)(2,1)S(1)} %get-tuple-element.43, bf16[512]{0:T(512)(128)(2,1)S(1)} %get-tuple-element.44, bf16[512]{0:T(512)(128)(2,1)S(1)} %get-tuple-element.45, ...), kind=kLoop, calls=%fused_computation.542 | loop fusion | flops 7340032 | bytes 1591296 | tf_op jit(solution)/shard_map/neg | solution.py:43
  43.8 1.7 %fusion.349 = (bf16[512,512]{1,0:T(8,128)(2,1)S(1)}, bf16[512,512]{1,0:T(8,128)(2,1)S(1)}, bf16[512,512]{1,0:T(8,128)(2,1)S(1)}) fusion(bf16[512]{0:T(512)(128)(2,1)S(1)} %get-tuple-element.26, bf16[512]{0:T(512)(128)(2,1)S(1)} %get-tuple-element.27, bf16[512]{0:T(512)(128)(2,1)S(1)} %get-tuple-element.28, bf16[512]{0:T(512)(128)(2,1)S(1)} %get-tuple-element.29, ...), kind=kLoop, calls=%fused_computation.547 | loop fusion | flops 7340032 | bytes 1591296 | tf_op jit(solution)/shard_map/neg | solution.py:43
  45.8 1.7 %fusion.351 = (bf16[512,512]{1,0:T(8,128)(2,1)S(1)}, bf16[512,512]{1,0:T(8,128)(2,1)S(1)}, bf16[512,512]{1,0:T(8,128)(2,1)S(1)}) fusion(bf16[512]{0:T(512)(128)(2,1)S(1)} %get-tuple-element.106, bf16[512]{0:T(512)(128)(2,1)S(1)} %get-tuple-element.107, bf16[512]{0:T(512)(128)(2,1)S(1)} %get-tuple-element.108, bf16[512]{0:T(512)(128)(2,1)S(1)} %get-tuple-element.109, ...), kind=kLoop, calls=%fused_computation.549 | loop fusion | flops 7340032 | bytes 1591296 | tf_op jit(solution)/shard_map/neg | solution.py:43
  47.6 16.8 %collective-permute-done.2 = bf16[1024,512]{1,0:T(8,128)(2,1)S(1)} collective-permute-done((bf16[1024,512]{1,0:T(8,128)(2,1)S(1)}, bf16[1024,512]{1,0:T(8,128)(2,1)S(1)}, u32[]{:S(2)}, u32[]{:S(2)}) %collective-permute-start.2) | collective-permute-done | bytes 1048608 | tf_op jit(solution)/shard_map/ppermute | solution.py:16
  64.4 1.2 add_convert_fusion
  65.6 0.9 constant_dynamic-slice_fusion
  66.5 2.4 %collective-permute-start.3 = (bf16[1024,256]{1,0:T(8,128)(2,1)}, bf16[1024,256]{1,0:T(8,128)(2,1)}, u32[]{:S(2)}, u32[]{:S(2)}) collective-permute-start(bf16[1024,256]{1,0:T(8,128)(2,1)} %constant_dynamic-slice_fusion), channel_id=1, source_target_pairs={{0,64},{16,80},{32,96},{48,112},{64,0},{80,16},{96,32},{112,48},{1... | collective-permute-start | bytes 1572872 | tf_op jit(solution)/shard_map/ppermute | solution.py:16
  69.0 2.7 %fusion.350 = (bf16[512,512]{1,0:T(8,128)(2,1)}, bf16[512,512]{1,0:T(8,128)(2,1)}, bf16[512,512]{1,0:T(8,128)(2,1)}) fusion(bf16[512]{0:T(512)(128)(2,1)S(1)} %get-tuple-element.58, bf16[512]{0:T(512)(128)(2,1)S(1)} %get-tuple-element.59, bf16[512]{0:T(512)(128)(2,1)S(1)} %get-tuple-element.60, bf16[512]{0:T(512)(128)(2,1)S(1)} %get-tuple-element.61, ...), kind=kLoop, calls=%fused_computation.548 | loop fusion | flops 7340032 | bytes 1591296 | tf_op jit(solution)/shard_map/neg | solution.py:43
  71.7 1.7 %fusion.29 = f32[1024,256]{1,0:T(8,128)} fusion(bf16[512,512]{1,0:T(8,128)(2,1)S(1)} %get-tuple-element.213, bf16[512,512]{1,0:T(8,128)(2,1)S(1)} %get-tuple-element.186, bf16[512,512]{1,0:T(8,128)(2,1)S(1)} %get-tuple-element.185, bf16[1024,512]{1,0:T(8,128)(2,1)S(1)} %add_convert_fusion, s32[]{:T(128)S(6)} %select_n.476), kind=kOutput, calls=%fused_computation.33 | convolution fusion | flops 545259520 | bytes 3145732 | tf_op jit(solution)/shard_map/dot_general | solution.py:115
  73.4 10.4 %all-to-all-start = ((s32[128,1,8]{2,1,0:T(1,128)}), s32[128,1,8]{2,1,0:T(1,128)S(1)}, u32[]{:S(2)}, u32[]{:S(2)}) async-start(s32[128,1,8]{2,1,0:T(1,128)} %bitcast.33), calls=%async_computation | async-start | bytes 131072 | tf_op jit(solution)/shard_map/all_to_all | solution.py:118
  83.8 1.9 %fusion.69 = f32[1024,256]{1,0:T(8,128)S(1)} fusion(bf16[512,512]{1,0:T(8,128)(2,1)S(1)} %get-tuple-element.217, bf16[512,512]{1,0:T(8,128)(2,1)S(1)} %get-tuple-element.194, bf16[512,512]{1,0:T(8,128)(2,1)S(1)} %get-tuple-element.193, bf16[1024,512]{1,0:T(8,128)(2,1)} %copy-done.6, s32[]{:T(128)S(6)} %select_n.476), kind=kOutput, calls=%fused_computation.73 | convolution fusion | flops 545259520 | bytes 3145732 | tf_op jit(solution)/shard_map/dot_general | solution.py:119
  85.7 1.8 %fusion.102 = bf16[1024,256]{1,0:T(8,128)(2,1)S(1)} fusion(f32[1024,256]{1,0:T(8,128)S(1)} %fusion.69, bf16[1024,256]{1,0:T(8,128)(2,1)} %collective-permute-done.3, bf16[512,512]{1,0:T(8,128)(2,1)S(1)} %copy-done.5, bf16[512,512]{1,0:T(8,128)(2,1)S(1)} %copy-done.4, bf16[512,512]{1,0:T(8,128)(2,1)S(1)} %copy-done.3), kind=kOutput, calls=%fused_computation.104 | convolution fusion | flops 545783808 | bytes 3670016 | tf_op jit(solution)/shard_map/dot_general | solution.py:115
  87.5 0.2 copy.47
  87.7 2.1 %fusion.99 = bf16[1024,256]{1,0:T(8,128)(2,1)S(1)} fusion(f32[1024,256]{1,0:T(8,128)} %fusion.29, bf16[1024,256]{1,0:T(8,128)(2,1)} %collective-permute-done.3, bf16[512,512]{1,0:T(8,128)(2,1)S(1)} %get-tuple-element.212, bf16[512,512]{1,0:T(8,128)(2,1)S(1)} %get-tuple-element.184, bf16[512,512]{1,0:T(8,128)(2,1)S(1)} %get-tuple-element.183), kind=kOutput, calls=%fused_computation.103 | convolution fusion | flops 545783808 | bytes 3670016 | tf_op jit(solution)/shard_map/dot_general | solution.py:119
  89.8 0.2 copy.46
  90.0 0.8 fusion.89
  90.8 0.7 fusion.90
  91.5 1.7 %pad_maximum_fusion.2 = bf16[128,16,512]{2,1,0:T(8,128)(2,1)} fusion(bf16[128,8,512]{2,1,0:T(8,128)(2,1)S(1)} %fusion.90, bf16[128,8,512]{2,1,0:T(8,128)(2,1)S(1)} %fusion.89), kind=kLoop, calls=%fused_computation.81 | loop fusion | flops 4194304 | bytes 4194304 | tf_op jit(solution)/shard_map/concatenate | solution.py:129
  93.4 9.6 %all-to-all-start.1 = ((bf16[128,16,512]{2,1,0:T(8,128)(2,1)}), bf16[128,16,512]{2,1,0:T(8,128)(2,1)S(1)}, u32[]{:S(2)}, u32[]{:S(2)}) async-start(bf16[128,16,512]{2,1,0:T(8,128)(2,1)} %pad_maximum_fusion.2), calls=%async_computation.1 | async-start | bytes 4194304 | tf_op jit(solution)/shard_map/all_to_all | solution.py:130
  104.7 27.9 %all-to-all-done.1 = bf16[128,16,512]{2,1,0:T(8,128)(2,1)S(1)} async-done(((bf16[128,16,512]{2,1,0:T(8,128)(2,1)}), bf16[128,16,512]{2,1,0:T(8,128)(2,1)S(1)}, u32[]{:S(2)}, u32[]{:S(2)}) %all-to-all-start.1) | async-done | bytes 2097184 | tf_op jit(solution)/shard_map/all_to_all | solution.py:130
  132.9 0.8 fusion.97
  133.8 0.8 fusion.98
  134.8 1.1 maximum_bitcast_fusion
  (93 shorter events, 4.4 us)
Async XLA Ops:
  0.0 3.7 %copy-start.7 = (bf16[3,1,2,2,512,8]{4,5,3,2,1,0:T(8,128)(2,1)S(1)}, bf16[3,1,2,2,512,8]{4,5,3,2,1,0:T(8,128)(2,1)}, u32[]{:S(2)}) copy-start(bf16[3,1,2,2,512,8]{4,5,3,2,1,0:T(8,128)(2,1)} %param.9) | copy-start | bytes 294916
  0.0 3.7 %copy-start.8 = (s32[1,1,512,1]{2,3,1,0:T(1,128)S(1)}, s32[1,1,512,1]{2,3,1,0:T(1,128)}, u32[]{:S(2)}) copy-start(s32[1,1,512,1]{2,3,1,0:T(1,128)} %param.10) | copy-start | bytes 6148
  0.0 4.4 %copy-start.10 = (bf16[2,512]{1,0:T(2,128)(2,1)S(1)}, bf16[2,512]{1,0:T(2,128)(2,1)}, u32[]{:S(2)}) copy-start(bf16[2,512]{1,0:T(2,128)(2,1)} %param.7) | copy-start | bytes 6148
  0.0 26.8 %collective-permute-start = (bf16[2,512,512]{2,1,0:T(8,128)(2,1)}, bf16[2,512,512]{2,1,0:T(8,128)(2,1)}, u32[]{:S(2)}, u32[]{:S(2)}) collective-permute-start(bf16[2,512,512]{2,1,0:T(8,128)(2,1)} %param.6), channel_id=1, source_target_pairs={{1,0},{2,1},{3,2},{4,3},{5,4},{6,5},{7,6},{8,7},{9,8},{10,9},{11,1... | collective-permute-start | bytes 3145736 | tf_op jit(solution)/shard_map/ppermute | solution.py:12
  9.0 1.6 %copy-start.9 = (s32[3,1,2,512]{3,2,1,0:T(2,128)S(1)}, s32[3,1,2,512]{3,2,1,0:T(2,128)}, u32[]{:S(2)}) copy-start(s32[3,1,2,512]{3,2,1,0:T(2,128)} %param.8) | copy-start | bytes 36868
  9.0 1.7 %copy-start.11 = (s32[1,1,512]{2,1,0:T(1,128)S(1)}, s32[1,1,512]{2,1,0:T(1,128)}, u32[]{:S(2)}) copy-start(s32[1,1,512]{2,1,0:T(1,128)} %param.11) | copy-start | bytes 6148
  29.4 3.6 %copy-start = (bf16[512,512]{1,0:T(8,128)(2,1)S(1)}, bf16[512,512]{1,0:T(8,128)(2,1)}, u32[]{:S(2)}) copy-start(bf16[512,512]{1,0:T(8,128)(2,1)} %get-tuple-element.197) | copy-start | bytes 1572868
  29.4 3.6 %copy-start.1 = (bf16[512,512]{1,0:T(8,128)(2,1)S(1)}, bf16[512,512]{1,0:T(8,128)(2,1)}, u32[]{:S(2)}) copy-start(bf16[512,512]{1,0:T(8,128)(2,1)} %get-tuple-element.198) | copy-start | bytes 1572868
  29.4 3.6 %copy-start.2 = (bf16[512,512]{1,0:T(8,128)(2,1)S(1)}, bf16[512,512]{1,0:T(8,128)(2,1)}, u32[]{:S(2)}) copy-start(bf16[512,512]{1,0:T(8,128)(2,1)} %get-tuple-element.219) | copy-start | bytes 1572868
  29.5 4.7 %collective-permute-start.1 = (bf16[1024,512]{1,0:T(8,128)(2,1)S(1)}, bf16[1024,512]{1,0:T(8,128)(2,1)S(1)}, u32[]{:S(2)}, u32[]{:S(2)}) collective-permute-start(bf16[1024,512]{1,0:T(8,128)(2,1)S(1)} %bitcast.124), channel_id=1, source_target_pairs={{0,16},{16,0},{32,48},{48,32},{64,80},{80,64},{96,112},{112,96},{1... | collective-permute-start | bytes 3145736 | tf_op jit(solution)/shard_map/ppermute | solution.py:16
  35.5 10.1 %collective-permute-start.5 = (bf16[2,2,512,8]{2,3,1,0:T(8,128)(2,1)S(1)}, bf16[2,2,512,8]{2,3,1,0:T(8,128)(2,1)S(1)}, u32[]{:S(2)}, u32[]{:S(2)}) collective-permute-start(bf16[2,2,512,8]{2,3,1,0:T(8,128)(2,1)S(1)} %slice_bitcast_fusion.4), channel_id=1, source_target_pairs={{0,64},{16,80},{32,96},{48,112},{64,0},{80,16},{96,32},{112,48},{1... | collective-permute-start | bytes 98312 | tf_op jit(solution)/shard_map/ppermute | solution.py:16
  39.5 6.1 %collective-permute-start.4 = (s32[1536]{0:T(1024)S(1)}, s32[1536]{0:T(1024)S(1)}, u32[]{:S(2)}, u32[]{:S(2)}) collective-permute-start(s32[1536]{0:T(1024)S(1)} %pad_add_fusion.2), channel_id=1, source_target_pairs={{0,64},{16,80},{32,96},{48,112},{64,0},{80,16},{96,32},{112,48},{1... | collective-permute-start | bytes 18440 | tf_op jit(solution)/shard_map/ppermute | solution.py:16
  39.6 24.8 %collective-permute-start.2 = (bf16[1024,512]{1,0:T(8,128)(2,1)S(1)}, bf16[1024,512]{1,0:T(8,128)(2,1)S(1)}, u32[]{:S(2)}, u32[]{:S(2)}) collective-permute-start(bf16[1024,512]{1,0:T(8,128)(2,1)S(1)} %add_convert_fusion.1), channel_id=1, source_target_pairs={{0,32},{16,48},{32,0},{48,16},{64,96},{80,112},{96,64},{112,80},{1... | collective-permute-start | bytes 3145736 | tf_op jit(solution)/shard_map/ppermute | solution.py:16
  65.6 7.8 %copy-start.6 = (bf16[1024,512]{1,0:T(8,128)(2,1)}, bf16[1024,512]{1,0:T(8,128)(2,1)S(1)}, u32[]{:S(2)}) copy-start(bf16[1024,512]{1,0:T(8,128)(2,1)S(1)} %add_convert_fusion) | copy-start | bytes 3145732
  66.5 19.2 %collective-permute-start.3 = (bf16[1024,256]{1,0:T(8,128)(2,1)}, bf16[1024,256]{1,0:T(8,128)(2,1)}, u32[]{:S(2)}, u32[]{:S(2)}) collective-permute-start(bf16[1024,256]{1,0:T(8,128)(2,1)} %constant_dynamic-slice_fusion), channel_id=1, source_target_pairs={{0,64},{16,80},{32,96},{48,112},{64,0},{80,16},{96,32},{112,48},{1... | collective-permute-start | bytes 1572872 | tf_op jit(solution)/shard_map/ppermute | solution.py:16
  73.4 20.0 %all-to-all-start = ((s32[128,1,8]{2,1,0:T(1,128)}), s32[128,1,8]{2,1,0:T(1,128)S(1)}, u32[]{:S(2)}, u32[]{:S(2)}) async-start(s32[128,1,8]{2,1,0:T(1,128)} %bitcast.33), calls=%async_computation | async-start | bytes 131072 | tf_op jit(solution)/shard_map/all_to_all | solution.py:118
  83.8 1.9 %copy-start.3 = (bf16[512,512]{1,0:T(8,128)(2,1)S(1)}, bf16[512,512]{1,0:T(8,128)(2,1)}, u32[]{:S(2)}) copy-start(bf16[512,512]{1,0:T(8,128)(2,1)} %get-tuple-element.187) | copy-start | bytes 1572868
  83.8 1.9 %copy-start.4 = (bf16[512,512]{1,0:T(8,128)(2,1)S(1)}, bf16[512,512]{1,0:T(8,128)(2,1)}, u32[]{:S(2)}) copy-start(bf16[512,512]{1,0:T(8,128)(2,1)} %get-tuple-element.188) | copy-start | bytes 1572868
  83.8 1.9 %copy-start.5 = (bf16[512,512]{1,0:T(8,128)(2,1)S(1)}, bf16[512,512]{1,0:T(8,128)(2,1)}, u32[]{:S(2)}) copy-start(bf16[512,512]{1,0:T(8,128)(2,1)} %get-tuple-element.214) | copy-start | bytes 1572868
  93.4 39.3 %all-to-all-start.1 = ((bf16[128,16,512]{2,1,0:T(8,128)(2,1)}), bf16[128,16,512]{2,1,0:T(8,128)(2,1)S(1)}, u32[]{:S(2)}, u32[]{:S(2)}) async-start(bf16[128,16,512]{2,1,0:T(8,128)(2,1)} %pad_maximum_fusion.2), calls=%async_computation.1 | async-start | bytes 4194304 | tf_op jit(solution)/shard_map/all_to_all | solution.py:130

commit v19 on v18

--- a/solution.py
+++ b/solution.py
@@ -87,8 +87,13 @@
         mine = merge_matrix(offsets[section, 0, 0], weights[section, 0, 0])
         theirs = merge_matrix(offsets[section, 0, 1], weights[section, 0, 1])
         merged = jnp.dot(mine, image, preferred_element_type=jnp.float32)
+        if section == 1:
+            labels, merged = lax.optimization_barrier((labels, merged))
+            marks = lax.all_to_all(labels, ("sub", "rng"), split_axis=0, concat_axis=0, tiled=True)
         merged = merged + jnp.dot(theirs, partner, preferred_element_type=jnp.float32)
         image = merged.astype(jnp.bfloat16)
+        if section == 1:
+            marks, image = lax.optimization_barrier((marks, image))
         if section == 0:
             late, image = lax.optimization_barrier((late, image))
             own_offsets, own_weights, slot = late
@@ -113,9 +118,6 @@
         mine = merge_matrix(starts[0], kernel[0])
         theirs = merge_matrix(starts[1], kernel[1])
         merged = jnp.dot(mine, old[m], preferred_element_type=jnp.float32)
-        if m == 0:
-            labels, merged = lax.optimization_barrier((labels, merged))
-            marks = lax.all_to_all(labels, ("sub", "rng"), split_axis=0, concat_axis=0, tiled=True)
         merged = merged + jnp.dot(theirs, old[m ^ bit], preferred_element_type=jnp.float32)
         piece = merged.astype(jnp.bfloat16)
         rows = piece.reshape(2, p_dev, half).transpose(1, 0, 2).reshape(p_dev, 2 * half)

time: 136 us -> 138 us (1.015)
  waiting for transfers between devices: 48.8 us -> 39.6 us
  starting transfers between devices: 30.6 us -> 35.9 us
  matrix products: 19.9 us -> 23.4 us
    ppermute x5, waiting for transfers between devices: 16.8 us -> 7.54 us  [from_partner(): lax.ppermute(value, axis, [(i, i ^ 1 << apart) for i in range(lax.axis_si...]
    dot_general x2, matrix products: 2.49 us -> 5.66 us  [on_device(): jnp.dot(theirs, partner, preferred_element_type=jnp.float32)]
    all_to_all x1, starting transfers between devices: 9.61 us -> 12.7 us  [on_device(): lax.all_to_all(payload, ('sub', 'rng'), split_axis=0, concat_axis=0, tile...]
    dot_general x2, matrix products: 2.48 us -> 5.09 us  [on_device(): merged = jnp.dot(mine, image, preferred_element_type=jnp.float32)]
    all_to_all x1, starting transfers between devices: 10.4 us -> 12.3 us  [on_device(): lax.all_to_all(labels, ('sub', 'rng'), split_axis=0, concat_axis=0, tiled...]
  transfers between devices with their start and end apart: 8 -> 8, of which waited for: 4 -> 4; matrix products, arithmetic and copies ran while one was open for 34% -> 33% of each run, Pallas kernels for 0% -> 0%
where the time goes in v19:
time: 138 us; the launch traced here: 137 us
  waiting for transfers between devices  39.6 us (29%)
  starting transfers between devices  35.9 us (26%)
  matrix products  23.4 us (17%)
  other arithmetic  22.4 us (16%)
  local copies, waits for them, and re-layouts  15.5 us (11%)
    all_to_all x1, waiting for transfers between devices, on_device(): lax.all_to_all(payload, ('sub', 'rng'), split_axis=0, concat_axis=0, tile...  28.1 us
    neg x8, other arithmetic, merge_matrix(): upper = jnp.concatenate([g_real, -g_imag], axis=1)  17 us
    all_to_all x1, starting transfers between devices, on_device(): lax.all_to_all(payload, ('sub', 'rng'), split_axis=0, concat_axis=0, tile...  12.7 us
    all_to_all x1, starting transfers between devices, on_device(): lax.all_to_all(labels, ('sub', 'rng'), split_axis=0, concat_axis=0, tiled...  12.3 us
    ppermute x5, starting transfers between devices, from_partner(): lax.ppermute(value, axis, [(i, i ^ 1 << apart) for i in range(lax.axis_si...  9.4 us
    ppermute x5, waiting for transfers between devices, from_partner(): lax.ppermute(value, axis, [(i, i ^ 1 << apart) for i in range(lax.axis_si...  7.54 us
    dot_general x2, matrix products, on_device(): jnp.dot(theirs, partner, preferred_element_type=jnp.float32)  5.66 us
    dot_general x2, matrix products, on_device(): merged = jnp.dot(mine, image, preferred_element_type=jnp.float32)  5.09 us
  transfers between devices with their start and end apart: 8, of which 4 were waited for; matrix products, arithmetic and copies ran while one was open for 33% of the time, Pallas kernels for 0%

profile of v19, /device:TPU:1, one launch (start us, length us, event | category | flops | bytes accessed | tf_op | source)
XLA Modules:
  0.0 137.3 jit_solution(3676175234944116958)
XLA Ops:
  0.0 1.4 %collective-permute-start = (bf16[2,512,512]{2,1,0:T(8,128)(2,1)}, bf16[2,512,512]{2,1,0:T(8,128)(2,1)}, u32[]{:S(2)}, u32[]{:S(2)}) collective-permute-start(bf16[2,512,512]{2,1,0:T(8,128)(2,1)} %param.6), channel_id=1, source_target_pairs={{1,0},{2,1},{3,2},{4,3},{5,4},{6,5},{7,6},{8,7},{9,8},{10,9},{11,1... | collective-permute-start | bytes 3145736 | tf_op jit(solution)/shard_map/ppermute | solution.py:12
  1.4 2.2 %slice_bitcast_fusion.3 = (bf16[512,512]{1,0:T(8,128)(2,1)}, bf16[512,512]{1,0:T(8,128)(2,1)}) fusion(bf16[2,512,512]{2,1,0:T(8,128)(2,1)} %param.6), kind=kLoop, calls=%fused_computation.323 | loop fusion | bytes 2097152 | tf_op jit(solution)/shard_map/squeeze | solution.py:66
  4.2 0.2 fusion.312
  4.5 1.3 tile.9
  6.0 0.5 reshape.160
  6.6 1.3 tile.21
  7.9 1.0 slice.1011
  9.0 1.5 %reshape.161 = bf16[512,1024]{1,0:T(8,128)(2,1)S(1)} reshape(bf16[524288]{0:T(1024)(128)(2,1)} %slice.1011) | data formatting | bytes 2097152 | tf_op jit(solution)/shard_map/reshape | solution.py:25
  10.6 0.3 select_reduce_fusion
  11.3 1.5 %fusion.105 = (bf16[512,1024]{0,1:T(8,128)(2,1)}, bf16[512,1024]{0,1:T(8,128)(2,1)}) fusion(bf16[1024,512]{0,1:T(8,128)(2,1)S(1)} %bitcast.124, bf16[1024,512]{0,1:T(8,128)(2,1)S(1)} %bitcast_negate_fusion, bf16[1024,512]{0,1:T(8,128)(2,1)S(1)} %bitcast.122), kind=kLoop, calls=%fused_computation.105 | loop fusion | flops 4194304 | bytes 5242880 | tf_op jit(solution)/shard_map/concatenate | solution.py:28
  12.8 2.7 %fusion.345 = (bf16[512,512]{1,0:T(8,128)(2,1)}, bf16[512,512]{1,0:T(8,128)(2,1)}, bf16[512,512]{1,0:T(8,128)(2,1)}) fusion(bf16[512]{0:T(512)(128)(2,1)S(1)} %get-tuple-element.134, bf16[512]{0:T(512)(128)(2,1)S(1)} %get-tuple-element.135, bf16[512]{0:T(512)(128)(2,1)S(1)} %get-tuple-element.136, bf16[512]{0:T(512)(128)(2,1)S(1)} %get-tuple-element.137, ...), kind=kLoop, calls=%fused_computation.535 | loop fusion | flops 7340032 | bytes 1591296 | tf_op jit(solution)/shard_map/neg | solution.py:43
  15.6 0.7 sub.137
  16.3 3.1 %fusion.25 = f32[512,1024]{1,0:T(8,128)S(1)} fusion(bf16[512,1024]{0,1:T(8,128)(2,1)} %get-tuple-element.158, bf16[512,1024]{0,1:T(8,128)(2,1)} %get-tuple-element.157, bf16[512,512]{1,0:T(8,128)(2,1)} %get-tuple-element.156, bf16[512,512]{1,0:T(8,128)(2,1)} %get-tuple-element.155), kind=kOutput, calls=%fused_computation.29 | convolution fusion | flops 1080033280 | bytes 5242880 | tf_op jit(solution)/shard_map/dot_general | solution.py:65
  19.4 1.7 %fusion.346 = (bf16[512,512]{1,0:T(8,128)(2,1)S(1)}, bf16[512,512]{1,0:T(8,128)(2,1)S(1)}, bf16[512,512]{1,0:T(8,128)(2,1)S(1)}) fusion(bf16[512]{0:T(512)(128)(2,1)S(1)} %get-tuple-element.118, bf16[512]{0:T(512)(128)(2,1)S(1)} %get-tuple-element.119, bf16[512]{0:T(512)(128)(2,1)S(1)} %get-tuple-element.120, bf16[512]{0:T(512)(128)(2,1)S(1)} %get-tuple-element.121, ...), kind=kLoop, calls=%fused_computation.536 | loop fusion | flops 7340032 | bytes 1591296 | tf_op jit(solution)/shard_map/neg | solution.py:43
  21.2 1.7 %fusion.344 = (bf16[512,512]{1,0:T(8,128)(2,1)S(1)}, bf16[512,512]{1,0:T(8,128)(2,1)S(1)}, bf16[512,512]{1,0:T(8,128)(2,1)S(1)}) fusion(bf16[512]{0:T(512)(128)(2,1)S(1)} %get-tuple-element.86, bf16[512]{0:T(512)(128)(2,1)S(1)} %get-tuple-element.87, bf16[512]{0:T(512)(128)(2,1)S(1)} %get-tuple-element.88, bf16[512]{0:T(512)(128)(2,1)S(1)} %get-tuple-element.89, ...), kind=kLoop, calls=%fused_computation.534 | loop fusion | flops 7340032 | bytes 1591296 | tf_op jit(solution)/shard_map/neg | solution.py:43
  22.9 3.9 %collective-permute-done = bf16[2,512,512]{2,1,0:T(8,128)(2,1)} collective-permute-done((bf16[2,512,512]{2,1,0:T(8,128)(2,1)}, bf16[2,512,512]{2,1,0:T(8,128)(2,1)}, u32[]{:S(2)}, u32[]{:S(2)}) %collective-permute-start) | collective-permute-done | bytes 1048608 | tf_op jit(solution)/shard_map/ppermute | solution.py:12
  26.9 1.3 slice_bitcast_fusion.1
  28.1 1.3 add_convert_fusion.2
  29.5 1.7 %collective-permute-start.1 = (bf16[1024,512]{1,0:T(8,128)(2,1)S(1)}, bf16[1024,512]{1,0:T(8,128)(2,1)S(1)}, u32[]{:S(2)}, u32[]{:S(2)}) collective-permute-start(bf16[1024,512]{1,0:T(8,128)(2,1)S(1)} %bitcast.126), channel_id=1, source_target_pairs={{0,16},{16,0},{32,48},{48,32},{64,80},{80,64},{96,112},{112,96},{1... | collective-permute-start | bytes 3145736 | tf_op jit(solution)/shard_map/ppermute | solution.py:16
  31.3 1.7 %fusion.347 = (bf16[512,512]{1,0:T(8,128)(2,1)S(1)}, bf16[512,512]{1,0:T(8,128)(2,1)S(1)}, bf16[512,512]{1,0:T(8,128)(2,1)S(1)}) fusion(bf16[512]{0:T(512)(128)(2,1)S(1)} %get-tuple-element.70, bf16[512]{0:T(512)(128)(2,1)S(1)} %get-tuple-element.71, bf16[512]{0:T(512)(128)(2,1)S(1)} %get-tuple-element.72, bf16[512]{0:T(512)(128)(2,1)S(1)} %get-tuple-element.73, ...), kind=kLoop, calls=%fused_computation.537 | loop fusion | flops 7340032 | bytes 1591296 | tf_op jit(solution)/shard_map/neg | solution.py:43
  33.0 1.2 fusion.17
  34.3 2.2 %add_convert_fusion.1 = bf16[1024,512]{1,0:T(8,128)(2,1)} fusion(f32[1024,512]{1,0:T(8,128)S(1)} %fusion.17, bf16[1024,512]{1,0:T(8,128)(2,1)S(1)} %collective-permute-done.1, bf16[512,512]{1,0:T(8,128)(2,1)S(1)} %get-tuple-element.222, bf16[512,512]{1,0:T(8,128)(2,1)S(1)} %get-tuple-element.200, bf16[512,512]{1,0:T(8,128)(2,1)S(1)} %get-tuple-element.199), kind=kOutput, calls=%fused_computation.86 | convolution fusion | flops 1083179008 | bytes 5767168 | tf_op jit(solution)/shard_map/dot_general | solution.py:93
  36.5 3.8 %collective-permute-start.5 = (bf16[2,2,512,8]{2,3,1,0:T(8,128)(2,1)S(1)}, bf16[2,2,512,8]{2,3,1,0:T(8,128)(2,1)S(1)}, u32[]{:S(2)}, u32[]{:S(2)}) collective-permute-start(bf16[2,2,512,8]{2,3,1,0:T(8,128)(2,1)S(1)} %slice_bitcast_fusion.4), channel_id=1, source_target_pairs={{0,64},{16,80},{32,96},{48,112},{64,0},{80,16},{96,32},{112,48},{1... | collective-permute-start | bytes 98312 | tf_op jit(solution)/shard_map/ppermute | solution.py:16
  40.4 1.0 collective-permute-start.2
  41.4 3.8 %fusion.9 = f32[1024,512]{1,0:T(8,128)} fusion(bf16[1024,512]{1,0:T(8,128)(2,1)} %add_convert_fusion.1, bf16[512,512]{1,0:T(8,128)(2,1)S(1)} %get-tuple-element.220, bf16[512,512]{1,0:T(8,128)(2,1)S(1)} %get-tuple-element.196, bf16[512,512]{1,0:T(8,128)(2,1)S(1)} %get-tuple-element.195), kind=kOutput, calls=%fused_computation.11 | convolution fusion | flops 1082130432 | bytes 4718592 | tf_op jit(solution)/shard_map/dot_general | solution.py:89
  45.3 12.3 %all-to-all-start = ((s32[128,1,8]{2,1,0:T(1,128)}), s32[128,1,8]{2,1,0:T(1,128)S(1)}, u32[]{:S(2)}, u32[]{:S(2)}) async-start(s32[128,1,8]{2,1,0:T(1,128)} %bitcast.27), calls=%async_computation | async-start | bytes 131072 | tf_op jit(solution)/shard_map/all_to_all | solution.py:92
  57.8 1.7 %fusion.348 = (bf16[512,512]{1,0:T(8,128)(2,1)S(1)}, bf16[512,512]{1,0:T(8,128)(2,1)S(1)}, bf16[512,512]{1,0:T(8,128)(2,1)S(1)}) fusion(bf16[512]{0:T(512)(128)(2,1)S(1)} %get-tuple-element.38, bf16[512]{0:T(512)(128)(2,1)S(1)} %get-tuple-element.39, bf16[512]{0:T(512)(128)(2,1)S(1)} %get-tuple-element.40, bf16[512]{0:T(512)(128)(2,1)S(1)} %get-tuple-element.41, ...), kind=kLoop, calls=%fused_computation.538 | loop fusion | flops 7340032 | bytes 1591296 | tf_op jit(solution)/shard_map/neg | solution.py:43
  59.6 2.8 %fusion.349 = (bf16[512,512]{1,0:T(8,128)(2,1)}, bf16[512,512]{1,0:T(8,128)(2,1)}, bf16[512,512]{1,0:T(8,128)(2,1)}) fusion(bf16[512]{0:T(512)(128)(2,1)S(1)} %get-tuple-element.22, bf16[512]{0:T(512)(128)(2,1)S(1)} %get-tuple-element.23, bf16[512]{0:T(512)(128)(2,1)S(1)} %get-tuple-element.24, bf16[512]{0:T(512)(128)(2,1)S(1)} %get-tuple-element.25, ...), kind=kLoop, calls=%fused_computation.539 | loop fusion | flops 7340032 | bytes 1591296 | tf_op jit(solution)/shard_map/neg | solution.py:43
  62.6 2.8 %fusion.351 = (bf16[512,512]{1,0:T(8,128)(2,1)}, bf16[512,512]{1,0:T(8,128)(2,1)}, bf16[512,512]{1,0:T(8,128)(2,1)}) fusion(bf16[512]{0:T(512)(128)(2,1)S(1)} %get-tuple-element.102, bf16[512]{0:T(512)(128)(2,1)S(1)} %get-tuple-element.103, bf16[512]{0:T(512)(128)(2,1)S(1)} %get-tuple-element.104, bf16[512]{0:T(512)(128)(2,1)S(1)} %get-tuple-element.105, ...), kind=kLoop, calls=%fused_computation.541 | loop fusion | flops 7340032 | bytes 1591296 | tf_op jit(solution)/shard_map/neg | solution.py:43
  65.5 0.6 collective-permute-done.2
  66.1 3.4 %add_convert_fusion = bf16[1024,512]{1,0:T(8,128)(2,1)} fusion(f32[1024,512]{1,0:T(8,128)S(1)} %copy-done.16, bf16[1024,512]{1,0:T(8,128)(2,1)} %collective-permute-done.2, bf16[512,512]{1,0:T(8,128)(2,1)S(1)} %get-tuple-element.219, bf16[512,512]{1,0:T(8,128)(2,1)S(1)} %get-tuple-element.194, bf16[512,512]{1,0:T(8,128)(2,1)S(1)} %get-tuple-element.193), kind=kOutput, calls=%fused_computation.85 | convolution fusion | flops 1083179008 | bytes 5767168 | tf_op jit(solution)/shard_map/dot_general | solution.py:93
  69.5 1.2 constant_dynamic-slice_fusion
  70.8 2.7 %collective-permute-start.3 = (bf16[1024,256]{1,0:T(8,128)(2,1)S(1)}, bf16[1024,256]{1,0:T(8,128)(2,1)S(1)}, u32[]{:S(2)}, u32[]{:S(2)}) collective-permute-start(bf16[1024,256]{1,0:T(8,128)(2,1)S(1)} %constant_dynamic-slice_fusion), channel_id=1, source_target_pairs={{0,64},{16,80},{32,96},{48,112},{64,0},{80,16},{96,32},{112,48},{1... | collective-permute-start | bytes 1572872 | tf_op jit(solution)/shard_map/ppermute | solution.py:16
  73.5 1.7 %fusion.350 = (bf16[512,512]{1,0:T(8,128)(2,1)S(1)}, bf16[512,512]{1,0:T(8,128)(2,1)S(1)}, bf16[512,512]{1,0:T(8,128)(2,1)S(1)}) fusion(bf16[512]{0:T(512)(128)(2,1)S(1)} %get-tuple-element.54, bf16[512]{0:T(512)(128)(2,1)S(1)} %get-tuple-element.55, bf16[512]{0:T(512)(128)(2,1)S(1)} %get-tuple-element.56, bf16[512]{0:T(512)(128)(2,1)S(1)} %get-tuple-element.57, ...), kind=kLoop, calls=%fused_computation.540 | loop fusion | flops 7340032 | bytes 1591296 | tf_op jit(solution)/shard_map/neg | solution.py:43
  75.3 0.7 fusion.69
  76.0 1.7 %fusion.45 = f32[1024,256]{1,0:T(8,128)} fusion(bf16[512,512]{1,0:T(8,128)(2,1)S(1)} %get-tuple-element.217, bf16[512,512]{1,0:T(8,128)(2,1)S(1)} %get-tuple-element.190, bf16[512,512]{1,0:T(8,128)(2,1)S(1)} %get-tuple-element.189, bf16[1024,512]{1,0:T(8,128)(2,1)S(1)} %copy-done.9, s32[]{:T(128)S(6)} %select_n.476), kind=kOutput, calls=%fused_computation.49 | convolution fusion | flops 545259520 | bytes 3145732 | tf_op jit(solution)/shard_map/dot_general | solution.py:120
  77.7 6.9 %collective-permute-done.3 = bf16[1024,256]{1,0:T(8,128)(2,1)S(1)} collective-permute-done((bf16[1024,256]{1,0:T(8,128)(2,1)S(1)}, bf16[1024,256]{1,0:T(8,128)(2,1)S(1)}, u32[]{:S(2)}, u32[]{:S(2)}) %collective-permute-start.3) | collective-permute-done | bytes 524320 | tf_op jit(solution)/shard_map/ppermute | solution.py:16
  84.6 0.7 fusion.102
  85.6 0.2 copy-done.3
  86.2 2.1 %fusion.99 = bf16[1024,256]{1,0:T(8,128)(2,1)S(1)} fusion(f32[1024,256]{1,0:T(8,128)} %fusion.45, bf16[1024,256]{1,0:T(8,128)(2,1)} %copy-done.15, bf16[512,512]{1,0:T(8,128)(2,1)S(1)} %copy-done.5, bf16[512,512]{1,0:T(8,128)(2,1)S(1)} %copy-done.4, bf16[512,512]{1,0:T(8,128)(2,1)S(1)} %copy-done.3), kind=kOutput, calls=%fused_computation.103 | convolution fusion | flops 545783808 | bytes 3670016 | tf_op jit(solution)/shard_map/dot_general | solution.py:121
  88.5 0.7 fusion.89
  89.2 0.8 fusion.90
  90.0 1.7 %pad_maximum_fusion.2 = bf16[128,16,512]{2,1,0:T(8,128)(2,1)} fusion(bf16[128,8,512]{2,1,0:T(8,128)(2,1)S(1)} %fusion.90, bf16[128,8,512]{2,1,0:T(8,128)(2,1)S(1)} %fusion.89), kind=kLoop, calls=%fused_computation.81 | loop fusion | flops 4194304 | bytes 4194304 | tf_op jit(solution)/shard_map/concatenate | solution.py:131
  91.7 12.7 %all-to-all-start.1 = ((bf16[128,16,512]{2,1,0:T(8,128)(2,1)}), bf16[128,16,512]{2,1,0:T(8,128)(2,1)S(1)}, u32[]{:S(2)}, u32[]{:S(2)}) async-start(bf16[128,16,512]{2,1,0:T(8,128)(2,1)} %pad_maximum_fusion.2), calls=%async_computation.1 | async-start | bytes 4194304 | tf_op jit(solution)/shard_map/all_to_all | solution.py:132
  106.0 28.1 %all-to-all-done.1 = bf16[128,16,512]{2,1,0:T(8,128)(2,1)S(1)} async-done(((bf16[128,16,512]{2,1,0:T(8,128)(2,1)}), bf16[128,16,512]{2,1,0:T(8,128)(2,1)S(1)}, u32[]{:S(2)}, u32[]{:S(2)}) %all-to-all-start.1) | async-done | bytes 2097184 | tf_op jit(solution)/shard_map/all_to_all | solution.py:132
  134.3 0.8 fusion.97
  135.3 0.8 fusion.98
  136.3 1.1 maximum_bitcast_fusion
  (103 shorter events, 4.8 us)
Async XLA Ops:
  0.0 3.7 %copy-start.10 = (bf16[3,1,2,2,512,8]{4,5,3,2,1,0:T(8,128)(2,1)S(1)}, bf16[3,1,2,2,512,8]{4,5,3,2,1,0:T(8,128)(2,1)}, u32[]{:S(2)}) copy-start(bf16[3,1,2,2,512,8]{4,5,3,2,1,0:T(8,128)(2,1)} %param.9) | copy-start | bytes 294916
  0.0 3.7 %copy-start.11 = (s32[1,1,512,1]{2,3,1,0:T(1,128)S(1)}, s32[1,1,512,1]{2,3,1,0:T(1,128)}, u32[]{:S(2)}) copy-start(s32[1,1,512,1]{2,3,1,0:T(1,128)} %param.10) | copy-start | bytes 6148
  0.0 4.4 %copy-start.13 = (bf16[2,512]{1,0:T(2,128)(2,1)S(1)}, bf16[2,512]{1,0:T(2,128)(2,1)}, u32[]{:S(2)}) copy-start(bf16[2,512]{1,0:T(2,128)(2,1)} %param.7) | copy-start | bytes 6148
  0.0 26.8 %collective-permute-start = (bf16[2,512,512]{2,1,0:T(8,128)(2,1)}, bf16[2,512,512]{2,1,0:T(8,128)(2,1)}, u32[]{:S(2)}, u32[]{:S(2)}) collective-permute-start(bf16[2,512,512]{2,1,0:T(8,128)(2,1)} %param.6), channel_id=1, source_target_pairs={{1,0},{2,1},{3,2},{4,3},{5,4},{6,5},{7,6},{8,7},{9,8},{10,9},{11,1... | collective-permute-start | bytes 3145736 | tf_op jit(solution)/shard_map/ppermute | solution.py:12
  9.0 1.6 %copy-start.12 = (s32[3,1,2,512]{3,2,1,0:T(2,128)S(1)}, s32[3,1,2,512]{3,2,1,0:T(2,128)}, u32[]{:S(2)}) copy-start(s32[3,1,2,512]{3,2,1,0:T(2,128)} %param.8) | copy-start | bytes 36868
  9.0 1.7 %copy-start.14 = (s32[1,1,512]{2,1,0:T(1,128)S(1)}, s32[1,1,512]{2,1,0:T(1,128)}, u32[]{:S(2)}) copy-start(s32[1,1,512]{2,1,0:T(1,128)} %param.11) | copy-start | bytes 6148
  29.4 3.6 %copy-start = (bf16[512,512]{1,0:T(8,128)(2,1)S(1)}, bf16[512,512]{1,0:T(8,128)(2,1)}, u32[]{:S(2)}) copy-start(bf16[512,512]{1,0:T(8,128)(2,1)} %get-tuple-element.201) | copy-start | bytes 1572868
  29.4 3.6 %copy-start.1 = (bf16[512,512]{1,0:T(8,128)(2,1)S(1)}, bf16[512,512]{1,0:T(8,128)(2,1)}, u32[]{:S(2)}) copy-start(bf16[512,512]{1,0:T(8,128)(2,1)} %get-tuple-element.202) | copy-start | bytes 1572868
  29.4 3.6 %copy-start.2 = (bf16[512,512]{1,0:T(8,128)(2,1)S(1)}, bf16[512,512]{1,0:T(8,128)(2,1)}, u32[]{:S(2)}) copy-start(bf16[512,512]{1,0:T(8,128)(2,1)} %get-tuple-element.223) | copy-start | bytes 1572868
  29.5 4.7 %collective-permute-start.1 = (bf16[1024,512]{1,0:T(8,128)(2,1)S(1)}, bf16[1024,512]{1,0:T(8,128)(2,1)S(1)}, u32[]{:S(2)}, u32[]{:S(2)}) collective-permute-start(bf16[1024,512]{1,0:T(8,128)(2,1)S(1)} %bitcast.126), channel_id=1, source_target_pairs={{0,16},{16,0},{32,48},{48,32},{64,80},{80,64},{96,112},{112,96},{1... | collective-permute-start | bytes 3145736 | tf_op jit(solution)/shard_map/ppermute | solution.py:16
  36.5 25.9 %collective-permute-start.5 = (bf16[2,2,512,8]{2,3,1,0:T(8,128)(2,1)S(1)}, bf16[2,2,512,8]{2,3,1,0:T(8,128)(2,1)S(1)}, u32[]{:S(2)}, u32[]{:S(2)}) collective-permute-start(bf16[2,2,512,8]{2,3,1,0:T(8,128)(2,1)S(1)} %slice_bitcast_fusion.4), channel_id=1, source_target_pairs={{0,64},{16,80},{32,96},{48,112},{64,0},{80,16},{96,32},{112,48},{1... | collective-permute-start | bytes 98312 | tf_op jit(solution)/shard_map/ppermute | solution.py:16
  40.4 22.0 %collective-permute-start.4 = (s32[1536]{0:T(1024)S(1)}, s32[1536]{0:T(1024)S(1)}, u32[]{:S(2)}, u32[]{:S(2)}) collective-permute-start(s32[1536]{0:T(1024)S(1)} %pad_add_fusion.2), channel_id=1, source_target_pairs={{0,64},{16,80},{32,96},{48,112},{64,0},{80,16},{96,32},{112,48},{1... | collective-permute-start | bytes 18440 | tf_op jit(solution)/shard_map/ppermute | solution.py:16
  40.4 25.6 %collective-permute-start.2 = (bf16[1024,512]{1,0:T(8,128)(2,1)}, bf16[1024,512]{1,0:T(8,128)(2,1)}, u32[]{:S(2)}, u32[]{:S(2)}) collective-permute-start(bf16[1024,512]{1,0:T(8,128)(2,1)} %add_convert_fusion.1), channel_id=1, source_target_pairs={{0,32},{16,48},{32,0},{48,16},{64,96},{80,112},{96,64},{112,80},{1... | collective-permute-start | bytes 3145736 | tf_op jit(solution)/shard_map/ppermute | solution.py:16
  45.3 24.2 %all-to-all-start = ((s32[128,1,8]{2,1,0:T(1,128)}), s32[128,1,8]{2,1,0:T(1,128)S(1)}, u32[]{:S(2)}, u32[]{:S(2)}) async-start(s32[128,1,8]{2,1,0:T(1,128)} %bitcast.27), calls=%async_computation | async-start | bytes 131072 | tf_op jit(solution)/shard_map/all_to_all | solution.py:92
  59.6 6.5 %copy-start.16 = (f32[1024,512]{1,0:T(8,128)S(1)}, f32[1024,512]{1,0:T(8,128)}, u32[]{:S(2)}) copy-start(f32[1024,512]{1,0:T(8,128)} %fusion.9) | copy-start | bytes 6291460
  69.5 5.7 %copy-start.6 = (bf16[512,512]{1,0:T(8,128)(2,1)S(1)}, bf16[512,512]{1,0:T(8,128)(2,1)}, u32[]{:S(2)}) copy-start(bf16[512,512]{1,0:T(8,128)(2,1)} %get-tuple-element.197) | copy-start | bytes 1572868
  69.5 5.7 %copy-start.7 = (bf16[512,512]{1,0:T(8,128)(2,1)S(1)}, bf16[512,512]{1,0:T(8,128)(2,1)}, u32[]{:S(2)}) copy-start(bf16[512,512]{1,0:T(8,128)(2,1)} %get-tuple-element.198) | copy-start | bytes 1572868
  69.5 5.7 %copy-start.8 = (bf16[512,512]{1,0:T(8,128)(2,1)S(1)}, bf16[512,512]{1,0:T(8,128)(2,1)}, u32[]{:S(2)}) copy-start(bf16[512,512]{1,0:T(8,128)(2,1)} %get-tuple-element.221) | copy-start | bytes 1572868
  69.5 5.7 %copy-start.9 = (bf16[1024,512]{1,0:T(8,128)(2,1)S(1)}, bf16[1024,512]{1,0:T(8,128)(2,1)}, u32[]{:S(2)}) copy-start(bf16[1024,512]{1,0:T(8,128)(2,1)} %add_convert_fusion) | copy-start | bytes 3145732
  70.8 13.8 %collective-permute-start.3 = (bf16[1024,256]{1,0:T(8,128)(2,1)S(1)}, bf16[1024,256]{1,0:T(8,128)(2,1)S(1)}, u32[]{:S(2)}, u32[]{:S(2)}) collective-permute-start(bf16[1024,256]{1,0:T(8,128)(2,1)S(1)} %constant_dynamic-slice_fusion), channel_id=1, source_target_pairs={{0,64},{16,80},{32,96},{48,112},{64,0},{80,16},{96,32},{112,48},{1... | collective-permute-start | bytes 1572872 | tf_op jit(solution)/shard_map/ppermute | solution.py:16
  84.6 0.8 copy-start.15
  84.6 1.2 copy-start.3
  84.6 1.4 %copy-start.4 = (bf16[512,512]{1,0:T(8,128)(2,1)S(1)}, bf16[512,512]{1,0:T(8,128)(2,1)}, u32[]{:S(2)}) copy-start(bf16[512,512]{1,0:T(8,128)(2,1)} %get-tuple-element.188) | copy-start | bytes 1572868
  84.6 1.5 %copy-start.5 = (bf16[512,512]{1,0:T(8,128)(2,1)S(1)}, bf16[512,512]{1,0:T(8,128)(2,1)}, u32[]{:S(2)}) copy-start(bf16[512,512]{1,0:T(8,128)(2,1)} %get-tuple-element.216) | copy-start | bytes 1572868
  91.7 42.4 %all-to-all-start.1 = ((bf16[128,16,512]{2,1,0:T(8,128)(2,1)}), bf16[128,16,512]{2,1,0:T(8,128)(2,1)S(1)}, u32[]{:S(2)}, u32[]{:S(2)}) async-start(bf16[128,16,512]{2,1,0:T(8,128)(2,1)} %pad_maximum_fusion.2), calls=%async_computation.1 | async-start | bytes 4194304 | tf_op jit(solution)/shard_map/all_to_all | solution.py:132

commit v20 on v18

--- a/solution.py
+++ b/solution.py
@@ -102,16 +102,16 @@
     keep_bit = (me_sub >> last) & 1
     kept = lax.dynamic_slice_in_dim(image, keep_bit * half, half, axis=1)
     sent = lax.dynamic_slice_in_dim(image, (1 - keep_bit) * half, half, axis=1)
-    old = {0: kept, bit: far(sent)}
     bands = {
         0: (own_offsets, own_weights),
         bit: (far_offsets, far_weights),
     }
     sends = []
+    built = {m: tuple(merge_matrix(bands[m][0][i], bands[m][1][i]) for i in range(2)) for m in (0, bit)}
+    built, kept = lax.optimization_barrier((built, kept))
+    old = {0: kept, bit: far(sent)}
     for m in (0, bit):
-        starts, kernel = bands[m]
-        mine = merge_matrix(starts[0], kernel[0])
-        theirs = merge_matrix(starts[1], kernel[1])
+        mine, theirs = built[m]
         merged = jnp.dot(mine, old[m], preferred_element_type=jnp.float32)
         if m == 0:
             labels, merged = lax.optimization_barrier((labels, merged))

time: 136 us -> 146 us (1.074)
  other arithmetic: 21.3 us -> 27.2 us
  local copies, waits for them, and re-layouts: 14.7 us -> 18.7 us
  waiting for transfers between devices: 48.8 us -> 44.8 us
  matrix products: 19.9 us -> 23 us
    concatenate x0 -> x4, other arithmetic: none -> 3.91 us  [merge_matrix(): return jnp.concatenate([upper, lower], axis=0)]
    ppermute x1, waiting for transfers between devices: 3.91 us -> 0.01 us  [shifted(): lax.ppermute(value, axis, [(source, source + steps) for source in range(f...]
    reshape x2, local copies, waits for them, and re-layouts: 0.42 us -> 2.26 us  [on_device(): piece.reshape(2, p_dev, half).transpose(1, 0, 2).reshape(p_dev, 2 * half)]
  transfers between devices with their start and end apart: 8 -> 8, of which waited for: 4 -> 2; matrix products, arithmetic and copies ran while one was open for 34% -> 41% of each run, Pallas kernels for 0% -> 0%
where the time goes in v20:
time: 146 us
  waiting for transfers between devices  44.8 us (31%)
  starting transfers between devices  31.5 us (22%)
  other arithmetic  27.2 us (19%)
  matrix products  23 us (16%)
  local copies, waits for them, and re-layouts  18.7 us (13%)
    all_to_all x1, waiting for transfers between devices, on_device(): lax.all_to_all(payload, ('sub', 'rng'), split_axis=0, concat_axis=0, tile...  27.9 us
    ppermute x5, waiting for transfers between devices, from_partner(): lax.ppermute(value, axis, [(i, i ^ 1 << apart) for i in range(lax.axis_si...  16.9 us
    neg x8, other arithmetic, merge_matrix(): upper = jnp.concatenate([g_real, -g_imag], axis=1)  14.8 us
    all_to_all x1, starting transfers between devices, on_device(): lax.all_to_all(labels, ('sub', 'rng'), split_axis=0, concat_axis=0, tiled...  10.6 us
    all_to_all x1, starting transfers between devices, on_device(): lax.all_to_all(payload, ('sub', 'rng'), split_axis=0, concat_axis=0, tile...  9.76 us
    ppermute x5, starting transfers between devices, from_partner(): lax.ppermute(value, axis, [(i, i ^ 1 << apart) for i in range(lax.axis_si...  9.66 us
    dot_general x2, matrix products, on_device(): jnp.dot(theirs, old[m ^ bit], preferred_element_type=jnp.float32)  5.12 us
    dot_general x2, matrix products, on_device(): merged = jnp.dot(mine, old[m], preferred_element_type=jnp.float32)  4.25 us
  transfers between devices with their start and end apart: 8, of which 2 were waited for; matrix products, arithmetic and copies ran while one was open for 41% of the time, Pallas kernels for 0%

profile of v20, /device:TPU:1, one launch (start us, length us, event | category | flops | bytes accessed | tf_op | source)
XLA Modules:
  0.0 145.7 jit_solution(8810202141171370934)
XLA Ops:
  0.0 1.4 collective-permute-start
  1.4 2.3 %slice_bitcast_fusion.3 = (bf16[512,512]{1,0:T(8,128)(2,1)}, bf16[512,512]{1,0:T(8,128)(2,1)}) fusion(bf16[2,512,512]{2,1,0:T(8,128)(2,1)} %param.6), kind=kLoop, calls=%fused_computation.295 | loop fusion | bytes 2097152 | tf_op jit(solution)/shard_map/squeeze | solution.py:66
  5.0 1.3 tile.21
  7.0 1.1 bitcast_negate_fusion
  8.2 1.3 tile.9
  9.5 1.0 slice.1002
  10.6 1.6 %reshape.177 = bf16[512,1024]{1,0:T(8,128)(2,1)S(1)} reshape(bf16[524288]{0:T(1024)(128)(2,1)} %slice.1002) | data formatting | bytes 2097152 | tf_op jit(solution)/shard_map/reshape | solution.py:25
  12.6 0.9 fusion.268
  15.2 1.1 slice_reduce_fusion.127
  16.6 1.5 %fusion.63 = (bf16[512,1024]{0,1:T(8,128)(2,1)}, bf16[512,1024]{0,1:T(8,128)(2,1)}) fusion(bf16[1024,512]{0,1:T(8,128)(2,1)S(1)} %bitcast.128, bf16[1024,512]{0,1:T(8,128)(2,1)S(1)} %copy-done, bf16[1024,512]{0,1:T(8,128)(2,1)S(1)} %bitcast.126), kind=kLoop, calls=%fused_computation.77 | loop fusion | flops 4194304 | bytes 5242880 | tf_op jit(solution)/shard_map/concatenate | solution.py:28
  18.1 2.7 %fusion.295 = (bf16[512,512]{1,0:T(8,128)(2,1)}, bf16[512,512]{1,0:T(8,128)(2,1)}, bf16[512,512]{1,0:T(8,128)(2,1)}) fusion(bf16[512]{0:T(512)(128)(2,1)S(1)} %get-tuple-element.148, bf16[512]{0:T(512)(128)(2,1)S(1)} %get-tuple-element.149, bf16[512]{0:T(512)(128)(2,1)S(1)} %get-tuple-element.150, bf16[512]{0:T(512)(128)(2,1)S(1)} %get-tuple-element.151, ...), kind=kLoop, calls=%fused_computation.508 | loop fusion | flops 7340032 | bytes 1591296 | tf_op jit(solution)/shard_map/neg | solution.py:43
  21.6 3.1 %fusion.17 = f32[512,1024]{1,0:T(8,128)S(1)} fusion(bf16[512,1024]{0,1:T(8,128)(2,1)} %get-tuple-element.174, bf16[512,1024]{0,1:T(8,128)(2,1)} %get-tuple-element.173, bf16[512,512]{1,0:T(8,128)(2,1)} %get-tuple-element.172, bf16[512,512]{1,0:T(8,128)(2,1)} %get-tuple-element.171), kind=kOutput, calls=%fused_computation.21 | convolution fusion | flops 1080033280 | bytes 5242880 | tf_op jit(solution)/shard_map/dot_general | solution.py:65
  24.8 1.7 %fusion.296 = (bf16[512,512]{1,0:T(8,128)(2,1)S(1)}, bf16[512,512]{1,0:T(8,128)(2,1)S(1)}, bf16[512,512]{1,0:T(8,128)(2,1)S(1)}) fusion(bf16[512]{0:T(512)(128)(2,1)S(1)} %get-tuple-element.132, bf16[512]{0:T(512)(128)(2,1)S(1)} %get-tuple-element.133, bf16[512]{0:T(512)(128)(2,1)S(1)} %get-tuple-element.134, bf16[512]{0:T(512)(128)(2,1)S(1)} %get-tuple-element.135, ...), kind=kLoop, calls=%fused_computation.509 | loop fusion | flops 7340032 | bytes 1591296 | tf_op jit(solution)/shard_map/neg | solution.py:43
  26.6 1.7 %fusion.300 = (bf16[512,512]{1,0:T(8,128)(2,1)S(1)}, bf16[512,512]{1,0:T(8,128)(2,1)S(1)}, bf16[512,512]{1,0:T(8,128)(2,1)S(1)}) fusion(bf16[512]{0:T(512)(128)(2,1)S(1)} %get-tuple-element.52, bf16[512]{0:T(512)(128)(2,1)S(1)} %get-tuple-element.53, bf16[512]{0:T(512)(128)(2,1)S(1)} %get-tuple-element.54, bf16[512]{0:T(512)(128)(2,1)S(1)} %get-tuple-element.55, ...), kind=kLoop, calls=%fused_computation.513 | loop fusion | flops 7340032 | bytes 1591296 | tf_op jit(solution)/shard_map/neg | solution.py:43
  28.3 1.3 slice_bitcast_fusion.1
  29.6 1.3 add_convert_fusion.2
  31.0 1.4 collective-permute-start.1
  33.1 1.7 %fusion.301 = (bf16[512,512]{1,0:T(8,128)(2,1)S(1)}, bf16[512,512]{1,0:T(8,128)(2,1)S(1)}, bf16[512,512]{1,0:T(8,128)(2,1)S(1)}) fusion(bf16[512]{0:T(512)(128)(2,1)S(1)} %get-tuple-element.36, bf16[512]{0:T(512)(128)(2,1)S(1)} %get-tuple-element.37, bf16[512]{0:T(512)(128)(2,1)S(1)} %get-tuple-element.38, bf16[512]{0:T(512)(128)(2,1)S(1)} %get-tuple-element.39, ...), kind=kLoop, calls=%fused_computation.514 | loop fusion | flops 7340032 | bytes 1591296 | tf_op jit(solution)/shard_map/neg | solution.py:43
  34.9 1.2 fusion.9
  36.1 1.2 add_convert_fusion.1
  37.4 3.8 %collective-permute-start.3 = (bf16[2,2,512,8]{2,3,1,0:T(8,128)(2,1)S(1)}, bf16[2,2,512,8]{2,3,1,0:T(8,128)(2,1)S(1)}, u32[]{:S(2)}, u32[]{:S(2)}) collective-permute-start(bf16[2,2,512,8]{2,3,1,0:T(8,128)(2,1)S(1)} %slice_bitcast_fusion.4), channel_id=1, source_target_pairs={{0,64},{16,80},{32,96},{48,112},{64,0},{80,16},{96,32},{112,48},{1... | collective-permute-start | bytes 98312 | tf_op jit(solution)/shard_map/ppermute | solution.py:16
  41.2 0.7 collective-permute-start.4
  41.9 1.1 collective-permute-start.2
  43.3 1.2 fusion.29
  44.6 1.7 %fusion.297 = (bf16[512,512]{1,0:T(8,128)(2,1)S(1)}, bf16[512,512]{1,0:T(8,128)(2,1)S(1)}, bf16[512,512]{1,0:T(8,128)(2,1)S(1)}) fusion(bf16[512]{0:T(512)(128)(2,1)S(1)} %get-tuple-element.100, bf16[512]{0:T(512)(128)(2,1)S(1)} %get-tuple-element.101, bf16[512]{0:T(512)(128)(2,1)S(1)} %get-tuple-element.102, bf16[512]{0:T(512)(128)(2,1)S(1)} %get-tuple-element.103, ...), kind=kLoop, calls=%fused_computation.510 | loop fusion | flops 7340032 | bytes 1591296 | tf_op jit(solution)/shard_map/neg | solution.py:43
  46.6 1.7 %fusion.294 = (bf16[512,512]{1,0:T(8,128)(2,1)S(1)}, bf16[512,512]{1,0:T(8,128)(2,1)S(1)}, bf16[512,512]{1,0:T(8,128)(2,1)S(1)}) fusion(bf16[512]{0:T(512)(128)(2,1)S(1)} %get-tuple-element.116, bf16[512]{0:T(512)(128)(2,1)S(1)} %get-tuple-element.117, bf16[512]{0:T(512)(128)(2,1)S(1)} %get-tuple-element.118, bf16[512]{0:T(512)(128)(2,1)S(1)} %get-tuple-element.119, ...), kind=kLoop, calls=%fused_computation.507 | loop fusion | flops 7340032 | bytes 1591296 | tf_op jit(solution)/shard_map/neg | solution.py:43
  48.7 16.9 %collective-permute-done.2 = s32[1536]{0:T(1024)S(1)} collective-permute-done((s32[1536]{0:T(1024)S(1)}, s32[1536]{0:T(1024)S(1)}, u32[]{:S(2)}, u32[]{:S(2)}) %collective-permute-start.2) | collective-permute-done | bytes 6176 | tf_op jit(solution)/shard_map/ppermute | solution.py:16
  65.7 1.7 %fusion.299 = (bf16[512,512]{1,0:T(8,128)(2,1)S(1)}, bf16[512,512]{1,0:T(8,128)(2,1)S(1)}, bf16[512,512]{1,0:T(8,128)(2,1)S(1)}) fusion(bf16[512]{0:T(512)(128)(2,1)S(1)} %get-tuple-element.68, bf16[512]{0:T(512)(128)(2,1)S(1)} %get-tuple-element.69, bf16[512]{0:T(512)(128)(2,1)S(1)} %get-tuple-element.70, bf16[512]{0:T(512)(128)(2,1)S(1)} %get-tuple-element.71, ...), kind=kLoop, calls=%fused_computation.512 | loop fusion | flops 7340032 | bytes 1591296 | tf_op jit(solution)/shard_map/neg | solution.py:43
  67.5 1.6 %maximum_maximum_fusion.3 = bf16[1024,1024]{1,0:T(8,128)(2,1)} fusion(bf16[512,512]{1,0:T(8,128)(2,1)S(1)} %get-tuple-element.226, bf16[512,512]{1,0:T(8,128)(2,1)S(1)} %get-tuple-element.200, bf16[512,512]{1,0:T(8,128)(2,1)S(1)} %get-tuple-element.199), kind=kLoop, calls=%fused_computation.36 | loop fusion | flops 8388608 | bytes 3670016 | tf_op jit(solution)/shard_map/concatenate | solution.py:45
  69.2 1.7 %fusion.298 = (bf16[512,512]{1,0:T(8,128)(2,1)S(1)}, bf16[512,512]{1,0:T(8,128)(2,1)S(1)}, bf16[512,512]{1,0:T(8,128)(2,1)S(1)}) fusion(bf16[512]{0:T(512)(128)(2,1)S(1)} %get-tuple-element.84, bf16[512]{0:T(512)(128)(2,1)S(1)} %get-tuple-element.85, bf16[512]{0:T(512)(128)(2,1)S(1)} %get-tuple-element.86, bf16[512]{0:T(512)(128)(2,1)S(1)} %get-tuple-element.87, ...), kind=kLoop, calls=%fused_computation.511 | loop fusion | flops 7340032 | bytes 1591296 | tf_op jit(solution)/shard_map/neg | solution.py:43
  70.9 1.7 %maximum_maximum_fusion.2 = bf16[1024,1024]{1,0:T(8,128)(2,1)} fusion(bf16[512,512]{1,0:T(8,128)(2,1)S(1)} %get-tuple-element.227, bf16[512,512]{1,0:T(8,128)(2,1)S(1)} %get-tuple-element.202, bf16[512,512]{1,0:T(8,128)(2,1)S(1)} %get-tuple-element.201), kind=kLoop, calls=%fused_computation.35 | loop fusion | flops 8388608 | bytes 3670016 | tf_op jit(solution)/shard_map/concatenate | solution.py:45
  72.5 1.2 add_convert_fusion
  73.9 2.5 %collective-permute-start.5 = (bf16[1024,256]{1,0:T(8,128)(2,1)S(1)}, bf16[1024,256]{1,0:T(8,128)(2,1)}, u32[]{:S(2)}, u32[]{:S(2)}) collective-permute-start(bf16[1024,256]{1,0:T(8,128)(2,1)S(1)} %get-tuple-element.167), channel_id=1, source_target_pairs={{0,64},{16,80},{32,96},{48,112},{64,0},{80,16},{96,32},{112,48},{1... | collective-permute-start | bytes 1572872 | tf_op jit(solution)/shard_map/ppermute | solution.py:16
  76.4 1.7 %fusion.306 = f32[1024,256]{1,0:T(8,128)} fusion(bf16[1024,1024]{1,0:T(8,128)(2,1)S(1)} %maximum_maximum_fusion, bf16[1024,256]{1,0:T(8,128)(2,1)S(1)} %get-tuple-element.21), kind=kOutput, calls=%fused_computation.519 | convolution fusion | flops 536870912 | bytes 3670016 | tf_op jit(solution)/shard_map/dot_general | solution.py:115
  78.1 10.6 %all-to-all-start = ((s32[128,1,8]{2,1,0:T(1,128)}), s32[128,1,8]{2,1,0:T(1,128)S(1)}, u32[]{:S(2)}, u32[]{:S(2)}) async-start(s32[128,1,8]{2,1,0:T(1,128)} %bitcast.40), calls=%async_computation | async-start | bytes 131072 | tf_op jit(solution)/shard_map/all_to_all | solution.py:118
  88.7 3.4 %fusion.307 = f32[1024,256]{1,0:T(8,128)} fusion(bf16[1024,1024]{1,0:T(8,128)(2,1)} %maximum_maximum_fusion.3, bf16[1024,256]{1,0:T(8,128)(2,1)S(1)} %get-tuple-element.21), kind=kOutput, calls=%fused_computation.520 | convolution fusion | flops 536870912 | bytes 3670016 | tf_op jit(solution)/shard_map/dot_general | solution.py:119
  92.1 1.8 %fusion.61 = bf16[1024,256]{1,0:T(8,128)(2,1)S(1)} fusion(f32[1024,256]{1,0:T(8,128)S(1)} %copy-done.14, bf16[1024,1024]{1,0:T(8,128)(2,1)S(1)} %maximum_maximum_fusion.1, bf16[1024,256]{1,0:T(8,128)(2,1)} %collective-permute-done.5), kind=kOutput, calls=%fused_computation.75 | convolution fusion | flops 537395200 | bytes 4194304 | tf_op jit(solution)/shard_map/dot_general | solution.py:119
  93.9 1.0 copy.46
  94.9 1.9 %fusion.57 = bf16[128,8,512]{2,1,0:T(8,128)(2,1)S(1)} fusion(bf16[512,512]{0,1:T(8,128)(2,1)} %bitcast.138, s32[512]{0:T(512)S(1)} %multiply_add_fusion), kind=kOutput, calls=%fused_computation.69 | convolution fusion | flops 537919488 | bytes 1574912 | tf_op jit(solution)/shard_map/dot_general | solution.py:122
  96.8 2.6 %fusion.62 = bf16[1024,256]{1,0:T(8,128)(2,1)} fusion(f32[1024,256]{1,0:T(8,128)S(1)} %copy-done.13, bf16[1024,1024]{1,0:T(8,128)(2,1)S(1)} %copy-done.1, bf16[1024,256]{1,0:T(8,128)(2,1)} %collective-permute-done.5), kind=kOutput, calls=%fused_computation.76 | convolution fusion | flops 537395200 | bytes 4194304 | tf_op jit(solution)/shard_map/dot_general | solution.py:115
  99.3 1.3 copy.47
  100.6 0.7 fusion.58
  101.3 1.7 %pad_maximum_fusion.2 = bf16[128,16,512]{2,1,0:T(8,128)(2,1)} fusion(bf16[128,8,512]{2,1,0:T(8,128)(2,1)S(1)} %fusion.58, bf16[128,8,512]{2,1,0:T(8,128)(2,1)S(1)} %fusion.57), kind=kLoop, calls=%fused_computation.53 | loop fusion | flops 4194304 | bytes 4194304 | tf_op jit(solution)/shard_map/concatenate | solution.py:129
  103.0 9.8 %all-to-all-start.1 = ((bf16[128,16,512]{2,1,0:T(8,128)(2,1)}), bf16[128,16,512]{2,1,0:T(8,128)(2,1)S(1)}, u32[]{:S(2)}, u32[]{:S(2)}) async-start(bf16[128,16,512]{2,1,0:T(8,128)(2,1)} %pad_maximum_fusion.2), calls=%async_computation.1 | async-start | bytes 4194304 | tf_op jit(solution)/shard_map/all_to_all | solution.py:130
  114.5 27.9 %all-to-all-done.1 = bf16[128,16,512]{2,1,0:T(8,128)(2,1)S(1)} async-done(((bf16[128,16,512]{2,1,0:T(8,128)(2,1)}), bf16[128,16,512]{2,1,0:T(8,128)(2,1)S(1)}, u32[]{:S(2)}, u32[]{:S(2)}) %all-to-all-start.1) | async-done | bytes 2097184 | tf_op jit(solution)/shard_map/all_to_all | solution.py:130
  142.7 0.8 fusion.60
  143.7 0.8 fusion.59
  144.7 1.1 maximum_bitcast_fusion
  (103 shorter events, 9.4 us)
Async XLA Ops:
  0.0 3.7 %copy-start.5 = (bf16[3,1,2,2,512,8]{4,5,3,2,1,0:T(8,128)(2,1)S(1)}, bf16[3,1,2,2,512,8]{4,5,3,2,1,0:T(8,128)(2,1)}, u32[]{:S(2)}) copy-start(bf16[3,1,2,2,512,8]{4,5,3,2,1,0:T(8,128)(2,1)} %param.9) | copy-start | bytes 294916
  0.0 4.3 %copy-start.7 = (s32[3,1,2,512]{3,2,1,0:T(2,128)S(1)}, s32[3,1,2,512]{3,2,1,0:T(2,128)}, u32[]{:S(2)}) copy-start(s32[3,1,2,512]{3,2,1,0:T(2,128)} %param.8) | copy-start | bytes 36868
  0.0 4.9 %copy-start.12 = (bf16[2,512]{1,0:T(2,128)(2,1)S(1)}, bf16[2,512]{1,0:T(2,128)(2,1)}, u32[]{:S(2)}) copy-start(bf16[2,512]{1,0:T(2,128)(2,1)} %param.7) | copy-start | bytes 6148
  0.0 28.3 %collective-permute-start = (bf16[2,512,512]{2,1,0:T(8,128)(2,1)}, bf16[2,512,512]{2,1,0:T(8,128)(2,1)}, u32[]{:S(2)}, u32[]{:S(2)}) collective-permute-start(bf16[2,512,512]{2,1,0:T(8,128)(2,1)} %param.6), channel_id=1, source_target_pairs={{1,0},{2,1},{3,2},{4,3},{5,4},{6,5},{7,6},{8,7},{9,8},{10,9},{11,1... | collective-permute-start | bytes 3145736 | tf_op jit(solution)/shard_map/ppermute | solution.py:12
  9.5 2.7 %copy-start.6 = (s32[1,1,512,1]{2,3,1,0:T(1,128)S(1)}, s32[1,1,512,1]{2,3,1,0:T(1,128)}, u32[]{:S(2)}) copy-start(s32[1,1,512,1]{2,3,1,0:T(1,128)} %param.10) | copy-start | bytes 6148
  10.6 6.0 %copy-start = (bf16[1024,512]{0,1:T(8,128)(2,1)S(1)}, bf16[1024,512]{0,1:T(8,128)(2,1)}, u32[]{:S(2)}) copy-start(bf16[1024,512]{0,1:T(8,128)(2,1)} %bitcast_negate_fusion) | copy-start | bytes 3145732
  16.6 1.5 %copy-start.11 = (s32[1,1,1,512]{3,2,1,0:T(1,128)S(1)}, s32[1,1,1,512]{3,2,1,0:T(1,128)}, u32[]{:S(2)}) copy-start(s32[1,1,1,512]{3,2,1,0:T(1,128)} %get-tuple-element.193) | copy-start | bytes 6148
  21.6 3.2 %copy-start.10 = (s32[1,1,1,512]{3,2,1,0:T(1,128)S(1)}, s32[1,1,1,512]{3,2,1,0:T(1,128)}, u32[]{:S(2)}) copy-start(s32[1,1,1,512]{3,2,1,0:T(1,128)} %get-tuple-element.192) | copy-start | bytes 6148
  21.6 4.9 %copy-start.9 = (s32[1,1,1,512]{3,2,1,0:T(1,128)S(1)}, s32[1,1,1,512]{3,2,1,0:T(1,128)}, u32[]{:S(2)}) copy-start(s32[1,1,1,512]{3,2,1,0:T(1,128)} %get-tuple-element.194) | copy-start | bytes 6148
  30.9 2.3 %copy-start.8 = (s32[1,1,1,512]{3,2,1,0:T(1,128)S(1)}, s32[1,1,1,512]{3,2,1,0:T(1,128)}, u32[]{:S(2)}) copy-start(s32[1,1,1,512]{3,2,1,0:T(1,128)} %get-tuple-element.191) | copy-start | bytes 6148
  30.9 4.0 %copy-start.2 = (bf16[512,512]{1,0:T(8,128)(2,1)S(1)}, bf16[512,512]{1,0:T(8,128)(2,1)}, u32[]{:S(2)}) copy-start(bf16[512,512]{1,0:T(8,128)(2,1)} %get-tuple-element.209) | copy-start | bytes 1572868
  30.9 4.0 %copy-start.3 = (bf16[512,512]{1,0:T(8,128)(2,1)S(1)}, bf16[512,512]{1,0:T(8,128)(2,1)}, u32[]{:S(2)}) copy-start(bf16[512,512]{1,0:T(8,128)(2,1)} %get-tuple-element.210) | copy-start | bytes 1572868
  30.9 4.0 %copy-start.4 = (bf16[512,512]{1,0:T(8,128)(2,1)S(1)}, bf16[512,512]{1,0:T(8,128)(2,1)}, u32[]{:S(2)}) copy-start(bf16[512,512]{1,0:T(8,128)(2,1)} %get-tuple-element.231) | copy-start | bytes 1572868
  31.0 5.1 %collective-permute-start.1 = (bf16[1024,512]{1,0:T(8,128)(2,1)S(1)}, bf16[1024,512]{1,0:T(8,128)(2,1)S(1)}, u32[]{:S(2)}, u32[]{:S(2)}) collective-permute-start(bf16[1024,512]{1,0:T(8,128)(2,1)S(1)} %bitcast.130), channel_id=1, source_target_pairs={{0,16},{16,0},{32,48},{48,32},{64,80},{80,64},{96,112},{112,96},{1... | collective-permute-start | bytes 3145736 | tf_op jit(solution)/shard_map/ppermute | solution.py:16
  37.4 28.2 %collective-permute-start.3 = (bf16[2,2,512,8]{2,3,1,0:T(8,128)(2,1)S(1)}, bf16[2,2,512,8]{2,3,1,0:T(8,128)(2,1)S(1)}, u32[]{:S(2)}, u32[]{:S(2)}) collective-permute-start(bf16[2,2,512,8]{2,3,1,0:T(8,128)(2,1)S(1)} %slice_bitcast_fusion.4), channel_id=1, source_target_pairs={{0,64},{16,80},{32,96},{48,112},{64,0},{80,16},{96,32},{112,48},{1... | collective-permute-start | bytes 98312 | tf_op jit(solution)/shard_map/ppermute | solution.py:16
  41.2 31.4 %collective-permute-start.4 = (bf16[1024,512]{1,0:T(8,128)(2,1)S(1)}, bf16[1024,512]{1,0:T(8,128)(2,1)S(1)}, u32[]{:S(2)}, u32[]{:S(2)}) collective-permute-start(bf16[1024,512]{1,0:T(8,128)(2,1)S(1)} %add_convert_fusion.1), channel_id=1, source_target_pairs={{0,32},{16,48},{32,0},{48,16},{64,96},{80,112},{96,64},{112,80},{1... | collective-permute-start | bytes 3145736 | tf_op jit(solution)/shard_map/ppermute | solution.py:16
  41.9 23.6 %collective-permute-start.2 = (s32[1536]{0:T(1024)S(1)}, s32[1536]{0:T(1024)S(1)}, u32[]{:S(2)}, u32[]{:S(2)}) collective-permute-start(s32[1536]{0:T(1024)S(1)} %pad_add_fusion.1), channel_id=1, source_target_pairs={{0,64},{16,80},{32,96},{48,112},{64,0},{80,16},{96,32},{112,48},{1... | collective-permute-start | bytes 18440 | tf_op jit(solution)/shard_map/ppermute | solution.py:16
  73.9 18.2 %collective-permute-start.5 = (bf16[1024,256]{1,0:T(8,128)(2,1)S(1)}, bf16[1024,256]{1,0:T(8,128)(2,1)}, u32[]{:S(2)}, u32[]{:S(2)}) collective-permute-start(bf16[1024,256]{1,0:T(8,128)(2,1)S(1)} %get-tuple-element.167), channel_id=1, source_target_pairs={{0,64},{16,80},{32,96},{48,112},{64,0},{80,16},{96,32},{112,48},{1... | collective-permute-start | bytes 1572872 | tf_op jit(solution)/shard_map/ppermute | solution.py:16
  78.1 24.9 %all-to-all-start = ((s32[128,1,8]{2,1,0:T(1,128)}), s32[128,1,8]{2,1,0:T(1,128)S(1)}, u32[]{:S(2)}, u32[]{:S(2)}) async-start(s32[128,1,8]{2,1,0:T(1,128)} %bitcast.40), calls=%async_computation | async-start | bytes 131072 | tf_op jit(solution)/shard_map/all_to_all | solution.py:118
  88.7 3.4 %copy-start.14 = (f32[1024,256]{1,0:T(8,128)S(1)}, f32[1024,256]{1,0:T(8,128)}, u32[]{:S(2)}) copy-start(f32[1024,256]{1,0:T(8,128)} %fusion.306) | copy-start | bytes 3145732
  93.9 2.9 %copy-start.1 = (bf16[1024,1024]{1,0:T(8,128)(2,1)S(1)}, bf16[1024,1024]{1,0:T(8,128)(2,1)}, u32[]{:S(2)}) copy-start(bf16[1024,1024]{1,0:T(8,128)(2,1)} %maximum_maximum_fusion.2) | copy-start | bytes 6291460
  94.9 1.9 %copy-start.13 = (f32[1024,256]{1,0:T(8,128)S(1)}, f32[1024,256]{1,0:T(8,128)}, u32[]{:S(2)}) copy-start(f32[1024,256]{1,0:T(8,128)} %fusion.307) | copy-start | bytes 3145732
  103.0 39.5 %all-to-all-start.1 = ((bf16[128,16,512]{2,1,0:T(8,128)(2,1)}), bf16[128,16,512]{2,1,0:T(8,128)(2,1)S(1)}, u32[]{:S(2)}, u32[]{:S(2)}) async-start(bf16[128,16,512]{2,1,0:T(8,128)(2,1)} %pad_maximum_fusion.2), calls=%async_computation.1 | async-start | bytes 4194304 | tf_op jit(solution)/shard_map/all_to_all | solution.py:130
